TPU v7x, 128 devices: a whole 4x4x4 slice. The times are simulated.
128 devices in a mesh: space: 8 (over z_hi, x), blk: 16 (over y, z_lo, core).
Axes of the slice: x: 4, y: 4, z: 4 (z_hi: 2, z_lo: 2; z = z_hi * 2 + z_lo), core: 2. Of those that a mesh axis runs over, the one named last changes fastest.
Arguments:
- density: bfloat16 [12288, 128, 128], P(('space', 'blk')), may hold values from -6 to 6
- bra_table: bfloat16 [12288, 128, 256], P(('space', 'blk')), may hold values from -0.5 to 0.5
- ket_table: bfloat16 [12288, 128, 256], P(('space', 'blk')), may hold values from -0.5 to 0.5
- box_of_block: int32 [12288], P(('space', 'blk')), may hold values from 0 to 127
- leaf_src: int32 [1024, 27], P(('space', 'blk')), may hold values from 0 to 383
- leaf_type: int32 [1024, 27], P(('space', 'blk')), may hold values from 0 to 15
- coarse_src: int32 [128, 27], P(('space', 'blk')), may hold values from 0 to 127
- coarse_type: int32 [128, 27], P(('space', 'blk')), may hold values from 0 to 15
- translation: float32 [16, 256, 256], replicated, may hold values from -0.375 to 0.375
- upward_translation_table: float32 [8, 256, 256], replicated, may hold values from -0.375 to 0.375
Outputs:
- coulomb: bfloat16 [12288, 128, 128], P(('space', 'blk'))
- box_locals: float32 [1024, 256], P(('space', 'blk'))
All inputs are finite; a program needn't handle non-finite values.
Results may differ from a plain program's by a relative error of at most 0.0049.
Values sent between devices are 32-bit elements; how exact they have to be, the bound alone decides.
No kernel may reach another device: no remote copies, remote signals or barrier semaphores. Data moves between devices by JAX's collectives and lax.ppermute only.
A program may use at most 128 MiB of HBM per device.

v0:
```python
import jax
import jax.numpy as jnp
from jax import lax
from jax.sharding import PartitionSpec as P


def padded(block, sides, width):
    for axis, dim in sides:
        count = lax.axis_size(axis)
        forward = [(i, i + 1) for i in range(count - 1)]
        backward = [(target, source) for source, target in forward]
        low = lax.ppermute(
            lax.slice_in_dim(block, block.shape[dim] - width, None, axis=dim), axis, forward
        )
        high = lax.ppermute(lax.slice_in_dim(block, 0, width, axis=dim), axis, backward)
        block = jnp.concatenate([low, block, high], axis=dim)
    return block


def shards(
    density,
    bra_table,
    ket_table,
    box_of_block,
    leaf_src,
    leaf_type,
    coarse_src,
    coarse_type,
    translation,
    upward_translation_table,
):
    top_level_index = lax.Precision.HIGHEST
    n_blk = lax.axis_size("blk")
    box_dom = 8 * n_blk
    n_types = translation.shape[0]
    inner = jnp.einsum("bmn,bmk->bnk", density, bra_table, preferred_element_type=jnp.float32)
    moments = jnp.sum(inner * ket_table.astype(jnp.float32), axis=1)
    box_hot = (box_of_block[:, None] == jnp.arange(box_dom, dtype=jnp.int32)[None, :]).astype(
        jnp.float32
    )
    partial_moments = lax.dot_general(
        box_hot, moments, (((0,), (0,)), ((), ())), precision=top_level_index
    )
    held_boxes = lax.psum_scatter(partial_moments, "blk", scatter_dimension=0, tiled=True)
    domain = lax.all_gather(held_boxes, "blk", axis=0, tiled=True)
    window = padded(domain, (("space", 0),), box_dom)
    self_parent_index = jnp.einsum(
        "oe,ode->d", held_boxes, upward_translation_table, precision=top_level_index
    )[None, :]
    all_parents = lax.all_gather(self_parent_index, ("space", "blk"), axis=0, tiled=True)
    src_hot = (leaf_src[..., None] == jnp.arange(3 * box_dom, dtype=jnp.int32)).astype(jnp.float32)
    type_hot = (leaf_type[..., None] == jnp.arange(n_types, dtype=jnp.int32)).astype(jnp.float32)
    counts = jnp.einsum("blt,blj->btj", type_hot, src_hot, precision=top_level_index)
    gathered = jnp.einsum("btj,jk->btk", counts, window, precision=top_level_index)
    leaf_far = jnp.einsum("btk,tlk->bl", gathered, translation, precision=top_level_index)
    n_parents = all_parents.shape[0]
    csrc_hot = (coarse_src[..., None] == jnp.arange(n_parents, dtype=jnp.int32)).astype(jnp.float32)
    ctype_hot = (coarse_type[..., None] == jnp.arange(n_types, dtype=jnp.int32)).astype(jnp.float32)
    ccounts = jnp.einsum("pet,peq->ptq", ctype_hot, csrc_hot, precision=top_level_index)
    cgathered = jnp.einsum("ptq,qk->ptk", ccounts, all_parents, precision=top_level_index)
    parent_local_expansion = jnp.einsum(
        "ptk,tlk->pl", cgathered, translation, precision=top_level_index
    )
    downward_sent = jnp.einsum(
        "d,uds->us", parent_local_expansion[0], upward_translation_table, precision=top_level_index
    )
    box_locals = leaf_far + downward_sent
    domain_local = lax.all_gather(box_locals, "blk", axis=0, tiled=True)
    block_locals = jnp.dot(box_hot, domain_local, precision=top_level_index)
    scaled = (bra_table.astype(jnp.float32) * block_locals[:, None, :]).astype(jnp.bfloat16)
    coulomb = jnp.einsum(
        "bmk,bnk->bmn", scaled, ket_table, preferred_element_type=jnp.float32
    ).astype(jnp.bfloat16)
    return (coulomb, box_locals)


def solution(mesh):
    placed = (
        P(("space", "blk"), None, None),
        P(("space", "blk"), None, None),
        P(("space", "blk"), None, None),
        P(("space", "blk")),
        P(("space", "blk"), None),
        P(("space", "blk"), None),
        P(("space", "blk"), None),
        P(("space", "blk"), None),
        P(),
        P(),
    )
    return jax.shard_map(
        shards,
        mesh=mesh,
        in_specs=placed,
        out_specs=(P(("space", "blk"), None, None), P(("space", "blk"), None)),
        check_vma=False,
    )
```

profile of v0, /device:TPU:0, one launch (start us, length us, event | category | flops | bytes accessed | tf_op | source)
XLA Modules:
  0.0 323.1 jit_solution(17972422086320185214)
XLA Ops:
  7.2 0.0 copy-start
  7.2 0.0 copy-start.6
  7.2 0.0 copy-start.8
  7.2 0.0 copy-start.7
  7.2 0.0 copy-start.5
  7.2 0.0 copy-start.4
  7.2 0.0 reduce-scatter.2.cloned.1.call-start
  7.3 1.8 copy-done
  9.1 6.8 %multiply_reduce_fusion = f32[96,256]{1,0:T(8,128)S(1)} fusion(bf16[96,128,256]{2,1,0:T(8,128)(2,1)} %param.12, bf16[96,128,128]{2,1,0:T(8,128)(2,1)S(1)} %copy-done, bf16[96,128,256]{2,1,0:T(8,128)(2,1)} %param.11), kind=kOutput, calls=%fused_computation.1 | convolution fusion | flops 814718976 | bytes 15826944 | tf_op jit(solution)/shard_map/bmn,bmk->bnk/dot_general | solution.py:36
  15.9 0.0 copy-done.6
  15.9 1.0 fusion.15
  16.9 0.0 reduce-scatter.2.cloned.1.call-update
  16.9 0.0 copy-done.8
  16.9 0.2 fusion.21
  17.1 0.0 copy-done.5
  17.1 0.2 fusion.9
  17.4 63.1 %reduce-scatter.2.cloned.1.call-done = f32[8,256]{1,0:T(8,128)} async-done(((f32[128,256]{1,0:T(8,128)}), f32[8,256]{1,0:T(8,128)}) %reduce-scatter.2.cloned.1.call-update) | async-done | bytes 8208 | tf_op jit(solution)/shard_map/reduce_scatter | solution.py:44
  80.4 16.7 %all_gather.9 = f32[128,256]{1,0:T(8,128)S(1)} all-gather(f32[8,256]{1,0:T(8,128)} %reduce-scatter.2.cloned.1.call-done), channel_id=1, replica_groups=mesh['space'=8,'blk'=16] {'blk'}, dimensions={0}, use_global_device_ids=true | all-gather | bytes 139264 | tf_op jit(solution)/shard_map/all_gather | solution.py:45
  97.1 1.3 collective-permute-start.1
  98.4 4.6 %collective-permute-start = (f32[128,256]{1,0:T(8,128)S(1)}, f32[128,256]{1,0:T(8,128)S(1)}, u32[]{:S(2)}, u32[]{:S(2)}) collective-permute-start(f32[128,256]{1,0:T(8,128)S(1)} %all_gather.9), channel_id=1, source_target_pairs={{0,16},{16,32},{32,48},{48,64},{64,80},{80,96},{96,112},{1,17},{17... | collective-permute-start | bytes 393224 | tf_op jit(solution)/shard_map/ppermute | solution.py:12
  103.0 3.3 %convolution_bitcast_fusion.3 = f32[1,1,256]{2,1,0:T(1,128)S(1)} fusion(f32[8,256,256]{2,1,0:T(8,128)} %param.19, f32[8,256,1]{1,0,2:T(8,128)} %bitcast.43), kind=kOutput, calls=%fused_computation.9 | convolution fusion | flops 6291456 | bytes 2106368 | tf_op jit(solution)/shard_map/oe,ode->d/dot_general | solution.py:47
  106.3 174.5 %all-gather.1 = f32[128,1,256]{2,1,0:T(1,128)S(1)} all-gather(f32[1,1,256]{2,1,0:T(1,128)S(1)} %convolution_bitcast_fusion.3), channel_id=2, replica_groups=mesh['space'=8,'blk'=16] {'space','blk'}, dimensions={0}, use_global_device_ids=true | all-gather | bytes 132096 | tf_op jit(solution)/shard_map/all_gather | solution.py:50
  280.7 0.2 convolution_bitcast_fusion
  280.9 5.5 %convolution_bitcast_fusion.2 = f32[256,1,1]{0,1,2:T(1,128)S(1)} fusion(f32[16,256,256]{2,1,0:T(8,128)} %param.18, f32[16,256,1]{1,0,2:T(8,128)S(1)} %convolution_bitcast_fusion), kind=kOutput, calls=%fused_computation.8 | convolution fusion | flops 12582912 | bytes 4211712 | tf_op jit(solution)/shard_map/ptk,tlk->pl/dot_general | solution.py:61
  286.5 1.1 fusion.29
  287.6 0.0 collective-permute-done.1
  287.6 0.0 collective-permute-done
  287.6 0.4 fusion.4
  288.0 3.3 %fusion.3 = f32[8,256]{1,0:T(8,128)S(1)} fusion(f32[8,16,256]{2,0,1:T(8,128)S(1)} %fusion.4, f32[16,256,256]{2,1,0:T(8,128)S(1)} %copy-done.1, f32[1,8,256]{2,0,1:T(1,128)S(1)} %fusion.29), kind=kOutput, calls=%fused_computation.7 | convolution fusion | flops 100665344 | bytes 4341760 | tf_op jit(solution)/shard_map/btk,tlk->bl/dot_general | solution.py:55
  291.4 16.6 %all_gather.11 = f32[128,256]{1,0:T(8,128)S(1)} all-gather(f32[8,256]{1,0:T(8,128)S(1)} %fusion.3), channel_id=1, replica_groups=mesh['space'=8,'blk'=16] {'blk'}, dimensions={0}, use_global_device_ids=true | all-gather | bytes 139264 | tf_op jit(solution)/shard_map/all_gather | solution.py:68
  308.0 0.2 fusion.14
  308.2 8.1 %fusion.2 = bf16[96,128,128]{2,1,0:T(8,128)(2,1)} fusion(bf16[96,128,256]{2,1,0:T(8,128)(2,1)} %param.12, bf16[96,128,256]{2,1,0:T(8,128)(2,1)} %param.11, f32[96,256]{1,0:T(8,128)S(1)} %fusion.14), kind=kOutput, calls=%fused_computation.4 | convolution fusion | flops 816316416 | bytes 15826944 | tf_op jit(solution)/shard_map/bmk,bnk->bmn/dot_general | solution.py:71
  (8 shorter events, 0.0 us)
Async XLA Ops:
  7.2 1.9 copy-start
  7.2 8.7 %copy-start.6 = (s32[96]{0:T(128)S(1)}, s32[96]{0:T(128)}, u32[]{:S(2)}) copy-start(s32[96]{0:T(128)} %param.13) | copy-start | bytes 1156
  7.2 9.7 %copy-start.8 = (s32[1,27]{1,0:T(1,128)S(1)}, s32[1,27]{1,0:T(1,128)}, u32[]{:S(2)}) copy-start(s32[1,27]{1,0:T(1,128)} %param.17) | copy-start | bytes 328
  7.2 9.7 %copy-start.7 = (s32[1,27]{1,0:T(1,128)S(1)}, s32[1,27]{1,0:T(1,128)}, u32[]{:S(2)}) copy-start(s32[1,27]{1,0:T(1,128)} %param.16) | copy-start | bytes 328
  7.2 9.9 %copy-start.5 = (s32[8,27]{1,0:T(8,128)S(1)}, s32[8,27]{1,0:T(8,128)}, u32[]{:S(2)}) copy-start(s32[8,27]{1,0:T(8,128)} %param.15) | copy-start | bytes 2596
  7.2 9.9 %copy-start.4 = (s32[8,27]{1,0:T(8,128)S(1)}, s32[8,27]{1,0:T(8,128)}, u32[]{:S(2)}) copy-start(s32[8,27]{1,0:T(8,128)} %param.14) | copy-start | bytes 2596
  7.2 73.2 %reduce-scatter.2.cloned.1.call-start = ((), (), s32[]{:S(2)}) async-start(), calls=%async_computation.1 | async-start | bytes 139264 | tf_op jit(solution)/shard_map/reduce_scatter | solution.py:44
  80.4 206.0 %copy-start.2 = (f32[8,256,256]{2,1,0:T(8,128)S(1)}, f32[8,256,256]{2,1,0:T(8,128)}, u32[]{:S(2)}) copy-start(f32[8,256,256]{2,1,0:T(8,128)} %param.19) | copy-start | bytes 6291460
  80.4 207.6 %copy-start.1 = (f32[16,256,256]{2,1,0:T(8,128)S(1)}, f32[16,256,256]{2,1,0:T(8,128)}, u32[]{:S(2)}) copy-start(f32[16,256,256]{2,1,0:T(8,128)} %param.18) | copy-start | bytes 12582916
  97.1 190.5 %collective-permute-start.1 = (f32[128,256]{1,0:T(8,128)S(1)}, f32[128,256]{1,0:T(8,128)S(1)}, u32[]{:S(2)}, u32[]{:S(2)}) collective-permute-start(f32[128,256]{1,0:T(8,128)S(1)} %all_gather.9), channel_id=1, source_target_pairs={{16,0},{32,16},{48,32},{64,48},{80,64},{96,80},{112,96},{17,1},{33... | collective-permute-start | bytes 393224 | tf_op jit(solution)/shard_map/ppermute | solution.py:15
  98.4 189.2 %collective-permute-start = (f32[128,256]{1,0:T(8,128)S(1)}, f32[128,256]{1,0:T(8,128)S(1)}, u32[]{:S(2)}, u32[]{:S(2)}) collective-permute-start(f32[128,256]{1,0:T(8,128)S(1)} %all_gather.9), channel_id=1, source_target_pairs={{0,16},{16,32},{32,48},{48,64},{64,80},{80,96},{96,112},{1,17},{17... | collective-permute-start | bytes 393224 | tf_op jit(solution)/shard_map/ppermute | solution.py:12
  291.4 24.9 %copy-start.3 = (f32[8,256]{1,0:T(8,128)}, f32[8,256]{1,0:T(8,128)S(1)}, u32[]{:S(2)}) copy-start(f32[8,256]{1,0:T(8,128)S(1)} %fusion.3) | copy-start | bytes 24580
Sparse Core Ops, SparseCore 0:
  17.0 63.3 reduce-scatter.1
where the time goes:
time: 325 us; the launch traced here: 323 us
  blocking collectives  208 us (64%)
  waiting for transfers between devices  63.1 us (19%)
  matrix products  30.5 us (9%)
  between operations  14.2 us (4%)
  starting transfers between devices  5.87 us (2%)
    all_gather x1, blocking collectives, shards(): lax.all_gather(self_parent_index, ('space', 'blk'), axis=0, tiled=True)  174 us
    reduce_scatter x1, waiting for transfers between devices, shards(): lax.psum_scatter(partial_moments, 'blk', scatter_dimension=0, tiled=True)  63.1 us
    all_gather x1, blocking collectives, shards(): domain = lax.all_gather(held_boxes, 'blk', axis=0, tiled=True)  16.7 us
    all_gather x1, blocking collectives, shards(): domain_local = lax.all_gather(box_locals, 'blk', axis=0, tiled=True)  16.6 us
    dot_general x1, matrix products, shards(): jnp.einsum('bmk,bnk->bmn', scaled, ket_table, preferred_element_type=jnp....  8.08 us
    dot_general x1, matrix products, shards(): jnp.einsum('bmn,bmk->bnk', density, bra_table, preferred_element_type=jnp...  6.82 us
  transfers between devices with their start and end apart: 3, of which 1 were waited for; matrix products, arithmetic and copies ran while one was open for 3% of the time, Pallas kernels for 0%

commit v1 on v0

v1 whole, which is shorter than its diff:
```python
import jax
import jax.numpy as jnp
from jax import lax
from jax.sharding import PartitionSpec as P


def exchange(x, axis, mask):
    count = lax.axis_size(axis)
    return lax.ppermute(x, axis, [(i, i ^ mask) for i in range(count)])


def butterfly_sum(x, axis):
    count = lax.axis_size(axis)
    mask = 1
    while mask < count:
        x = x + exchange(x, axis, mask)
        mask *= 2
    return x


def butterfly_gather(x, axis):
    count = lax.axis_size(axis)
    me = lax.axis_index(axis)
    mask = 1
    while mask < count:
        other = exchange(x, axis, mask)
        low = (me // mask) % 2 == 0
        x = jnp.where(low, jnp.concatenate([x, other], 0), jnp.concatenate([other, x], 0))
        mask *= 2
    return x


def neighbours(block, axis):
    count = lax.axis_size(axis)
    forward = [(i, i + 1) for i in range(count - 1)]
    backward = [(target, source) for source, target in forward]
    low = lax.ppermute(block, axis, forward)
    high = lax.ppermute(block, axis, backward)
    return jnp.concatenate([low, block, high], axis=0)


def shards(
    density,
    bra_table,
    ket_table,
    box_of_block,
    leaf_src,
    leaf_type,
    coarse_src,
    coarse_type,
    translation,
    upward_translation_table,
):
    top = lax.Precision.HIGHEST
    n_blk = lax.axis_size("blk")
    box_dom = 8 * n_blk
    n_types = translation.shape[0]
    inner = jnp.einsum("bmn,bmk->bnk", density, bra_table, preferred_element_type=jnp.float32)
    moments = jnp.sum(inner * ket_table.astype(jnp.float32), axis=1)
    box_hot = (box_of_block[:, None] == jnp.arange(box_dom, dtype=jnp.int32)[None, :]).astype(
        jnp.float32
    )
    partial_moments = lax.dot_general(
        box_hot, moments, (((0,), (0,)), ((), ())), precision=top
    )
    domain = butterfly_sum(partial_moments, "blk")
    window = neighbours(domain, "space")
    domain_parents = jnp.einsum(
        "qce,cde->qd", domain.reshape(n_blk, 8, -1), upward_translation_table, precision=top
    )
    all_parents = butterfly_gather(domain_parents, "space")
    src_hot = (leaf_src[..., None] == jnp.arange(3 * box_dom, dtype=jnp.int32)).astype(jnp.float32)
    type_hot = (leaf_type[..., None] == jnp.arange(n_types, dtype=jnp.int32)).astype(jnp.float32)
    counts = jnp.einsum("blt,blj->btj", type_hot, src_hot, precision=top)
    gathered = jnp.einsum("btj,jk->btk", counts, window, precision=top)
    leaf_far = jnp.einsum("btk,tlk->bl", gathered, translation, precision=top)
    n_parents = all_parents.shape[0]
    csrc_hot = (coarse_src[..., None] == jnp.arange(n_parents, dtype=jnp.int32)).astype(jnp.float32)
    ctype_hot = (coarse_type[..., None] == jnp.arange(n_types, dtype=jnp.int32)).astype(jnp.float32)
    ccounts = jnp.einsum("pet,peq->ptq", ctype_hot, csrc_hot, precision=top)
    cgathered = jnp.einsum("ptq,qk->ptk", ccounts, all_parents, precision=top)
    parent_local_expansion = jnp.einsum("ptk,tlk->pl", cgathered, translation, precision=top)
    downward_sent = jnp.einsum(
        "d,uds->us", parent_local_expansion[0], upward_translation_table, precision=top
    )
    box_locals = leaf_far + downward_sent
    domain_local = butterfly_gather(box_locals, "blk")
    block_locals = jnp.dot(box_hot, domain_local, precision=top)
    scaled = (bra_table.astype(jnp.float32) * block_locals[:, None, :]).astype(jnp.bfloat16)
    coulomb = jnp.einsum(
        "bmk,bnk->bmn", scaled, ket_table, preferred_element_type=jnp.float32
    ).astype(jnp.bfloat16)
    return (coulomb, box_locals)


def solution(mesh):
    placed = (
        P(("space", "blk"), None, None),
        P(("space", "blk"), None, None),
        P(("space", "blk"), None, None),
        P(("space", "blk")),
        P(("space", "blk"), None),
        P(("space", "blk"), None),
        P(("space", "blk"), None),
        P(("space", "blk"), None),
        P(),
        P(),
    )
    return jax.shard_map(
        shards,
        mesh=mesh,
        in_specs=placed,
        out_specs=(P(("space", "blk"), None, None), P(("space", "blk"), None)),
        check_vma=False,
    )
```

time: 325 us -> 91.6 us (0.28)
  the two profiles are of different devices: /device:TPU:0 before, /device:TPU:30 now
where the time goes in v1:
time: 91.6 us; the launch traced here: 91.3 us
  waiting for transfers between devices  33.7 us (37%)
  matrix products  31.5 us (34%)
  starting transfers between devices  22.7 us (25%)
  local copies, waits for them, and re-layouts  1.87 us (2%)
    ppermute x11, waiting for transfers between devices, exchange(): return lax.ppermute(x, axis, [(i, i ^ mask) for i in range(count)])  33.7 us
    ppermute x11, starting transfers between devices, exchange(): return lax.ppermute(x, axis, [(i, i ^ mask) for i in range(count)])  12.9 us
    dot_general x1, matrix products, shards(): jnp.einsum('bmk,bnk->bmn', scaled, ket_table, preferred_element_type=jnp....  8.08 us
    ppermute x1, starting transfers between devices, neighbours(): low = lax.ppermute(block, axis, forward)  6.9 us
    dot_general x1, matrix products, shards(): jnp.einsum('bmn,bmk->bnk', density, bra_table, preferred_element_type=jnp...  6.82 us
    dot_general x1, matrix products, shards(): jnp.einsum('ptk,tlk->pl', cgathered, translation, precision=top)  5.55 us
    dot_general x1, matrix products, shards(): leaf_far = jnp.einsum('btk,tlk->bl', gathered, translation, precision=top)  3.34 us
    ppermute x1, starting transfers between devices, neighbours(): high = lax.ppermute(block, axis, backward)  2.99 us
  transfers between devices with their start and end apart: 13, of which 10 were waited for; matrix products, arithmetic and copies ran while one was open for 12% of the time, Pallas kernels for 0%

profile of v1, /device:TPU:30, one launch (start us, length us, event | category | flops | bytes accessed | tf_op | source)
XLA Modules:
  0.0 91.3 jit_solution(6597391217173759673)
XLA Ops:
  0.7 1.8 %copy-done = bf16[96,128,128]{2,1,0:T(8,128)(2,1)S(1)} copy-done((bf16[96,128,128]{2,1,0:T(8,128)(2,1)S(1)}, bf16[96,128,128]{2,1,0:T(8,128)(2,1)}, u32[]{:S(2)}) %copy-start) | copy-done | bytes 3145752
  2.5 6.8 %multiply_reduce_fusion = f32[96,256]{1,0:T(8,128)S(1)} fusion(bf16[96,128,256]{2,1,0:T(8,128)(2,1)} %param.12, bf16[96,128,128]{2,1,0:T(8,128)(2,1)S(1)} %copy-done, bf16[96,128,256]{2,1,0:T(8,128)(2,1)} %param.11), kind=kOutput, calls=%fused_computation.1 | convolution fusion | flops 814718976 | bytes 15826944 | tf_op jit(solution)/shard_map/bmn,bmk->bnk/dot_general | solution.py:58
  9.8 1.3 %collective-permute-done = f32[128,256]{1,0:T(8,128)S(1)} collective-permute-done((f32[128,256]{1,0:T(8,128)S(1)}, f32[128,256]{1,0:T(8,128)S(1)}, u32[]{:S(2)}, u32[]{:S(2)}) %collective-permute-start) | collective-permute-done | bytes 131104 | tf_op jit(solution)/shard_map/ppermute | solution.py:9
  11.1 2.0 %collective-permute-start.1 = (f32[128,256]{1,0:T(8,128)S(1)}, f32[128,256]{1,0:T(8,128)S(1)}, u32[]{:S(2)}, u32[]{:S(2)}) collective-permute-start(f32[128,256]{1,0:T(8,128)S(1)} %add.48), channel_id=1, source_target_pairs={{0,2},{1,3},{2,0},{3,1},{4,6},{5,7},{6,4},{7,5},{8,10},{9,11},{10,... | collective-permute-start | bytes 393224 | tf_op jit(solution)/shard_map/ppermute | solution.py:9
  13.1 3.8 %collective-permute-done.1 = f32[128,256]{1,0:T(8,128)S(1)} collective-permute-done((f32[128,256]{1,0:T(8,128)S(1)}, f32[128,256]{1,0:T(8,128)S(1)}, u32[]{:S(2)}, u32[]{:S(2)}) %collective-permute-start.1) | collective-permute-done | bytes 131104 | tf_op jit(solution)/shard_map/ppermute | solution.py:9
  17.0 0.8 collective-permute-start.2
  17.8 4.2 %collective-permute-done.2 = f32[128,256]{1,0:T(8,128)S(1)} collective-permute-done((f32[128,256]{1,0:T(8,128)S(1)}, f32[128,256]{1,0:T(8,128)S(1)}, u32[]{:S(2)}, u32[]{:S(2)}) %collective-permute-start.2) | collective-permute-done | bytes 131104 | tf_op jit(solution)/shard_map/ppermute | solution.py:9
  22.0 1.3 %collective-permute-start.3 = (f32[128,256]{1,0:T(8,128)S(1)}, f32[128,256]{1,0:T(8,128)S(1)}, u32[]{:S(2)}, u32[]{:S(2)}) collective-permute-start(f32[128,256]{1,0:T(8,128)S(1)} %add.50), channel_id=1, source_target_pairs={{0,8},{1,9},{2,10},{3,11},{4,12},{5,13},{6,14},{7,15},{8,0},{9,1},... | collective-permute-start | bytes 393224 | tf_op jit(solution)/shard_map/ppermute | solution.py:9
  23.4 5.2 %collective-permute-done.3 = f32[128,256]{1,0:T(8,128)S(1)} collective-permute-done((f32[128,256]{1,0:T(8,128)S(1)}, f32[128,256]{1,0:T(8,128)S(1)}, u32[]{:S(2)}, u32[]{:S(2)}) %collective-permute-start.3) | collective-permute-done | bytes 131104 | tf_op jit(solution)/shard_map/ppermute | solution.py:9
  28.6 1.7 %convolution_bitcast_fusion.1 = f32[16,256]{1,0:T(8,128)S(1)} fusion(f32[8,256,256]{2,1,0:T(8,128)S(1)} %copy-done.2, f32[16,8,256]{2,1,0:T(8,128)S(1)} %bitcast.37), kind=kOutput, calls=%fused_computation.6 | convolution fusion | flops 100663296 | bytes 2244608 | tf_op jit(solution)/shard_map/qce,cde->qd/dot_general | solution.py:68
  30.4 0.8 collective-permute-start.6
  31.2 2.9 %collective-permute-done.6 = f32[16,256]{1,0:T(8,128)S(1)} collective-permute-done((f32[16,256]{1,0:T(8,128)S(1)}, f32[16,256]{1,0:T(8,128)S(1)}, u32[]{:S(2)}, u32[]{:S(2)}) %collective-permute-start.6) | collective-permute-done | bytes 16416 | tf_op jit(solution)/shard_map/ppermute | solution.py:9
  34.1 1.4 %collective-permute-start.7 = (f32[32,256]{1,0:T(8,128)S(1)}, f32[32,256]{1,0:T(8,128)S(1)}, u32[]{:S(2)}, u32[]{:S(2)}) collective-permute-start(f32[32,256]{1,0:T(8,128)S(1)} %maximum_select_fusion.6), channel_id=1, source_target_pairs={{0,32},{16,48},{32,0},{48,16},{64,96},{80,112},{96,64},{112,80},{1... | collective-permute-start | bytes 98312 | tf_op jit(solution)/shard_map/ppermute | solution.py:9
  35.9 3.6 %collective-permute-done.7 = f32[32,256]{1,0:T(8,128)S(1)} collective-permute-done((f32[32,256]{1,0:T(8,128)S(1)}, f32[32,256]{1,0:T(8,128)S(1)}, u32[]{:S(2)}, u32[]{:S(2)}) %collective-permute-start.7) | collective-permute-done | bytes 32800 | tf_op jit(solution)/shard_map/ppermute | solution.py:9
  39.5 0.6 maximum_select_fusion.4
  40.2 3.8 %collective-permute-start.8 = (f32[64,256]{1,0:T(8,128)}, f32[64,256]{1,0:T(8,128)S(1)}, u32[]{:S(2)}, u32[]{:S(2)}) collective-permute-start(f32[64,256]{1,0:T(8,128)} %maximum_select_fusion.4), channel_id=1, source_target_pairs={{0,64},{16,80},{32,96},{48,112},{64,0},{80,16},{96,32},{112,48},{1... | collective-permute-start | bytes 196616 | tf_op jit(solution)/shard_map/ppermute | solution.py:9
  44.0 0.8 fusion.32
  44.8 3.0 %collective-permute-start.5 = (f32[128,256]{1,0:T(8,128)S(1)}, f32[128,256]{1,0:T(8,128)S(1)}, u32[]{:S(2)}, u32[]{:S(2)}) collective-permute-start(f32[128,256]{1,0:T(8,128)S(1)} %add.51), channel_id=1, source_target_pairs={{16,0},{32,16},{48,32},{64,48},{80,64},{96,80},{112,96},{17,1},{33... | collective-permute-start | bytes 393224 | tf_op jit(solution)/shard_map/ppermute | solution.py:38
  47.8 6.9 %collective-permute-start.4 = (f32[128,256]{1,0:T(8,128)S(1)}, f32[128,256]{1,0:T(8,128)S(1)}, u32[]{:S(2)}, u32[]{:S(2)}) collective-permute-start(f32[128,256]{1,0:T(8,128)S(1)} %add.51), channel_id=1, source_target_pairs={{0,16},{16,32},{32,48},{48,64},{64,80},{80,96},{96,112},{1,17},{17... | collective-permute-start | bytes 393224 | tf_op jit(solution)/shard_map/ppermute | solution.py:37
  54.8 1.1 %convolution_bitcast_fusion = f32[16,256,1]{1,0,2:T(8,128)S(1)} fusion(f32[16,128]{1,0:T(8,128)S(1)} %fusion.32, f32[64,256]{1,0:T(8,128)S(1)} %collective-permute-done.8, f32[64,256]{1,0:T(8,128)} %maximum_select_fusion.4, pred[]{:T(512)S(6)} %eq.151), kind=kOutput, calls=%fused_computation.5 | convolution fusion | flops 6389760 | bytes 155649 | tf_op jit(solution)/shard_map/ptq,qk->ptk/dot_general | solution.py:81
  55.8 5.6 %convolution_bitcast_fusion.3 = f32[256,1,1]{0,1,2:T(1,128)S(1)} fusion(f32[16,256,256]{2,1,0:T(8,128)} %param.18, f32[16,256,1]{1,0,2:T(8,128)S(1)} %convolution_bitcast_fusion), kind=kOutput, calls=%fused_computation.9 | convolution fusion | flops 12582912 | bytes 4211712 | tf_op jit(solution)/shard_map/ptk,tlk->pl/dot_general | solution.py:82
  61.4 2.7 %fusion.41 = f32[1,8,256]{2,0,1:T(1,128)S(1)} fusion(f32[256,1,1]{0,1,2:T(1,128)S(1)} %convolution_bitcast_fusion.3, f32[8,256,256]{2,1,0:T(8,128)} %param.19), kind=kOutput, calls=%fused_computation.58 | convolution fusion | flops 6291456 | bytes 2106368 | tf_op jit(solution)/shard_map/d,uds->us/dot_general | solution.py:83
  64.1 0.4 fusion.4
  64.5 3.3 %fusion.3 = f32[8,256]{1,0:T(8,128)S(1)} fusion(f32[8,16,256]{2,0,1:T(8,128)S(1)} %fusion.4, f32[16,256,256]{2,1,0:T(8,128)S(1)} %copy-done.1, f32[1,8,256]{2,0,1:T(1,128)S(1)} %fusion.41), kind=kOutput, calls=%fused_computation.8 | convolution fusion | flops 100665344 | bytes 4341760 | tf_op jit(solution)/shard_map/btk,tlk->bl/dot_general | solution.py:76
  68.0 1.1 %collective-permute-done.9 = f32[8,256]{1,0:T(8,128)S(1)} collective-permute-done((f32[8,256]{1,0:T(8,128)S(1)}, f32[8,256]{1,0:T(8,128)S(1)}, u32[]{:S(2)}, u32[]{:S(2)}) %collective-permute-start.9) | collective-permute-done | bytes 8224 | tf_op jit(solution)/shard_map/ppermute | solution.py:9
  69.1 1.0 %collective-permute-start.10 = (f32[16,256]{1,0:T(8,128)S(1)}, f32[16,256]{1,0:T(8,128)S(1)}, u32[]{:S(2)}, u32[]{:S(2)}) collective-permute-start(f32[16,256]{1,0:T(8,128)S(1)} %maximum_select_fusion.8), channel_id=1, source_target_pairs={{0,2},{1,3},{2,0},{3,1},{4,6},{5,7},{6,4},{7,5},{8,10},{9,11},{10,... | collective-permute-start | bytes 49160 | tf_op jit(solution)/shard_map/ppermute | solution.py:9
  70.1 2.7 %collective-permute-done.10 = f32[16,256]{1,0:T(8,128)S(1)} collective-permute-done((f32[16,256]{1,0:T(8,128)S(1)}, f32[16,256]{1,0:T(8,128)S(1)}, u32[]{:S(2)}, u32[]{:S(2)}) %collective-permute-start.10) | collective-permute-done | bytes 16416 | tf_op jit(solution)/shard_map/ppermute | solution.py:9
  72.9 0.6 collective-permute-start.11
  73.5 3.6 %collective-permute-done.11 = f32[32,256]{1,0:T(8,128)S(1)} collective-permute-done((f32[32,256]{1,0:T(8,128)S(1)}, f32[32,256]{1,0:T(8,128)S(1)}, u32[]{:S(2)}, u32[]{:S(2)}) %collective-permute-start.11) | collective-permute-done | bytes 32800 | tf_op jit(solution)/shard_map/ppermute | solution.py:9
  77.1 0.9 collective-permute-start.12
  78.0 5.0 %collective-permute-done.12 = f32[64,256]{1,0:T(8,128)S(1)} collective-permute-done((f32[64,256]{1,0:T(8,128)S(1)}, f32[64,256]{1,0:T(8,128)S(1)}, u32[]{:S(2)}, u32[]{:S(2)}) %collective-permute-start.12) | collective-permute-done | bytes 65568 | tf_op jit(solution)/shard_map/ppermute | solution.py:9
  83.2 8.1 %fusion.2 = bf16[96,128,128]{2,1,0:T(8,128)(2,1)} fusion(bf16[96,128,256]{2,1,0:T(8,128)(2,1)} %param.12, bf16[96,128,256]{2,1,0:T(8,128)(2,1)} %param.11, f32[96,256]{1,0:T(8,128)S(1)} %fusion.17), kind=kOutput, calls=%fused_computation.4 | convolution fusion | flops 816316416 | bytes 15826944 | tf_op jit(solution)/shard_map/bmk,bnk->bmn/dot_general | solution.py:90
  (31 shorter events, 1.2 us)
Async XLA Ops:
  0.6 1.9 %copy-start = (bf16[96,128,128]{2,1,0:T(8,128)(2,1)S(1)}, bf16[96,128,128]{2,1,0:T(8,128)(2,1)}, u32[]{:S(2)}) copy-start(bf16[96,128,128]{2,1,0:T(8,128)(2,1)} %param.10) | copy-start | bytes 9437188
  0.6 8.7 %copy-start.6 = (s32[96]{0:T(128)S(1)}, s32[96]{0:T(128)}, u32[]{:S(2)}) copy-start(s32[96]{0:T(128)} %param.13) | copy-start | bytes 1156
  0.7 28.0 %copy-start.2 = (f32[8,256,256]{2,1,0:T(8,128)S(1)}, f32[8,256,256]{2,1,0:T(8,128)}, u32[]{:S(2)}) copy-start(f32[8,256,256]{2,1,0:T(8,128)} %param.19) | copy-start | bytes 6291460
  0.7 34.9 %copy-start.5 = (s32[8,27]{1,0:T(8,128)S(1)}, s32[8,27]{1,0:T(8,128)}, u32[]{:S(2)}) copy-start(s32[8,27]{1,0:T(8,128)} %param.15) | copy-start | bytes 2596
  0.7 34.9 %copy-start.4 = (s32[8,27]{1,0:T(8,128)S(1)}, s32[8,27]{1,0:T(8,128)}, u32[]{:S(2)}) copy-start(s32[8,27]{1,0:T(8,128)} %param.14) | copy-start | bytes 2596
  0.7 43.3 %copy-start.7 = (s32[1,27]{1,0:T(1,128)S(1)}, s32[1,27]{1,0:T(1,128)}, u32[]{:S(2)}) copy-start(s32[1,27]{1,0:T(1,128)} %param.16) | copy-start | bytes 328
  9.7 1.4 %collective-permute-start = (f32[128,256]{1,0:T(8,128)S(1)}, f32[128,256]{1,0:T(8,128)S(1)}, u32[]{:S(2)}, u32[]{:S(2)}) collective-permute-start(f32[128,256]{1,0:T(8,128)S(1)} %fusion.27), channel_id=1, source_target_pairs={{0,1},{1,0},{2,3},{3,2},{4,5},{5,4},{6,7},{7,6},{8,9},{9,8},{10,11... | collective-permute-start | bytes 393224 | tf_op jit(solution)/shard_map/ppermute | solution.py:9
  11.1 5.8 %collective-permute-start.1 = (f32[128,256]{1,0:T(8,128)S(1)}, f32[128,256]{1,0:T(8,128)S(1)}, u32[]{:S(2)}, u32[]{:S(2)}) collective-permute-start(f32[128,256]{1,0:T(8,128)S(1)} %add.48), channel_id=1, source_target_pairs={{0,2},{1,3},{2,0},{3,1},{4,6},{5,7},{6,4},{7,5},{8,10},{9,11},{10,... | collective-permute-start | bytes 393224 | tf_op jit(solution)/shard_map/ppermute | solution.py:9
  17.0 5.0 %collective-permute-start.2 = (f32[128,256]{1,0:T(8,128)S(1)}, f32[128,256]{1,0:T(8,128)S(1)}, u32[]{:S(2)}, u32[]{:S(2)}) collective-permute-start(f32[128,256]{1,0:T(8,128)S(1)} %add.49), channel_id=1, source_target_pairs={{0,4},{1,5},{2,6},{3,7},{4,0},{5,1},{6,2},{7,3},{8,12},{9,13},{10,... | collective-permute-start | bytes 393224 | tf_op jit(solution)/shard_map/ppermute | solution.py:9
  22.0 6.6 %collective-permute-start.3 = (f32[128,256]{1,0:T(8,128)S(1)}, f32[128,256]{1,0:T(8,128)S(1)}, u32[]{:S(2)}, u32[]{:S(2)}) collective-permute-start(f32[128,256]{1,0:T(8,128)S(1)} %add.50), channel_id=1, source_target_pairs={{0,8},{1,9},{2,10},{3,11},{4,12},{5,13},{6,14},{7,15},{8,0},{9,1},... | collective-permute-start | bytes 393224 | tf_op jit(solution)/shard_map/ppermute | solution.py:9
  30.4 3.8 %collective-permute-start.6 = (f32[16,256]{1,0:T(8,128)S(1)}, f32[16,256]{1,0:T(8,128)S(1)}, u32[]{:S(2)}, u32[]{:S(2)}) collective-permute-start(f32[16,256]{1,0:T(8,128)S(1)} %convolution_bitcast_fusion.1), channel_id=1, source_target_pairs={{0,16},{16,0},{32,48},{48,32},{64,80},{80,64},{96,112},{112,96},{1... | collective-permute-start | bytes 49160 | tf_op jit(solution)/shard_map/ppermute | solution.py:9
  34.1 5.4 %collective-permute-start.7 = (f32[32,256]{1,0:T(8,128)S(1)}, f32[32,256]{1,0:T(8,128)S(1)}, u32[]{:S(2)}, u32[]{:S(2)}) collective-permute-start(f32[32,256]{1,0:T(8,128)S(1)} %maximum_select_fusion.6), channel_id=1, source_target_pairs={{0,32},{16,48},{32,0},{48,16},{64,96},{80,112},{96,64},{112,80},{1... | collective-permute-start | bytes 98312 | tf_op jit(solution)/shard_map/ppermute | solution.py:9
  40.2 14.6 %collective-permute-start.8 = (f32[64,256]{1,0:T(8,128)}, f32[64,256]{1,0:T(8,128)S(1)}, u32[]{:S(2)}, u32[]{:S(2)}) collective-permute-start(f32[64,256]{1,0:T(8,128)} %maximum_select_fusion.4), channel_id=1, source_target_pairs={{0,64},{16,80},{32,96},{48,112},{64,0},{80,16},{96,32},{112,48},{1... | collective-permute-start | bytes 196616 | tf_op jit(solution)/shard_map/ppermute | solution.py:9
  44.8 19.7 %copy-start.1 = (f32[16,256,256]{2,1,0:T(8,128)S(1)}, f32[16,256,256]{2,1,0:T(8,128)}, u32[]{:S(2)}) copy-start(f32[16,256,256]{2,1,0:T(8,128)} %param.18) | copy-start | bytes 12582916
  44.8 19.3 %collective-permute-start.5 = (f32[128,256]{1,0:T(8,128)S(1)}, f32[128,256]{1,0:T(8,128)S(1)}, u32[]{:S(2)}, u32[]{:S(2)}) collective-permute-start(f32[128,256]{1,0:T(8,128)S(1)} %add.51), channel_id=1, source_target_pairs={{16,0},{32,16},{48,32},{64,48},{80,64},{96,80},{112,96},{17,1},{33... | collective-permute-start | bytes 393224 | tf_op jit(solution)/shard_map/ppermute | solution.py:38
  47.8 16.3 %collective-permute-start.4 = (f32[128,256]{1,0:T(8,128)S(1)}, f32[128,256]{1,0:T(8,128)S(1)}, u32[]{:S(2)}, u32[]{:S(2)}) collective-permute-start(f32[128,256]{1,0:T(8,128)S(1)} %add.51), channel_id=1, source_target_pairs={{0,16},{16,32},{32,48},{48,64},{64,80},{80,96},{96,112},{1,17},{17... | collective-permute-start | bytes 393224 | tf_op jit(solution)/shard_map/ppermute | solution.py:37
  67.9 23.4 %copy-start.3 = (f32[8,256]{1,0:T(8,128)}, f32[8,256]{1,0:T(8,128)S(1)}, u32[]{:S(2)}) copy-start(f32[8,256]{1,0:T(8,128)S(1)} %fusion.3) | copy-start | bytes 24580
  67.9 1.2 %collective-permute-start.9 = (f32[8,256]{1,0:T(8,128)S(1)}, f32[8,256]{1,0:T(8,128)S(1)}, u32[]{:S(2)}, u32[]{:S(2)}) collective-permute-start(f32[8,256]{1,0:T(8,128)S(1)} %fusion.3), channel_id=1, source_target_pairs={{0,1},{1,0},{2,3},{3,2},{4,5},{5,4},{6,7},{7,6},{8,9},{9,8},{10,11... | collective-permute-start | bytes 24584 | tf_op jit(solution)/shard_map/ppermute | solution.py:9
  69.1 3.7 %collective-permute-start.10 = (f32[16,256]{1,0:T(8,128)S(1)}, f32[16,256]{1,0:T(8,128)S(1)}, u32[]{:S(2)}, u32[]{:S(2)}) collective-permute-start(f32[16,256]{1,0:T(8,128)S(1)} %maximum_select_fusion.8), channel_id=1, source_target_pairs={{0,2},{1,3},{2,0},{3,1},{4,6},{5,7},{6,4},{7,5},{8,10},{9,11},{10,... | collective-permute-start | bytes 49160 | tf_op jit(solution)/shard_map/ppermute | solution.py:9
  72.9 4.3 %collective-permute-start.11 = (f32[32,256]{1,0:T(8,128)S(1)}, f32[32,256]{1,0:T(8,128)S(1)}, u32[]{:S(2)}, u32[]{:S(2)}) collective-permute-start(f32[32,256]{1,0:T(8,128)S(1)} %maximum_select_fusion.7), channel_id=1, source_target_pairs={{0,4},{1,5},{2,6},{3,7},{4,0},{5,1},{6,2},{7,3},{8,12},{9,13},{10,... | collective-permute-start | bytes 98312 | tf_op jit(solution)/shard_map/ppermute | solution.py:9
  77.1 5.8 %collective-permute-start.12 = (f32[64,256]{1,0:T(8,128)S(1)}, f32[64,256]{1,0:T(8,128)S(1)}, u32[]{:S(2)}, u32[]{:S(2)}) collective-permute-start(f32[64,256]{1,0:T(8,128)S(1)} %maximum_select_fusion.5), channel_id=1, source_target_pairs={{0,8},{1,9},{2,10},{3,11},{4,12},{5,13},{6,14},{7,15},{8,0},{9,1},... | collective-permute-start | bytes 196616 | tf_op jit(solution)/shard_map/ppermute | solution.py:9

commit v2 on v1

v2 whole, which is shorter than its diff:
```python
import jax
import jax.numpy as jnp
from jax import lax
from jax.sharding import PartitionSpec as P


def exchange(x, axis, mask):
    count = lax.axis_size(axis)
    return lax.ppermute(x, axis, [(i, i ^ mask) for i in range(count)])


def shift(x, axis, step):
    count = lax.axis_size(axis)
    return lax.ppermute(x, axis, [(i, (i + step) % count) for i in range(count)])


def group_sum(x, axis):
    count = lax.axis_size(axis)
    stride = 1
    while stride < count:
        if count % (4 * stride) == 0:
            near = x + exchange(x, axis, stride)
            far = exchange(x, axis, 2 * stride) + exchange(x, axis, 3 * stride)
            x = near + far
            stride *= 4
        else:
            x = x + exchange(x, axis, stride)
            stride *= 2
    return x


def shards(
    density,
    bra_table,
    ket_table,
    box_of_block,
    leaf_src,
    leaf_type,
    coarse_src,
    coarse_type,
    translation,
    upward_translation_table,
):
    top = lax.Precision.HIGHEST
    n_blk = lax.axis_size("blk")
    n_space = lax.axis_size("space")
    me = lax.axis_index("blk")
    here = lax.axis_index("space")
    leaves = leaf_src.shape[0]
    box_dom = leaves * n_blk
    n_types = translation.shape[0]
    coeffs = translation.shape[1]

    lists = jnp.concatenate([leaf_src, leaf_type, coarse_src, coarse_type], axis=0)
    table = jnp.zeros((n_blk,) + lists.shape, jnp.int32)
    table = lax.dynamic_update_index_in_dim(table, lists, me, 0)
    table = group_sum(table, "blk")
    dom_src = table[:, :leaves].reshape(box_dom, -1)
    dom_type = table[:, leaves : 2 * leaves].reshape(box_dom, -1)
    dom_csrc = table[:, 2 * leaves]
    dom_ctype = table[:, 2 * leaves + 1]

    inner = jnp.einsum("bmn,bmk->bnk", density, bra_table, preferred_element_type=jnp.float32)
    moments = jnp.sum(inner * ket_table.astype(jnp.float32), axis=1)
    box_hot = (box_of_block[:, None] == jnp.arange(box_dom, dtype=jnp.int32)[None, :]).astype(
        jnp.float32
    )
    partial_moments = lax.dot_general(
        box_hot, moments, (((0,), (0,)), ((), ())), precision=top
    )
    domain = group_sum(partial_moments, "blk")
    domain_parents = jnp.einsum(
        "qce,cde->qd", domain.reshape(n_blk, leaves, coeffs), upward_translation_table, precision=top
    )
    near = jnp.concatenate([domain, domain_parents], axis=0)
    from_low = shift(near, "space", 1)
    from_high = shift(near, "space", n_space - 1)
    low = jnp.where(here > 0, from_low[:box_dom], 0.0)
    high = jnp.where(here < n_space - 1, from_high[:box_dom], 0.0)
    window = jnp.concatenate([low, domain, high], axis=0)
    by_step = [domain_parents, from_low[box_dom:]]
    by_step += [shift(domain_parents, "space", k) for k in range(2, n_space - 1)]
    by_step += [from_high[box_dom:]]
    all_parents = jnp.concatenate(by_step, axis=0)
    csrc = ((here - dom_csrc // n_blk) % n_space) * n_blk + dom_csrc % n_blk

    src_hot = (dom_src[..., None] == jnp.arange(3 * box_dom, dtype=jnp.int32)).astype(jnp.bfloat16)
    type_hot = (dom_type[..., None] == jnp.arange(n_types, dtype=jnp.int32)).astype(jnp.bfloat16)
    counts = jnp.einsum("blt,blj->btj", type_hot, src_hot, preferred_element_type=jnp.float32)
    gathered = jnp.einsum("btj,jk->btk", counts, window, precision=top)
    n_parents = all_parents.shape[0]
    csrc_hot = (csrc[..., None] == jnp.arange(n_parents, dtype=jnp.int32)).astype(jnp.bfloat16)
    ctype_hot = (dom_ctype[..., None] == jnp.arange(n_types, dtype=jnp.int32)).astype(jnp.bfloat16)
    ccounts = jnp.einsum("pet,peq->ptq", ctype_hot, csrc_hot, preferred_element_type=jnp.float32)
    cgathered = jnp.einsum("ptq,qk->ptk", ccounts, all_parents, precision=top)
    rows = jnp.concatenate([gathered, cgathered], axis=0)
    far = jnp.einsum("btk,tlk->bl", rows, translation, precision=top)
    leaf_far = far[:box_dom]
    parent_locals = far[box_dom:]
    downward = jnp.einsum(
        "qd,cds->qcs", parent_locals, upward_translation_table, precision=top
    ).reshape(box_dom, coeffs)
    domain_local = leaf_far + downward
    box_locals = lax.dynamic_slice_in_dim(domain_local, me * leaves, leaves, axis=0)
    block_locals = jnp.dot(box_hot, domain_local, precision=top)
    scaled = (bra_table.astype(jnp.float32) * block_locals[:, None, :]).astype(jnp.bfloat16)
    coulomb = jnp.einsum(
        "bmk,bnk->bmn", scaled, ket_table, preferred_element_type=jnp.float32
    ).astype(jnp.bfloat16)
    return (coulomb, box_locals)


def solution(mesh):
    placed = (
        P(("space", "blk"), None, None),
        P(("space", "blk"), None, None),
        P(("space", "blk"), None, None),
        P(("space", "blk")),
        P(("space", "blk"), None),
        P(("space", "blk"), None),
        P(("space", "blk"), None),
        P(("space", "blk"), None),
        P(),
        P(),
    )
    return jax.shard_map(
        shards,
        mesh=mesh,
        in_specs=placed,
        out_specs=(P(("space", "blk"), None, None), P(("space", "blk"), None)),
        check_vma=False,
    )
```

time: 91.6 us -> 95 us (1.037)
  the two profiles are of different devices: /device:TPU:30 before, /device:TPU:0 now
where the time goes in v2:
time: 95 us; the launch traced here: 94.2 us
  matrix products  31 us (33%)
  starting transfers between devices  29.4 us (31%)
  waiting for transfers between devices  24.5 us (26%)
  local copies, waits for them, and re-layouts  4.35 us (5%)
  other arithmetic  4.05 us (4%)
  between operations  0.98 us (1%)
    ppermute x7, starting transfers between devices, shift(): lax.ppermute(x, axis, [(i, (i + step) % count) for i in range(count)])  16.7 us
    ppermute x12, waiting for transfers between devices, exchange(): return lax.ppermute(x, axis, [(i, i ^ mask) for i in range(count)])  15.2 us
    ppermute x12, starting transfers between devices, exchange(): return lax.ppermute(x, axis, [(i, i ^ mask) for i in range(count)])  12.8 us
    ppermute x7, waiting for transfers between devices, shift(): lax.ppermute(x, axis, [(i, (i + step) % count) for i in range(count)])  9.27 us
    dot_general x1, matrix products, shards(): jnp.einsum('bmk,bnk->bmn', scaled, ket_table, preferred_element_type=jnp....  8.08 us
    dot_general x1, matrix products, shards(): jnp.einsum('bmn,bmk->bnk', density, bra_table, preferred_element_type=jnp...  6.82 us
    dot_general x1, matrix products, shards(): gathered = jnp.einsum('btj,jk->btk', counts, window, precision=top)  4.52 us
    dot_general x1, matrix products, shards(): far = jnp.einsum('btk,tlk->bl', rows, translation, precision=top)  4.39 us
  transfers between devices with their start and end apart: 19, of which 8 were waited for; matrix products, arithmetic and copies ran while one was open for 16% of the time, Pallas kernels for 0%

profile of v2, /device:TPU:0, one launch (start us, length us, event | category | flops | bytes accessed | tf_op | source)
XLA Modules:
  0.0 94.2 jit_solution(183233512951921268)
XLA Ops:
  0.7 0.9 fusion.30
  1.6 1.5 %collective-permute-start.2 = (s32[16,18,27]{2,1,0:T(8,128)S(1)}, s32[16,18,27]{2,1,0:T(8,128)S(1)}, u32[]{:S(2)}, u32[]{:S(2)}) collective-permute-start(s32[16,18,27]{2,1,0:T(8,128)S(1)} %fusion.30), channel_id=1, source_target_pairs={{0,3},{1,2},{2,1},{3,0},{4,7},{5,6},{6,5},{7,4},{8,11},{9,10},{10,... | collective-permute-start | bytes 93320 | tf_op jit(solution)/shard_map/ppermute | solution.py:9
  3.9 6.8 %multiply_reduce_fusion = f32[96,256]{1,0:T(8,128)S(1)} fusion(bf16[96,128,256]{2,1,0:T(8,128)(2,1)} %param.12, bf16[96,128,128]{2,1,0:T(8,128)(2,1)S(1)} %copy-done, bf16[96,128,256]{2,1,0:T(8,128)(2,1)} %param.11), kind=kOutput, calls=%fused_computation.1 | convolution fusion | flops 814718976 | bytes 15826944 | tf_op jit(solution)/shard_map/bmn,bmk->bnk/dot_general | solution.py:63
  10.8 2.4 %collective-permute-done.1 = s32[16,18,27]{2,1,0:T(8,128)S(1)} collective-permute-done((s32[16,18,27]{2,1,0:T(8,128)S(1)}, s32[16,18,27]{2,1,0:T(8,128)S(1)}, u32[]{:S(2)}, u32[]{:S(2)}) %collective-permute-start.1) | collective-permute-done | bytes 31136 | tf_op jit(solution)/shard_map/ppermute | solution.py:9
  13.2 3.2 %collective-permute-start.5 = (s32[16,18,27]{2,1,0:T(8,128)S(1)}, s32[16,18,27]{2,1,0:T(8,128)}, u32[]{:S(2)}, u32[]{:S(2)}) collective-permute-start(s32[16,18,27]{2,1,0:T(8,128)S(1)} %add_add_fusion.1), channel_id=1, source_target_pairs={{0,12},{1,13},{2,14},{3,15},{4,8},{5,9},{6,10},{7,11},{8,4},{9,5},... | collective-permute-start | bytes 93320 | tf_op jit(solution)/shard_map/ppermute | solution.py:9
  17.7 1.1 %collective-permute-start.8 = (f32[128,256]{1,0:T(8,128)S(1)}, f32[128,256]{1,0:T(8,128)}, u32[]{:S(2)}, u32[]{:S(2)}) collective-permute-start(f32[128,256]{1,0:T(8,128)S(1)} %fusion.26), channel_id=1, source_target_pairs={{0,3},{1,2},{2,1},{3,0},{4,7},{5,6},{6,5},{7,4},{8,11},{9,10},{10,... | collective-permute-start | bytes 393224 | tf_op jit(solution)/shard_map/ppermute | solution.py:9
  18.8 1.1 %collective-permute-start.7 = (f32[128,256]{1,0:T(8,128)S(1)}, f32[128,256]{1,0:T(8,128)}, u32[]{:S(2)}, u32[]{:S(2)}) collective-permute-start(f32[128,256]{1,0:T(8,128)S(1)} %fusion.26), channel_id=1, source_target_pairs={{0,2},{1,3},{2,0},{3,1},{4,6},{5,7},{6,4},{7,5},{8,10},{9,11},{10,... | collective-permute-start | bytes 393224 | tf_op jit(solution)/shard_map/ppermute | solution.py:9
  19.9 5.2 %collective-permute-done.5 = s32[16,18,27]{2,1,0:T(8,128)} collective-permute-done((s32[16,18,27]{2,1,0:T(8,128)S(1)}, s32[16,18,27]{2,1,0:T(8,128)}, u32[]{:S(2)}, u32[]{:S(2)}) %collective-permute-start.5) | collective-permute-done | bytes 31136 | tf_op jit(solution)/shard_map/ppermute | solution.py:9
  25.0 0.7 collective-permute-done.4
  26.1 1.2 %add_add_fusion = s32[16,18,27]{2,1,0:T(8,128)S(1)} fusion(s32[16,18,27]{2,1,0:T(8,128)} %collective-permute-done.4, s32[16,18,27]{2,1,0:T(8,128)} %collective-permute-done.5, s32[16,18,27]{2,1,0:T(8,128)S(1)} %add_add_fusion.1, s32[16,18,27]{2,1,0:T(8,128)} %collective-permute-done.3), kind=kLoop, calls=%fused_computation.25 | loop fusion | flops 23328 | bytes 155520 | tf_op jit(solution)/shard_map/add | solution.py:24
  27.3 0.7 copy-done.3
  28.6 0.7 iota_compare_fusion.6
  29.3 1.4 %copy.17 = pred[128,27,16]{1,2,0:T(8,128)(4,1)S(1)} copy(pred[128,27,16]{0,2,1:T(8,128)(4,1)} %iota_compare_fusion.6) | data formatting | bytes 110592 | tf_op jit(solution)/shard_map/eq | solution.py:88
  30.7 3.0 %fusion.2 = f32[128,16,384]{2,1,0:T(8,128)S(1)} fusion(pred[128,27,16]{1,2,0:T(8,128)(4,1)S(1)} %copy.17, s32[128,27]{1,0:T(8,128)} %get-tuple-element.2), kind=kOutput, calls=%fused_computation.5 | convolution fusion | flops 43794432 | bytes 3214848 | tf_op jit(solution)/shard_map/blt,blj->btj/dot_general | solution.py:89
  33.7 0.9 fusion.38
  34.7 1.1 %add_add_fusion.3 = f32[128,256]{1,0:T(8,128)S(1)} fusion(f32[128,256]{1,0:T(8,128)} %collective-permute-done.7, f32[128,256]{1,0:T(8,128)} %collective-permute-done.8, f32[128,256]{1,0:T(8,128)S(1)} %fusion.26, f32[128,256]{1,0:T(8,128)} %collective-permute-done.6), kind=kLoop, calls=%fused_computation.38 | loop fusion | flops 98304 | bytes 655360 | tf_op jit(solution)/shard_map/add | solution.py:24
  35.7 2.9 %collective-permute-start.11 = (f32[128,256]{1,0:T(8,128)S(1)}, f32[128,256]{1,0:T(8,128)S(1)}, u32[]{:S(2)}, u32[]{:S(2)}) collective-permute-start(f32[128,256]{1,0:T(8,128)S(1)} %add_add_fusion.3), channel_id=1, source_target_pairs={{0,12},{1,13},{2,14},{3,15},{4,8},{5,9},{6,10},{7,11},{8,4},{9,5},... | collective-permute-start | bytes 393224 | tf_op jit(solution)/shard_map/ppermute | solution.py:9
  39.9 4.4 %collective-permute-done.11 = f32[128,256]{1,0:T(8,128)S(1)} collective-permute-done((f32[128,256]{1,0:T(8,128)S(1)}, f32[128,256]{1,0:T(8,128)S(1)}, u32[]{:S(2)}, u32[]{:S(2)}) %collective-permute-start.11) | collective-permute-done | bytes 131104 | tf_op jit(solution)/shard_map/ppermute | solution.py:9
  44.3 2.2 %collective-permute-done.10 = f32[128,256]{1,0:T(8,128)S(1)} collective-permute-done((f32[128,256]{1,0:T(8,128)S(1)}, f32[128,256]{1,0:T(8,128)S(1)}, u32[]{:S(2)}, u32[]{:S(2)}) %collective-permute-start.10) | collective-permute-done | bytes 131104 | tf_op jit(solution)/shard_map/ppermute | solution.py:9
  46.6 1.7 %constant_dynamic-update-slice_fusion.7 = (f32[128,256]{1,0:T(8,128)S(1)}, f32[16,256]{1,0:T(8,128)S(1)}) fusion(f32[8,256,256]{2,1,0:T(8,128)S(1)} %copy-done.1, f32[16,8,256]{2,1,0:T(8,128)S(1)} %bitcast.37), kind=kOutput, calls=%fused_computation.53 | convolution fusion | flops 100663296 | bytes 2260992 | tf_op jit(solution)/shard_map/qce,cde->qd/dot_general | solution.py:72
  48.4 1.6 %collective-permute-start.12 = (f32[144,256]{1,0:T(8,128)S(1)}, f32[144,256]{1,0:T(8,128)S(1)}, u32[]{:S(2)}, u32[]{:S(2)}) collective-permute-start(f32[144,256]{1,0:T(8,128)S(1)} %pad_maximum_fusion), channel_id=1, source_target_pairs={{0,16},{16,32},{32,48},{48,64},{64,80},{80,96},{96,112},{112,0},{1... | collective-permute-start | bytes 442376 | tf_op jit(solution)/shard_map/ppermute | solution.py:14
  50.3 6.4 %collective-permute-start.18 = (f32[16,256]{1,0:T(8,128)S(1)}, f32[16,256]{1,0:T(8,128)S(1)}, u32[]{:S(2)}, u32[]{:S(2)}) collective-permute-start(f32[16,256]{1,0:T(8,128)S(1)} %get-tuple-element.7), channel_id=1, source_target_pairs={{0,96},{16,112},{32,0},{48,16},{64,32},{80,48},{96,64},{112,80},{1... | collective-permute-start | bytes 49160 | tf_op jit(solution)/shard_map/ppermute | solution.py:14
  56.7 2.3 %collective-permute-start.17 = (f32[16,256]{1,0:T(8,128)S(1)}, f32[16,256]{1,0:T(8,128)S(1)}, u32[]{:S(2)}, u32[]{:S(2)}) collective-permute-start(f32[16,256]{1,0:T(8,128)S(1)} %get-tuple-element.7), channel_id=1, source_target_pairs={{0,80},{16,96},{32,112},{48,0},{64,16},{80,32},{96,48},{112,64},{1... | collective-permute-start | bytes 49160 | tf_op jit(solution)/shard_map/ppermute | solution.py:14
  59.1 0.9 collective-permute-start.15
  60.0 2.6 %collective-permute-start.14 = (f32[16,256]{1,0:T(8,128)S(1)}, f32[16,256]{1,0:T(8,128)S(1)}, u32[]{:S(2)}, u32[]{:S(2)}) collective-permute-start(f32[16,256]{1,0:T(8,128)S(1)} %get-tuple-element.7), channel_id=1, source_target_pairs={{0,32},{16,48},{32,64},{48,80},{64,96},{80,112},{96,0},{112,16},{1... | collective-permute-start | bytes 49160 | tf_op jit(solution)/shard_map/ppermute | solution.py:14
  62.5 5.1 %collective-permute-done.14 = f32[16,256]{1,0:T(8,128)S(1)} collective-permute-done((f32[16,256]{1,0:T(8,128)S(1)}, f32[16,256]{1,0:T(8,128)S(1)}, u32[]{:S(2)}, u32[]{:S(2)}) %collective-permute-start.14) | collective-permute-done | bytes 16416 | tf_op jit(solution)/shard_map/ppermute | solution.py:14
  67.6 2.9 %collective-permute-start.13 = (f32[144,256]{1,0:T(8,128)S(1)}, f32[144,256]{1,0:T(8,128)S(1)}, u32[]{:S(2)}, u32[]{:S(2)}) collective-permute-start(f32[144,256]{1,0:T(8,128)S(1)} %pad_maximum_fusion), channel_id=1, source_target_pairs={{0,112},{16,0},{32,16},{48,32},{64,48},{80,64},{96,80},{112,96},{1... | collective-permute-start | bytes 442376 | tf_op jit(solution)/shard_map/ppermute | solution.py:14
  70.6 4.2 %collective-permute-done.13 = f32[144,256]{1,0:T(8,128)S(1)} collective-permute-done((f32[144,256]{1,0:T(8,128)S(1)}, f32[144,256]{1,0:T(8,128)S(1)}, u32[]{:S(2)}, u32[]{:S(2)}) %collective-permute-start.13) | collective-permute-done | bytes 147488 | tf_op jit(solution)/shard_map/ppermute | solution.py:14
  75.2 4.5 %fusion.3 = f32[128,16,256]{2,0,1:T(8,128)S(1)} fusion(f32[128,16,384]{2,1,0:T(8,128)S(1)} %fusion.2, f32[128,256]{1,0:T(8,128)S(1)} %slice_select_fusion, f32[128,256]{1,0:T(8,128)S(1)} %add_add_fusion.2, f32[128,256]{1,0:T(8,128)S(1)} %slice_select_fusion.1), kind=kOutput, calls=%fused_computation.6 | convolution fusion | flops 2416115712 | bytes 5636096 | tf_op jit(solution)/shard_map/btj,jk->btk/dot_general | solution.py:90
  79.7 4.4 %fusion.11 = f32[144,256]{1,0:T(8,128)S(1)} fusion(f32[16,256,256]{2,1,0:T(8,128)S(1)} %copy-done.2, f32[16,16,256]{2,0,1:T(8,128)S(1)} %fusion.19, f32[128,16,256]{2,0,1:T(8,128)S(1)} %fusion.3), kind=kOutput, calls=%fused_computation.14 | convolution fusion | flops 1812529152 | bytes 6701056 | tf_op jit(solution)/shard_map/btk,tlk->bl/dot_general | solution.py:97
  84.1 1.1 %fusion.29 = f32[16,8,256]{2,0,1:T(8,128)S(1)} fusion(f32[8,256,256]{2,1,0:T(8,128)S(1)} %copy-done.1, f32[144,256]{1,0:T(8,128)S(1)} %fusion.11), kind=kOutput, calls=%fused_computation.55 | convolution fusion | flops 100663296 | bytes 2244608 | tf_op jit(solution)/shard_map/qd,cds->qcs/dot_general | solution.py:100
  86.2 8.1 %fusion.10 = bf16[96,128,128]{2,1,0:T(8,128)(2,1)} fusion(bf16[96,128,256]{2,1,0:T(8,128)(2,1)} %param.12, bf16[96,128,256]{2,1,0:T(8,128)(2,1)} %param.11, f32[96,256]{1,0:T(8,128)S(1)} %fusion.25), kind=kOutput, calls=%fused_computation.13 | convolution fusion | flops 816316416 | bytes 15826944 | tf_op jit(solution)/shard_map/bmk,bnk->bmn/dot_general | solution.py:107
  (60 shorter events, 6.3 us)
Async XLA Ops:
  0.6 3.2 %copy-start = (bf16[96,128,128]{2,1,0:T(8,128)(2,1)S(1)}, bf16[96,128,128]{2,1,0:T(8,128)(2,1)}, u32[]{:S(2)}) copy-start(bf16[96,128,128]{2,1,0:T(8,128)(2,1)} %param.10) | copy-start | bytes 9437188
  1.6 9.1 %copy-start.4 = (s32[8,27]{1,0:T(8,128)S(1)}, s32[8,27]{1,0:T(8,128)}, u32[]{:S(2)}) copy-start(s32[8,27]{1,0:T(8,128)} %param.15) | copy-start | bytes 2596
  1.6 9.1 %copy-start.5 = (s32[8,27]{1,0:T(8,128)S(1)}, s32[8,27]{1,0:T(8,128)}, u32[]{:S(2)}) copy-start(s32[8,27]{1,0:T(8,128)} %param.14) | copy-start | bytes 2596
  1.6 9.1 %copy-start.7 = (s32[1,27]{1,0:T(1,128)S(1)}, s32[1,27]{1,0:T(1,128)}, u32[]{:S(2)}) copy-start(s32[1,27]{1,0:T(1,128)} %param.17) | copy-start | bytes 328
  1.6 9.1 %copy-start.8 = (s32[1,27]{1,0:T(1,128)S(1)}, s32[1,27]{1,0:T(1,128)}, u32[]{:S(2)}) copy-start(s32[1,27]{1,0:T(1,128)} %param.16) | copy-start | bytes 328
  1.6 15.7 %copy-start.6 = (s32[96]{0:T(128)S(1)}, s32[96]{0:T(128)}, u32[]{:S(2)}) copy-start(s32[96]{0:T(128)} %param.13) | copy-start | bytes 1156
  1.6 9.1 %collective-permute-start.2 = (s32[16,18,27]{2,1,0:T(8,128)S(1)}, s32[16,18,27]{2,1,0:T(8,128)S(1)}, u32[]{:S(2)}, u32[]{:S(2)}) collective-permute-start(s32[16,18,27]{2,1,0:T(8,128)S(1)} %fusion.30), channel_id=1, source_target_pairs={{0,3},{1,2},{2,1},{3,0},{4,7},{5,6},{6,5},{7,4},{8,11},{9,10},{10,... | collective-permute-start | bytes 93320 | tf_op jit(solution)/shard_map/ppermute | solution.py:9
  3.2 9.9 %collective-permute-start.1 = (s32[16,18,27]{2,1,0:T(8,128)S(1)}, s32[16,18,27]{2,1,0:T(8,128)S(1)}, u32[]{:S(2)}, u32[]{:S(2)}) collective-permute-start(s32[16,18,27]{2,1,0:T(8,128)S(1)} %fusion.30), channel_id=1, source_target_pairs={{0,2},{1,3},{2,0},{3,1},{4,6},{5,7},{6,4},{7,5},{8,10},{9,11},{10,... | collective-permute-start | bytes 93320 | tf_op jit(solution)/shard_map/ppermute | solution.py:9
  3.8 6.9 %collective-permute-start = (s32[16,18,27]{2,1,0:T(8,128)S(1)}, s32[16,18,27]{2,1,0:T(8,128)S(1)}, u32[]{:S(2)}, u32[]{:S(2)}) collective-permute-start(s32[16,18,27]{2,1,0:T(8,128)S(1)} %fusion.30), channel_id=1, source_target_pairs={{0,1},{1,0},{2,3},{3,2},{4,5},{5,4},{6,7},{7,6},{8,9},{9,8},{10,11... | collective-permute-start | bytes 93320 | tf_op jit(solution)/shard_map/ppermute | solution.py:9
  13.2 11.9 %collective-permute-start.5 = (s32[16,18,27]{2,1,0:T(8,128)S(1)}, s32[16,18,27]{2,1,0:T(8,128)}, u32[]{:S(2)}, u32[]{:S(2)}) collective-permute-start(s32[16,18,27]{2,1,0:T(8,128)S(1)} %add_add_fusion.1), channel_id=1, source_target_pairs={{0,12},{1,13},{2,14},{3,15},{4,8},{5,9},{6,10},{7,11},{8,4},{9,5},... | collective-permute-start | bytes 93320 | tf_op jit(solution)/shard_map/ppermute | solution.py:9
  16.4 9.4 %collective-permute-start.4 = (s32[16,18,27]{2,1,0:T(8,128)S(1)}, s32[16,18,27]{2,1,0:T(8,128)}, u32[]{:S(2)}, u32[]{:S(2)}) collective-permute-start(s32[16,18,27]{2,1,0:T(8,128)S(1)} %add_add_fusion.1), channel_id=1, source_target_pairs={{0,8},{1,9},{2,10},{3,11},{4,12},{5,13},{6,14},{7,15},{8,0},{9,1},... | collective-permute-start | bytes 93320 | tf_op jit(solution)/shard_map/ppermute | solution.py:9
  17.0 9.1 %collective-permute-start.3 = (s32[16,18,27]{2,1,0:T(8,128)S(1)}, s32[16,18,27]{2,1,0:T(8,128)}, u32[]{:S(2)}, u32[]{:S(2)}) collective-permute-start(s32[16,18,27]{2,1,0:T(8,128)S(1)} %add_add_fusion.1), channel_id=1, source_target_pairs={{0,4},{1,5},{2,6},{3,7},{4,0},{5,1},{6,2},{7,3},{8,12},{9,13},{10,... | collective-permute-start | bytes 93320 | tf_op jit(solution)/shard_map/ppermute | solution.py:9
  17.7 17.0 %collective-permute-start.8 = (f32[128,256]{1,0:T(8,128)S(1)}, f32[128,256]{1,0:T(8,128)}, u32[]{:S(2)}, u32[]{:S(2)}) collective-permute-start(f32[128,256]{1,0:T(8,128)S(1)} %fusion.26), channel_id=1, source_target_pairs={{0,3},{1,2},{2,1},{3,0},{4,7},{5,6},{6,5},{7,4},{8,11},{9,10},{10,... | collective-permute-start | bytes 393224 | tf_op jit(solution)/shard_map/ppermute | solution.py:9
  18.8 15.8 %collective-permute-start.7 = (f32[128,256]{1,0:T(8,128)S(1)}, f32[128,256]{1,0:T(8,128)}, u32[]{:S(2)}, u32[]{:S(2)}) collective-permute-start(f32[128,256]{1,0:T(8,128)S(1)} %fusion.26), channel_id=1, source_target_pairs={{0,2},{1,3},{2,0},{3,1},{4,6},{5,7},{6,4},{7,5},{8,10},{9,11},{10,... | collective-permute-start | bytes 393224 | tf_op jit(solution)/shard_map/ppermute | solution.py:9
  25.0 9.6 %collective-permute-start.6 = (f32[128,256]{1,0:T(8,128)S(1)}, f32[128,256]{1,0:T(8,128)}, u32[]{:S(2)}, u32[]{:S(2)}) collective-permute-start(f32[128,256]{1,0:T(8,128)S(1)} %fusion.26), channel_id=1, source_target_pairs={{0,1},{1,0},{2,3},{3,2},{4,5},{5,4},{6,7},{7,6},{8,9},{9,8},{10,11... | collective-permute-start | bytes 393224 | tf_op jit(solution)/shard_map/ppermute | solution.py:9
  27.3 0.7 copy-start.3
  30.7 15.9 %copy-start.1 = (f32[8,256,256]{2,1,0:T(8,128)S(1)}, f32[8,256,256]{2,1,0:T(8,128)}, u32[]{:S(2)}) copy-start(f32[8,256,256]{2,1,0:T(8,128)} %param.19) | copy-start | bytes 6291460
  35.7 8.6 %collective-permute-start.11 = (f32[128,256]{1,0:T(8,128)S(1)}, f32[128,256]{1,0:T(8,128)S(1)}, u32[]{:S(2)}, u32[]{:S(2)}) collective-permute-start(f32[128,256]{1,0:T(8,128)S(1)} %add_add_fusion.3), channel_id=1, source_target_pairs={{0,12},{1,13},{2,14},{3,15},{4,8},{5,9},{6,10},{7,11},{8,4},{9,5},... | collective-permute-start | bytes 393224 | tf_op jit(solution)/shard_map/ppermute | solution.py:9
  38.7 7.9 %collective-permute-start.10 = (f32[128,256]{1,0:T(8,128)S(1)}, f32[128,256]{1,0:T(8,128)S(1)}, u32[]{:S(2)}, u32[]{:S(2)}) collective-permute-start(f32[128,256]{1,0:T(8,128)S(1)} %add_add_fusion.3), channel_id=1, source_target_pairs={{0,8},{1,9},{2,10},{3,11},{4,12},{5,13},{6,14},{7,15},{8,0},{9,1},... | collective-permute-start | bytes 393224 | tf_op jit(solution)/shard_map/ppermute | solution.py:9
  39.3 7.2 %collective-permute-start.9 = (f32[128,256]{1,0:T(8,128)S(1)}, f32[128,256]{1,0:T(8,128)S(1)}, u32[]{:S(2)}, u32[]{:S(2)}) collective-permute-start(f32[128,256]{1,0:T(8,128)S(1)} %add_add_fusion.3), channel_id=1, source_target_pairs={{0,4},{1,5},{2,6},{3,7},{4,0},{5,1},{6,2},{7,3},{8,12},{9,13},{10,... | collective-permute-start | bytes 393224 | tf_op jit(solution)/shard_map/ppermute | solution.py:9
  48.4 11.6 %collective-permute-start.12 = (f32[144,256]{1,0:T(8,128)S(1)}, f32[144,256]{1,0:T(8,128)S(1)}, u32[]{:S(2)}, u32[]{:S(2)}) collective-permute-start(f32[144,256]{1,0:T(8,128)S(1)} %pad_maximum_fusion), channel_id=1, source_target_pairs={{0,16},{16,32},{32,48},{48,64},{64,80},{80,96},{96,112},{112,0},{1... | collective-permute-start | bytes 442376 | tf_op jit(solution)/shard_map/ppermute | solution.py:14
  50.3 20.2 %collective-permute-start.18 = (f32[16,256]{1,0:T(8,128)S(1)}, f32[16,256]{1,0:T(8,128)S(1)}, u32[]{:S(2)}, u32[]{:S(2)}) collective-permute-start(f32[16,256]{1,0:T(8,128)S(1)} %get-tuple-element.7), channel_id=1, source_target_pairs={{0,96},{16,112},{32,0},{48,16},{64,32},{80,48},{96,64},{112,80},{1... | collective-permute-start | bytes 49160 | tf_op jit(solution)/shard_map/ppermute | solution.py:14
  56.7 13.8 %collective-permute-start.17 = (f32[16,256]{1,0:T(8,128)S(1)}, f32[16,256]{1,0:T(8,128)S(1)}, u32[]{:S(2)}, u32[]{:S(2)}) collective-permute-start(f32[16,256]{1,0:T(8,128)S(1)} %get-tuple-element.7), channel_id=1, source_target_pairs={{0,80},{16,96},{32,112},{48,0},{64,16},{80,32},{96,48},{112,64},{1... | collective-permute-start | bytes 49160 | tf_op jit(solution)/shard_map/ppermute | solution.py:14
  59.0 11.5 %collective-permute-start.16 = (f32[16,256]{1,0:T(8,128)S(1)}, f32[16,256]{1,0:T(8,128)S(1)}, u32[]{:S(2)}, u32[]{:S(2)}) collective-permute-start(f32[16,256]{1,0:T(8,128)S(1)} %get-tuple-element.7), channel_id=1, source_target_pairs={{0,64},{16,80},{32,96},{48,112},{64,0},{80,16},{96,32},{112,48},{1... | collective-permute-start | bytes 49160 | tf_op jit(solution)/shard_map/ppermute | solution.py:14
  59.1 11.4 %collective-permute-start.15 = (f32[16,256]{1,0:T(8,128)S(1)}, f32[16,256]{1,0:T(8,128)S(1)}, u32[]{:S(2)}, u32[]{:S(2)}) collective-permute-start(f32[16,256]{1,0:T(8,128)S(1)} %get-tuple-element.7), channel_id=1, source_target_pairs={{0,48},{16,64},{32,80},{48,96},{64,112},{80,0},{96,16},{112,32},{1... | collective-permute-start | bytes 49160 | tf_op jit(solution)/shard_map/ppermute | solution.py:14
  60.0 7.6 %collective-permute-start.14 = (f32[16,256]{1,0:T(8,128)S(1)}, f32[16,256]{1,0:T(8,128)S(1)}, u32[]{:S(2)}, u32[]{:S(2)}) collective-permute-start(f32[16,256]{1,0:T(8,128)S(1)} %get-tuple-element.7), channel_id=1, source_target_pairs={{0,32},{16,48},{32,64},{48,80},{64,96},{80,112},{96,0},{112,16},{1... | collective-permute-start | bytes 49160 | tf_op jit(solution)/shard_map/ppermute | solution.py:14
  67.6 7.2 %collective-permute-start.13 = (f32[144,256]{1,0:T(8,128)S(1)}, f32[144,256]{1,0:T(8,128)S(1)}, u32[]{:S(2)}, u32[]{:S(2)}) collective-permute-start(f32[144,256]{1,0:T(8,128)S(1)} %pad_maximum_fusion), channel_id=1, source_target_pairs={{0,112},{16,0},{32,16},{48,32},{64,48},{80,64},{96,80},{112,96},{1... | collective-permute-start | bytes 442376 | tf_op jit(solution)/shard_map/ppermute | solution.py:14
  75.1 4.6 %copy-start.2 = (f32[16,256,256]{2,1,0:T(8,128)S(1)}, f32[16,256,256]{2,1,0:T(8,128)}, u32[]{:S(2)}) copy-start(f32[16,256,256]{2,1,0:T(8,128)} %param.18) | copy-start | bytes 12582916

commit v3 on v2

--- a/solution.py
+++ b/solution.py
@@ -9,23 +9,24 @@
     return lax.ppermute(x, axis, [(i, i ^ mask) for i in range(count)])
 
 
-def shift(x, axis, step):
+def butterfly_sum(x, axis):
     count = lax.axis_size(axis)
-    return lax.ppermute(x, axis, [(i, (i + step) % count) for i in range(count)])
+    mask = 1
+    while mask < count:
+        x = x + exchange(x, axis, mask)
+        mask *= 2
+    return x
 
 
-def group_sum(x, axis):
+def butterfly_gather(x, axis):
     count = lax.axis_size(axis)
-    stride = 1
-    while stride < count:
-        if count % (4 * stride) == 0:
-            near = x + exchange(x, axis, stride)
-            far = exchange(x, axis, 2 * stride) + exchange(x, axis, 3 * stride)
-            x = near + far
-            stride *= 4
-        else:
-            x = x + exchange(x, axis, stride)
-            stride *= 2
+    me = lax.axis_index(axis)
+    mask = 1
+    while mask < count:
+        other = exchange(x, axis, mask)
+        low = (me // mask) % 2 == 0
+        x = jnp.where(low, jnp.concatenate([x, other], 0), jnp.concatenate([other, x], 0))
+        mask *= 2
     return x
 
 
@@ -52,13 +53,12 @@
     coeffs = translation.shape[1]
 
     lists = jnp.concatenate([leaf_src, leaf_type, coarse_src, coarse_type], axis=0)
-    table = jnp.zeros((n_blk,) + lists.shape, jnp.int32)
-    table = lax.dynamic_update_index_in_dim(table, lists, me, 0)
-    table = group_sum(table, "blk")
-    dom_src = table[:, :leaves].reshape(box_dom, -1)
-    dom_type = table[:, leaves : 2 * leaves].reshape(box_dom, -1)
-    dom_csrc = table[:, 2 * leaves]
-    dom_ctype = table[:, 2 * leaves + 1]
+    flat = lists.size
+    table = jnp.zeros((n_blk, flat), jnp.float32)
+    table = lax.dynamic_update_index_in_dim(table, lists.reshape(flat).astype(jnp.float32), me, 0)
+    table_rows = -(-n_blk * flat // coeffs)
+    table = jnp.pad(table.reshape(-1), (0, table_rows * coeffs - n_blk * flat))
+    table = table.reshape(table_rows, coeffs)
 
     inner = jnp.einsum("bmn,bmk->bnk", density, bra_table, preferred_element_type=jnp.float32)
     moments = jnp.sum(inner * ket_table.astype(jnp.float32), axis=1)
@@ -68,28 +68,33 @@
     partial_moments = lax.dot_general(
         box_hot, moments, (((0,), (0,)), ((), ())), precision=top
     )
-    domain = group_sum(partial_moments, "blk")
+    summed = butterfly_sum(jnp.concatenate([partial_moments, table], axis=0), "blk")
+    domain = summed[:box_dom]
+    table = summed[box_dom:].reshape(-1)[: n_blk * flat].reshape((n_blk,) + lists.shape)
+    table = table.astype(jnp.int32)
+    dom_src = table[:, :leaves].reshape(box_dom, -1)
+    dom_type = table[:, leaves : 2 * leaves].reshape(box_dom, -1)
+    dom_csrc = table[:, 2 * leaves]
+    dom_ctype = table[:, 2 * leaves + 1]
+
     domain_parents = jnp.einsum(
         "qce,cde->qd", domain.reshape(n_blk, leaves, coeffs), upward_translation_table, precision=top
     )
-    near = jnp.concatenate([domain, domain_parents], axis=0)
-    from_low = shift(near, "space", 1)
-    from_high = shift(near, "space", n_space - 1)
-    low = jnp.where(here > 0, from_low[:box_dom], 0.0)
-    high = jnp.where(here < n_space - 1, from_high[:box_dom], 0.0)
-    window = jnp.concatenate([low, domain, high], axis=0)
-    by_step = [domain_parents, from_low[box_dom:]]
-    by_step += [shift(domain_parents, "space", k) for k in range(2, n_space - 1)]
-    by_step += [from_high[box_dom:]]
-    all_parents = jnp.concatenate(by_step, axis=0)
-    csrc = ((here - dom_csrc // n_blk) % n_space) * n_blk + dom_csrc % n_blk
+    everything = butterfly_gather(
+        jnp.concatenate([domain, domain_parents], axis=0)[None], "space"
+    )
+    all_leaves = everything[:, :box_dom]
+    all_parents = everything[:, box_dom:].reshape(-1, coeffs)
+    zero = jnp.zeros((1, box_dom, coeffs), jnp.float32)
+    padded = jnp.concatenate([zero, all_leaves, zero], axis=0)
+    window = lax.dynamic_slice_in_dim(padded, here, 3, axis=0).reshape(3 * box_dom, coeffs)
 
     src_hot = (dom_src[..., None] == jnp.arange(3 * box_dom, dtype=jnp.int32)).astype(jnp.bfloat16)
     type_hot = (dom_type[..., None] == jnp.arange(n_types, dtype=jnp.int32)).astype(jnp.bfloat16)
     counts = jnp.einsum("blt,blj->btj", type_hot, src_hot, preferred_element_type=jnp.float32)
     gathered = jnp.einsum("btj,jk->btk", counts, window, precision=top)
     n_parents = all_parents.shape[0]
-    csrc_hot = (csrc[..., None] == jnp.arange(n_parents, dtype=jnp.int32)).astype(jnp.bfloat16)
+    csrc_hot = (dom_csrc[..., None] == jnp.arange(n_parents, dtype=jnp.int32)).astype(jnp.bfloat16)
     ctype_hot = (dom_ctype[..., None] == jnp.arange(n_types, dtype=jnp.int32)).astype(jnp.bfloat16)
     ccounts = jnp.einsum("pet,peq->ptq", ctype_hot, csrc_hot, preferred_element_type=jnp.float32)
     cgathered = jnp.einsum("ptq,qk->ptk", ccounts, all_parents, precision=top)

time: 95 us -> 85.6 us (0.901)
  starting transfers between devices: 29.4 us -> 14.9 us
  local copies, waits for them, and re-layouts: 4.35 us -> 7.35 us
  other arithmetic: 4.05 us -> 6.75 us
    ppermute x7 -> x0, starting transfers between devices: 16.7 us -> none  [shift(): lax.ppermute(x, axis, [(i, (i + step) % count) for i in range(count)])]
    ppermute x7 -> x0, waiting for transfers between devices: 9.27 us -> none  [shift(): lax.ppermute(x, axis, [(i, (i + step) % count) for i in range(count)])]
    ppermute x12 -> x7, waiting for transfers between devices: 15.2 us -> 23.8 us  [exchange(): return lax.ppermute(x, axis, [(i, i ^ mask) for i in range(count)])]
    select_n x2 -> x3, other arithmetic: 0.03 us -> 4.93 us  [butterfly_gather(): jnp.where(low, jnp.concatenate([x, other], 0), jnp.concatenate([other, x]...]
    add x6 -> x4, other arithmetic: 2.32 us -> 0.08 us  [butterfly_sum(): x = x + exchange(x, axis, mask)]
    ppermute x12 -> x7, starting transfers between devices: 12.8 us -> 14.9 us  [exchange(): return lax.ppermute(x, axis, [(i, i ^ mask) for i in range(count)])]
    dot_general x1, matrix products: 1.74 us -> 3.32 us  [shards(): jnp.einsum('qce,cde->qd', domain.reshape(n_blk, leaves, coeffs), upward_t...]
    dot_general x1, matrix products: 2.99 us -> 2.02 us  [shards(): jnp.einsum('blt,blj->btj', type_hot, src_hot, preferred_element_type=jnp....]
  transfers between devices with their start and end apart: 19 -> 7, of which waited for: 8 -> 7; matrix products, arithmetic and copies ran while one was open for 16% -> 10% of each run, Pallas kernels for 0% -> 0%
where the time goes in v3:
time: 85.6 us; the launch traced here: 85.2 us
  matrix products  31.4 us (37%)
  waiting for transfers between devices  23.8 us (28%)
  starting transfers between devices  14.9 us (17%)
  local copies, waits for them, and re-layouts  7.35 us (9%)
  other arithmetic  6.75 us (8%)
  between operations  0.9 us (1%)
    ppermute x7, waiting for transfers between devices, exchange(): return lax.ppermute(x, axis, [(i, i ^ mask) for i in range(count)])  23.8 us
    ppermute x7, starting transfers between devices, exchange(): return lax.ppermute(x, axis, [(i, i ^ mask) for i in range(count)])  14.9 us
    dot_general x1, matrix products, shards(): jnp.einsum('bmk,bnk->bmn', scaled, ket_table, preferred_element_type=jnp....  8.08 us
    dot_general x1, matrix products, shards(): jnp.einsum('bmn,bmk->bnk', density, bra_table, preferred_element_type=jnp...  6.82 us
    select_n x3, other arithmetic, butterfly_gather(): jnp.where(low, jnp.concatenate([x, other], 0), jnp.concatenate([other, x]...  4.93 us
    dot_general x1, matrix products, shards(): gathered = jnp.einsum('btj,jk->btk', counts, window, precision=top)  4.52 us
    dot_general x1, matrix products, shards(): far = jnp.einsum('btk,tlk->bl', rows, translation, precision=top)  4.38 us
    dot_general x1, matrix products, shards(): jnp.einsum('qce,cde->qd', domain.reshape(n_blk, leaves, coeffs), upward_t...  3.32 us
  transfers between devices with their start and end apart: 7, of which 7 were waited for; matrix products, arithmetic and copies ran while one was open for 10% of the time, Pallas kernels for 0%

profile of v3, /device:TPU:0, one launch (start us, length us, event | category | flops | bytes accessed | tf_op | source)
XLA Modules:
  0.0 85.2 jit_solution(18107715886679520753)
XLA Ops:
  0.6 0.9 %add_convert_fusion = f32[18,27]{1,0:T(8,128)S(1)} fusion(s32[1,27]{1,0:T(1,128)} %param.17, s32[1,27]{1,0:T(1,128)} %param.16, s32[8,27]{1,0:T(8,128)} %param.15, s32[8,27]{1,0:T(8,128)} %param.14), kind=kLoop, calls=%fused_computation.46 | loop fusion | flops 1944 | bytes 3888 | tf_op jit(solution)/shard_map/convert_element_type | solution.py:58
  1.9 0.7 copy-done
  2.6 6.8 %multiply_reduce_fusion = f32[96,256]{1,0:T(8,128)S(1)} fusion(bf16[96,128,256]{2,1,0:T(8,128)(2,1)} %param.12, bf16[96,128,128]{2,1,0:T(8,128)(2,1)S(1)} %copy-done, bf16[96,128,256]{2,1,0:T(8,128)(2,1)} %param.11), kind=kOutput, calls=%fused_computation.1 | convolution fusion | flops 814718976 | bytes 15826944 | tf_op jit(solution)/shard_map/bmn,bmk->bnk/dot_general | solution.py:63
  9.9 1.4 %collective-permute-done = f32[159,256]{1,0:T(8,128)S(1)} collective-permute-done((f32[159,256]{1,0:T(8,128)S(1)}, f32[159,256]{1,0:T(8,128)S(1)}, u32[]{:S(2)}, u32[]{:S(2)}) %collective-permute-start) | collective-permute-done | bytes 162848 | tf_op jit(solution)/shard_map/ppermute | solution.py:9
  11.3 2.1 %collective-permute-start.1 = (f32[159,256]{1,0:T(8,128)S(1)}, f32[159,256]{1,0:T(8,128)S(1)}, u32[]{:S(2)}, u32[]{:S(2)}) collective-permute-start(f32[159,256]{1,0:T(8,128)S(1)} %fusion.28), channel_id=1, source_target_pairs={{0,2},{1,3},{2,0},{3,1},{4,6},{5,7},{6,4},{7,5},{8,10},{9,11},{10,... | collective-permute-start | bytes 488456 | tf_op jit(solution)/shard_map/ppermute | solution.py:9
  13.4 4.5 %collective-permute-done.1 = f32[159,256]{1,0:T(8,128)S(1)} collective-permute-done((f32[159,256]{1,0:T(8,128)S(1)}, f32[159,256]{1,0:T(8,128)S(1)}, u32[]{:S(2)}, u32[]{:S(2)}) %collective-permute-start.1) | collective-permute-done | bytes 162848 | tf_op jit(solution)/shard_map/ppermute | solution.py:9
  17.9 1.7 %collective-permute-start.2 = (f32[159,256]{1,0:T(8,128)S(1)}, f32[159,256]{1,0:T(8,128)S(1)}, u32[]{:S(2)}, u32[]{:S(2)}) collective-permute-start(f32[159,256]{1,0:T(8,128)S(1)} %add.42), channel_id=1, source_target_pairs={{0,4},{1,5},{2,6},{3,7},{4,0},{5,1},{6,2},{7,3},{8,12},{9,13},{10,... | collective-permute-start | bytes 488456 | tf_op jit(solution)/shard_map/ppermute | solution.py:9
  19.6 4.1 %collective-permute-done.2 = f32[159,256]{1,0:T(8,128)S(1)} collective-permute-done((f32[159,256]{1,0:T(8,128)S(1)}, f32[159,256]{1,0:T(8,128)S(1)}, u32[]{:S(2)}, u32[]{:S(2)}) %collective-permute-start.2) | collective-permute-done | bytes 162848 | tf_op jit(solution)/shard_map/ppermute | solution.py:9
  23.7 3.2 %collective-permute-start.3 = (f32[159,256]{1,0:T(8,128)S(1)}, f32[159,256]{1,0:T(8,128)S(1)}, u32[]{:S(2)}, u32[]{:S(2)}) collective-permute-start(f32[159,256]{1,0:T(8,128)S(1)} %add.43), channel_id=1, source_target_pairs={{0,8},{1,9},{2,10},{3,11},{4,12},{5,13},{6,14},{7,15},{8,0},{9,1},... | collective-permute-start | bytes 488456 | tf_op jit(solution)/shard_map/ppermute | solution.py:9
  26.9 3.7 %collective-permute-done.3 = f32[159,256]{1,0:T(8,128)S(1)} collective-permute-done((f32[159,256]{1,0:T(8,128)S(1)}, f32[159,256]{1,0:T(8,128)S(1)}, u32[]{:S(2)}, u32[]{:S(2)}) %collective-permute-start.3) | collective-permute-done | bytes 162848 | tf_op jit(solution)/shard_map/ppermute | solution.py:9
  30.7 3.3 %convolution_bitcast_fusion = f32[16,256]{1,0:T(8,128)S(1)} fusion(f32[8,256,256]{2,1,0:T(8,128)} %param.19, f32[16,8,256]{2,1,0:T(8,128)S(1)} %get-tuple-element.7), kind=kOutput, calls=%fused_computation.19 | convolution fusion | flops 100663296 | bytes 2244608 | tf_op jit(solution)/shard_map/qce,cde->qd/dot_general | solution.py:80
  34.0 1.5 %collective-permute-start.4 = (f32[1,144,256]{2,1,0:T(8,128)S(1)}, f32[1,144,256]{2,1,0:T(8,128)}, u32[]{:S(2)}, u32[]{:S(2)}) collective-permute-start(f32[1,144,256]{2,1,0:T(8,128)S(1)} %maximum_bitcast_fusion), channel_id=1, source_target_pairs={{0,16},{16,0},{32,48},{48,32},{64,80},{80,64},{96,112},{112,96},{1... | collective-permute-start | bytes 442376 | tf_op jit(solution)/shard_map/ppermute | solution.py:9
  35.5 0.9 %convert_element_type.43 = s32[16,18,27]{2,1,0:T(8,128)} reshape(s32[7776]{0:T(1024)S(1)} %slice_convert_fusion) | data formatting | bytes 62208 | tf_op jit(solution)/shard_map/convert_element_type | solution.py:74
  36.4 3.0 %collective-permute-done.4 = f32[1,144,256]{2,1,0:T(8,128)} collective-permute-done((f32[1,144,256]{2,1,0:T(8,128)S(1)}, f32[1,144,256]{2,1,0:T(8,128)}, u32[]{:S(2)}, u32[]{:S(2)}) %collective-permute-start.4) | collective-permute-done | bytes 147488 | tf_op jit(solution)/shard_map/ppermute | solution.py:9
  39.4 1.2 %maximum_select_fusion.2 = f32[2,144,256]{2,1,0:T(8,128)S(1)} fusion(f32[1,144,256]{2,1,0:T(8,128)} %collective-permute-done.4, f32[1,144,256]{2,1,0:T(8,128)} %copy-done.3, pred[]{:T(512)S(6)} %eq.99), kind=kLoop, calls=%fused_computation.23 | loop fusion | flops 221184 | bytes 589825 | tf_op jit(solution)/shard_map/jit(_where)/select_n | solution.py:28
  40.5 3.0 %collective-permute-start.5 = (f32[2,144,256]{2,1,0:T(8,128)S(1)}, f32[2,144,256]{2,1,0:T(8,128)}, u32[]{:S(2)}, u32[]{:S(2)}) collective-permute-start(f32[2,144,256]{2,1,0:T(8,128)S(1)} %maximum_select_fusion.2), channel_id=1, source_target_pairs={{0,32},{16,48},{32,0},{48,16},{64,96},{80,112},{96,64},{112,80},{1... | collective-permute-start | bytes 884744 | tf_op jit(solution)/shard_map/ppermute | solution.py:9
  43.5 1.5 %slice_bitcast_fusion = (s32[128,27]{1,0:T(8,128)S(1)}, s32[128,27]{1,0:T(8,128)}) fusion(s32[16,18,27]{2,1,0:T(8,128)} %convert_element_type.43), kind=kLoop, calls=%fused_computation.35 | loop fusion | bytes 55296 | tf_op jit(solution)/shard_map/eq | solution.py:92
  45.0 0.9 %copy.17 = s32[128,27]{0,1:T(8,128)S(1)} copy(s32[128,27]{1,0:T(8,128)} %get-tuple-element.3) | data formatting | bytes 27648 | tf_op jit(solution)/shard_map/eq | solution.py:93
  46.0 0.9 %fusion.29 = (s32[16,1,27]{2,1,0:T(1,128)S(1)}, s32[16,1,27]{2,1,0:T(1,128)S(1)}) fusion(s32[16,18,27]{2,1,0:T(8,128)} %convert_element_type.43), kind=kLoop, calls=%fused_computation.51 | loop fusion | bytes 6912 | tf_op jit(solution)/shard_map/slice | solution.py:78
  46.9 2.0 %collective-permute-done.5 = f32[2,144,256]{2,1,0:T(8,128)} collective-permute-done((f32[2,144,256]{2,1,0:T(8,128)S(1)}, f32[2,144,256]{2,1,0:T(8,128)}, u32[]{:S(2)}, u32[]{:S(2)}) %collective-permute-start.5) | collective-permute-done | bytes 294944 | tf_op jit(solution)/shard_map/ppermute | solution.py:9
  48.9 1.9 %maximum_select_fusion.1 = f32[4,144,256]{2,1,0:T(8,128)} fusion(f32[2,144,256]{2,1,0:T(8,128)} %collective-permute-done.5, f32[2,144,256]{2,1,0:T(8,128)S(1)} %maximum_select_fusion.2, pred[]{:T(512)S(6)} %eq.98), kind=kLoop, calls=%fused_computation.20 | loop fusion | flops 442368 | bytes 1179649 | tf_op jit(solution)/shard_map/jit(_where)/select_n | solution.py:28
  50.9 3.4 %collective-permute-start.6 = (f32[4,144,256]{2,1,0:T(8,128)}, f32[4,144,256]{2,1,0:T(8,128)}, u32[]{:S(2)}, u32[]{:S(2)}) collective-permute-start(f32[4,144,256]{2,1,0:T(8,128)} %maximum_select_fusion.1), channel_id=1, source_target_pairs={{0,64},{16,80},{32,96},{48,112},{64,0},{80,16},{96,32},{112,48},{1... | collective-permute-start | bytes 1769480 | tf_op jit(solution)/shard_map/ppermute | solution.py:9
  54.3 0.7 iota_compare_fusion.4
  55.0 1.4 %copy.18 = pred[128,27,16]{1,2,0:T(8,128)(4,1)S(1)} copy(pred[128,27,16]{0,2,1:T(8,128)(4,1)} %iota_compare_fusion.4) | data formatting | bytes 110592 | tf_op jit(solution)/shard_map/eq | solution.py:93
  56.6 2.0 %fusion.2 = f32[128,16,384]{2,1,0:T(8,128)S(1)} fusion(pred[128,27,16]{1,2,0:T(8,128)(4,1)S(1)} %copy.18, s32[128,27]{1,0:T(8,128)S(1)} %get-tuple-element.2), kind=kOutput, calls=%fused_computation.5 | convolution fusion | flops 43794432 | bytes 3214848 | tf_op jit(solution)/shard_map/blt,blj->btj/dot_general | solution.py:94
  58.6 5.1 %collective-permute-done.6 = f32[4,144,256]{2,1,0:T(8,128)} collective-permute-done((f32[4,144,256]{2,1,0:T(8,128)}, f32[4,144,256]{2,1,0:T(8,128)}, u32[]{:S(2)}, u32[]{:S(2)}) %collective-permute-start.6) | collective-permute-done | bytes 589856 | tf_op jit(solution)/shard_map/ppermute | solution.py:9
  63.7 1.8 %maximum_select_fusion = f32[8,144,256]{2,1,0:T(8,128)S(1)} fusion(f32[4,144,256]{2,1,0:T(8,128)} %collective-permute-done.6, f32[4,144,256]{2,1,0:T(8,128)} %maximum_select_fusion.1, pred[]{:T(512)S(6)} %eq.97), kind=kLoop, calls=%fused_computation.17 | loop fusion | flops 884736 | bytes 2359297 | tf_op jit(solution)/shard_map/jit(_where)/select_n | solution.py:28
  66.1 4.5 %fusion.3 = f32[128,16,256]{2,0,1:T(8,128)S(1)} fusion(f32[384,256,1]{1,0,2:T(8,128)S(1)} %bitcast.36, f32[128,16,384]{2,1,0:T(8,128)S(1)} %fusion.2), kind=kOutput, calls=%fused_computation.6 | convolution fusion | flops 2415919104 | bytes 5636096 | tf_op jit(solution)/shard_map/btj,jk->btk/dot_general | solution.py:95
  70.7 4.4 %fusion.11 = f32[144,256]{1,0:T(8,128)S(1)} fusion(f32[16,256,256]{2,1,0:T(8,128)S(1)} %copy-done.2, f32[16,16,256]{2,0,1:T(8,128)S(1)} %fusion.17, f32[128,16,256]{2,0,1:T(8,128)S(1)} %fusion.3), kind=kOutput, calls=%fused_computation.18 | convolution fusion | flops 1812529152 | bytes 6701056 | tf_op jit(solution)/shard_map/btk,tlk->bl/dot_general | solution.py:102
  75.1 1.1 %fusion.26 = f32[16,8,256]{2,0,1:T(8,128)S(1)} fusion(f32[8,256,256]{2,1,0:T(8,128)S(1)} %copy-done.1, f32[144,256]{1,0:T(8,128)S(1)} %fusion.11), kind=kOutput, calls=%fused_computation.45 | convolution fusion | flops 100663296 | bytes 2244608 | tf_op jit(solution)/shard_map/qd,cds->qcs/dot_general | solution.py:105
  76.5 0.6 constant_dynamic-slice_fusion
  77.1 8.1 %fusion.10 = bf16[96,128,128]{2,1,0:T(8,128)(2,1)} fusion(bf16[96,128,256]{2,1,0:T(8,128)(2,1)} %param.12, bf16[96,128,256]{2,1,0:T(8,128)(2,1)} %param.11, f32[96,256]{1,0:T(8,128)S(1)} %fusion.22), kind=kOutput, calls=%fused_computation.13 | convolution fusion | flops 816316416 | bytes 15826944 | tf_op jit(solution)/shard_map/bmk,bnk->bmn/dot_general | solution.py:112
  (35 shorter events, 2.0 us)
Async XLA Ops:
  0.6 2.0 %copy-start = (bf16[96,128,128]{2,1,0:T(8,128)(2,1)S(1)}, bf16[96,128,128]{2,1,0:T(8,128)(2,1)}, u32[]{:S(2)}) copy-start(bf16[96,128,128]{2,1,0:T(8,128)(2,1)} %param.10) | copy-start | bytes 9437188
  2.6 6.8 %copy-start.4 = (s32[96]{0:T(128)S(1)}, s32[96]{0:T(128)}, u32[]{:S(2)}) copy-start(s32[96]{0:T(128)} %param.13) | copy-start | bytes 1156
  9.8 1.5 %collective-permute-start = (f32[159,256]{1,0:T(8,128)S(1)}, f32[159,256]{1,0:T(8,128)S(1)}, u32[]{:S(2)}, u32[]{:S(2)}) collective-permute-start(f32[159,256]{1,0:T(8,128)S(1)} %pad_maximum_fusion), channel_id=1, source_target_pairs={{0,1},{1,0},{2,3},{3,2},{4,5},{5,4},{6,7},{7,6},{8,9},{9,8},{10,11... | collective-permute-start | bytes 488456 | tf_op jit(solution)/shard_map/ppermute | solution.py:9
  11.3 6.6 %collective-permute-start.1 = (f32[159,256]{1,0:T(8,128)S(1)}, f32[159,256]{1,0:T(8,128)S(1)}, u32[]{:S(2)}, u32[]{:S(2)}) collective-permute-start(f32[159,256]{1,0:T(8,128)S(1)} %fusion.28), channel_id=1, source_target_pairs={{0,2},{1,3},{2,0},{3,1},{4,6},{5,7},{6,4},{7,5},{8,10},{9,11},{10,... | collective-permute-start | bytes 488456 | tf_op jit(solution)/shard_map/ppermute | solution.py:9
  17.9 5.8 %collective-permute-start.2 = (f32[159,256]{1,0:T(8,128)S(1)}, f32[159,256]{1,0:T(8,128)S(1)}, u32[]{:S(2)}, u32[]{:S(2)}) collective-permute-start(f32[159,256]{1,0:T(8,128)S(1)} %add.42), channel_id=1, source_target_pairs={{0,4},{1,5},{2,6},{3,7},{4,0},{5,1},{6,2},{7,3},{8,12},{9,13},{10,... | collective-permute-start | bytes 488456 | tf_op jit(solution)/shard_map/ppermute | solution.py:9
  23.7 6.9 %collective-permute-start.3 = (f32[159,256]{1,0:T(8,128)S(1)}, f32[159,256]{1,0:T(8,128)S(1)}, u32[]{:S(2)}, u32[]{:S(2)}) collective-permute-start(f32[159,256]{1,0:T(8,128)S(1)} %add.43), channel_id=1, source_target_pairs={{0,8},{1,9},{2,10},{3,11},{4,12},{5,13},{6,14},{7,15},{8,0},{9,1},... | collective-permute-start | bytes 488456 | tf_op jit(solution)/shard_map/ppermute | solution.py:9
  34.0 2.4 %copy-start.3 = (f32[1,144,256]{2,1,0:T(8,128)}, f32[1,144,256]{2,1,0:T(8,128)S(1)}, u32[]{:S(2)}) copy-start(f32[1,144,256]{2,1,0:T(8,128)S(1)} %maximum_bitcast_fusion) | copy-start | bytes 442372
  34.0 5.3 %collective-permute-start.4 = (f32[1,144,256]{2,1,0:T(8,128)S(1)}, f32[1,144,256]{2,1,0:T(8,128)}, u32[]{:S(2)}, u32[]{:S(2)}) collective-permute-start(f32[1,144,256]{2,1,0:T(8,128)S(1)} %maximum_bitcast_fusion), channel_id=1, source_target_pairs={{0,16},{16,0},{32,48},{48,32},{64,80},{80,64},{96,112},{112,96},{1... | collective-permute-start | bytes 442376 | tf_op jit(solution)/shard_map/ppermute | solution.py:9
  40.5 8.4 %collective-permute-start.5 = (f32[2,144,256]{2,1,0:T(8,128)S(1)}, f32[2,144,256]{2,1,0:T(8,128)}, u32[]{:S(2)}, u32[]{:S(2)}) collective-permute-start(f32[2,144,256]{2,1,0:T(8,128)S(1)} %maximum_select_fusion.2), channel_id=1, source_target_pairs={{0,32},{16,48},{32,0},{48,16},{64,96},{80,112},{96,64},{112,80},{1... | collective-permute-start | bytes 884744 | tf_op jit(solution)/shard_map/ppermute | solution.py:9
  50.9 12.8 %collective-permute-start.6 = (f32[4,144,256]{2,1,0:T(8,128)}, f32[4,144,256]{2,1,0:T(8,128)}, u32[]{:S(2)}, u32[]{:S(2)}) collective-permute-start(f32[4,144,256]{2,1,0:T(8,128)} %maximum_select_fusion.1), channel_id=1, source_target_pairs={{0,64},{16,80},{32,96},{48,112},{64,0},{80,16},{96,32},{112,48},{1... | collective-permute-start | bytes 1769480 | tf_op jit(solution)/shard_map/ppermute | solution.py:9
  66.1 4.5 %copy-start.2 = (f32[16,256,256]{2,1,0:T(8,128)S(1)}, f32[16,256,256]{2,1,0:T(8,128)}, u32[]{:S(2)}) copy-start(f32[16,256,256]{2,1,0:T(8,128)} %param.18) | copy-start | bytes 12582916
  70.7 4.4 %copy-start.1 = (f32[8,256,256]{2,1,0:T(8,128)S(1)}, f32[8,256,256]{2,1,0:T(8,128)}, u32[]{:S(2)}) copy-start(f32[8,256,256]{2,1,0:T(8,128)} %param.19) | copy-start | bytes 6291460

commit v4 on v3

--- a/solution.py
+++ b/solution.py
@@ -42,7 +42,7 @@
     translation,
     upward_translation_table,
 ):
-    top = lax.Precision.HIGHEST
+    top = lax.Precision.HIGH
     n_blk = lax.axis_size("blk")
     n_space = lax.axis_size("space")
     me = lax.axis_index("blk")
@@ -80,14 +80,28 @@
     domain_parents = jnp.einsum(
         "qce,cde->qd", domain.reshape(n_blk, leaves, coeffs), upward_translation_table, precision=top
     )
-    everything = butterfly_gather(
-        jnp.concatenate([domain, domain_parents], axis=0)[None], "space"
-    )
-    all_leaves = everything[:, :box_dom]
-    all_parents = everything[:, box_dom:].reshape(-1, coeffs)
-    zero = jnp.zeros((1, box_dom, coeffs), jnp.float32)
-    padded = jnp.concatenate([zero, all_leaves, zero], axis=0)
-    window = lax.dynamic_slice_in_dim(padded, here, 3, axis=0).reshape(3 * box_dom, coeffs)
+    parents = domain_parents
+    carried = domain
+    delivered = []
+    mask = 1
+    while mask < n_space:
+        got = exchange(jnp.concatenate([carried, parents], axis=0), "space", mask)
+        carried = got[:box_dom]
+        delivered.append(carried)
+        parents = jnp.concatenate([parents, got[box_dom:]], axis=0)
+        mask *= 2
+    all_parents = parents
+
+    def neighbour(step):
+        other = here + step
+        pick = jnp.zeros_like(domain)
+        for r, block in enumerate(delivered):
+            pick = jnp.where((here ^ other) == 2 ** (r + 1) - 1, block, pick)
+        inside = (other >= 0) & (other < n_space)
+        return jnp.where(inside, pick, 0.0)
+
+    window = jnp.concatenate([neighbour(-1), domain, neighbour(1)], axis=0)
+    dom_csrc = (dom_csrc // n_blk ^ here) * n_blk + dom_csrc % n_blk
 
     src_hot = (dom_src[..., None] == jnp.arange(3 * box_dom, dtype=jnp.int32)).astype(jnp.bfloat16)
     type_hot = (dom_type[..., None] == jnp.arange(n_types, dtype=jnp.int32)).astype(jnp.bfloat16)

time: 85.6 us -> 75.9 us (0.89)
  matrix products: 31.4 us -> 26.8 us
  waiting for transfers between devices: 23.8 us -> 21.2 us
  other arithmetic: 6.75 us -> 4.29 us
    select_n x3 -> x1, other arithmetic: 4.93 us -> 1.1 us  [neighbour(): return jnp.where(inside, pick, 0.0)]
    ppermute x7, waiting for transfers between devices: 23.8 us -> 21.2 us  [exchange(): return lax.ppermute(x, axis, [(i, i ^ mask) for i in range(count)])]
    dot_general x1, matrix products: 4.38 us -> 2.28 us  [shards(): far = jnp.einsum('btk,tlk->bl', rows, translation, precision=top)]
    dot_general x1, matrix products: 4.52 us -> 2.48 us  [shards(): gathered = jnp.einsum('btj,jk->btk', counts, window, precision=top)]
    slice x2 -> x5, local copies, waits for them, and re-layouts: 0.08 us -> 1.65 us  [the longest x2 0.92 us: shards(): carried = got[:box_dom]]
  transfers between devices with their start and end apart: 7 -> 7, of which waited for: 7 -> 6; matrix products, arithmetic and copies ran while one was open for 10% -> 11% of each run, Pallas kernels for 0% -> 0%
where the time goes in v4:
time: 75.9 us; the launch traced here: 75.4 us
  matrix products  26.8 us (35%)
  waiting for transfers between devices  21.2 us (28%)
  starting transfers between devices  15 us (20%)
  local copies, waits for them, and re-layouts  7.2 us (9%)
  other arithmetic  4.29 us (6%)
  between operations  0.93 us (1%)
    ppermute x7, waiting for transfers between devices, exchange(): return lax.ppermute(x, axis, [(i, i ^ mask) for i in range(count)])  21.2 us
    ppermute x7, starting transfers between devices, exchange(): return lax.ppermute(x, axis, [(i, i ^ mask) for i in range(count)])  15 us
    dot_general x1, matrix products, shards(): jnp.einsum('bmk,bnk->bmn', scaled, ket_table, preferred_element_type=jnp....  8.08 us
    dot_general x1, matrix products, shards(): jnp.einsum('bmn,bmk->bnk', density, bra_table, preferred_element_type=jnp...  6.82 us
    dot_general x1, matrix products, shards(): jnp.einsum('blt,blj->btj', type_hot, src_hot, preferred_element_type=jnp....  2.84 us
    dot_general x1, matrix products, shards(): jnp.einsum('qce,cde->qd', domain.reshape(n_blk, leaves, coeffs), upward_t...  2.51 us
    dot_general x1, matrix products, shards(): gathered = jnp.einsum('btj,jk->btk', counts, window, precision=top)  2.48 us
    dot_general x1, matrix products, shards(): far = jnp.einsum('btk,tlk->bl', rows, translation, precision=top)  2.28 us
  transfers between devices with their start and end apart: 7, of which 6 were waited for; matrix products, arithmetic and copies ran while one was open for 11% of the time, Pallas kernels for 0%

profile of v4, /device:TPU:0, one launch (start us, length us, event | category | flops | bytes accessed | tf_op | source)
XLA Modules:
  0.0 75.4 jit_solution(18138146147743653004)
XLA Ops:
  0.6 0.9 %add_convert_fusion = f32[18,27]{1,0:T(8,128)S(1)} fusion(s32[1,27]{1,0:T(1,128)} %param.17, s32[1,27]{1,0:T(1,128)} %param.16, s32[8,27]{1,0:T(8,128)} %param.15, s32[8,27]{1,0:T(8,128)} %param.14), kind=kLoop, calls=%fused_computation.54 | loop fusion | flops 1944 | bytes 3888 | tf_op jit(solution)/shard_map/convert_element_type | solution.py:58
  1.9 0.7 copy-done
  2.6 6.8 %multiply_reduce_fusion = f32[96,256]{1,0:T(8,128)S(1)} fusion(bf16[96,128,256]{2,1,0:T(8,128)(2,1)} %param.12, bf16[96,128,128]{2,1,0:T(8,128)(2,1)S(1)} %copy-done, bf16[96,128,256]{2,1,0:T(8,128)(2,1)} %param.11), kind=kOutput, calls=%fused_computation.1 | convolution fusion | flops 814718976 | bytes 15826944 | tf_op jit(solution)/shard_map/bmn,bmk->bnk/dot_general | solution.py:63
  9.4 0.3 fusion.31
  9.9 1.4 %collective-permute-done = f32[159,256]{1,0:T(8,128)S(1)} collective-permute-done((f32[159,256]{1,0:T(8,128)S(1)}, f32[159,256]{1,0:T(8,128)S(1)}, u32[]{:S(2)}, u32[]{:S(2)}) %collective-permute-start) | collective-permute-done | bytes 162848 | tf_op jit(solution)/shard_map/ppermute | solution.py:9
  11.3 2.1 %collective-permute-start.1 = (f32[159,256]{1,0:T(8,128)S(1)}, f32[159,256]{1,0:T(8,128)S(1)}, u32[]{:S(2)}, u32[]{:S(2)}) collective-permute-start(f32[159,256]{1,0:T(8,128)S(1)} %fusion.45), channel_id=1, source_target_pairs={{0,2},{1,3},{2,0},{3,1},{4,6},{5,7},{6,4},{7,5},{8,10},{9,11},{10,... | collective-permute-start | bytes 488456 | tf_op jit(solution)/shard_map/ppermute | solution.py:9
  13.4 4.5 %collective-permute-done.1 = f32[159,256]{1,0:T(8,128)S(1)} collective-permute-done((f32[159,256]{1,0:T(8,128)S(1)}, f32[159,256]{1,0:T(8,128)S(1)}, u32[]{:S(2)}, u32[]{:S(2)}) %collective-permute-start.1) | collective-permute-done | bytes 162848 | tf_op jit(solution)/shard_map/ppermute | solution.py:9
  17.9 1.7 %collective-permute-start.2 = (f32[159,256]{1,0:T(8,128)S(1)}, f32[159,256]{1,0:T(8,128)S(1)}, u32[]{:S(2)}, u32[]{:S(2)}) collective-permute-start(f32[159,256]{1,0:T(8,128)S(1)} %add.54), channel_id=1, source_target_pairs={{0,4},{1,5},{2,6},{3,7},{4,0},{5,1},{6,2},{7,3},{8,12},{9,13},{10,... | collective-permute-start | bytes 488456 | tf_op jit(solution)/shard_map/ppermute | solution.py:9
  19.6 4.1 %collective-permute-done.2 = f32[159,256]{1,0:T(8,128)S(1)} collective-permute-done((f32[159,256]{1,0:T(8,128)S(1)}, f32[159,256]{1,0:T(8,128)S(1)}, u32[]{:S(2)}, u32[]{:S(2)}) %collective-permute-start.2) | collective-permute-done | bytes 162848 | tf_op jit(solution)/shard_map/ppermute | solution.py:9
  23.7 3.2 %collective-permute-start.3 = (f32[159,256]{1,0:T(8,128)S(1)}, f32[159,256]{1,0:T(8,128)S(1)}, u32[]{:S(2)}, u32[]{:S(2)}) collective-permute-start(f32[159,256]{1,0:T(8,128)S(1)} %add.55), channel_id=1, source_target_pairs={{0,8},{1,9},{2,10},{3,11},{4,12},{5,13},{6,14},{7,15},{8,0},{9,1},... | collective-permute-start | bytes 488456 | tf_op jit(solution)/shard_map/ppermute | solution.py:9
  26.8 3.7 %collective-permute-done.3 = f32[159,256]{1,0:T(8,128)S(1)} collective-permute-done((f32[159,256]{1,0:T(8,128)S(1)}, f32[159,256]{1,0:T(8,128)S(1)}, u32[]{:S(2)}, u32[]{:S(2)}) %collective-permute-start.3) | collective-permute-done | bytes 162848 | tf_op jit(solution)/shard_map/ppermute | solution.py:9
  30.7 2.5 %convolution_bitcast_fusion = f32[16,256]{1,0:T(8,128)S(1)} fusion(f32[8,256,256]{2,1,0:T(8,128)} %param.19, f32[16,8,256]{2,1,0:T(8,128)S(1)} %get-tuple-element.9), kind=kOutput, calls=%fused_computation.15 | convolution fusion | flops 50331648 | bytes 2244608 | tf_op jit(solution)/shard_map/qce,cde->qd/dot_general | solution.py:80
  33.2 0.7 pad_maximum_fusion.3
  33.9 1.4 %collective-permute-start.4 = (f32[144,256]{1,0:T(8,128)}, f32[144,256]{1,0:T(8,128)}, u32[]{:S(2)}, u32[]{:S(2)}) collective-permute-start(f32[144,256]{1,0:T(8,128)} %pad_maximum_fusion.3), channel_id=1, source_target_pairs={{0,16},{16,0},{32,48},{48,32},{64,80},{80,64},{96,112},{112,96},{1... | collective-permute-start | bytes 442376 | tf_op jit(solution)/shard_map/ppermute | solution.py:9
  35.5 0.7 slice_bitcast_fusion
  36.2 0.7 copy.17
  36.9 1.4 %iota_compare_fusion.4 = pred[128,27,16]{0,2,1:T(8,128)(4,1)} fusion(s32[128,27]{0,1:T(8,128)} %copy.17), kind=kLoop, calls=%fused_computation.23 | loop fusion | flops 55296 | bytes 69120 | tf_op jit(solution)/shard_map/eq | solution.py:107
  38.2 1.4 %copy.18 = pred[128,27,16]{1,2,0:T(8,128)(4,1)S(1)} copy(pred[128,27,16]{0,2,1:T(8,128)(4,1)} %iota_compare_fusion.4) | data formatting | bytes 110592 | tf_op jit(solution)/shard_map/eq | solution.py:107
  39.6 2.8 %fusion.2 = f32[128,16,384]{2,1,0:T(8,128)S(1)} fusion(pred[128,27,16]{1,2,0:T(8,128)(4,1)S(1)} %copy.18, s32[128,27]{1,0:T(8,128)} %get-tuple-element.4), kind=kOutput, calls=%fused_computation.5 | convolution fusion | flops 43794432 | bytes 3214848 | tf_op jit(solution)/shard_map/blt,blj->btj/dot_general | solution.py:108
  42.4 0.9 %fusion.46 = (s32[16,1,27]{2,1,0:T(1,128)S(1)}, s32[16,1,27]{2,1,0:T(1,128)S(1)}) fusion(s32[16,18,27]{2,1,0:T(8,128)} %copy-done.3), kind=kLoop, calls=%fused_computation.74 | loop fusion | bytes 6912 | tf_op jit(solution)/shard_map/slice | solution.py:78
  43.4 0.7 slice.66
  44.1 0.9 %slice.65 = f32[128,256]{1,0:T(8,128)S(1)} slice(f32[144,256]{1,0:T(8,128)} %collective-permute-done.4), slice={[0:128], [0:256]} | slice | bytes 262144 | tf_op jit(solution)/shard_map/slice | solution.py:89
  45.0 2.8 %collective-permute-start.5 = (f32[160,256]{1,0:T(8,128)S(1)}, f32[160,256]{1,0:T(8,128)S(1)}, u32[]{:S(2)}, u32[]{:S(2)}) collective-permute-start(f32[160,256]{1,0:T(8,128)S(1)} %pad_maximum_fusion.2), channel_id=1, source_target_pairs={{0,32},{16,48},{32,0},{48,16},{64,96},{80,112},{96,64},{112,80},{1... | collective-permute-start | bytes 491528 | tf_op jit(solution)/shard_map/ppermute | solution.py:9
  47.9 4.1 %collective-permute-done.5 = f32[160,256]{1,0:T(8,128)S(1)} collective-permute-done((f32[160,256]{1,0:T(8,128)S(1)}, f32[160,256]{1,0:T(8,128)S(1)}, u32[]{:S(2)}, u32[]{:S(2)}) %collective-permute-start.5) | collective-permute-done | bytes 163872 | tf_op jit(solution)/shard_map/ppermute | solution.py:9
  52.0 3.8 %collective-permute-start.6 = (f32[192,256]{1,0:T(8,128)S(1)}, f32[192,256]{1,0:T(8,128)S(1)}, u32[]{:S(2)}, u32[]{:S(2)}) collective-permute-start(f32[192,256]{1,0:T(8,128)S(1)} %pad_maximum_fusion), channel_id=1, source_target_pairs={{0,64},{16,80},{32,96},{48,112},{64,0},{80,16},{96,32},{112,48},{1... | collective-permute-start | bytes 589832 | tf_op jit(solution)/shard_map/ppermute | solution.py:9
  56.0 3.4 %collective-permute-done.6 = f32[192,256]{1,0:T(8,128)S(1)} collective-permute-done((f32[192,256]{1,0:T(8,128)S(1)}, f32[192,256]{1,0:T(8,128)S(1)}, u32[]{:S(2)}, u32[]{:S(2)}) %collective-permute-start.6) | collective-permute-done | bytes 196640 | tf_op jit(solution)/shard_map/ppermute | solution.py:9
  59.7 1.1 %select_select_fusion.1 = (f32[128,256]{1,0:T(8,128)S(1)}, f32[128,256]{1,0:T(8,128)S(1)}) fusion(f32[192,256]{1,0:T(8,128)S(1)} %collective-permute-done.6, pred[]{:T(512)S(6)} %eq.104, pred[]{:T(512)S(6)} %eq.103, pred[]{:T(512)S(6)} %eq.102, pred[]{:T(512)S(6)} %and.33, f32[160,256]{1,0:T(8,128)S(1)} %collective-permute-done.5, ...), kind=kLoop, calls=%fused_computation.42 | loop fusion | flops 262144 | bytes 655368 | tf_op jit(solution)/shard_map/jit(_where)/select_n | solution.py:101
  60.8 2.5 %fusion.3 = f32[128,16,256]{2,0,1:T(8,128)S(1)} fusion(f32[128,16,384]{2,1,0:T(8,128)S(1)} %fusion.2, f32[128,256]{1,0:T(8,128)S(1)} %get-tuple-element.3, f32[128,256]{1,0:T(8,128)S(1)} %get-tuple-element.8, f32[128,256]{1,0:T(8,128)S(1)} %get-tuple-element.2), kind=kOutput, calls=%fused_computation.6 | convolution fusion | flops 1208156160 | bytes 5636096 | tf_op jit(solution)/shard_map/btj,jk->btk/dot_general | solution.py:109
  63.3 2.3 %fusion.11 = f32[144,256]{1,0:T(8,128)S(1)} fusion(f32[16,256,256]{2,1,0:T(8,128)S(1)} %copy-done.2, f32[16,16,256]{2,0,1:T(8,128)S(1)} %fusion.19, f32[128,16,256]{2,0,1:T(8,128)S(1)} %fusion.3), kind=kOutput, calls=%fused_computation.14 | convolution fusion | flops 906559488 | bytes 6701056 | tf_op jit(solution)/shard_map/btk,tlk->bl/dot_general | solution.py:116
  65.6 0.7 fusion.34
  66.7 0.6 constant_dynamic-slice_fusion
  67.3 8.1 %fusion.10 = bf16[96,128,128]{2,1,0:T(8,128)(2,1)} fusion(bf16[96,128,256]{2,1,0:T(8,128)(2,1)} %param.12, bf16[96,128,256]{2,1,0:T(8,128)(2,1)} %param.11, f32[96,256]{1,0:T(8,128)S(1)} %fusion.30), kind=kOutput, calls=%fused_computation.13 | convolution fusion | flops 816316416 | bytes 15826944 | tf_op jit(solution)/shard_map/bmk,bnk->bmn/dot_general | solution.py:126
  (39 shorter events, 1.6 us)
Async XLA Ops:
  0.6 2.0 %copy-start = (bf16[96,128,128]{2,1,0:T(8,128)(2,1)S(1)}, bf16[96,128,128]{2,1,0:T(8,128)(2,1)}, u32[]{:S(2)}) copy-start(bf16[96,128,128]{2,1,0:T(8,128)(2,1)} %param.10) | copy-start | bytes 9437188
  2.6 6.8 %copy-start.4 = (s32[96]{0:T(128)S(1)}, s32[96]{0:T(128)}, u32[]{:S(2)}) copy-start(s32[96]{0:T(128)} %param.13) | copy-start | bytes 1156
  9.8 1.5 %collective-permute-start = (f32[159,256]{1,0:T(8,128)S(1)}, f32[159,256]{1,0:T(8,128)S(1)}, u32[]{:S(2)}, u32[]{:S(2)}) collective-permute-start(f32[159,256]{1,0:T(8,128)S(1)} %pad_maximum_fusion.1), channel_id=1, source_target_pairs={{0,1},{1,0},{2,3},{3,2},{4,5},{5,4},{6,7},{7,6},{8,9},{9,8},{10,11... | collective-permute-start | bytes 488456 | tf_op jit(solution)/shard_map/ppermute | solution.py:9
  11.3 6.6 %collective-permute-start.1 = (f32[159,256]{1,0:T(8,128)S(1)}, f32[159,256]{1,0:T(8,128)S(1)}, u32[]{:S(2)}, u32[]{:S(2)}) collective-permute-start(f32[159,256]{1,0:T(8,128)S(1)} %fusion.45), channel_id=1, source_target_pairs={{0,2},{1,3},{2,0},{3,1},{4,6},{5,7},{6,4},{7,5},{8,10},{9,11},{10,... | collective-permute-start | bytes 488456 | tf_op jit(solution)/shard_map/ppermute | solution.py:9
  17.9 5.8 %collective-permute-start.2 = (f32[159,256]{1,0:T(8,128)S(1)}, f32[159,256]{1,0:T(8,128)S(1)}, u32[]{:S(2)}, u32[]{:S(2)}) collective-permute-start(f32[159,256]{1,0:T(8,128)S(1)} %add.54), channel_id=1, source_target_pairs={{0,4},{1,5},{2,6},{3,7},{4,0},{5,1},{6,2},{7,3},{8,12},{9,13},{10,... | collective-permute-start | bytes 488456 | tf_op jit(solution)/shard_map/ppermute | solution.py:9
  23.7 6.9 %collective-permute-start.3 = (f32[159,256]{1,0:T(8,128)S(1)}, f32[159,256]{1,0:T(8,128)S(1)}, u32[]{:S(2)}, u32[]{:S(2)}) collective-permute-start(f32[159,256]{1,0:T(8,128)S(1)} %add.55), channel_id=1, source_target_pairs={{0,8},{1,9},{2,10},{3,11},{4,12},{5,13},{6,14},{7,15},{8,0},{9,1},... | collective-permute-start | bytes 488456 | tf_op jit(solution)/shard_map/ppermute | solution.py:9
  33.9 9.5 %collective-permute-start.4 = (f32[144,256]{1,0:T(8,128)}, f32[144,256]{1,0:T(8,128)}, u32[]{:S(2)}, u32[]{:S(2)}) collective-permute-start(f32[144,256]{1,0:T(8,128)} %pad_maximum_fusion.3), channel_id=1, source_target_pairs={{0,16},{16,0},{32,48},{48,32},{64,80},{80,64},{96,112},{112,96},{1... | collective-permute-start | bytes 442376 | tf_op jit(solution)/shard_map/ppermute | solution.py:9
  35.5 1.4 %copy-start.3 = (s32[16,18,27]{2,1,0:T(8,128)}, s32[16,18,27]{2,1,0:T(8,128)S(1)}, u32[]{:S(2)}) copy-start(s32[16,18,27]{2,1,0:T(8,128)S(1)} %convert_element_type.43) | copy-start | bytes 93316
  45.0 6.9 %collective-permute-start.5 = (f32[160,256]{1,0:T(8,128)S(1)}, f32[160,256]{1,0:T(8,128)S(1)}, u32[]{:S(2)}, u32[]{:S(2)}) collective-permute-start(f32[160,256]{1,0:T(8,128)S(1)} %pad_maximum_fusion.2), channel_id=1, source_target_pairs={{0,32},{16,48},{32,0},{48,16},{64,96},{80,112},{96,64},{112,80},{1... | collective-permute-start | bytes 491528 | tf_op jit(solution)/shard_map/ppermute | solution.py:9
  52.0 7.4 %collective-permute-start.6 = (f32[192,256]{1,0:T(8,128)S(1)}, f32[192,256]{1,0:T(8,128)S(1)}, u32[]{:S(2)}, u32[]{:S(2)}) collective-permute-start(f32[192,256]{1,0:T(8,128)S(1)} %pad_maximum_fusion), channel_id=1, source_target_pairs={{0,64},{16,80},{32,96},{48,112},{64,0},{80,16},{96,32},{112,48},{1... | collective-permute-start | bytes 589832 | tf_op jit(solution)/shard_map/ppermute | solution.py:9
  59.7 3.6 %copy-start.2 = (f32[16,256,256]{2,1,0:T(8,128)S(1)}, f32[16,256,256]{2,1,0:T(8,128)}, u32[]{:S(2)}) copy-start(f32[16,256,256]{2,1,0:T(8,128)} %param.18) | copy-start | bytes 12582916
  63.3 2.3 %copy-start.1 = (f32[8,256,256]{2,1,0:T(8,128)S(1)}, f32[8,256,256]{2,1,0:T(8,128)}, u32[]{:S(2)}) copy-start(f32[8,256,256]{2,1,0:T(8,128)} %param.19) | copy-start | bytes 6291460
  63.3 3.1 %copy-start.5 = (s32[96]{0:T(128)S(1)}, s32[96]{0:T(128)}, u32[]{:S(2)}) copy-start(s32[96]{0:T(128)} %param.13) | copy-start | bytes 1156

commit v5 on v4

--- a/solution.py
+++ b/solution.py
@@ -1,7 +1,67 @@
 import jax
 import jax.numpy as jnp
 from jax import lax
+from jax.experimental import pallas as pl
+from jax.experimental.pallas import tpu as pltpu
 from jax.sharding import PartitionSpec as P
+
+TILE = 8
+
+
+def moments_kernel(dens_ref, bra_ref, ket_ref, out_ref):
+    mixed = jnp.einsum(
+        "bmn,bnk->bmk", dens_ref[...], ket_ref[...], preferred_element_type=jnp.float32
+    )
+    out_ref[...] = jnp.sum(bra_ref[...].astype(jnp.float32) * mixed, axis=1)
+
+
+def block_moments(density, bra_table, ket_table):
+    blocks, rows, cols = density.shape
+    coeffs = bra_table.shape[2]
+    return pl.pallas_call(
+        moments_kernel,
+        out_shape=jax.ShapeDtypeStruct((blocks, coeffs), jnp.float32),
+        grid=(blocks // TILE,),
+        in_specs=[
+            pl.BlockSpec((TILE, rows, cols), lambda i: (i, 0, 0)),
+            pl.BlockSpec((TILE, rows, coeffs), lambda i: (i, 0, 0)),
+            pl.BlockSpec((TILE, cols, coeffs), lambda i: (i, 0, 0)),
+        ],
+        out_specs=pl.BlockSpec((TILE, coeffs), lambda i: (i, 0)),
+        cost_estimate=pl.CostEstimate(
+            flops=2 * blocks * rows * cols * coeffs,
+            transcendentals=0,
+            bytes_accessed=2 * blocks * (rows * cols + 2 * rows * coeffs) + 4 * blocks * coeffs,
+        ),
+    )(density, bra_table, ket_table)
+
+
+def coulomb_kernel(bra_ref, ket_ref, local_ref, out_ref):
+    scaled = (bra_ref[...].astype(jnp.float32) * local_ref[...][:, None, :]).astype(jnp.bfloat16)
+    out_ref[...] = jnp.einsum(
+        "bmk,bnk->bmn", scaled, ket_ref[...], preferred_element_type=jnp.float32
+    ).astype(jnp.bfloat16)
+
+
+def block_coulomb(bra_table, ket_table, block_locals):
+    blocks, rows, coeffs = bra_table.shape
+    cols = ket_table.shape[1]
+    return pl.pallas_call(
+        coulomb_kernel,
+        out_shape=jax.ShapeDtypeStruct((blocks, rows, cols), jnp.bfloat16),
+        grid=(blocks // TILE,),
+        in_specs=[
+            pl.BlockSpec((TILE, rows, coeffs), lambda i: (i, 0, 0)),
+            pl.BlockSpec((TILE, cols, coeffs), lambda i: (i, 0, 0)),
+            pl.BlockSpec((TILE, coeffs), lambda i: (i, 0)),
+        ],
+        out_specs=pl.BlockSpec((TILE, rows, cols), lambda i: (i, 0, 0)),
+        cost_estimate=pl.CostEstimate(
+            flops=2 * blocks * rows * cols * coeffs,
+            transcendentals=0,
+            bytes_accessed=2 * blocks * (rows * cols + 2 * rows * coeffs) + 4 * blocks * coeffs,
+        ),
+    )(bra_table, ket_table, block_locals)
 
 
 def exchange(x, axis, mask):
@@ -60,8 +120,7 @@
     table = jnp.pad(table.reshape(-1), (0, table_rows * coeffs - n_blk * flat))
     table = table.reshape(table_rows, coeffs)
 
-    inner = jnp.einsum("bmn,bmk->bnk", density, bra_table, preferred_element_type=jnp.float32)
-    moments = jnp.sum(inner * ket_table.astype(jnp.float32), axis=1)
+    moments = block_moments(density, bra_table, ket_table)
     box_hot = (box_of_block[:, None] == jnp.arange(box_dom, dtype=jnp.int32)[None, :]).astype(
         jnp.float32
     )
@@ -122,10 +181,7 @@
     domain_local = leaf_far + downward
     box_locals = lax.dynamic_slice_in_dim(domain_local, me * leaves, leaves, axis=0)
     block_locals = jnp.dot(box_hot, domain_local, precision=top)
-    scaled = (bra_table.astype(jnp.float32) * block_locals[:, None, :]).astype(jnp.bfloat16)
-    coulomb = jnp.einsum(
-        "bmk,bnk->bmn", scaled, ket_table, preferred_element_type=jnp.float32
-    ).astype(jnp.bfloat16)
+    coulomb = block_coulomb(bra_table, ket_table, block_locals)
     return (coulomb, box_locals)
 
 

time: 75.9 us -> 76.2 us (level)
  the two profiles are of different devices: /device:TPU:0 before, /device:TPU:30 now
where the time goes in v5:
time: 76.2 us; the launch traced here: 75.5 us
  waiting for transfers between devices  29.5 us (39%)
  Pallas kernels  22.5 us (30%)
  matrix products  10.7 us (14%)
  starting transfers between devices  8.83 us (12%)
  local copies, waits for them, and re-layouts  1.86 us (2%)
  other arithmetic  1.25 us (2%)
  between operations  0.92 us (1%)
    ppermute x7, waiting for transfers between devices, exchange(): return lax.ppermute(x, axis, [(i, i ^ mask) for i in range(count)])  29.5 us
    pallas_call x1, Pallas kernels, block_coulomb(): pl.pallas_call(coulomb_kernel, out_shape=jax.ShapeDtypeStruct((blocks, ro...  11.3 us
    pallas_call x1, Pallas kernels, block_moments(): pl.pallas_call(moments_kernel, out_shape=jax.ShapeDtypeStruct((blocks, co...  11.2 us
    ppermute x7, starting transfers between devices, exchange(): return lax.ppermute(x, axis, [(i, i ^ mask) for i in range(count)])  8.83 us
    dot_general x1, matrix products, shards(): gathered = jnp.einsum('btj,jk->btk', counts, window, precision=top)  2.48 us
    dot_general x1, matrix products, shards(): far = jnp.einsum('btk,tlk->bl', rows, translation, precision=top)  2.29 us
    dot_general x1, matrix products, shards(): jnp.einsum('blt,blj->btj', type_hot, src_hot, preferred_element_type=jnp....  1.85 us
  transfers between devices with their start and end apart: 7, of which 7 were waited for; matrix products, arithmetic and copies ran while one was open for 4% of the time, Pallas kernels for 0%

profile of v5, /device:TPU:30, one launch (start us, length us, event | category | flops | bytes accessed | tf_op | source)
XLA Modules:
  0.0 75.5 jit_solution(13542035919410842638)
XLA Ops:
  0.7 0.9 %add_convert_fusion = f32[18,27]{1,0:T(8,128)S(1)} fusion(s32[1,27]{1,0:T(1,128)} %param.17, s32[1,27]{1,0:T(1,128)} %param.16, s32[8,27]{1,0:T(8,128)} %param.15, s32[8,27]{1,0:T(8,128)} %param.14), kind=kLoop, calls=%fused_computation.49 | loop fusion | flops 1944 | bytes 3888 | tf_op jit(solution)/shard_map/convert_element_type | solution.py:118
  1.5 0.1 convert_element_type.27
  1.7 0.1 reshape.88
  1.9 11.2 %shard_map.113 = f32[96,256]{1,0:T(8,128)} custom-call(bf16[96,128,128]{2,1,0:T(8,128)(2,1)} %dens_ref.1, bf16[96,128,256]{2,1,0:T(8,128)(2,1)} %bra_ref.3, bf16[96,128,256]{2,1,0:T(8,128)(2,1)} %ket_ref.3), custom_call_target="tpu_custom_call" | custom-call | flops 805306368 | bytes 15826944 | tf_op jit(solution)/shard_map/pallas_call | solution.py:21
  13.0 1.2 %fusion.28 = f32[128,256]{1,0:T(8,128)S(1)} fusion(f32[96,256]{1,0:T(8,128)} %shard_map.113, s32[96]{0:T(128)S(1)} %copy-done.2), kind=kOutput, calls=%fused_computation.43 | convolution fusion | flops 18886656 | bytes 229760 | tf_op jit(solution)/shard_map/dot_general | solution.py:127
  14.3 0.1 collective-permute-start
  14.4 1.4 %collective-permute-done = f32[159,256]{1,0:T(8,128)S(1)} collective-permute-done((f32[159,256]{1,0:T(8,128)S(1)}, f32[159,256]{1,0:T(8,128)S(1)}, u32[]{:S(2)}, u32[]{:S(2)}) %collective-permute-start) | collective-permute-done | bytes 162848 | tf_op jit(solution)/shard_map/ppermute | solution.py:69
  15.8 2.0 %collective-permute-start.1 = (f32[159,256]{1,0:T(8,128)S(1)}, f32[159,256]{1,0:T(8,128)S(1)}, u32[]{:S(2)}, u32[]{:S(2)}) collective-permute-start(f32[159,256]{1,0:T(8,128)S(1)} %fusion.42), channel_id=1, source_target_pairs={{0,2},{1,3},{2,0},{3,1},{4,6},{5,7},{6,4},{7,5},{8,10},{9,11},{10,... | collective-permute-start | bytes 488456 | tf_op jit(solution)/shard_map/ppermute | solution.py:69
  17.8 4.5 %collective-permute-done.1 = f32[159,256]{1,0:T(8,128)S(1)} collective-permute-done((f32[159,256]{1,0:T(8,128)S(1)}, f32[159,256]{1,0:T(8,128)S(1)}, u32[]{:S(2)}, u32[]{:S(2)}) %collective-permute-start.1) | collective-permute-done | bytes 162848 | tf_op jit(solution)/shard_map/ppermute | solution.py:69
  22.3 0.8 %collective-permute-start.2 = (f32[159,256]{1,0:T(8,128)S(1)}, f32[159,256]{1,0:T(8,128)S(1)}, u32[]{:S(2)}, u32[]{:S(2)}) collective-permute-start(f32[159,256]{1,0:T(8,128)S(1)} %add.54), channel_id=1, source_target_pairs={{0,4},{1,5},{2,6},{3,7},{4,0},{5,1},{6,2},{7,3},{8,12},{9,13},{10,... | collective-permute-start | bytes 488456 | tf_op jit(solution)/shard_map/ppermute | solution.py:69
  23.1 4.8 %collective-permute-done.2 = f32[159,256]{1,0:T(8,128)S(1)} collective-permute-done((f32[159,256]{1,0:T(8,128)S(1)}, f32[159,256]{1,0:T(8,128)S(1)}, u32[]{:S(2)}, u32[]{:S(2)}) %collective-permute-start.2) | collective-permute-done | bytes 162848 | tf_op jit(solution)/shard_map/ppermute | solution.py:69
  28.0 1.3 %collective-permute-start.3 = (f32[159,256]{1,0:T(8,128)S(1)}, f32[159,256]{1,0:T(8,128)S(1)}, u32[]{:S(2)}, u32[]{:S(2)}) collective-permute-start(f32[159,256]{1,0:T(8,128)S(1)} %add.55), channel_id=1, source_target_pairs={{0,8},{1,9},{2,10},{3,11},{4,12},{5,13},{6,14},{7,15},{8,0},{9,1},... | collective-permute-start | bytes 488456 | tf_op jit(solution)/shard_map/ppermute | solution.py:69
  29.3 5.6 %collective-permute-done.3 = f32[159,256]{1,0:T(8,128)S(1)} collective-permute-done((f32[159,256]{1,0:T(8,128)S(1)}, f32[159,256]{1,0:T(8,128)S(1)}, u32[]{:S(2)}, u32[]{:S(2)}) %collective-permute-start.3) | collective-permute-done | bytes 162848 | tf_op jit(solution)/shard_map/ppermute | solution.py:69
  35.0 0.9 %convolution_bitcast_fusion = f32[16,256]{1,0:T(8,128)S(1)} fusion(f32[8,256,256]{2,1,0:T(8,128)S(1)} %copy-done, f32[16,8,256]{2,1,0:T(8,128)S(1)} %get-tuple-element.9), kind=kOutput, calls=%fused_computation.10 | convolution fusion | flops 50331648 | bytes 2244608 | tf_op jit(solution)/shard_map/qce,cde->qd/dot_general | solution.py:139
  35.9 0.9 %collective-permute-start.4 = (f32[144,256]{1,0:T(8,128)S(1)}, f32[144,256]{1,0:T(8,128)S(1)}, u32[]{:S(2)}, u32[]{:S(2)}) collective-permute-start(f32[144,256]{1,0:T(8,128)S(1)} %pad_maximum_fusion.3), channel_id=1, source_target_pairs={{0,16},{16,0},{32,48},{48,32},{64,80},{80,64},{96,112},{112,96},{1... | collective-permute-start | bytes 442376 | tf_op jit(solution)/shard_map/ppermute | solution.py:69
  36.8 0.2 convert_element_type.29
  37.2 0.6 copy.17
  37.8 1.9 %fusion = f32[128,16,384]{2,1,0:T(8,128)S(1)} fusion(pred[128,27,16]{1,2,0:T(8,128)(4,1)S(1)} %copy.17, s32[128,27]{1,0:T(8,128)S(1)} %get-tuple-element.4), kind=kOutput, calls=%fused_computation.1 | convolution fusion | flops 43794432 | bytes 3214848 | tf_op jit(solution)/shard_map/blt,blj->btj/dot_general | solution.py:167
  39.7 3.0 %collective-permute-done.4 = f32[144,256]{1,0:T(8,128)S(1)} collective-permute-done((f32[144,256]{1,0:T(8,128)S(1)}, f32[144,256]{1,0:T(8,128)S(1)}, u32[]{:S(2)}, u32[]{:S(2)}) %collective-permute-start.4) | collective-permute-done | bytes 147488 | tf_op jit(solution)/shard_map/ppermute | solution.py:69
  42.7 0.1 collective-permute-start.5
  42.9 6.8 %collective-permute-done.5 = f32[160,256]{1,0:T(8,128)S(1)} collective-permute-done((f32[160,256]{1,0:T(8,128)S(1)}, f32[160,256]{1,0:T(8,128)S(1)}, u32[]{:S(2)}, u32[]{:S(2)}) %collective-permute-start.5) | collective-permute-done | bytes 163872 | tf_op jit(solution)/shard_map/ppermute | solution.py:69
  49.7 3.6 %collective-permute-start.6 = (f32[192,256]{1,0:T(8,128)S(1)}, f32[192,256]{1,0:T(8,128)S(1)}, u32[]{:S(2)}, u32[]{:S(2)}) collective-permute-start(f32[192,256]{1,0:T(8,128)S(1)} %pad_maximum_fusion), channel_id=1, source_target_pairs={{0,64},{16,80},{32,96},{48,112},{64,0},{80,16},{96,32},{112,48},{1... | collective-permute-start | bytes 589832 | tf_op jit(solution)/shard_map/ppermute | solution.py:69
  53.3 0.2 fusion.15
  53.5 3.4 %collective-permute-done.6 = f32[192,256]{1,0:T(8,128)S(1)} collective-permute-done((f32[192,256]{1,0:T(8,128)S(1)}, f32[192,256]{1,0:T(8,128)S(1)}, u32[]{:S(2)}, u32[]{:S(2)}) %collective-permute-start.6) | collective-permute-done | bytes 196640 | tf_op jit(solution)/shard_map/ppermute | solution.py:69
  57.0 0.3 fusion.16
  57.3 2.5 %fusion.1 = f32[128,16,256]{2,0,1:T(8,128)S(1)} fusion(f32[128,16,384]{2,1,0:T(8,128)S(1)} %fusion, f32[128,256]{1,0:T(8,128)S(1)} %get-tuple-element.3, f32[128,256]{1,0:T(8,128)S(1)} %get-tuple-element.8, f32[128,256]{1,0:T(8,128)S(1)} %get-tuple-element.2), kind=kOutput, calls=%fused_computation.2 | convolution fusion | flops 1208156160 | bytes 5636096 | tf_op jit(solution)/shard_map/btj,jk->btk/dot_general | solution.py:168
  59.8 2.3 %fusion.8 = f32[144,256]{1,0:T(8,128)S(1)} fusion(f32[16,256,256]{2,1,0:T(8,128)S(1)} %copy-done.1, f32[16,16,256]{2,0,1:T(8,128)S(1)} %fusion.16, f32[128,16,256]{2,0,1:T(8,128)S(1)} %fusion.1), kind=kOutput, calls=%fused_computation.9 | convolution fusion | flops 906559488 | bytes 6701056 | tf_op jit(solution)/shard_map/btk,tlk->bl/dot_general | solution.py:175
  62.1 0.6 fusion.31
  62.7 0.1 slice_add_fusion
  62.8 0.8 %fusion.27.local_ref = f32[96,256]{1,0:T(8,128)} fusion(f32[128,256]{1,0:T(8,128)S(1)} %slice_add_fusion, s32[96]{0:T(128)S(1)} %copy-done.2), kind=kOutput, calls=%fused_computation.42 | convolution fusion | flops 18886656 | bytes 229760 | tf_op jit(solution)/shard_map/dot_general | solution.py:183
  63.6 0.6 constant_dynamic-slice_fusion
  64.2 11.3 %shard_map.114 = bf16[96,128,128]{2,1,0:T(8,128)(2,1)} custom-call(bf16[96,128,256]{2,1,0:T(8,128)(2,1)} %bra_ref.3, bf16[96,128,256]{2,1,0:T(8,128)(2,1)} %ket_ref.3, f32[96,256]{1,0:T(8,128)} %fusion.27.local_ref), custom_call_target="tpu_custom_call" | custom-call | flops 805306368 | bytes 15826944 | tf_op jit(solution)/shard_map/pallas_call | solution.py:49
  (33 shorter events, 0.5 us)
Async XLA Ops:
  0.6 34.3 %copy-start = (f32[8,256,256]{2,1,0:T(8,128)S(1)}, f32[8,256,256]{2,1,0:T(8,128)}, u32[]{:S(2)}) copy-start(f32[8,256,256]{2,1,0:T(8,128)} %param.19) | copy-start | bytes 6291460
  1.9 11.2 %copy-start.2 = (s32[96]{0:T(128)S(1)}, s32[96]{0:T(128)}, u32[]{:S(2)}) copy-start(s32[96]{0:T(128)} %param.13) | copy-start | bytes 1156
  14.3 1.5 %collective-permute-start = (f32[159,256]{1,0:T(8,128)S(1)}, f32[159,256]{1,0:T(8,128)S(1)}, u32[]{:S(2)}, u32[]{:S(2)}) collective-permute-start(f32[159,256]{1,0:T(8,128)S(1)} %pad_maximum_fusion.1), channel_id=1, source_target_pairs={{0,1},{1,0},{2,3},{3,2},{4,5},{5,4},{6,7},{7,6},{8,9},{9,8},{10,11... | collective-permute-start | bytes 488456 | tf_op jit(solution)/shard_map/ppermute | solution.py:69
  15.8 6.5 %collective-permute-start.1 = (f32[159,256]{1,0:T(8,128)S(1)}, f32[159,256]{1,0:T(8,128)S(1)}, u32[]{:S(2)}, u32[]{:S(2)}) collective-permute-start(f32[159,256]{1,0:T(8,128)S(1)} %fusion.42), channel_id=1, source_target_pairs={{0,2},{1,3},{2,0},{3,1},{4,6},{5,7},{6,4},{7,5},{8,10},{9,11},{10,... | collective-permute-start | bytes 488456 | tf_op jit(solution)/shard_map/ppermute | solution.py:69
  22.3 5.6 %collective-permute-start.2 = (f32[159,256]{1,0:T(8,128)S(1)}, f32[159,256]{1,0:T(8,128)S(1)}, u32[]{:S(2)}, u32[]{:S(2)}) collective-permute-start(f32[159,256]{1,0:T(8,128)S(1)} %add.54), channel_id=1, source_target_pairs={{0,4},{1,5},{2,6},{3,7},{4,0},{5,1},{6,2},{7,3},{8,12},{9,13},{10,... | collective-permute-start | bytes 488456 | tf_op jit(solution)/shard_map/ppermute | solution.py:69
  28.0 6.9 %collective-permute-start.3 = (f32[159,256]{1,0:T(8,128)S(1)}, f32[159,256]{1,0:T(8,128)S(1)}, u32[]{:S(2)}, u32[]{:S(2)}) collective-permute-start(f32[159,256]{1,0:T(8,128)S(1)} %add.55), channel_id=1, source_target_pairs={{0,8},{1,9},{2,10},{3,11},{4,12},{5,13},{6,14},{7,15},{8,0},{9,1},... | collective-permute-start | bytes 488456 | tf_op jit(solution)/shard_map/ppermute | solution.py:69
  35.9 6.8 %collective-permute-start.4 = (f32[144,256]{1,0:T(8,128)S(1)}, f32[144,256]{1,0:T(8,128)S(1)}, u32[]{:S(2)}, u32[]{:S(2)}) collective-permute-start(f32[144,256]{1,0:T(8,128)S(1)} %pad_maximum_fusion.3), channel_id=1, source_target_pairs={{0,16},{16,0},{32,48},{48,32},{64,80},{80,64},{96,112},{112,96},{1... | collective-permute-start | bytes 442376 | tf_op jit(solution)/shard_map/ppermute | solution.py:69
  42.7 6.9 %collective-permute-start.5 = (f32[160,256]{1,0:T(8,128)S(1)}, f32[160,256]{1,0:T(8,128)S(1)}, u32[]{:S(2)}, u32[]{:S(2)}) collective-permute-start(f32[160,256]{1,0:T(8,128)S(1)} %pad_maximum_fusion.2), channel_id=1, source_target_pairs={{0,32},{16,48},{32,0},{48,16},{64,96},{80,112},{96,64},{112,80},{1... | collective-permute-start | bytes 491528 | tf_op jit(solution)/shard_map/ppermute | solution.py:69
  49.7 7.3 %collective-permute-start.6 = (f32[192,256]{1,0:T(8,128)S(1)}, f32[192,256]{1,0:T(8,128)S(1)}, u32[]{:S(2)}, u32[]{:S(2)}) collective-permute-start(f32[192,256]{1,0:T(8,128)S(1)} %pad_maximum_fusion), channel_id=1, source_target_pairs={{0,64},{16,80},{32,96},{48,112},{64,0},{80,16},{96,32},{112,48},{1... | collective-permute-start | bytes 589832 | tf_op jit(solution)/shard_map/ppermute | solution.py:69
  57.3 2.5 %copy-start.1 = (f32[16,256,256]{2,1,0:T(8,128)S(1)}, f32[16,256,256]{2,1,0:T(8,128)}, u32[]{:S(2)}) copy-start(f32[16,256,256]{2,1,0:T(8,128)} %param.18) | copy-start | bytes 12582916

commit v6 on v5

--- a/solution.py
+++ b/solution.py
@@ -5,29 +5,35 @@
 from jax.experimental.pallas import tpu as pltpu
 from jax.sharding import PartitionSpec as P
 
-TILE = 8
+def tile_of(blocks, most=48):
+    for tile in range(most, 7, -8):
+        if blocks % tile == 0:
+            return tile
+    return blocks
 
 
 def moments_kernel(dens_ref, bra_ref, ket_ref, out_ref):
-    mixed = jnp.einsum(
-        "bmn,bnk->bmk", dens_ref[...], ket_ref[...], preferred_element_type=jnp.float32
-    )
-    out_ref[...] = jnp.sum(bra_ref[...].astype(jnp.float32) * mixed, axis=1)
+    for j in range(out_ref.shape[0]):
+        mixed = jnp.dot(dens_ref[j], ket_ref[j], preferred_element_type=jnp.float32)
+        out_ref[pl.ds(j, 1), :] = jnp.sum(
+            bra_ref[j].astype(jnp.float32) * mixed, axis=0, keepdims=True
+        )
 
 
 def block_moments(density, bra_table, ket_table):
     blocks, rows, cols = density.shape
     coeffs = bra_table.shape[2]
+    tile = tile_of(blocks)
     return pl.pallas_call(
         moments_kernel,
         out_shape=jax.ShapeDtypeStruct((blocks, coeffs), jnp.float32),
-        grid=(blocks // TILE,),
+        grid=(blocks // tile,),
         in_specs=[
-            pl.BlockSpec((TILE, rows, cols), lambda i: (i, 0, 0)),
-            pl.BlockSpec((TILE, rows, coeffs), lambda i: (i, 0, 0)),
-            pl.BlockSpec((TILE, cols, coeffs), lambda i: (i, 0, 0)),
+            pl.BlockSpec((tile, rows, cols), lambda i: (i, 0, 0)),
+            pl.BlockSpec((tile, rows, coeffs), lambda i: (i, 0, 0)),
+            pl.BlockSpec((tile, cols, coeffs), lambda i: (i, 0, 0)),
         ],
-        out_specs=pl.BlockSpec((TILE, coeffs), lambda i: (i, 0)),
+        out_specs=pl.BlockSpec((tile, coeffs), lambda i: (i, 0)),
         cost_estimate=pl.CostEstimate(
             flops=2 * blocks * rows * cols * coeffs,
             transcendentals=0,
@@ -37,25 +43,27 @@
 
 
 def coulomb_kernel(bra_ref, ket_ref, local_ref, out_ref):
-    scaled = (bra_ref[...].astype(jnp.float32) * local_ref[...][:, None, :]).astype(jnp.bfloat16)
-    out_ref[...] = jnp.einsum(
-        "bmk,bnk->bmn", scaled, ket_ref[...], preferred_element_type=jnp.float32
-    ).astype(jnp.bfloat16)
+    for j in range(out_ref.shape[0]):
+        scaled = (bra_ref[j].astype(jnp.float32) * local_ref[pl.ds(j, 1), :]).astype(jnp.bfloat16)
+        out_ref[j] = lax.dot_general(
+            scaled, ket_ref[j], (((1,), (1,)), ((), ())), preferred_element_type=jnp.float32
+        ).astype(jnp.bfloat16)
 
 
 def block_coulomb(bra_table, ket_table, block_locals):
     blocks, rows, coeffs = bra_table.shape
     cols = ket_table.shape[1]
+    tile = tile_of(blocks)
     return pl.pallas_call(
         coulomb_kernel,
         out_shape=jax.ShapeDtypeStruct((blocks, rows, cols), jnp.bfloat16),
-        grid=(blocks // TILE,),
+        grid=(blocks // tile,),
         in_specs=[
-            pl.BlockSpec((TILE, rows, coeffs), lambda i: (i, 0, 0)),
-            pl.BlockSpec((TILE, cols, coeffs), lambda i: (i, 0, 0)),
-            pl.BlockSpec((TILE, coeffs), lambda i: (i, 0)),
+            pl.BlockSpec((tile, rows, coeffs), lambda i: (i, 0, 0)),
+            pl.BlockSpec((tile, cols, coeffs), lambda i: (i, 0, 0)),
+            pl.BlockSpec((tile, coeffs), lambda i: (i, 0)),
         ],
-        out_specs=pl.BlockSpec((TILE, rows, cols), lambda i: (i, 0, 0)),
+        out_specs=pl.BlockSpec((tile, rows, cols), lambda i: (i, 0, 0)),
         cost_estimate=pl.CostEstimate(
             flops=2 * blocks * rows * cols * coeffs,
             transcendentals=0,

time: 76.2 us -> 67.4 us (0.88)
  the two profiles are of different devices: /device:TPU:30 before, /device:TPU:22 now
where the time goes in v6:
time: 67.4 us; the launch traced here: 67.3 us
  waiting for transfers between devices  29.9 us (44%)
  Pallas kernels  14 us (21%)
  matrix products  10.7 us (16%)
  starting transfers between devices  8.65 us (13%)
  local copies, waits for them, and re-layouts  1.86 us (3%)
  other arithmetic  1.25 us (2%)
  between operations  0.92 us (1%)
    ppermute x7, waiting for transfers between devices, exchange(): return lax.ppermute(x, axis, [(i, i ^ mask) for i in range(count)])  29.9 us
    ppermute x7, starting transfers between devices, exchange(): return lax.ppermute(x, axis, [(i, i ^ mask) for i in range(count)])  8.65 us
    pallas_call x1, Pallas kernels, block_moments(): pl.pallas_call(moments_kernel, out_shape=jax.ShapeDtypeStruct((blocks, co...  7.2 us
    pallas_call x1, Pallas kernels, block_coulomb(): pl.pallas_call(coulomb_kernel, out_shape=jax.ShapeDtypeStruct((blocks, ro...  6.81 us
    dot_general x1, matrix products, shards(): gathered = jnp.einsum('btj,jk->btk', counts, window, precision=top)  2.48 us
    dot_general x1, matrix products, shards(): far = jnp.einsum('btk,tlk->bl', rows, translation, precision=top)  2.29 us
    dot_general x1, matrix products, shards(): jnp.einsum('blt,blj->btj', type_hot, src_hot, preferred_element_type=jnp....  1.85 us
  transfers between devices with their start and end apart: 7, of which 7 were waited for; matrix products, arithmetic and copies ran while one was open for 5% of the time, Pallas kernels for 0%

profile of v6, /device:TPU:22, one launch (start us, length us, event | category | flops | bytes accessed | tf_op | source)
XLA Modules:
  0.0 67.3 jit_solution(1764654811463548036)
XLA Ops:
  0.7 0.9 %add_convert_fusion = f32[18,27]{1,0:T(8,128)S(1)} fusion(s32[1,27]{1,0:T(1,128)} %param.17, s32[1,27]{1,0:T(1,128)} %param.16, s32[8,27]{1,0:T(8,128)} %param.15, s32[8,27]{1,0:T(8,128)} %param.14), kind=kLoop, calls=%fused_computation.49 | loop fusion | flops 1944 | bytes 3888 | tf_op jit(solution)/shard_map/convert_element_type | solution.py:126
  1.5 0.1 convert_element_type.27
  1.7 0.1 reshape.88
  1.9 7.2 %shard_map.113 = f32[96,256]{1,0:T(8,128)} custom-call(bf16[96,128,128]{2,1,0:T(8,128)(2,1)} %dens_ref.1, bf16[96,128,256]{2,1,0:T(8,128)(2,1)} %bra_ref.3, bf16[96,128,256]{2,1,0:T(8,128)(2,1)} %ket_ref.3), custom_call_target="tpu_custom_call" | custom-call | flops 805306368 | bytes 15826944 | tf_op jit(solution)/shard_map/pallas_call | solution.py:27
  9.1 1.2 %fusion.28 = f32[128,256]{1,0:T(8,128)S(1)} fusion(f32[96,256]{1,0:T(8,128)} %shard_map.113, s32[96]{0:T(128)S(1)} %copy-done.2), kind=kOutput, calls=%fused_computation.43 | convolution fusion | flops 18886656 | bytes 229760 | tf_op jit(solution)/shard_map/dot_general | solution.py:135
  10.3 0.1 collective-permute-start
  10.4 1.4 %collective-permute-done = f32[159,256]{1,0:T(8,128)S(1)} collective-permute-done((f32[159,256]{1,0:T(8,128)S(1)}, f32[159,256]{1,0:T(8,128)S(1)}, u32[]{:S(2)}, u32[]{:S(2)}) %collective-permute-start) | collective-permute-done | bytes 162848 | tf_op jit(solution)/shard_map/ppermute | solution.py:77
  11.8 2.0 %collective-permute-start.1 = (f32[159,256]{1,0:T(8,128)S(1)}, f32[159,256]{1,0:T(8,128)S(1)}, u32[]{:S(2)}, u32[]{:S(2)}) collective-permute-start(f32[159,256]{1,0:T(8,128)S(1)} %fusion.42), channel_id=1, source_target_pairs={{0,2},{1,3},{2,0},{3,1},{4,6},{5,7},{6,4},{7,5},{8,10},{9,11},{10,... | collective-permute-start | bytes 488456 | tf_op jit(solution)/shard_map/ppermute | solution.py:77
  13.8 4.5 %collective-permute-done.1 = f32[159,256]{1,0:T(8,128)S(1)} collective-permute-done((f32[159,256]{1,0:T(8,128)S(1)}, f32[159,256]{1,0:T(8,128)S(1)}, u32[]{:S(2)}, u32[]{:S(2)}) %collective-permute-start.1) | collective-permute-done | bytes 162848 | tf_op jit(solution)/shard_map/ppermute | solution.py:77
  18.3 1.4 %collective-permute-start.2 = (f32[159,256]{1,0:T(8,128)S(1)}, f32[159,256]{1,0:T(8,128)S(1)}, u32[]{:S(2)}, u32[]{:S(2)}) collective-permute-start(f32[159,256]{1,0:T(8,128)S(1)} %add.54), channel_id=1, source_target_pairs={{0,4},{1,5},{2,6},{3,7},{4,0},{5,1},{6,2},{7,3},{8,12},{9,13},{10,... | collective-permute-start | bytes 488456 | tf_op jit(solution)/shard_map/ppermute | solution.py:77
  19.7 4.3 %collective-permute-done.2 = f32[159,256]{1,0:T(8,128)S(1)} collective-permute-done((f32[159,256]{1,0:T(8,128)S(1)}, f32[159,256]{1,0:T(8,128)S(1)}, u32[]{:S(2)}, u32[]{:S(2)}) %collective-permute-start.2) | collective-permute-done | bytes 162848 | tf_op jit(solution)/shard_map/ppermute | solution.py:77
  24.0 0.4 collective-permute-start.3
  24.4 6.5 %collective-permute-done.3 = f32[159,256]{1,0:T(8,128)S(1)} collective-permute-done((f32[159,256]{1,0:T(8,128)S(1)}, f32[159,256]{1,0:T(8,128)S(1)}, u32[]{:S(2)}, u32[]{:S(2)}) %collective-permute-start.3) | collective-permute-done | bytes 162848 | tf_op jit(solution)/shard_map/ppermute | solution.py:77
  31.0 0.9 %convolution_bitcast_fusion = f32[16,256]{1,0:T(8,128)S(1)} fusion(f32[8,256,256]{2,1,0:T(8,128)S(1)} %copy-done, f32[16,8,256]{2,1,0:T(8,128)S(1)} %get-tuple-element.9), kind=kOutput, calls=%fused_computation.10 | convolution fusion | flops 50331648 | bytes 2244608 | tf_op jit(solution)/shard_map/qce,cde->qd/dot_general | solution.py:147
  31.9 0.9 %collective-permute-start.4 = (f32[144,256]{1,0:T(8,128)S(1)}, f32[144,256]{1,0:T(8,128)S(1)}, u32[]{:S(2)}, u32[]{:S(2)}) collective-permute-start(f32[144,256]{1,0:T(8,128)S(1)} %pad_maximum_fusion.3), channel_id=1, source_target_pairs={{0,16},{16,0},{32,48},{48,32},{64,80},{80,64},{96,112},{112,96},{1... | collective-permute-start | bytes 442376 | tf_op jit(solution)/shard_map/ppermute | solution.py:77
  32.8 0.2 convert_element_type.29
  33.2 0.6 copy.17
  33.8 1.9 %fusion = f32[128,16,384]{2,1,0:T(8,128)S(1)} fusion(pred[128,27,16]{1,2,0:T(8,128)(4,1)S(1)} %copy.17, s32[128,27]{1,0:T(8,128)S(1)} %get-tuple-element.4), kind=kOutput, calls=%fused_computation.1 | convolution fusion | flops 43794432 | bytes 3214848 | tf_op jit(solution)/shard_map/blt,blj->btj/dot_general | solution.py:175
  35.7 3.0 %collective-permute-done.4 = f32[144,256]{1,0:T(8,128)S(1)} collective-permute-done((f32[144,256]{1,0:T(8,128)S(1)}, f32[144,256]{1,0:T(8,128)S(1)}, u32[]{:S(2)}, u32[]{:S(2)}) %collective-permute-start.4) | collective-permute-done | bytes 147488 | tf_op jit(solution)/shard_map/ppermute | solution.py:77
  38.8 0.1 collective-permute-start.5
  38.9 6.8 %collective-permute-done.5 = f32[160,256]{1,0:T(8,128)S(1)} collective-permute-done((f32[160,256]{1,0:T(8,128)S(1)}, f32[160,256]{1,0:T(8,128)S(1)}, u32[]{:S(2)}, u32[]{:S(2)}) %collective-permute-start.5) | collective-permute-done | bytes 163872 | tf_op jit(solution)/shard_map/ppermute | solution.py:77
  45.7 3.8 %collective-permute-start.6 = (f32[192,256]{1,0:T(8,128)S(1)}, f32[192,256]{1,0:T(8,128)S(1)}, u32[]{:S(2)}, u32[]{:S(2)}) collective-permute-start(f32[192,256]{1,0:T(8,128)S(1)} %pad_maximum_fusion), channel_id=1, source_target_pairs={{0,64},{16,80},{32,96},{48,112},{64,0},{80,16},{96,32},{112,48},{1... | collective-permute-start | bytes 589832 | tf_op jit(solution)/shard_map/ppermute | solution.py:77
  49.5 0.2 fusion.15
  49.8 3.4 %collective-permute-done.6 = f32[192,256]{1,0:T(8,128)S(1)} collective-permute-done((f32[192,256]{1,0:T(8,128)S(1)}, f32[192,256]{1,0:T(8,128)S(1)}, u32[]{:S(2)}, u32[]{:S(2)}) %collective-permute-start.6) | collective-permute-done | bytes 196640 | tf_op jit(solution)/shard_map/ppermute | solution.py:77
  53.2 0.3 fusion.16
  53.5 2.5 %fusion.1 = f32[128,16,256]{2,0,1:T(8,128)S(1)} fusion(f32[128,16,384]{2,1,0:T(8,128)S(1)} %fusion, f32[128,256]{1,0:T(8,128)S(1)} %get-tuple-element.3, f32[128,256]{1,0:T(8,128)S(1)} %get-tuple-element.8, f32[128,256]{1,0:T(8,128)S(1)} %get-tuple-element.2), kind=kOutput, calls=%fused_computation.2 | convolution fusion | flops 1208156160 | bytes 5636096 | tf_op jit(solution)/shard_map/btj,jk->btk/dot_general | solution.py:176
  56.0 2.3 %fusion.8 = f32[144,256]{1,0:T(8,128)S(1)} fusion(f32[16,256,256]{2,1,0:T(8,128)S(1)} %copy-done.1, f32[16,16,256]{2,0,1:T(8,128)S(1)} %fusion.16, f32[128,16,256]{2,0,1:T(8,128)S(1)} %fusion.1), kind=kOutput, calls=%fused_computation.9 | convolution fusion | flops 906559488 | bytes 6701056 | tf_op jit(solution)/shard_map/btk,tlk->bl/dot_general | solution.py:183
  58.3 0.6 fusion.31
  58.9 0.1 slice_add_fusion
  59.0 0.8 %fusion.27.local_ref = f32[96,256]{1,0:T(8,128)} fusion(f32[128,256]{1,0:T(8,128)S(1)} %slice_add_fusion, s32[96]{0:T(128)S(1)} %copy-done.2), kind=kOutput, calls=%fused_computation.42 | convolution fusion | flops 18886656 | bytes 229760 | tf_op jit(solution)/shard_map/dot_general | solution.py:191
  59.8 0.6 constant_dynamic-slice_fusion
  60.4 6.8 %shard_map.114 = bf16[96,128,128]{2,1,0:T(8,128)(2,1)} custom-call(bf16[96,128,256]{2,1,0:T(8,128)(2,1)} %bra_ref.3, bf16[96,128,256]{2,1,0:T(8,128)(2,1)} %ket_ref.3, f32[96,256]{1,0:T(8,128)} %fusion.27.local_ref), custom_call_target="tpu_custom_call" | custom-call | flops 805306368 | bytes 15826944 | tf_op jit(solution)/shard_map/pallas_call | solution.py:57
  (33 shorter events, 0.5 us)
Async XLA Ops:
  0.6 30.3 %copy-start = (f32[8,256,256]{2,1,0:T(8,128)S(1)}, f32[8,256,256]{2,1,0:T(8,128)}, u32[]{:S(2)}) copy-start(f32[8,256,256]{2,1,0:T(8,128)} %param.19) | copy-start | bytes 6291460
  1.9 7.2 %copy-start.2 = (s32[96]{0:T(128)S(1)}, s32[96]{0:T(128)}, u32[]{:S(2)}) copy-start(s32[96]{0:T(128)} %param.13) | copy-start | bytes 1156
  10.3 1.5 %collective-permute-start = (f32[159,256]{1,0:T(8,128)S(1)}, f32[159,256]{1,0:T(8,128)S(1)}, u32[]{:S(2)}, u32[]{:S(2)}) collective-permute-start(f32[159,256]{1,0:T(8,128)S(1)} %pad_maximum_fusion.1), channel_id=1, source_target_pairs={{0,1},{1,0},{2,3},{3,2},{4,5},{5,4},{6,7},{7,6},{8,9},{9,8},{10,11... | collective-permute-start | bytes 488456 | tf_op jit(solution)/shard_map/ppermute | solution.py:77
  11.8 6.5 %collective-permute-start.1 = (f32[159,256]{1,0:T(8,128)S(1)}, f32[159,256]{1,0:T(8,128)S(1)}, u32[]{:S(2)}, u32[]{:S(2)}) collective-permute-start(f32[159,256]{1,0:T(8,128)S(1)} %fusion.42), channel_id=1, source_target_pairs={{0,2},{1,3},{2,0},{3,1},{4,6},{5,7},{6,4},{7,5},{8,10},{9,11},{10,... | collective-permute-start | bytes 488456 | tf_op jit(solution)/shard_map/ppermute | solution.py:77
  18.3 5.6 %collective-permute-start.2 = (f32[159,256]{1,0:T(8,128)S(1)}, f32[159,256]{1,0:T(8,128)S(1)}, u32[]{:S(2)}, u32[]{:S(2)}) collective-permute-start(f32[159,256]{1,0:T(8,128)S(1)} %add.54), channel_id=1, source_target_pairs={{0,4},{1,5},{2,6},{3,7},{4,0},{5,1},{6,2},{7,3},{8,12},{9,13},{10,... | collective-permute-start | bytes 488456 | tf_op jit(solution)/shard_map/ppermute | solution.py:77
  24.0 6.9 %collective-permute-start.3 = (f32[159,256]{1,0:T(8,128)S(1)}, f32[159,256]{1,0:T(8,128)S(1)}, u32[]{:S(2)}, u32[]{:S(2)}) collective-permute-start(f32[159,256]{1,0:T(8,128)S(1)} %add.55), channel_id=1, source_target_pairs={{0,8},{1,9},{2,10},{3,11},{4,12},{5,13},{6,14},{7,15},{8,0},{9,1},... | collective-permute-start | bytes 488456 | tf_op jit(solution)/shard_map/ppermute | solution.py:77
  31.9 6.8 %collective-permute-start.4 = (f32[144,256]{1,0:T(8,128)S(1)}, f32[144,256]{1,0:T(8,128)S(1)}, u32[]{:S(2)}, u32[]{:S(2)}) collective-permute-start(f32[144,256]{1,0:T(8,128)S(1)} %pad_maximum_fusion.3), channel_id=1, source_target_pairs={{0,16},{16,0},{32,48},{48,32},{64,80},{80,64},{96,112},{112,96},{1... | collective-permute-start | bytes 442376 | tf_op jit(solution)/shard_map/ppermute | solution.py:77
  38.8 6.9 %collective-permute-start.5 = (f32[160,256]{1,0:T(8,128)S(1)}, f32[160,256]{1,0:T(8,128)S(1)}, u32[]{:S(2)}, u32[]{:S(2)}) collective-permute-start(f32[160,256]{1,0:T(8,128)S(1)} %pad_maximum_fusion.2), channel_id=1, source_target_pairs={{0,32},{16,48},{32,0},{48,16},{64,96},{80,112},{96,64},{112,80},{1... | collective-permute-start | bytes 491528 | tf_op jit(solution)/shard_map/ppermute | solution.py:77
  45.7 7.4 %collective-permute-start.6 = (f32[192,256]{1,0:T(8,128)S(1)}, f32[192,256]{1,0:T(8,128)S(1)}, u32[]{:S(2)}, u32[]{:S(2)}) collective-permute-start(f32[192,256]{1,0:T(8,128)S(1)} %pad_maximum_fusion), channel_id=1, source_target_pairs={{0,64},{16,80},{32,96},{48,112},{64,0},{80,16},{96,32},{112,48},{1... | collective-permute-start | bytes 589832 | tf_op jit(solution)/shard_map/ppermute | solution.py:77
  53.5 2.5 %copy-start.1 = (f32[16,256,256]{2,1,0:T(8,128)S(1)}, f32[16,256,256]{2,1,0:T(8,128)}, u32[]{:S(2)}) copy-start(f32[16,256,256]{2,1,0:T(8,128)} %param.18) | copy-start | bytes 12582916

commit v7 on v6

--- a/solution.py
+++ b/solution.py
@@ -75,6 +75,43 @@
 def exchange(x, axis, mask):
     count = lax.axis_size(axis)
     return lax.ppermute(x, axis, [(i, i ^ mask) for i in range(count)])
+
+
+def joint(x, target_of):
+    n_space = lax.axis_size("space")
+    n_blk = lax.axis_size("blk")
+    pairs = []
+    for a in range(n_space):
+        for b in range(n_blk):
+            ta, tb = target_of(a, b)
+            pairs.append((a * n_blk + b, ta * n_blk + tb))
+    return lax.ppermute(x, ("space", "blk"), pairs)
+
+
+def two_port(x, first, second, axis):
+    n_blk = lax.axis_size("blk")
+    chips = n_blk // 2 if axis == "blk" else lax.axis_size("space")
+
+    def target_of(a, b):
+        step = first if b % 2 == 0 else second
+        if axis == "blk":
+            return a, 2 * ((b // 2 + step) % chips) + b % 2
+        return (a + step) % chips, b
+
+    got = joint(x, target_of)
+    other = exchange(got, "blk", 1)
+    core0 = lax.axis_index("blk") % 2 == 0
+    return jnp.where(core0, got, other), jnp.where(core0, other, got)
+
+
+def chip_sum(x):
+    chip = x + exchange(x, "blk", 1)
+    behind1, behind2 = two_port(chip, 1, 2, "blk")
+    pair = chip + behind1
+    three = pair + behind2
+    core0 = lax.axis_index("blk") % 2 == 0
+    behind3, behind6 = two_port(jnp.where(core0, three, pair), 3, 6, "blk")
+    return (three + behind3) + behind6
 
 
 def butterfly_sum(x, axis):
@@ -135,7 +172,11 @@
     partial_moments = lax.dot_general(
         box_hot, moments, (((0,), (0,)), ((), ())), precision=top
     )
-    summed = butterfly_sum(jnp.concatenate([partial_moments, table], axis=0), "blk")
+    stacked = jnp.concatenate([partial_moments, table], axis=0)
+    if n_blk == 16:
+        summed = chip_sum(stacked)
+    else:
+        summed = butterfly_sum(stacked, "blk")
     domain = summed[:box_dom]
     table = summed[box_dom:].reshape(-1)[: n_blk * flat].reshape((n_blk,) + lists.shape)
     table = table.astype(jnp.int32)
@@ -147,28 +188,44 @@
     domain_parents = jnp.einsum(
         "qce,cde->qd", domain.reshape(n_blk, leaves, coeffs), upward_translation_table, precision=top
     )
-    parents = domain_parents
-    carried = domain
-    delivered = []
-    mask = 1
-    while mask < n_space:
-        got = exchange(jnp.concatenate([carried, parents], axis=0), "space", mask)
-        carried = got[:box_dom]
-        delivered.append(carried)
-        parents = jnp.concatenate([parents, got[box_dom:]], axis=0)
-        mask *= 2
-    all_parents = parents
-
-    def neighbour(step):
-        other = here + step
-        pick = jnp.zeros_like(domain)
-        for r, block in enumerate(delivered):
-            pick = jnp.where((here ^ other) == 2 ** (r + 1) - 1, block, pick)
-        inside = (other >= 0) & (other < n_space)
-        return jnp.where(inside, pick, 0.0)
-
-    window = jnp.concatenate([neighbour(-1), domain, neighbour(1)], axis=0)
-    dom_csrc = (dom_csrc // n_blk ^ here) * n_blk + dom_csrc % n_blk
+    if n_space == 8 and n_blk % 2 == 0:
+        first = jnp.concatenate([domain, domain_parents], axis=0)
+        behind1, behind2 = two_port(first, 1, 2, "space")
+        low_block = behind1[:box_dom]
+        parents = jnp.concatenate([domain_parents, behind1[box_dom:], behind2[box_dom:]], axis=0)
+        second = jnp.concatenate([low_block, parents], axis=0)
+        behind3, behind6 = two_port(second, 3, 6, "space")
+        high_block = behind6[:box_dom]
+        all_parents = jnp.concatenate(
+            [parents, behind3[box_dom:], behind6[box_dom : box_dom + 2 * n_blk]], axis=0
+        )
+        low = jnp.where(here > 0, low_block, 0.0)
+        high = jnp.where(here < n_space - 1, high_block, 0.0)
+        window = jnp.concatenate([low, domain, high], axis=0)
+        dom_csrc = ((here - dom_csrc // n_blk) % n_space) * n_blk + dom_csrc % n_blk
+    else:
+        parents = domain_parents
+        carried = domain
+        delivered = []
+        mask = 1
+        while mask < n_space:
+            got = exchange(jnp.concatenate([carried, parents], axis=0), "space", mask)
+            carried = got[:box_dom]
+            delivered.append(carried)
+            parents = jnp.concatenate([parents, got[box_dom:]], axis=0)
+            mask *= 2
+        all_parents = parents
+
+        def neighbour(step):
+            other = here + step
+            pick = jnp.zeros_like(domain)
+            for r, block in enumerate(delivered):
+                pick = jnp.where((here ^ other) == 2 ** (r + 1) - 1, block, pick)
+            inside = (other >= 0) & (other < n_space)
+            return jnp.where(inside, pick, 0.0)
+
+        window = jnp.concatenate([neighbour(-1), domain, neighbour(1)], axis=0)
+        dom_csrc = (dom_csrc // n_blk ^ here) * n_blk + dom_csrc % n_blk
 
     src_hot = (dom_src[..., None] == jnp.arange(3 * box_dom, dtype=jnp.int32)).astype(jnp.bfloat16)
     type_hot = (dom_type[..., None] == jnp.arange(n_types, dtype=jnp.int32)).astype(jnp.bfloat16)

time: 67.4 us -> 69 us (1.024)
  the two profiles are of different devices: /device:TPU:22 before, /device:TPU:0 now
where the time goes in v7:
time: 69 us; the launch traced here: 67.8 us
  waiting for transfers between devices  35.1 us (51%)
  Pallas kernels  14 us (20%)
  matrix products  10.7 us (16%)
  starting transfers between devices  3.9 us (6%)
  local copies, waits for them, and re-layouts  1.84 us (3%)
  other arithmetic  1.32 us (2%)
  between operations  0.95 us (1%)
    ppermute x4, waiting for transfers between devices, joint(): return lax.ppermute(x, ('space', 'blk'), pairs)  28.4 us
    pallas_call x1, Pallas kernels, block_moments(): pl.pallas_call(moments_kernel, out_shape=jax.ShapeDtypeStruct((blocks, co...  7.2 us
    pallas_call x1, Pallas kernels, block_coulomb(): pl.pallas_call(coulomb_kernel, out_shape=jax.ShapeDtypeStruct((blocks, ro...  6.8 us
    ppermute x5, waiting for transfers between devices, exchange(): return lax.ppermute(x, axis, [(i, i ^ mask) for i in range(count)])  6.68 us
    ppermute x4, starting transfers between devices, joint(): return lax.ppermute(x, ('space', 'blk'), pairs)  3.81 us
    dot_general x1, matrix products, shards(): gathered = jnp.einsum('btj,jk->btk', counts, window, precision=top)  2.48 us
    dot_general x1, matrix products, shards(): far = jnp.einsum('btk,tlk->bl', rows, translation, precision=top)  2.29 us
    dot_general x1, matrix products, shards(): jnp.einsum('blt,blj->btj', type_hot, src_hot, preferred_element_type=jnp....  1.85 us
  transfers between devices with their start and end apart: 9, of which 9 were waited for; matrix products, arithmetic and copies ran while one was open for 5% of the time, Pallas kernels for 0%

profile of v7, /device:TPU:0, one launch (start us, length us, event | category | flops | bytes accessed | tf_op | source)
XLA Modules:
  0.0 67.8 jit_solution(1525429116783882571)
XLA Ops:
  0.7 0.9 %add_convert_fusion = f32[18,27]{1,0:T(8,128)S(1)} fusion(s32[1,27]{1,0:T(1,128)} %param.17, s32[1,27]{1,0:T(1,128)} %param.16, s32[8,27]{1,0:T(8,128)} %param.15, s32[8,27]{1,0:T(8,128)} %param.14), kind=kLoop, calls=%fused_computation.52 | loop fusion | flops 1944 | bytes 3888 | tf_op jit(solution)/shard_map/convert_element_type | solution.py:163
  1.5 0.1 convert_element_type.27
  1.7 0.1 reshape.99
  1.9 7.2 %shard_map.113 = f32[96,256]{1,0:T(8,128)} custom-call(bf16[96,128,128]{2,1,0:T(8,128)(2,1)} %dens_ref.1, bf16[96,128,256]{2,1,0:T(8,128)(2,1)} %bra_ref.3, bf16[96,128,256]{2,1,0:T(8,128)(2,1)} %ket_ref.3), custom_call_target="tpu_custom_call" | custom-call | flops 805306368 | bytes 15826944 | tf_op jit(solution)/shard_map/pallas_call | solution.py:27
  9.1 1.2 %fusion.25 = f32[128,256]{1,0:T(8,128)S(1)} fusion(f32[96,256]{1,0:T(8,128)} %shard_map.113, s32[96]{0:T(128)S(1)} %copy-done.2), kind=kOutput, calls=%fused_computation.44 | convolution fusion | flops 18886656 | bytes 229760 | tf_op jit(solution)/shard_map/dot_general | solution.py:172
  10.3 0.1 collective-permute-start
  10.4 1.4 %collective-permute-done = f32[159,256]{1,0:T(8,128)S(1)} collective-permute-done((f32[159,256]{1,0:T(8,128)S(1)}, f32[159,256]{1,0:T(8,128)S(1)}, u32[]{:S(2)}, u32[]{:S(2)}) %collective-permute-start) | collective-permute-done | bytes 162848 | tf_op jit(solution)/shard_map/ppermute | solution.py:77
  11.8 2.1 %collective-permute-start.1 = (f32[159,256]{1,0:T(8,128)S(1)}, f32[159,256]{1,0:T(8,128)S(1)}, u32[]{:S(2)}, u32[]{:S(2)}) collective-permute-start(f32[159,256]{1,0:T(8,128)S(1)} %fusion.36), channel_id=1, source_target_pairs={{0,2},{1,5},{2,4},{3,7},{4,6},{5,9},{6,8},{7,11},{8,10},{9,13},{10... | collective-permute-start | bytes 488456 | tf_op jit(solution)/shard_map/ppermute | solution.py:88
  13.9 7.0 %collective-permute-done.1 = f32[159,256]{1,0:T(8,128)S(1)} collective-permute-done((f32[159,256]{1,0:T(8,128)S(1)}, f32[159,256]{1,0:T(8,128)S(1)}, u32[]{:S(2)}, u32[]{:S(2)}) %collective-permute-start.1) | collective-permute-done | bytes 162848 | tf_op jit(solution)/shard_map/ppermute | solution.py:88
  20.8 1.4 %collective-permute-done.2 = f32[159,256]{1,0:T(8,128)S(1)} collective-permute-done((f32[159,256]{1,0:T(8,128)S(1)}, f32[159,256]{1,0:T(8,128)S(1)}, u32[]{:S(2)}, u32[]{:S(2)}) %collective-permute-start.2) | collective-permute-done | bytes 162848 | tf_op jit(solution)/shard_map/ppermute | solution.py:77
  22.3 0.1 collective-permute-start.3
  22.4 7.7 %collective-permute-done.3 = f32[159,256]{1,0:T(8,128)S(1)} collective-permute-done((f32[159,256]{1,0:T(8,128)S(1)}, f32[159,256]{1,0:T(8,128)S(1)}, u32[]{:S(2)}, u32[]{:S(2)}) %collective-permute-start.3) | collective-permute-done | bytes 162848 | tf_op jit(solution)/shard_map/ppermute | solution.py:88
  30.1 1.4 %collective-permute-done.4 = f32[159,256]{1,0:T(8,128)S(1)} collective-permute-done((f32[159,256]{1,0:T(8,128)S(1)}, f32[159,256]{1,0:T(8,128)S(1)}, u32[]{:S(2)}, u32[]{:S(2)}) %collective-permute-start.4) | collective-permute-done | bytes 162848 | tf_op jit(solution)/shard_map/ppermute | solution.py:77
  31.6 0.9 %constant_dynamic-update-slice_fusion.2 = (f32[128,256]{1,0:T(8,128)S(1)}, f32[16,256]{1,0:T(8,128)S(1)}) fusion(f32[8,256,256]{2,1,0:T(8,128)S(1)} %copy-done, f32[16,8,256]{2,1,0:T(8,128)S(1)} %get-tuple-element.9), kind=kOutput, calls=%fused_computation.63 | convolution fusion | flops 50331648 | bytes 2260992 | tf_op jit(solution)/shard_map/qce,cde->qd/dot_general | solution.py:188
  32.5 1.6 %collective-permute-start.5 = (f32[144,256]{1,0:T(8,128)S(1)}, f32[144,256]{1,0:T(8,128)S(1)}, u32[]{:S(2)}, u32[]{:S(2)}) collective-permute-start(f32[144,256]{1,0:T(8,128)S(1)} %pad_maximum_fusion.2), channel_id=1, source_target_pairs={{0,16},{1,33},{2,18},{3,35},{4,20},{5,37},{6,22},{7,39},{8,24},{9,... | collective-permute-start | bytes 442376 | tf_op jit(solution)/shard_map/ppermute | solution.py:88
  34.1 0.2 convert_element_type.29
  34.5 0.6 copy.17
  35.1 1.9 %fusion = f32[128,16,384]{2,1,0:T(8,128)S(1)} fusion(pred[128,27,16]{1,2,0:T(8,128)(4,1)S(1)} %copy.17, s32[128,27]{1,0:T(8,128)S(1)} %get-tuple-element.4), kind=kOutput, calls=%fused_computation.1 | convolution fusion | flops 43794432 | bytes 3214848 | tf_op jit(solution)/shard_map/blt,blj->btj/dot_general | solution.py:232
  36.9 5.9 %collective-permute-done.5 = f32[144,256]{1,0:T(8,128)S(1)} collective-permute-done((f32[144,256]{1,0:T(8,128)S(1)}, f32[144,256]{1,0:T(8,128)S(1)}, u32[]{:S(2)}, u32[]{:S(2)}) %collective-permute-start.5) | collective-permute-done | bytes 147488 | tf_op jit(solution)/shard_map/ppermute | solution.py:88
  42.8 1.4 %collective-permute-done.6 = f32[144,256]{1,0:T(8,128)S(1)} collective-permute-done((f32[144,256]{1,0:T(8,128)S(1)}, f32[144,256]{1,0:T(8,128)S(1)}, u32[]{:S(2)}, u32[]{:S(2)}) %collective-permute-start.6) | collective-permute-done | bytes 147488 | tf_op jit(solution)/shard_map/ppermute | solution.py:77
  44.3 0.1 collective-permute-start.7
  44.4 7.9 %collective-permute-done.7 = f32[176,256]{1,0:T(8,128)S(1)} collective-permute-done((f32[176,256]{1,0:T(8,128)S(1)}, f32[176,256]{1,0:T(8,128)S(1)}, u32[]{:S(2)}, u32[]{:S(2)}) %collective-permute-start.7) | collective-permute-done | bytes 180256 | tf_op jit(solution)/shard_map/ppermute | solution.py:88
  52.3 0.2 fusion.15
  52.5 1.2 %collective-permute-done.8 = f32[176,256]{1,0:T(8,128)S(1)} collective-permute-done((f32[176,256]{1,0:T(8,128)S(1)}, f32[176,256]{1,0:T(8,128)S(1)}, u32[]{:S(2)}, u32[]{:S(2)}) %collective-permute-start.8) | collective-permute-done | bytes 180256 | tf_op jit(solution)/shard_map/ppermute | solution.py:77
  53.8 0.3 fusion.17
  54.0 2.5 %fusion.1 = f32[128,16,256]{2,0,1:T(8,128)S(1)} fusion(f32[128,16,384]{2,1,0:T(8,128)S(1)} %fusion, f32[128,256]{1,0:T(8,128)S(1)} %slice_select_fusion, f32[128,256]{1,0:T(8,128)S(1)} %get-tuple-element.8, f32[128,256]{1,0:T(8,128)S(1)} %get-tuple-element.10), kind=kOutput, calls=%fused_computation.2 | convolution fusion | flops 1208156160 | bytes 5636096 | tf_op jit(solution)/shard_map/btj,jk->btk/dot_general | solution.py:233
  56.5 2.3 %fusion.8 = f32[144,256]{1,0:T(8,128)S(1)} fusion(f32[16,256,256]{2,1,0:T(8,128)S(1)} %copy-done.1, f32[16,16,256]{2,0,1:T(8,128)S(1)} %fusion.17, f32[128,16,256]{2,0,1:T(8,128)S(1)} %fusion.1), kind=kOutput, calls=%fused_computation.9 | convolution fusion | flops 906559488 | bytes 6701056 | tf_op jit(solution)/shard_map/btk,tlk->bl/dot_general | solution.py:240
  58.8 0.6 fusion.28
  59.4 0.1 slice_add_fusion
  59.5 0.9 %fusion.24.local_ref = f32[96,256]{1,0:T(8,128)} fusion(f32[128,256]{1,0:T(8,128)S(1)} %slice_add_fusion, s32[96]{0:T(128)S(1)} %copy-done.2), kind=kOutput, calls=%fused_computation.43 | convolution fusion | flops 18886656 | bytes 229760 | tf_op jit(solution)/shard_map/dot_general | solution.py:248
  60.4 0.6 constant_dynamic-slice_fusion
  61.0 6.8 %shard_map.114 = bf16[96,128,128]{2,1,0:T(8,128)(2,1)} custom-call(bf16[96,128,256]{2,1,0:T(8,128)(2,1)} %bra_ref.3, bf16[96,128,256]{2,1,0:T(8,128)(2,1)} %ket_ref.3, f32[96,256]{1,0:T(8,128)} %fusion.24.local_ref), custom_call_target="tpu_custom_call" | custom-call | flops 805306368 | bytes 15826944 | tf_op jit(solution)/shard_map/pallas_call | solution.py:57
  (37 shorter events, 0.6 us)
Async XLA Ops:
  0.6 31.0 %copy-start = (f32[8,256,256]{2,1,0:T(8,128)S(1)}, f32[8,256,256]{2,1,0:T(8,128)}, u32[]{:S(2)}) copy-start(f32[8,256,256]{2,1,0:T(8,128)} %param.19) | copy-start | bytes 6291460
  1.9 7.2 %copy-start.2 = (s32[96]{0:T(128)S(1)}, s32[96]{0:T(128)}, u32[]{:S(2)}) copy-start(s32[96]{0:T(128)} %param.13) | copy-start | bytes 1156
  10.3 1.5 %collective-permute-start = (f32[159,256]{1,0:T(8,128)S(1)}, f32[159,256]{1,0:T(8,128)S(1)}, u32[]{:S(2)}, u32[]{:S(2)}) collective-permute-start(f32[159,256]{1,0:T(8,128)S(1)} %pad_maximum_fusion.1), channel_id=1, source_target_pairs={{0,1},{1,0},{2,3},{3,2},{4,5},{5,4},{6,7},{7,6},{8,9},{9,8},{10,11... | collective-permute-start | bytes 488456 | tf_op jit(solution)/shard_map/ppermute | solution.py:77
  11.8 9.1 %collective-permute-start.1 = (f32[159,256]{1,0:T(8,128)S(1)}, f32[159,256]{1,0:T(8,128)S(1)}, u32[]{:S(2)}, u32[]{:S(2)}) collective-permute-start(f32[159,256]{1,0:T(8,128)S(1)} %fusion.36), channel_id=1, source_target_pairs={{0,2},{1,5},{2,4},{3,7},{4,6},{5,9},{6,8},{7,11},{8,10},{9,13},{10... | collective-permute-start | bytes 488456 | tf_op jit(solution)/shard_map/ppermute | solution.py:88
  20.8 1.4 %collective-permute-start.2 = (f32[159,256]{1,0:T(8,128)S(1)}, f32[159,256]{1,0:T(8,128)S(1)}, u32[]{:S(2)}, u32[]{:S(2)}) collective-permute-start(f32[159,256]{1,0:T(8,128)S(1)} %collective-permute-done.1), channel_id=1, source_target_pairs={{0,1},{1,0},{2,3},{3,2},{4,5},{5,4},{6,7},{7,6},{8,9},{9,8},{10,11... | collective-permute-start | bytes 488456 | tf_op jit(solution)/shard_map/ppermute | solution.py:77
  22.3 7.8 %collective-permute-start.3 = (f32[159,256]{1,0:T(8,128)S(1)}, f32[159,256]{1,0:T(8,128)S(1)}, u32[]{:S(2)}, u32[]{:S(2)}) collective-permute-start(f32[159,256]{1,0:T(8,128)S(1)} %fusion.16), channel_id=1, source_target_pairs={{0,6},{1,13},{2,8},{3,15},{4,10},{5,1},{6,12},{7,3},{8,14},{9,5},{... | collective-permute-start | bytes 488456 | tf_op jit(solution)/shard_map/ppermute | solution.py:88
  30.1 1.4 %collective-permute-start.4 = (f32[159,256]{1,0:T(8,128)S(1)}, f32[159,256]{1,0:T(8,128)S(1)}, u32[]{:S(2)}, u32[]{:S(2)}) collective-permute-start(f32[159,256]{1,0:T(8,128)S(1)} %collective-permute-done.3), channel_id=1, source_target_pairs={{0,1},{1,0},{2,3},{3,2},{4,5},{5,4},{6,7},{7,6},{8,9},{9,8},{10,11... | collective-permute-start | bytes 488456 | tf_op jit(solution)/shard_map/ppermute | solution.py:77
  32.5 10.3 %collective-permute-start.5 = (f32[144,256]{1,0:T(8,128)S(1)}, f32[144,256]{1,0:T(8,128)S(1)}, u32[]{:S(2)}, u32[]{:S(2)}) collective-permute-start(f32[144,256]{1,0:T(8,128)S(1)} %pad_maximum_fusion.2), channel_id=1, source_target_pairs={{0,16},{1,33},{2,18},{3,35},{4,20},{5,37},{6,22},{7,39},{8,24},{9,... | collective-permute-start | bytes 442376 | tf_op jit(solution)/shard_map/ppermute | solution.py:88
  42.8 1.4 %collective-permute-start.6 = (f32[144,256]{1,0:T(8,128)S(1)}, f32[144,256]{1,0:T(8,128)S(1)}, u32[]{:S(2)}, u32[]{:S(2)}) collective-permute-start(f32[144,256]{1,0:T(8,128)S(1)} %collective-permute-done.5), channel_id=1, source_target_pairs={{0,1},{1,0},{2,3},{3,2},{4,5},{5,4},{6,7},{7,6},{8,9},{9,8},{10,11... | collective-permute-start | bytes 442376 | tf_op jit(solution)/shard_map/ppermute | solution.py:77
  44.3 8.0 %collective-permute-start.7 = (f32[176,256]{1,0:T(8,128)S(1)}, f32[176,256]{1,0:T(8,128)S(1)}, u32[]{:S(2)}, u32[]{:S(2)}) collective-permute-start(f32[176,256]{1,0:T(8,128)S(1)} %pad_maximum_fusion), channel_id=1, source_target_pairs={{0,48},{1,97},{2,50},{3,99},{4,52},{5,101},{6,54},{7,103},{8,56},{... | collective-permute-start | bytes 540680 | tf_op jit(solution)/shard_map/ppermute | solution.py:88
  52.3 1.4 %collective-permute-start.8 = (f32[176,256]{1,0:T(8,128)S(1)}, f32[176,256]{1,0:T(8,128)S(1)}, u32[]{:S(2)}, u32[]{:S(2)}) collective-permute-start(f32[176,256]{1,0:T(8,128)S(1)} %collective-permute-done.7), channel_id=1, source_target_pairs={{0,1},{1,0},{2,3},{3,2},{4,5},{5,4},{6,7},{7,6},{8,9},{9,8},{10,11... | collective-permute-start | bytes 540680 | tf_op jit(solution)/shard_map/ppermute | solution.py:77
  54.0 2.5 %copy-start.1 = (f32[16,256,256]{2,1,0:T(8,128)S(1)}, f32[16,256,256]{2,1,0:T(8,128)}, u32[]{:S(2)}) copy-start(f32[16,256,256]{2,1,0:T(8,128)} %param.18) | copy-start | bytes 12582916

commit v8 on v6

--- a/solution.py
+++ b/solution.py
@@ -120,13 +120,18 @@
     n_types = translation.shape[0]
     coeffs = translation.shape[1]
 
+    core = me % 2
+    core0 = core == 0
+    half = box_dom // 2
+
     lists = jnp.concatenate([leaf_src, leaf_type, coarse_src, coarse_type], axis=0)
     flat = lists.size
     table = jnp.zeros((n_blk, flat), jnp.float32)
     table = lax.dynamic_update_index_in_dim(table, lists.reshape(flat).astype(jnp.float32), me, 0)
-    table_rows = -(-n_blk * flat // coeffs)
+    table_rows = 2 * -(-n_blk * flat // (2 * coeffs))
     table = jnp.pad(table.reshape(-1), (0, table_rows * coeffs - n_blk * flat))
     table = table.reshape(table_rows, coeffs)
+    t_half = table_rows // 2
 
     moments = block_moments(density, bra_table, ket_table)
     box_hot = (box_of_block[:, None] == jnp.arange(box_dom, dtype=jnp.int32)[None, :]).astype(
@@ -135,40 +140,65 @@
     partial_moments = lax.dot_general(
         box_hot, moments, (((0,), (0,)), ((), ())), precision=top
     )
-    summed = butterfly_sum(jnp.concatenate([partial_moments, table], axis=0), "blk")
-    domain = summed[:box_dom]
-    table = summed[box_dom:].reshape(-1)[: n_blk * flat].reshape((n_blk,) + lists.shape)
+    first = jnp.concatenate([partial_moments[:half], table[:t_half]], axis=0)
+    second = jnp.concatenate([partial_moments[half:], table[t_half:]], axis=0)
+    mine = jnp.where(core0, first, second)
+    summed = mine + exchange(jnp.where(core0, second, first), "blk", 1)
+    mask = 2
+    while mask < n_blk:
+        summed = summed + exchange(summed, "blk", mask)
+        mask *= 2
+    leaf_half = summed[:half]
+    table_half = summed[half:]
+
+    parent_half = jnp.einsum(
+        "qce,cde->qd", leaf_half.reshape(-1, 8, coeffs), upward_translation_table, precision=top
+    )
+    p_half = parent_half.shape[0]
+    parents = parent_half
+    carried = leaf_half
+    delivered = []
+    mask = 1
+    while mask < n_space:
+        got = exchange(jnp.concatenate([carried, parents], axis=0), "space", mask)
+        carried = got[:half]
+        delivered.append(carried)
+        parents = jnp.concatenate([parents, got[half:]], axis=0)
+        mask *= 2
+
+    def neighbour(step):
+        other = here + step
+        pick = jnp.zeros_like(leaf_half)
+        for r, block in enumerate(delivered):
+            pick = jnp.where((here ^ other) == 2 ** (r + 1) - 1, block, pick)
+        inside = (other >= 0) & (other < n_space)
+        return jnp.where(inside, pick, 0.0)
+
+    own = jnp.concatenate([neighbour(-1), leaf_half, neighbour(1), parents, table_half], axis=0)
+    theirs = exchange(own, "blk", 1)
+    low_part = jnp.where(core0, own, theirs)
+    high_part = jnp.where(core0, theirs, own)
+
+    def joined(start, size):
+        return jnp.concatenate(
+            [low_part[start : start + size], high_part[start : start + size]], axis=0
+        )
+
+    window = jnp.concatenate([joined(0, half), joined(half, half), joined(2 * half, half)], axis=0)
+    domain = joined(half, half)
+    slots = parents.shape[0] // p_half
+    all_parents = jnp.concatenate(
+        [joined(3 * half + j * p_half, p_half) for j in range(slots)], axis=0
+    )
+    table = joined(3 * half + slots * p_half, t_half)
+    table = table.reshape(-1)[: n_blk * flat].reshape((n_blk,) + lists.shape)
     table = table.astype(jnp.int32)
     dom_src = table[:, :leaves].reshape(box_dom, -1)
     dom_type = table[:, leaves : 2 * leaves].reshape(box_dom, -1)
     dom_csrc = table[:, 2 * leaves]
     dom_ctype = table[:, 2 * leaves + 1]
-
-    domain_parents = jnp.einsum(
-        "qce,cde->qd", domain.reshape(n_blk, leaves, coeffs), upward_translation_table, precision=top
-    )
-    parents = domain_parents
-    carried = domain
-    delivered = []
-    mask = 1
-    while mask < n_space:
-        got = exchange(jnp.concatenate([carried, parents], axis=0), "space", mask)
-        carried = got[:box_dom]
-        delivered.append(carried)
-        parents = jnp.concatenate([parents, got[box_dom:]], axis=0)
-        mask *= 2
-    all_parents = parents
-
-    def neighbour(step):
-        other = here + step
-        pick = jnp.zeros_like(domain)
-        for r, block in enumerate(delivered):
-            pick = jnp.where((here ^ other) == 2 ** (r + 1) - 1, block, pick)
-        inside = (other >= 0) & (other < n_space)
-        return jnp.where(inside, pick, 0.0)
-
-    window = jnp.concatenate([neighbour(-1), domain, neighbour(1)], axis=0)
     dom_csrc = (dom_csrc // n_blk ^ here) * n_blk + dom_csrc % n_blk
+    del domain
 
     src_hot = (dom_src[..., None] == jnp.arange(3 * box_dom, dtype=jnp.int32)).astype(jnp.bfloat16)
     type_hot = (dom_type[..., None] == jnp.arange(n_types, dtype=jnp.int32)).astype(jnp.bfloat16)

time: 67.4 us -> 67.4 us (level)
  the two profiles are of different devices: /device:TPU:22 before, /device:TPU:0 now
where the time goes in v8:
time: 67.4 us; the launch traced here: 66.3 us
  waiting for transfers between devices  19.1 us (28%)
  starting transfers between devices  16.6 us (25%)
  Pallas kernels  14 us (21%)
  matrix products  11.6 us (17%)
  local copies, waits for them, and re-layouts  2.54 us (4%)
  other arithmetic  1.22 us (2%)
  between operations  1.19 us (2%)
    ppermute x8, waiting for transfers between devices, exchange(): return lax.ppermute(x, axis, [(i, i ^ mask) for i in range(count)])  19.1 us
    ppermute x8, starting transfers between devices, exchange(): return lax.ppermute(x, axis, [(i, i ^ mask) for i in range(count)])  16.6 us
    pallas_call x1, Pallas kernels, block_moments(): pl.pallas_call(moments_kernel, out_shape=jax.ShapeDtypeStruct((blocks, co...  7.2 us
    pallas_call x1, Pallas kernels, block_coulomb(): pl.pallas_call(coulomb_kernel, out_shape=jax.ShapeDtypeStruct((blocks, ro...  6.81 us
    dot_general x1, matrix products, shards(): gathered = jnp.einsum('btj,jk->btk', counts, window, precision=top)  2.48 us
    dot_general x1, matrix products, shards(): far = jnp.einsum('btk,tlk->bl', rows, translation, precision=top)  2.29 us
    dot_general x1, matrix products, shards(): jnp.einsum('blt,blj->btj', type_hot, src_hot, preferred_element_type=jnp....  1.85 us
  transfers between devices with their start and end apart: 8, of which 8 were waited for; matrix products, arithmetic and copies ran while one was open for 0% of the time, Pallas kernels for 0%

profile of v8, /device:TPU:0, one launch (start us, length us, event | category | flops | bytes accessed | tf_op | source)
XLA Modules:
  0.0 66.3 jit_solution(15595768933727056964)
XLA Ops:
  0.7 0.9 %add_convert_fusion = f32[18,27]{1,0:T(8,128)S(1)} fusion(s32[1,27]{1,0:T(1,128)} %param.17, s32[1,27]{1,0:T(1,128)} %param.16, s32[8,27]{1,0:T(8,128)} %param.15, s32[8,27]{1,0:T(8,128)} %param.14), kind=kLoop, calls=%fused_computation.74 | loop fusion | flops 1944 | bytes 3888 | tf_op jit(solution)/shard_map/convert_element_type | solution.py:130
  1.7 0.1 reshape.98
  1.9 7.2 %shard_map.113 = f32[96,256]{1,0:T(8,128)} custom-call(bf16[96,128,128]{2,1,0:T(8,128)(2,1)} %dens_ref.1, bf16[96,128,256]{2,1,0:T(8,128)(2,1)} %bra_ref.3, bf16[96,128,256]{2,1,0:T(8,128)(2,1)} %ket_ref.3), custom_call_target="tpu_custom_call" | custom-call | flops 805306368 | bytes 15826944 | tf_op jit(solution)/shard_map/pallas_call | solution.py:27
  9.1 1.2 %fusion.21 = f32[128,256]{1,0:T(8,128)S(1)} fusion(f32[96,256]{1,0:T(8,128)} %shard_map.113, s32[96]{0:T(128)S(1)} %copy-done.3), kind=kOutput, calls=%fused_computation.66 | convolution fusion | flops 18886656 | bytes 229760 | tf_op jit(solution)/shard_map/dot_general | solution.py:140
  10.4 1.3 %collective-permute-done = f32[80,256]{1,0:T(8,128)S(1)} collective-permute-done((f32[80,256]{1,0:T(8,128)S(1)}, f32[80,256]{1,0:T(8,128)S(1)}, u32[]{:S(2)}, u32[]{:S(2)}) %collective-permute-start) | collective-permute-done | bytes 81952 | tf_op jit(solution)/shard_map/ppermute | solution.py:77
  11.7 2.1 %collective-permute-start.1 = (f32[80,256]{1,0:T(8,128)S(1)}, f32[80,256]{1,0:T(8,128)S(1)}, u32[]{:S(2)}, u32[]{:S(2)}) collective-permute-start(f32[80,256]{1,0:T(8,128)S(1)} %select_add_fusion), channel_id=1, source_target_pairs={{0,2},{1,3},{2,0},{3,1},{4,6},{5,7},{6,4},{7,5},{8,10},{9,11},{10,... | collective-permute-start | bytes 245768 | tf_op jit(solution)/shard_map/ppermute | solution.py:77
  13.8 2.8 %collective-permute-done.1 = f32[80,256]{1,0:T(8,128)S(1)} collective-permute-done((f32[80,256]{1,0:T(8,128)S(1)}, f32[80,256]{1,0:T(8,128)S(1)}, u32[]{:S(2)}, u32[]{:S(2)}) %collective-permute-start.1) | collective-permute-done | bytes 81952 | tf_op jit(solution)/shard_map/ppermute | solution.py:77
  16.6 1.7 %collective-permute-start.2 = (f32[80,256]{1,0:T(8,128)S(1)}, f32[80,256]{1,0:T(8,128)S(1)}, u32[]{:S(2)}, u32[]{:S(2)}) collective-permute-start(f32[80,256]{1,0:T(8,128)S(1)} %add.60), channel_id=1, source_target_pairs={{0,4},{1,5},{2,6},{3,7},{4,0},{5,1},{6,2},{7,3},{8,12},{9,13},{10,... | collective-permute-start | bytes 245768 | tf_op jit(solution)/shard_map/ppermute | solution.py:77
  18.2 2.9 %collective-permute-done.2 = f32[80,256]{1,0:T(8,128)S(1)} collective-permute-done((f32[80,256]{1,0:T(8,128)S(1)}, f32[80,256]{1,0:T(8,128)S(1)}, u32[]{:S(2)}, u32[]{:S(2)}) %collective-permute-start.2) | collective-permute-done | bytes 81952 | tf_op jit(solution)/shard_map/ppermute | solution.py:77
  21.1 3.3 %collective-permute-start.3 = (f32[80,256]{1,0:T(8,128)S(1)}, f32[80,256]{1,0:T(8,128)S(1)}, u32[]{:S(2)}, u32[]{:S(2)}) collective-permute-start(f32[80,256]{1,0:T(8,128)S(1)} %add.61), channel_id=1, source_target_pairs={{0,8},{1,9},{2,10},{3,11},{4,12},{5,13},{6,14},{7,15},{8,0},{9,1},... | collective-permute-start | bytes 245768 | tf_op jit(solution)/shard_map/ppermute | solution.py:77
  24.4 2.8 %collective-permute-done.3 = f32[80,256]{1,0:T(8,128)S(1)} collective-permute-done((f32[80,256]{1,0:T(8,128)S(1)}, f32[80,256]{1,0:T(8,128)S(1)}, u32[]{:S(2)}, u32[]{:S(2)}) %collective-permute-start.3) | collective-permute-done | bytes 81952 | tf_op jit(solution)/shard_map/ppermute | solution.py:77
  27.2 0.9 %convolution_bitcast_fusion = f32[8,256]{1,0:T(8,128)S(1)} fusion(f32[8,256,256]{2,1,0:T(8,128)S(1)} %copy-done, f32[8,8,256]{2,1,0:T(8,128)S(1)} %get-tuple-element.11), kind=kOutput, calls=%fused_computation.10 | convolution fusion | flops 25165824 | bytes 2170880 | tf_op jit(solution)/shard_map/qce,cde->qd/dot_general | solution.py:154
  28.1 1.6 %collective-permute-start.4 = (f32[72,256]{1,0:T(8,128)S(1)}, f32[72,256]{1,0:T(8,128)S(1)}, u32[]{:S(2)}, u32[]{:S(2)}) collective-permute-start(f32[72,256]{1,0:T(8,128)S(1)} %pad_maximum_fusion.4), channel_id=1, source_target_pairs={{0,16},{16,0},{32,48},{48,32},{64,80},{80,64},{96,112},{112,96},{1... | collective-permute-start | bytes 221192 | tf_op jit(solution)/shard_map/ppermute | solution.py:77
  29.7 2.9 %collective-permute-done.4 = f32[72,256]{1,0:T(8,128)S(1)} collective-permute-done((f32[72,256]{1,0:T(8,128)S(1)}, f32[72,256]{1,0:T(8,128)S(1)}, u32[]{:S(2)}, u32[]{:S(2)}) %collective-permute-start.4) | collective-permute-done | bytes 73760 | tf_op jit(solution)/shard_map/ppermute | solution.py:77
  32.6 3.8 %collective-permute-start.5 = (f32[80,256]{1,0:T(8,128)S(1)}, f32[80,256]{1,0:T(8,128)S(1)}, u32[]{:S(2)}, u32[]{:S(2)}) collective-permute-start(f32[80,256]{1,0:T(8,128)S(1)} %pad_maximum_fusion.3), channel_id=1, source_target_pairs={{0,32},{16,48},{32,0},{48,16},{64,96},{80,112},{96,64},{112,80},{1... | collective-permute-start | bytes 245768 | tf_op jit(solution)/shard_map/ppermute | solution.py:77
  36.4 2.4 %collective-permute-done.5 = f32[80,256]{1,0:T(8,128)S(1)} collective-permute-done((f32[80,256]{1,0:T(8,128)S(1)}, f32[80,256]{1,0:T(8,128)S(1)}, u32[]{:S(2)}, u32[]{:S(2)}) %collective-permute-start.5) | collective-permute-done | bytes 81952 | tf_op jit(solution)/shard_map/ppermute | solution.py:77
  38.8 3.8 %collective-permute-start.6 = (f32[96,256]{1,0:T(8,128)S(1)}, f32[96,256]{1,0:T(8,128)S(1)}, u32[]{:S(2)}, u32[]{:S(2)}) collective-permute-start(f32[96,256]{1,0:T(8,128)S(1)} %pad_maximum_fusion), channel_id=1, source_target_pairs={{0,64},{16,80},{32,96},{48,112},{64,0},{80,16},{96,32},{112,48},{1... | collective-permute-start | bytes 294920 | tf_op jit(solution)/shard_map/ppermute | solution.py:77
  42.7 2.6 %collective-permute-done.6 = f32[96,256]{1,0:T(8,128)S(1)} collective-permute-done((f32[96,256]{1,0:T(8,128)S(1)}, f32[96,256]{1,0:T(8,128)S(1)}, u32[]{:S(2)}, u32[]{:S(2)}) %collective-permute-start.6) | collective-permute-done | bytes 98336 | tf_op jit(solution)/shard_map/ppermute | solution.py:77
  45.4 0.3 collective-permute-start.7
  45.7 1.5 %collective-permute-done.7 = f32[272,256]{1,0:T(8,128)S(1)} collective-permute-done((f32[272,256]{1,0:T(8,128)S(1)}, f32[272,256]{1,0:T(8,128)S(1)}, u32[]{:S(2)}, u32[]{:S(2)}) %collective-permute-start.7) | collective-permute-done | bytes 278560 | tf_op jit(solution)/shard_map/ppermute | solution.py:77
  47.4 0.2 convert_element_type.29
  47.9 0.6 copy-done.2
  48.5 0.6 copy.18
  49.2 0.2 fusion.12
  49.4 1.2 %fusion.13 = f32[16,16,256]{2,0,1:T(8,128)S(1)} fusion(f32[128,256]{1,0:T(8,128)} %copy-done.2, f32[16,16,128]{2,1,0:T(8,128)S(1)} %fusion.12), kind=kOutput, calls=%fused_computation.18 | convolution fusion | flops 50331648 | bytes 524288 | tf_op jit(solution)/shard_map/ptq,qk->ptk/dot_general | solution.py:211
  50.6 1.9 %fusion = f32[128,16,384]{2,1,0:T(8,128)S(1)} fusion(pred[128,27,16]{1,2,0:T(8,128)(4,1)S(1)} %copy.18, s32[128,27]{1,0:T(8,128)S(1)} %get-tuple-element.4), kind=kOutput, calls=%fused_computation.1 | convolution fusion | flops 43794432 | bytes 3214848 | tf_op jit(solution)/shard_map/blt,blj->btj/dot_general | solution.py:205
  52.5 2.5 %fusion.1 = f32[128,16,256]{2,0,1:T(8,128)S(1)} fusion(f32[128,16,384]{2,1,0:T(8,128)S(1)} %fusion, f32[384,256]{1,0:T(8,128)S(1)} %slice_dynamic-update-slice_fusion), kind=kOutput, calls=%fused_computation.2 | convolution fusion | flops 1207959552 | bytes 5636096 | tf_op jit(solution)/shard_map/btj,jk->btk/dot_general | solution.py:206
  55.0 2.3 %fusion.8 = f32[144,256]{1,0:T(8,128)S(1)} fusion(f32[16,256,256]{2,1,0:T(8,128)S(1)} %copy-done.1, f32[16,16,256]{2,0,1:T(8,128)S(1)} %fusion.13, f32[128,16,256]{2,0,1:T(8,128)S(1)} %fusion.1), kind=kOutput, calls=%fused_computation.9 | convolution fusion | flops 906559488 | bytes 6701056 | tf_op jit(solution)/shard_map/btk,tlk->bl/dot_general | solution.py:213
  57.3 0.6 fusion.24
  58.0 0.9 %fusion.20.local_ref = f32[96,256]{1,0:T(8,128)} fusion(f32[128,256]{1,0:T(8,128)S(1)} %slice_add_fusion, s32[96]{0:T(128)S(1)} %copy-done.3), kind=kOutput, calls=%fused_computation.65 | convolution fusion | flops 18886656 | bytes 229760 | tf_op jit(solution)/shard_map/dot_general | solution.py:221
  58.8 0.6 constant_dynamic-slice_fusion
  59.4 6.8 %shard_map.114 = bf16[96,128,128]{2,1,0:T(8,128)(2,1)} custom-call(bf16[96,128,256]{2,1,0:T(8,128)(2,1)} %bra_ref.3, bf16[96,128,256]{2,1,0:T(8,128)(2,1)} %ket_ref.3, f32[96,256]{1,0:T(8,128)} %fusion.20.local_ref), custom_call_target="tpu_custom_call" | custom-call | flops 805306368 | bytes 15826944 | tf_op jit(solution)/shard_map/pallas_call | solution.py:57
  (70 shorter events, 0.9 us)
Async XLA Ops:
  0.6 26.6 %copy-start = (f32[8,256,256]{2,1,0:T(8,128)S(1)}, f32[8,256,256]{2,1,0:T(8,128)}, u32[]{:S(2)}) copy-start(f32[8,256,256]{2,1,0:T(8,128)} %param.19) | copy-start | bytes 6291460
  1.9 7.2 %copy-start.3 = (s32[96]{0:T(128)S(1)}, s32[96]{0:T(128)}, u32[]{:S(2)}) copy-start(s32[96]{0:T(128)} %param.13) | copy-start | bytes 1156
  10.3 1.4 %collective-permute-start = (f32[80,256]{1,0:T(8,128)S(1)}, f32[80,256]{1,0:T(8,128)S(1)}, u32[]{:S(2)}, u32[]{:S(2)}) collective-permute-start(f32[80,256]{1,0:T(8,128)S(1)} %fusion.17), channel_id=1, source_target_pairs={{0,1},{1,0},{2,3},{3,2},{4,5},{5,4},{6,7},{7,6},{8,9},{9,8},{10,11... | collective-permute-start | bytes 245768 | tf_op jit(solution)/shard_map/ppermute | solution.py:77
  11.7 4.9 %collective-permute-start.1 = (f32[80,256]{1,0:T(8,128)S(1)}, f32[80,256]{1,0:T(8,128)S(1)}, u32[]{:S(2)}, u32[]{:S(2)}) collective-permute-start(f32[80,256]{1,0:T(8,128)S(1)} %select_add_fusion), channel_id=1, source_target_pairs={{0,2},{1,3},{2,0},{3,1},{4,6},{5,7},{6,4},{7,5},{8,10},{9,11},{10,... | collective-permute-start | bytes 245768 | tf_op jit(solution)/shard_map/ppermute | solution.py:77
  16.6 4.5 %collective-permute-start.2 = (f32[80,256]{1,0:T(8,128)S(1)}, f32[80,256]{1,0:T(8,128)S(1)}, u32[]{:S(2)}, u32[]{:S(2)}) collective-permute-start(f32[80,256]{1,0:T(8,128)S(1)} %add.60), channel_id=1, source_target_pairs={{0,4},{1,5},{2,6},{3,7},{4,0},{5,1},{6,2},{7,3},{8,12},{9,13},{10,... | collective-permute-start | bytes 245768 | tf_op jit(solution)/shard_map/ppermute | solution.py:77
  21.1 6.0 %collective-permute-start.3 = (f32[80,256]{1,0:T(8,128)S(1)}, f32[80,256]{1,0:T(8,128)S(1)}, u32[]{:S(2)}, u32[]{:S(2)}) collective-permute-start(f32[80,256]{1,0:T(8,128)S(1)} %add.61), channel_id=1, source_target_pairs={{0,8},{1,9},{2,10},{3,11},{4,12},{5,13},{6,14},{7,15},{8,0},{9,1},... | collective-permute-start | bytes 245768 | tf_op jit(solution)/shard_map/ppermute | solution.py:77
  28.1 4.4 %collective-permute-start.4 = (f32[72,256]{1,0:T(8,128)S(1)}, f32[72,256]{1,0:T(8,128)S(1)}, u32[]{:S(2)}, u32[]{:S(2)}) collective-permute-start(f32[72,256]{1,0:T(8,128)S(1)} %pad_maximum_fusion.4), channel_id=1, source_target_pairs={{0,16},{16,0},{32,48},{48,32},{64,80},{80,64},{96,112},{112,96},{1... | collective-permute-start | bytes 221192 | tf_op jit(solution)/shard_map/ppermute | solution.py:77
  32.6 6.2 %collective-permute-start.5 = (f32[80,256]{1,0:T(8,128)S(1)}, f32[80,256]{1,0:T(8,128)S(1)}, u32[]{:S(2)}, u32[]{:S(2)}) collective-permute-start(f32[80,256]{1,0:T(8,128)S(1)} %pad_maximum_fusion.3), channel_id=1, source_target_pairs={{0,32},{16,48},{32,0},{48,16},{64,96},{80,112},{96,64},{112,80},{1... | collective-permute-start | bytes 245768 | tf_op jit(solution)/shard_map/ppermute | solution.py:77
  38.8 6.4 %collective-permute-start.6 = (f32[96,256]{1,0:T(8,128)S(1)}, f32[96,256]{1,0:T(8,128)S(1)}, u32[]{:S(2)}, u32[]{:S(2)}) collective-permute-start(f32[96,256]{1,0:T(8,128)S(1)} %pad_maximum_fusion), channel_id=1, source_target_pairs={{0,64},{16,80},{32,96},{48,112},{64,0},{80,16},{96,32},{112,48},{1... | collective-permute-start | bytes 294920 | tf_op jit(solution)/shard_map/ppermute | solution.py:77
  45.4 1.8 %collective-permute-start.7 = (f32[272,256]{1,0:T(8,128)S(1)}, f32[272,256]{1,0:T(8,128)S(1)}, u32[]{:S(2)}, u32[]{:S(2)}) collective-permute-start(f32[272,256]{1,0:T(8,128)S(1)} %constant_dynamic-update-slice_fusion), channel_id=1, source_target_pairs={{0,1},{1,0},{2,3},{3,2},{4,5},{5,4},{6,7},{7,6},{8,9},{9,8},{10,11... | collective-permute-start | bytes 835592 | tf_op jit(solution)/shard_map/ppermute | solution.py:77
  47.8 0.7 copy-start.2
  52.5 2.5 %copy-start.1 = (f32[16,256,256]{2,1,0:T(8,128)S(1)}, f32[16,256,256]{2,1,0:T(8,128)}, u32[]{:S(2)}) copy-start(f32[16,256,256]{2,1,0:T(8,128)} %param.18) | copy-start | bytes 12582916

commit v9 on v8

--- a/solution.py
+++ b/solution.py
@@ -131,7 +131,6 @@
     table_rows = 2 * -(-n_blk * flat // (2 * coeffs))
     table = jnp.pad(table.reshape(-1), (0, table_rows * coeffs - n_blk * flat))
     table = table.reshape(table_rows, coeffs)
-    t_half = table_rows // 2
 
     moments = block_moments(density, bra_table, ket_table)
     box_hot = (box_of_block[:, None] == jnp.arange(box_dom, dtype=jnp.int32)[None, :]).astype(
@@ -140,8 +139,8 @@
     partial_moments = lax.dot_general(
         box_hot, moments, (((0,), (0,)), ((), ())), precision=top
     )
-    first = jnp.concatenate([partial_moments[:half], table[:t_half]], axis=0)
-    second = jnp.concatenate([partial_moments[half:], table[t_half:]], axis=0)
+    first = jnp.concatenate([partial_moments[:half], table], axis=0)
+    second = jnp.concatenate([partial_moments[half:], table], axis=0)
     mine = jnp.where(core0, first, second)
     summed = mine + exchange(jnp.where(core0, second, first), "blk", 1)
     mask = 2
@@ -149,7 +148,7 @@
         summed = summed + exchange(summed, "blk", mask)
         mask *= 2
     leaf_half = summed[:half]
-    table_half = summed[half:]
+    table = summed[half:]
 
     parent_half = jnp.einsum(
         "qce,cde->qd", leaf_half.reshape(-1, 8, coeffs), upward_translation_table, precision=top
@@ -174,7 +173,7 @@
         inside = (other >= 0) & (other < n_space)
         return jnp.where(inside, pick, 0.0)
 
-    own = jnp.concatenate([neighbour(-1), leaf_half, neighbour(1), parents, table_half], axis=0)
+    own = jnp.concatenate([neighbour(-1), leaf_half, neighbour(1), parents], axis=0)
     theirs = exchange(own, "blk", 1)
     low_part = jnp.where(core0, own, theirs)
     high_part = jnp.where(core0, theirs, own)
@@ -190,7 +189,6 @@
     all_parents = jnp.concatenate(
         [joined(3 * half + j * p_half, p_half) for j in range(slots)], axis=0
     )
-    table = joined(3 * half + slots * p_half, t_half)
     table = table.reshape(-1)[: n_blk * flat].reshape((n_blk,) + lists.shape)
     table = table.astype(jnp.int32)
     dom_src = table[:, :leaves].reshape(box_dom, -1)

time: 67.4 us -> 63.5 us (0.942)
  waiting for transfers between devices: 19.1 us -> 16.7 us
  matrix products: 11.6 us -> 10.7 us
    ppermute x8, waiting for transfers between devices: 19.1 us -> 16.7 us  [exchange(): return lax.ppermute(x, axis, [(i, i ^ mask) for i in range(count)])]
    dot_general x1, matrix products: 1.17 us -> 0.26 us  [shards(): cgathered = jnp.einsum('ptq,qk->ptk', ccounts, all_parents, precision=top)]
  transfers between devices with their start and end apart: 8 -> 8, of which waited for: 8 -> 8; matrix products, arithmetic and copies ran while one was open for 0% -> 5% of each run, Pallas kernels for 0% -> 0%
where the time goes in v9:
time: 63.5 us; the launch traced here: 62.3 us
  waiting for transfers between devices  16.7 us (26%)
  starting transfers between devices  16.6 us (26%)
  Pallas kernels  14 us (22%)
  matrix products  10.7 us (17%)
  local copies, waits for them, and re-layouts  1.97 us (3%)
  other arithmetic  1.24 us (2%)
  between operations  1.15 us (2%)
    ppermute x8, waiting for transfers between devices, exchange(): return lax.ppermute(x, axis, [(i, i ^ mask) for i in range(count)])  16.7 us
    ppermute x8, starting transfers between devices, exchange(): return lax.ppermute(x, axis, [(i, i ^ mask) for i in range(count)])  16.6 us
    pallas_call x1, Pallas kernels, block_moments(): pl.pallas_call(moments_kernel, out_shape=jax.ShapeDtypeStruct((blocks, co...  7.2 us
    pallas_call x1, Pallas kernels, block_coulomb(): pl.pallas_call(coulomb_kernel, out_shape=jax.ShapeDtypeStruct((blocks, ro...  6.81 us
    dot_general x1, matrix products, shards(): gathered = jnp.einsum('btj,jk->btk', counts, window, precision=top)  2.46 us
    dot_general x1, matrix products, shards(): far = jnp.einsum('btk,tlk->bl', rows, translation, precision=top)  2.28 us
    dot_general x1, matrix products, shards(): jnp.einsum('blt,blj->btj', type_hot, src_hot, preferred_element_type=jnp....  1.84 us
  transfers between devices with their start and end apart: 8, of which 8 were waited for; matrix products, arithmetic and copies ran while one was open for 5% of the time, Pallas kernels for 0%

profile of v9, /device:TPU:0, one launch (start us, length us, event | category | flops | bytes accessed | tf_op | source)
XLA Modules:
  0.0 62.3 jit_solution(546255092308392579)
XLA Ops:
  0.7 0.9 %add_convert_fusion = f32[18,27]{1,0:T(8,128)S(1)} fusion(s32[1,27]{1,0:T(1,128)} %param.17, s32[1,27]{1,0:T(1,128)} %param.16, s32[8,27]{1,0:T(8,128)} %param.15, s32[8,27]{1,0:T(8,128)} %param.14), kind=kLoop, calls=%fused_computation.72 | loop fusion | flops 1944 | bytes 3888 | tf_op jit(solution)/shard_map/convert_element_type | solution.py:130
  1.7 0.1 reshape.88
  1.9 7.2 %shard_map.113 = f32[96,256]{1,0:T(8,128)} custom-call(bf16[96,128,128]{2,1,0:T(8,128)(2,1)} %dens_ref.1, bf16[96,128,256]{2,1,0:T(8,128)(2,1)} %bra_ref.3, bf16[96,128,256]{2,1,0:T(8,128)(2,1)} %ket_ref.3), custom_call_target="tpu_custom_call" | custom-call | flops 805306368 | bytes 15826944 | tf_op jit(solution)/shard_map/pallas_call | solution.py:27
  9.1 1.2 %fusion.21 = f32[128,256]{1,0:T(8,128)S(1)} fusion(f32[96,256]{1,0:T(8,128)} %shard_map.113, s32[96]{0:T(128)S(1)} %copy-done.2), kind=kOutput, calls=%fused_computation.65 | convolution fusion | flops 18886656 | bytes 229760 | tf_op jit(solution)/shard_map/dot_general | solution.py:139
  10.4 1.3 %collective-permute-done = f32[96,256]{1,0:T(8,128)S(1)} collective-permute-done((f32[96,256]{1,0:T(8,128)S(1)}, f32[96,256]{1,0:T(8,128)S(1)}, u32[]{:S(2)}, u32[]{:S(2)}) %collective-permute-start) | collective-permute-done | bytes 98336 | tf_op jit(solution)/shard_map/ppermute | solution.py:77
  11.7 2.1 %collective-permute-start.1 = (f32[96,256]{1,0:T(8,128)S(1)}, f32[96,256]{1,0:T(8,128)S(1)}, u32[]{:S(2)}, u32[]{:S(2)}) collective-permute-start(f32[96,256]{1,0:T(8,128)S(1)} %select_add_fusion), channel_id=1, source_target_pairs={{0,2},{1,3},{2,0},{3,1},{4,6},{5,7},{6,4},{7,5},{8,10},{9,11},{10,... | collective-permute-start | bytes 294920 | tf_op jit(solution)/shard_map/ppermute | solution.py:77
  13.8 3.1 %collective-permute-done.1 = f32[96,256]{1,0:T(8,128)S(1)} collective-permute-done((f32[96,256]{1,0:T(8,128)S(1)}, f32[96,256]{1,0:T(8,128)S(1)}, u32[]{:S(2)}, u32[]{:S(2)}) %collective-permute-start.1) | collective-permute-done | bytes 98336 | tf_op jit(solution)/shard_map/ppermute | solution.py:77
  16.9 1.7 %collective-permute-start.2 = (f32[96,256]{1,0:T(8,128)S(1)}, f32[96,256]{1,0:T(8,128)S(1)}, u32[]{:S(2)}, u32[]{:S(2)}) collective-permute-start(f32[96,256]{1,0:T(8,128)S(1)} %add.59), channel_id=1, source_target_pairs={{0,4},{1,5},{2,6},{3,7},{4,0},{5,1},{6,2},{7,3},{8,12},{9,13},{10,... | collective-permute-start | bytes 294920 | tf_op jit(solution)/shard_map/ppermute | solution.py:77
  18.6 3.0 %collective-permute-done.2 = f32[96,256]{1,0:T(8,128)S(1)} collective-permute-done((f32[96,256]{1,0:T(8,128)S(1)}, f32[96,256]{1,0:T(8,128)S(1)}, u32[]{:S(2)}, u32[]{:S(2)}) %collective-permute-start.2) | collective-permute-done | bytes 98336 | tf_op jit(solution)/shard_map/ppermute | solution.py:77
  21.7 3.3 %collective-permute-start.3 = (f32[96,256]{1,0:T(8,128)S(1)}, f32[96,256]{1,0:T(8,128)S(1)}, u32[]{:S(2)}, u32[]{:S(2)}) collective-permute-start(f32[96,256]{1,0:T(8,128)S(1)} %add.60), channel_id=1, source_target_pairs={{0,8},{1,9},{2,10},{3,11},{4,12},{5,13},{6,14},{7,15},{8,0},{9,1},... | collective-permute-start | bytes 294920 | tf_op jit(solution)/shard_map/ppermute | solution.py:77
  24.9 2.9 %collective-permute-done.3 = f32[96,256]{1,0:T(8,128)S(1)} collective-permute-done((f32[96,256]{1,0:T(8,128)S(1)}, f32[96,256]{1,0:T(8,128)S(1)}, u32[]{:S(2)}, u32[]{:S(2)}) %collective-permute-start.3) | collective-permute-done | bytes 98336 | tf_op jit(solution)/shard_map/ppermute | solution.py:77
  28.0 0.9 %convolution_bitcast_fusion = f32[8,256]{1,0:T(8,128)S(1)} fusion(f32[8,256,256]{2,1,0:T(8,128)S(1)} %copy-done, f32[8,8,256]{2,1,0:T(8,128)S(1)} %get-tuple-element.11), kind=kOutput, calls=%fused_computation.10 | convolution fusion | flops 25165824 | bytes 2170880 | tf_op jit(solution)/shard_map/qce,cde->qd/dot_general | solution.py:153
  28.9 1.6 %collective-permute-start.4 = (f32[72,256]{1,0:T(8,128)S(1)}, f32[72,256]{1,0:T(8,128)S(1)}, u32[]{:S(2)}, u32[]{:S(2)}) collective-permute-start(f32[72,256]{1,0:T(8,128)S(1)} %pad_maximum_fusion.4), channel_id=1, source_target_pairs={{0,16},{16,0},{32,48},{48,32},{64,80},{80,64},{96,112},{112,96},{1... | collective-permute-start | bytes 221192 | tf_op jit(solution)/shard_map/ppermute | solution.py:77
  30.5 0.2 convert_element_type.29
  30.8 0.6 %copy.17 = pred[128,27,16]{1,2,0:T(8,128)(4,1)S(1)} copy(pred[128,27,16]{0,2,1:T(8,128)(4,1)S(1)} %iota_compare_fusion.4) | data formatting | bytes 110592 | tf_op jit(solution)/shard_map/eq | solution.py:202
  31.5 1.9 %collective-permute-done.4 = f32[72,256]{1,0:T(8,128)S(1)} collective-permute-done((f32[72,256]{1,0:T(8,128)S(1)}, f32[72,256]{1,0:T(8,128)S(1)}, u32[]{:S(2)}, u32[]{:S(2)}) %collective-permute-start.4) | collective-permute-done | bytes 73760 | tf_op jit(solution)/shard_map/ppermute | solution.py:77
  33.4 3.8 %collective-permute-start.5 = (f32[80,256]{1,0:T(8,128)S(1)}, f32[80,256]{1,0:T(8,128)S(1)}, u32[]{:S(2)}, u32[]{:S(2)}) collective-permute-start(f32[80,256]{1,0:T(8,128)S(1)} %pad_maximum_fusion.3), channel_id=1, source_target_pairs={{0,32},{16,48},{32,0},{48,16},{64,96},{80,112},{96,64},{112,80},{1... | collective-permute-start | bytes 245768 | tf_op jit(solution)/shard_map/ppermute | solution.py:77
  37.2 1.8 %fusion = f32[128,16,384]{2,1,0:T(8,128)S(1)} fusion(pred[128,27,16]{1,2,0:T(8,128)(4,1)S(1)} %copy.17, s32[128,27]{1,0:T(8,128)S(1)} %get-tuple-element.4), kind=kOutput, calls=%fused_computation.1 | convolution fusion | flops 43794432 | bytes 3214848 | tf_op jit(solution)/shard_map/blt,blj->btj/dot_general | solution.py:203
  39.0 0.6 collective-permute-done.5
  39.6 3.8 %collective-permute-start.6 = (f32[96,256]{1,0:T(8,128)S(1)}, f32[96,256]{1,0:T(8,128)S(1)}, u32[]{:S(2)}, u32[]{:S(2)}) collective-permute-start(f32[96,256]{1,0:T(8,128)S(1)} %pad_maximum_fusion.2), channel_id=1, source_target_pairs={{0,64},{16,80},{32,96},{48,112},{64,0},{80,16},{96,32},{112,48},{1... | collective-permute-start | bytes 294920 | tf_op jit(solution)/shard_map/ppermute | solution.py:77
  43.5 2.6 %collective-permute-done.6 = f32[96,256]{1,0:T(8,128)S(1)} collective-permute-done((f32[96,256]{1,0:T(8,128)S(1)}, f32[96,256]{1,0:T(8,128)S(1)}, u32[]{:S(2)}, u32[]{:S(2)}) %collective-permute-start.6) | collective-permute-done | bytes 98336 | tf_op jit(solution)/shard_map/ppermute | solution.py:77
  46.2 0.3 collective-permute-start.7
  46.5 0.2 fusion.12
  46.7 1.2 %collective-permute-done.7 = f32[256,256]{1,0:T(8,128)S(1)} collective-permute-done((f32[256,256]{1,0:T(8,128)S(1)}, f32[256,256]{1,0:T(8,128)S(1)}, u32[]{:S(2)}, u32[]{:S(2)}) %collective-permute-start.7) | collective-permute-done | bytes 262176 | tf_op jit(solution)/shard_map/ppermute | solution.py:77
  48.3 0.3 fusion.13
  48.5 2.5 %fusion.1 = f32[128,16,256]{2,0,1:T(8,128)S(1)} fusion(f32[128,16,384]{2,1,0:T(8,128)S(1)} %fusion, f32[384,256]{1,0:T(8,128)S(1)} %slice_dynamic-update-slice_fusion), kind=kOutput, calls=%fused_computation.2 | convolution fusion | flops 1207959552 | bytes 5636096 | tf_op jit(solution)/shard_map/btj,jk->btk/dot_general | solution.py:204
  51.0 2.3 %fusion.8 = f32[144,256]{1,0:T(8,128)S(1)} fusion(f32[16,256,256]{2,1,0:T(8,128)S(1)} %copy-done.1, f32[16,16,256]{2,0,1:T(8,128)S(1)} %fusion.13, f32[128,16,256]{2,0,1:T(8,128)S(1)} %fusion.1), kind=kOutput, calls=%fused_computation.9 | convolution fusion | flops 906559488 | bytes 6701056 | tf_op jit(solution)/shard_map/btk,tlk->bl/dot_general | solution.py:211
  53.3 0.6 fusion.24
  53.9 0.1 slice_add_fusion
  54.0 0.9 %fusion.20.local_ref = f32[96,256]{1,0:T(8,128)} fusion(f32[128,256]{1,0:T(8,128)S(1)} %slice_add_fusion, s32[96]{0:T(128)S(1)} %copy-done.2), kind=kOutput, calls=%fused_computation.64 | convolution fusion | flops 18886656 | bytes 229760 | tf_op jit(solution)/shard_map/dot_general | solution.py:219
  54.9 0.6 constant_dynamic-slice_fusion
  55.5 6.8 %shard_map.114 = bf16[96,128,128]{2,1,0:T(8,128)(2,1)} custom-call(bf16[96,128,256]{2,1,0:T(8,128)(2,1)} %bra_ref.3, bf16[96,128,256]{2,1,0:T(8,128)(2,1)} %ket_ref.3, f32[96,256]{1,0:T(8,128)} %fusion.20.local_ref), custom_call_target="tpu_custom_call" | custom-call | flops 805306368 | bytes 15826944 | tf_op jit(solution)/shard_map/pallas_call | solution.py:57
  (64 shorter events, 0.8 us)
Async XLA Ops:
  0.6 27.3 %copy-start = (f32[8,256,256]{2,1,0:T(8,128)S(1)}, f32[8,256,256]{2,1,0:T(8,128)}, u32[]{:S(2)}) copy-start(f32[8,256,256]{2,1,0:T(8,128)} %param.19) | copy-start | bytes 6291460
  1.9 7.2 %copy-start.2 = (s32[96]{0:T(128)S(1)}, s32[96]{0:T(128)}, u32[]{:S(2)}) copy-start(s32[96]{0:T(128)} %param.13) | copy-start | bytes 1156
  10.3 1.4 %collective-permute-start = (f32[96,256]{1,0:T(8,128)S(1)}, f32[96,256]{1,0:T(8,128)S(1)}, u32[]{:S(2)}, u32[]{:S(2)}) collective-permute-start(f32[96,256]{1,0:T(8,128)S(1)} %fusion.17), channel_id=1, source_target_pairs={{0,1},{1,0},{2,3},{3,2},{4,5},{5,4},{6,7},{7,6},{8,9},{9,8},{10,11... | collective-permute-start | bytes 294920 | tf_op jit(solution)/shard_map/ppermute | solution.py:77
  11.7 5.2 %collective-permute-start.1 = (f32[96,256]{1,0:T(8,128)S(1)}, f32[96,256]{1,0:T(8,128)S(1)}, u32[]{:S(2)}, u32[]{:S(2)}) collective-permute-start(f32[96,256]{1,0:T(8,128)S(1)} %select_add_fusion), channel_id=1, source_target_pairs={{0,2},{1,3},{2,0},{3,1},{4,6},{5,7},{6,4},{7,5},{8,10},{9,11},{10,... | collective-permute-start | bytes 294920 | tf_op jit(solution)/shard_map/ppermute | solution.py:77
  16.9 4.7 %collective-permute-start.2 = (f32[96,256]{1,0:T(8,128)S(1)}, f32[96,256]{1,0:T(8,128)S(1)}, u32[]{:S(2)}, u32[]{:S(2)}) collective-permute-start(f32[96,256]{1,0:T(8,128)S(1)} %add.59), channel_id=1, source_target_pairs={{0,4},{1,5},{2,6},{3,7},{4,0},{5,1},{6,2},{7,3},{8,12},{9,13},{10,... | collective-permute-start | bytes 294920 | tf_op jit(solution)/shard_map/ppermute | solution.py:77
  21.7 6.2 %collective-permute-start.3 = (f32[96,256]{1,0:T(8,128)S(1)}, f32[96,256]{1,0:T(8,128)S(1)}, u32[]{:S(2)}, u32[]{:S(2)}) collective-permute-start(f32[96,256]{1,0:T(8,128)S(1)} %add.60), channel_id=1, source_target_pairs={{0,8},{1,9},{2,10},{3,11},{4,12},{5,13},{6,14},{7,15},{8,0},{9,1},... | collective-permute-start | bytes 294920 | tf_op jit(solution)/shard_map/ppermute | solution.py:77
  28.9 4.4 %collective-permute-start.4 = (f32[72,256]{1,0:T(8,128)S(1)}, f32[72,256]{1,0:T(8,128)S(1)}, u32[]{:S(2)}, u32[]{:S(2)}) collective-permute-start(f32[72,256]{1,0:T(8,128)S(1)} %pad_maximum_fusion.4), channel_id=1, source_target_pairs={{0,16},{16,0},{32,48},{48,32},{64,80},{80,64},{96,112},{112,96},{1... | collective-permute-start | bytes 221192 | tf_op jit(solution)/shard_map/ppermute | solution.py:77
  33.4 6.2 %collective-permute-start.5 = (f32[80,256]{1,0:T(8,128)S(1)}, f32[80,256]{1,0:T(8,128)S(1)}, u32[]{:S(2)}, u32[]{:S(2)}) collective-permute-start(f32[80,256]{1,0:T(8,128)S(1)} %pad_maximum_fusion.3), channel_id=1, source_target_pairs={{0,32},{16,48},{32,0},{48,16},{64,96},{80,112},{96,64},{112,80},{1... | collective-permute-start | bytes 245768 | tf_op jit(solution)/shard_map/ppermute | solution.py:77
  39.6 6.4 %collective-permute-start.6 = (f32[96,256]{1,0:T(8,128)S(1)}, f32[96,256]{1,0:T(8,128)S(1)}, u32[]{:S(2)}, u32[]{:S(2)}) collective-permute-start(f32[96,256]{1,0:T(8,128)S(1)} %pad_maximum_fusion.2), channel_id=1, source_target_pairs={{0,64},{16,80},{32,96},{48,112},{64,0},{80,16},{96,32},{112,48},{1... | collective-permute-start | bytes 294920 | tf_op jit(solution)/shard_map/ppermute | solution.py:77
  46.2 1.8 %collective-permute-start.7 = (f32[256,256]{1,0:T(8,128)S(1)}, f32[256,256]{1,0:T(8,128)S(1)}, u32[]{:S(2)}, u32[]{:S(2)}) collective-permute-start(f32[256,256]{1,0:T(8,128)S(1)} %constant_dynamic-update-slice_fusion), channel_id=1, source_target_pairs={{0,1},{1,0},{2,3},{3,2},{4,5},{5,4},{6,7},{7,6},{8,9},{9,8},{10,11... | collective-permute-start | bytes 786440 | tf_op jit(solution)/shard_map/ppermute | solution.py:77
  48.5 2.5 %copy-start.1 = (f32[16,256,256]{2,1,0:T(8,128)S(1)}, f32[16,256,256]{2,1,0:T(8,128)}, u32[]{:S(2)}) copy-start(f32[16,256,256]{2,1,0:T(8,128)} %param.18) | copy-start | bytes 12582916

commit v10 on v9

--- a/solution.py
+++ b/solution.py
@@ -173,22 +173,14 @@
         inside = (other >= 0) & (other < n_space)
         return jnp.where(inside, pick, 0.0)
 
-    own = jnp.concatenate([neighbour(-1), leaf_half, neighbour(1), parents], axis=0)
-    theirs = exchange(own, "blk", 1)
-    low_part = jnp.where(core0, own, theirs)
-    high_part = jnp.where(core0, theirs, own)
-
-    def joined(start, size):
-        return jnp.concatenate(
-            [low_part[start : start + size], high_part[start : start + size]], axis=0
-        )
-
-    window = jnp.concatenate([joined(0, half), joined(half, half), joined(2 * half, half)], axis=0)
-    domain = joined(half, half)
+    window = jnp.concatenate([neighbour(-1), leaf_half, neighbour(1)], axis=0)
+    rows_held = (
+        jnp.arange(3)[:, None] * box_dom + core * half + jnp.arange(half)[None, :]
+    ).reshape(-1)
     slots = parents.shape[0] // p_half
-    all_parents = jnp.concatenate(
-        [joined(3 * half + j * p_half, p_half) for j in range(slots)], axis=0
-    )
+    parents_held = (
+        jnp.arange(slots)[:, None] * n_blk + core * p_half + jnp.arange(p_half)[None, :]
+    ).reshape(-1)
     table = table.reshape(-1)[: n_blk * flat].reshape((n_blk,) + lists.shape)
     table = table.astype(jnp.int32)
     dom_src = table[:, :leaves].reshape(box_dom, -1)
@@ -196,19 +188,18 @@
     dom_csrc = table[:, 2 * leaves]
     dom_ctype = table[:, 2 * leaves + 1]
     dom_csrc = (dom_csrc // n_blk ^ here) * n_blk + dom_csrc % n_blk
-    del domain
-
-    src_hot = (dom_src[..., None] == jnp.arange(3 * box_dom, dtype=jnp.int32)).astype(jnp.bfloat16)
+
+    src_hot = (dom_src[..., None] == rows_held).astype(jnp.bfloat16)
     type_hot = (dom_type[..., None] == jnp.arange(n_types, dtype=jnp.int32)).astype(jnp.bfloat16)
     counts = jnp.einsum("blt,blj->btj", type_hot, src_hot, preferred_element_type=jnp.float32)
     gathered = jnp.einsum("btj,jk->btk", counts, window, precision=top)
-    n_parents = all_parents.shape[0]
-    csrc_hot = (dom_csrc[..., None] == jnp.arange(n_parents, dtype=jnp.int32)).astype(jnp.bfloat16)
+    csrc_hot = (dom_csrc[..., None] == parents_held).astype(jnp.bfloat16)
     ctype_hot = (dom_ctype[..., None] == jnp.arange(n_types, dtype=jnp.int32)).astype(jnp.bfloat16)
     ccounts = jnp.einsum("pet,peq->ptq", ctype_hot, csrc_hot, preferred_element_type=jnp.float32)
-    cgathered = jnp.einsum("ptq,qk->ptk", ccounts, all_parents, precision=top)
+    cgathered = jnp.einsum("ptq,qk->ptk", ccounts, parents, precision=top)
     rows = jnp.concatenate([gathered, cgathered], axis=0)
-    far = jnp.einsum("btk,tlk->bl", rows, translation, precision=top)
+    far_part = jnp.einsum("btk,tlk->bl", rows, translation, precision=top)
+    far = far_part + exchange(far_part, "blk", 1)
     leaf_far = far[:box_dom]
     parent_locals = far[box_dom:]
     downward = jnp.einsum(

time: 63.5 us -> 62.5 us (0.984)
  matrix products: 10.7 us -> 9.41 us
    dot_general x1, matrix products: 1.84 us -> 0.95 us  [shards(): jnp.einsum('blt,blj->btj', type_hot, src_hot, preferred_element_type=jnp....]
  transfers between devices with their start and end apart: 8 -> 8, of which waited for: 8 -> 8; matrix products, arithmetic and copies ran while one was open for 5% -> 4% of each run, Pallas kernels for 0% -> 0%
where the time goes in v10:
time: 62.5 us; the launch traced here: 61.3 us
  waiting for transfers between devices  17.1 us (27%)
  starting transfers between devices  16.4 us (26%)
  Pallas kernels  14 us (22%)
  matrix products  9.41 us (15%)
  local copies, waits for them, and re-layouts  2.09 us (3%)
  other arithmetic  1.36 us (2%)
  between operations  0.93 us (1%)
    ppermute x8, waiting for transfers between devices, exchange(): return lax.ppermute(x, axis, [(i, i ^ mask) for i in range(count)])  17.1 us
    ppermute x8, starting transfers between devices, exchange(): return lax.ppermute(x, axis, [(i, i ^ mask) for i in range(count)])  16.4 us
    pallas_call x1, Pallas kernels, block_moments(): pl.pallas_call(moments_kernel, out_shape=jax.ShapeDtypeStruct((blocks, co...  7.2 us
    pallas_call x1, Pallas kernels, block_coulomb(): pl.pallas_call(coulomb_kernel, out_shape=jax.ShapeDtypeStruct((blocks, ro...  6.81 us
    dot_general x1, matrix products, shards(): far_part = jnp.einsum('btk,tlk->bl', rows, translation, precision=top)  2.29 us
    dot_general x1, matrix products, shards(): gathered = jnp.einsum('btj,jk->btk', counts, window, precision=top)  2.1 us
  transfers between devices with their start and end apart: 8, of which 8 were waited for; matrix products, arithmetic and copies ran while one was open for 4% of the time, Pallas kernels for 0%

profile of v10, /device:TPU:0, one launch (start us, length us, event | category | flops | bytes accessed | tf_op | source)
XLA Modules:
  0.0 61.3 jit_solution(2765734129450429274)
XLA Ops:
  0.7 0.9 %add_convert_fusion = f32[18,27]{1,0:T(8,128)S(1)} fusion(s32[1,27]{1,0:T(1,128)} %param.17, s32[1,27]{1,0:T(1,128)} %param.16, s32[8,27]{1,0:T(8,128)} %param.15, s32[8,27]{1,0:T(8,128)} %param.14), kind=kLoop, calls=%fused_computation.55 | loop fusion | flops 1944 | bytes 3888 | tf_op jit(solution)/shard_map/convert_element_type | solution.py:130
  1.6 0.1 convert_element_type.27
  1.7 0.1 reshape.130
  1.9 7.2 %shard_map.113 = f32[96,256]{1,0:T(8,128)} custom-call(bf16[96,128,128]{2,1,0:T(8,128)(2,1)} %dens_ref.1, bf16[96,128,256]{2,1,0:T(8,128)(2,1)} %bra_ref.3, bf16[96,128,256]{2,1,0:T(8,128)(2,1)} %ket_ref.3), custom_call_target="tpu_custom_call" | custom-call | flops 805306368 | bytes 15826944 | tf_op jit(solution)/shard_map/pallas_call | solution.py:27
  9.1 1.2 %fusion.33 = f32[128,256]{1,0:T(8,128)S(1)} fusion(f32[96,256]{1,0:T(8,128)} %shard_map.113, s32[96]{0:T(128)S(1)} %copy-done.2), kind=kOutput, calls=%fused_computation.48 | convolution fusion | flops 18886656 | bytes 229760 | tf_op jit(solution)/shard_map/dot_general | solution.py:139
  10.4 1.3 %collective-permute-done = f32[96,256]{1,0:T(8,128)S(1)} collective-permute-done((f32[96,256]{1,0:T(8,128)S(1)}, f32[96,256]{1,0:T(8,128)S(1)}, u32[]{:S(2)}, u32[]{:S(2)}) %collective-permute-start) | collective-permute-done | bytes 98336 | tf_op jit(solution)/shard_map/ppermute | solution.py:77
  11.7 2.1 %collective-permute-start.1 = (f32[96,256]{1,0:T(8,128)S(1)}, f32[96,256]{1,0:T(8,128)S(1)}, u32[]{:S(2)}, u32[]{:S(2)}) collective-permute-start(f32[96,256]{1,0:T(8,128)S(1)} %select_add_fusion), channel_id=1, source_target_pairs={{0,2},{1,3},{2,0},{3,1},{4,6},{5,7},{6,4},{7,5},{8,10},{9,11},{10,... | collective-permute-start | bytes 294920 | tf_op jit(solution)/shard_map/ppermute | solution.py:77
  13.9 3.0 %collective-permute-done.1 = f32[96,256]{1,0:T(8,128)S(1)} collective-permute-done((f32[96,256]{1,0:T(8,128)S(1)}, f32[96,256]{1,0:T(8,128)S(1)}, u32[]{:S(2)}, u32[]{:S(2)}) %collective-permute-start.1) | collective-permute-done | bytes 98336 | tf_op jit(solution)/shard_map/ppermute | solution.py:77
  16.9 1.7 %collective-permute-start.2 = (f32[96,256]{1,0:T(8,128)S(1)}, f32[96,256]{1,0:T(8,128)S(1)}, u32[]{:S(2)}, u32[]{:S(2)}) collective-permute-start(f32[96,256]{1,0:T(8,128)S(1)} %add.124), channel_id=1, source_target_pairs={{0,4},{1,5},{2,6},{3,7},{4,0},{5,1},{6,2},{7,3},{8,12},{9,13},{10,... | collective-permute-start | bytes 294920 | tf_op jit(solution)/shard_map/ppermute | solution.py:77
  18.6 3.0 %collective-permute-done.2 = f32[96,256]{1,0:T(8,128)S(1)} collective-permute-done((f32[96,256]{1,0:T(8,128)S(1)}, f32[96,256]{1,0:T(8,128)S(1)}, u32[]{:S(2)}, u32[]{:S(2)}) %collective-permute-start.2) | collective-permute-done | bytes 98336 | tf_op jit(solution)/shard_map/ppermute | solution.py:77
  21.7 3.3 %collective-permute-start.3 = (f32[96,256]{1,0:T(8,128)S(1)}, f32[96,256]{1,0:T(8,128)S(1)}, u32[]{:S(2)}, u32[]{:S(2)}) collective-permute-start(f32[96,256]{1,0:T(8,128)S(1)} %add.125), channel_id=1, source_target_pairs={{0,8},{1,9},{2,10},{3,11},{4,12},{5,13},{6,14},{7,15},{8,0},{9,1},... | collective-permute-start | bytes 294920 | tf_op jit(solution)/shard_map/ppermute | solution.py:77
  25.2 2.7 %collective-permute-done.3 = f32[96,256]{1,0:T(8,128)S(1)} collective-permute-done((f32[96,256]{1,0:T(8,128)S(1)}, f32[96,256]{1,0:T(8,128)S(1)}, u32[]{:S(2)}, u32[]{:S(2)}) %collective-permute-start.3) | collective-permute-done | bytes 98336 | tf_op jit(solution)/shard_map/ppermute | solution.py:77
  28.0 0.9 %convolution_bitcast_fusion = f32[8,256]{1,0:T(8,128)S(1)} fusion(f32[8,256,256]{2,1,0:T(8,128)S(1)} %copy-done, f32[8,8,256]{2,1,0:T(8,128)S(1)} %get-tuple-element.11), kind=kOutput, calls=%fused_computation.11 | convolution fusion | flops 25165824 | bytes 2170880 | tf_op jit(solution)/shard_map/qce,cde->qd/dot_general | solution.py:153
  28.9 1.6 %collective-permute-start.4 = (f32[72,256]{1,0:T(8,128)S(1)}, f32[72,256]{1,0:T(8,128)S(1)}, u32[]{:S(2)}, u32[]{:S(2)}) collective-permute-start(f32[72,256]{1,0:T(8,128)S(1)} %pad_maximum_fusion.4), channel_id=1, source_target_pairs={{0,16},{16,0},{32,48},{48,32},{64,80},{80,64},{96,112},{112,96},{1... | collective-permute-start | bytes 221192 | tf_op jit(solution)/shard_map/ppermute | solution.py:77
  30.5 0.2 convert_element_type.29
  30.8 0.6 %copy.17 = pred[128,27,16]{1,2,0:T(8,128)(4,1)S(1)} copy(pred[128,27,16]{0,2,1:T(8,128)(4,1)S(1)} %iota_compare_fusion) | data formatting | bytes 110592 | tf_op jit(solution)/shard_map/eq | solution.py:193
  31.5 0.9 %fusion = f32[128,16,192]{2,1,0:T(8,128)S(1)} fusion(pred[128,27,16]{1,2,0:T(8,128)(4,1)S(1)} %copy.17, s32[192]{0:T(256)S(1)} %add.132, s32[128,27]{1,0:T(8,128)S(1)} %get-tuple-element.4), kind=kOutput, calls=%fused_computation | convolution fusion | flops 21897216 | bytes 1642752 | tf_op jit(solution)/shard_map/blt,blj->btj/dot_general | solution.py:194
  32.4 0.9 %collective-permute-done.4 = f32[72,256]{1,0:T(8,128)S(1)} collective-permute-done((f32[72,256]{1,0:T(8,128)S(1)}, f32[72,256]{1,0:T(8,128)S(1)}, u32[]{:S(2)}, u32[]{:S(2)}) %collective-permute-start.4) | collective-permute-done | bytes 73760 | tf_op jit(solution)/shard_map/ppermute | solution.py:77
  33.4 3.8 %collective-permute-start.5 = (f32[80,256]{1,0:T(8,128)S(1)}, f32[80,256]{1,0:T(8,128)S(1)}, u32[]{:S(2)}, u32[]{:S(2)}) collective-permute-start(f32[80,256]{1,0:T(8,128)S(1)} %pad_maximum_fusion.3), channel_id=1, source_target_pairs={{0,32},{16,48},{32,0},{48,16},{64,96},{80,112},{96,64},{112,80},{1... | collective-permute-start | bytes 245768 | tf_op jit(solution)/shard_map/ppermute | solution.py:77
  37.2 2.4 %collective-permute-done.5 = f32[80,256]{1,0:T(8,128)S(1)} collective-permute-done((f32[80,256]{1,0:T(8,128)S(1)}, f32[80,256]{1,0:T(8,128)S(1)}, u32[]{:S(2)}, u32[]{:S(2)}) %collective-permute-start.5) | collective-permute-done | bytes 81952 | tf_op jit(solution)/shard_map/ppermute | solution.py:77
  39.6 3.8 %collective-permute-start.6 = (f32[96,256]{1,0:T(8,128)S(1)}, f32[96,256]{1,0:T(8,128)S(1)}, u32[]{:S(2)}, u32[]{:S(2)}) collective-permute-start(f32[96,256]{1,0:T(8,128)S(1)} %pad_maximum_fusion.2), channel_id=1, source_target_pairs={{0,64},{16,80},{32,96},{48,112},{64,0},{80,16},{96,32},{112,48},{1... | collective-permute-start | bytes 294920 | tf_op jit(solution)/shard_map/ppermute | solution.py:77
  43.5 0.2 fusion.13
  43.7 2.3 %collective-permute-done.6 = f32[96,256]{1,0:T(8,128)S(1)} collective-permute-done((f32[96,256]{1,0:T(8,128)S(1)}, f32[96,256]{1,0:T(8,128)S(1)}, u32[]{:S(2)}, u32[]{:S(2)}) %collective-permute-start.6) | collective-permute-done | bytes 98336 | tf_op jit(solution)/shard_map/ppermute | solution.py:77
  46.1 0.2 fusion.19
  46.4 2.1 %fusion.6 = f32[128,16,256]{2,0,1:T(8,128)S(1)} fusion(f32[128,16,192]{2,1,0:T(8,128)S(1)} %fusion, f32[64,256]{1,0:T(8,128)S(1)} %get-tuple-element.3, f32[64,256]{1,0:T(8,128)S(1)} %get-tuple-element.10, f32[64,256]{1,0:T(8,128)S(1)} %get-tuple-element.2), kind=kOutput, calls=%fused_computation.6 | convolution fusion | flops 604078080 | bytes 3866624 | tf_op jit(solution)/shard_map/btj,jk->btk/dot_general | solution.py:195
  48.5 2.3 %fusion.10 = f32[144,256]{1,0:T(8,128)S(1)} fusion(f32[16,256,256]{2,1,0:T(8,128)S(1)} %copy-done.1, f32[16,16,256]{2,0,1:T(8,128)S(1)} %fusion.19, f32[128,16,256]{2,0,1:T(8,128)S(1)} %fusion.6), kind=kOutput, calls=%fused_computation.10 | convolution fusion | flops 906559488 | bytes 6701056 | tf_op jit(solution)/shard_map/btk,tlk->bl/dot_general | solution.py:201
  50.9 1.4 %collective-permute-done.7 = f32[144,256]{1,0:T(8,128)S(1)} collective-permute-done((f32[144,256]{1,0:T(8,128)S(1)}, f32[144,256]{1,0:T(8,128)S(1)}, u32[]{:S(2)}, u32[]{:S(2)}) %collective-permute-start.7) | collective-permute-done | bytes 147488 | tf_op jit(solution)/shard_map/ppermute | solution.py:77
  52.3 0.6 %fusion.36 = f32[16,8,256]{2,0,1:T(8,128)S(1)} fusion(f32[8,256,256]{2,1,0:T(8,128)S(1)} %copy-done, f32[144,256]{1,0:T(8,128)S(1)} %add.143), kind=kOutput, calls=%fused_computation.54 | convolution fusion | flops 50331648 | bytes 2244608 | tf_op jit(solution)/shard_map/qd,cds->qcs/dot_general | solution.py:205
  52.9 0.1 slice_add_fusion
  53.0 0.9 %fusion.32.local_ref = f32[96,256]{1,0:T(8,128)} fusion(f32[128,256]{1,0:T(8,128)S(1)} %slice_add_fusion, s32[96]{0:T(128)S(1)} %copy-done.2), kind=kOutput, calls=%fused_computation.47 | convolution fusion | flops 18886656 | bytes 229760 | tf_op jit(solution)/shard_map/dot_general | solution.py:210
  53.9 0.6 constant_dynamic-slice_fusion
  54.5 6.8 %shard_map.114 = bf16[96,128,128]{2,1,0:T(8,128)(2,1)} custom-call(bf16[96,128,256]{2,1,0:T(8,128)(2,1)} %bra_ref.3, bf16[96,128,256]{2,1,0:T(8,128)(2,1)} %ket_ref.3, f32[96,256]{1,0:T(8,128)} %fusion.32.local_ref), custom_call_target="tpu_custom_call" | custom-call | flops 805306368 | bytes 15826944 | tf_op jit(solution)/shard_map/pallas_call | solution.py:57
  (43 shorter events, 1.0 us)
Async XLA Ops:
  0.6 27.3 %copy-start = (f32[8,256,256]{2,1,0:T(8,128)S(1)}, f32[8,256,256]{2,1,0:T(8,128)}, u32[]{:S(2)}) copy-start(f32[8,256,256]{2,1,0:T(8,128)} %param.19) | copy-start | bytes 6291460
  1.9 7.2 %copy-start.2 = (s32[96]{0:T(128)S(1)}, s32[96]{0:T(128)}, u32[]{:S(2)}) copy-start(s32[96]{0:T(128)} %param.13) | copy-start | bytes 1156
  10.3 1.4 %collective-permute-start = (f32[96,256]{1,0:T(8,128)S(1)}, f32[96,256]{1,0:T(8,128)S(1)}, u32[]{:S(2)}, u32[]{:S(2)}) collective-permute-start(f32[96,256]{1,0:T(8,128)S(1)} %fusion.23), channel_id=1, source_target_pairs={{0,1},{1,0},{2,3},{3,2},{4,5},{5,4},{6,7},{7,6},{8,9},{9,8},{10,11... | collective-permute-start | bytes 294920 | tf_op jit(solution)/shard_map/ppermute | solution.py:77
  11.7 5.2 %collective-permute-start.1 = (f32[96,256]{1,0:T(8,128)S(1)}, f32[96,256]{1,0:T(8,128)S(1)}, u32[]{:S(2)}, u32[]{:S(2)}) collective-permute-start(f32[96,256]{1,0:T(8,128)S(1)} %select_add_fusion), channel_id=1, source_target_pairs={{0,2},{1,3},{2,0},{3,1},{4,6},{5,7},{6,4},{7,5},{8,10},{9,11},{10,... | collective-permute-start | bytes 294920 | tf_op jit(solution)/shard_map/ppermute | solution.py:77
  16.9 4.7 %collective-permute-start.2 = (f32[96,256]{1,0:T(8,128)S(1)}, f32[96,256]{1,0:T(8,128)S(1)}, u32[]{:S(2)}, u32[]{:S(2)}) collective-permute-start(f32[96,256]{1,0:T(8,128)S(1)} %add.124), channel_id=1, source_target_pairs={{0,4},{1,5},{2,6},{3,7},{4,0},{5,1},{6,2},{7,3},{8,12},{9,13},{10,... | collective-permute-start | bytes 294920 | tf_op jit(solution)/shard_map/ppermute | solution.py:77
  21.7 6.2 %collective-permute-start.3 = (f32[96,256]{1,0:T(8,128)S(1)}, f32[96,256]{1,0:T(8,128)S(1)}, u32[]{:S(2)}, u32[]{:S(2)}) collective-permute-start(f32[96,256]{1,0:T(8,128)S(1)} %add.125), channel_id=1, source_target_pairs={{0,8},{1,9},{2,10},{3,11},{4,12},{5,13},{6,14},{7,15},{8,0},{9,1},... | collective-permute-start | bytes 294920 | tf_op jit(solution)/shard_map/ppermute | solution.py:77
  28.9 4.4 %collective-permute-start.4 = (f32[72,256]{1,0:T(8,128)S(1)}, f32[72,256]{1,0:T(8,128)S(1)}, u32[]{:S(2)}, u32[]{:S(2)}) collective-permute-start(f32[72,256]{1,0:T(8,128)S(1)} %pad_maximum_fusion.4), channel_id=1, source_target_pairs={{0,16},{16,0},{32,48},{48,32},{64,80},{80,64},{96,112},{112,96},{1... | collective-permute-start | bytes 221192 | tf_op jit(solution)/shard_map/ppermute | solution.py:77
  33.4 6.2 %collective-permute-start.5 = (f32[80,256]{1,0:T(8,128)S(1)}, f32[80,256]{1,0:T(8,128)S(1)}, u32[]{:S(2)}, u32[]{:S(2)}) collective-permute-start(f32[80,256]{1,0:T(8,128)S(1)} %pad_maximum_fusion.3), channel_id=1, source_target_pairs={{0,32},{16,48},{32,0},{48,16},{64,96},{80,112},{96,64},{112,80},{1... | collective-permute-start | bytes 245768 | tf_op jit(solution)/shard_map/ppermute | solution.py:77
  39.6 6.4 %collective-permute-start.6 = (f32[96,256]{1,0:T(8,128)S(1)}, f32[96,256]{1,0:T(8,128)S(1)}, u32[]{:S(2)}, u32[]{:S(2)}) collective-permute-start(f32[96,256]{1,0:T(8,128)S(1)} %pad_maximum_fusion.2), channel_id=1, source_target_pairs={{0,64},{16,80},{32,96},{48,112},{64,0},{80,16},{96,32},{112,48},{1... | collective-permute-start | bytes 294920 | tf_op jit(solution)/shard_map/ppermute | solution.py:77
  46.4 2.2 %copy-start.1 = (f32[16,256,256]{2,1,0:T(8,128)S(1)}, f32[16,256,256]{2,1,0:T(8,128)}, u32[]{:S(2)}) copy-start(f32[16,256,256]{2,1,0:T(8,128)} %param.18) | copy-start | bytes 12582916
  50.8 1.5 %collective-permute-start.7 = (f32[144,256]{1,0:T(8,128)S(1)}, f32[144,256]{1,0:T(8,128)S(1)}, u32[]{:S(2)}, u32[]{:S(2)}) collective-permute-start(f32[144,256]{1,0:T(8,128)S(1)} %fusion.10), channel_id=1, source_target_pairs={{0,1},{1,0},{2,3},{3,2},{4,5},{5,4},{6,7},{7,6},{8,9},{9,8},{10,11... | collective-permute-start | bytes 442376 | tf_op jit(solution)/shard_map/ppermute | solution.py:77

commit v11 on v10

--- a/solution.py
+++ b/solution.py
@@ -126,11 +126,9 @@
 
     lists = jnp.concatenate([leaf_src, leaf_type, coarse_src, coarse_type], axis=0)
     flat = lists.size
-    table = jnp.zeros((n_blk, flat), jnp.float32)
-    table = lax.dynamic_update_index_in_dim(table, lists.reshape(flat).astype(jnp.float32), me, 0)
-    table_rows = 2 * -(-n_blk * flat // (2 * coeffs))
-    table = jnp.pad(table.reshape(-1), (0, table_rows * coeffs - n_blk * flat))
-    table = table.reshape(table_rows, coeffs)
+    slot_rows = -(-flat // coeffs)
+    slot = jnp.pad(lists.reshape(flat).astype(jnp.float32), (0, slot_rows * coeffs - flat))
+    slot = slot.reshape(slot_rows, coeffs)
 
     moments = block_moments(density, bra_table, ket_table)
     box_hot = (box_of_block[:, None] == jnp.arange(box_dom, dtype=jnp.int32)[None, :]).astype(
@@ -139,16 +137,22 @@
     partial_moments = lax.dot_general(
         box_hot, moments, (((0,), (0,)), ((), ())), precision=top
     )
-    first = jnp.concatenate([partial_moments[:half], table], axis=0)
-    second = jnp.concatenate([partial_moments[half:], table], axis=0)
-    mine = jnp.where(core0, first, second)
-    summed = mine + exchange(jnp.where(core0, second, first), "blk", 1)
+    first = partial_moments[:half]
+    second = partial_moments[half:]
+    got = exchange(jnp.concatenate([jnp.where(core0, second, first), slot], axis=0), "blk", 1)
+    summed = jnp.where(core0, first, second) + got[:half]
+    gathered_lists = jnp.concatenate([slot, got[half:]], axis=0)
     mask = 2
     while mask < n_blk:
-        summed = summed + exchange(summed, "blk", mask)
-        mask *= 2
-    leaf_half = summed[:half]
-    table = summed[half:]
+        got = exchange(jnp.concatenate([summed, gathered_lists], axis=0), "blk", mask)
+        summed = summed + got[:half]
+        gathered_lists = jnp.concatenate([gathered_lists, got[half:]], axis=0)
+        mask *= 2
+    leaf_half = summed
+    base = me - core
+    by_slot = gathered_lists.reshape(n_blk, slot_rows * coeffs)
+    paired = by_slot.reshape(n_blk // 2, 2, -1)[:, ::-1].reshape(n_blk, -1)
+    by_slot = jnp.where(core0, by_slot, paired)
 
     parent_half = jnp.einsum(
         "qce,cde->qd", leaf_half.reshape(-1, 8, coeffs), upward_translation_table, precision=top
@@ -181,8 +185,7 @@
     parents_held = (
         jnp.arange(slots)[:, None] * n_blk + core * p_half + jnp.arange(p_half)[None, :]
     ).reshape(-1)
-    table = table.reshape(-1)[: n_blk * flat].reshape((n_blk,) + lists.shape)
-    table = table.astype(jnp.int32)
+    table = by_slot[:, :flat].reshape((n_blk,) + lists.shape).astype(jnp.int32)
     dom_src = table[:, :leaves].reshape(box_dom, -1)
     dom_type = table[:, leaves : 2 * leaves].reshape(box_dom, -1)
     dom_csrc = table[:, 2 * leaves]
@@ -206,8 +209,12 @@
         "qd,cds->qcs", parent_locals, upward_translation_table, precision=top
     ).reshape(box_dom, coeffs)
     domain_local = leaf_far + downward
-    box_locals = lax.dynamic_slice_in_dim(domain_local, me * leaves, leaves, axis=0)
-    block_locals = jnp.dot(box_hot, domain_local, precision=top)
+    box_locals = lax.dynamic_slice_in_dim(domain_local, core * leaves, leaves, axis=0)
+    relabelled = ((box_of_block // leaves) ^ base) * leaves + box_of_block % leaves
+    slot_hot = (relabelled[:, None] == jnp.arange(box_dom, dtype=jnp.int32)[None, :]).astype(
+        jnp.float32
+    )
+    block_locals = jnp.dot(slot_hot, domain_local, precision=top)
     coulomb = block_coulomb(bra_table, ket_table, block_locals)
     return (coulomb, box_locals)
 

time: 62.5 us -> 61.7 us (0.987)
  waiting for transfers between devices: 17.1 us -> 16.1 us
    ppermute x8, waiting for transfers between devices: 17.1 us -> 16.1 us  [exchange(): return lax.ppermute(x, axis, [(i, i ^ mask) for i in range(count)])]
where the time goes in v11:
time: 61.7 us; the launch traced here: 60.5 us
  starting transfers between devices  16.5 us (27%)
  waiting for transfers between devices  16.1 us (26%)
  Pallas kernels  14 us (23%)
  matrix products  9.39 us (15%)
  local copies, waits for them, and re-layouts  2.14 us (3%)
  other arithmetic  1.39 us (2%)
  between operations  0.95 us (2%)
    ppermute x8, starting transfers between devices, exchange(): return lax.ppermute(x, axis, [(i, i ^ mask) for i in range(count)])  16.5 us
    ppermute x8, waiting for transfers between devices, exchange(): return lax.ppermute(x, axis, [(i, i ^ mask) for i in range(count)])  16.1 us
    pallas_call x1, Pallas kernels, block_moments(): pl.pallas_call(moments_kernel, out_shape=jax.ShapeDtypeStruct((blocks, co...  7.2 us
    pallas_call x1, Pallas kernels, block_coulomb(): pl.pallas_call(coulomb_kernel, out_shape=jax.ShapeDtypeStruct((blocks, ro...  6.81 us
    dot_general x1, matrix products, shards(): far_part = jnp.einsum('btk,tlk->bl', rows, translation, precision=top)  2.29 us
    dot_general x1, matrix products, shards(): gathered = jnp.einsum('btj,jk->btk', counts, window, precision=top)  2.1 us
  transfers between devices with their start and end apart: 8, of which 8 were waited for; matrix products, arithmetic and copies ran while one was open for 4% of the time, Pallas kernels for 0%

profile of v11, /device:TPU:0, one launch (start us, length us, event | category | flops | bytes accessed | tf_op | source)
XLA Modules:
  0.0 60.5 jit_solution(18432681528279425199)
XLA Ops:
  0.7 0.9 %add_convert_fusion = f32[18,27]{1,0:T(8,128)S(1)} fusion(s32[1,27]{1,0:T(1,128)} %param.17, s32[1,27]{1,0:T(1,128)} %param.16, s32[8,27]{1,0:T(8,128)} %param.15, s32[8,27]{1,0:T(8,128)} %param.14), kind=kLoop, calls=%fused_computation.60 | loop fusion | flops 1944 | bytes 3888 | tf_op jit(solution)/shard_map/convert_element_type | solution.py:130
  1.6 0.1 convert_element_type.21
  1.7 7.2 %shard_map.113 = f32[96,256]{1,0:T(8,128)} custom-call(bf16[96,128,128]{2,1,0:T(8,128)(2,1)} %dens_ref.1, bf16[96,128,256]{2,1,0:T(8,128)(2,1)} %bra_ref.3, bf16[96,128,256]{2,1,0:T(8,128)(2,1)} %ket_ref.3), custom_call_target="tpu_custom_call" | custom-call | flops 805306368 | bytes 15826944 | tf_op jit(solution)/shard_map/pallas_call | solution.py:27
  8.9 1.2 %fusion.32 = f32[128,256]{1,0:T(8,128)S(1)} fusion(f32[96,256]{1,0:T(8,128)} %shard_map.113, s32[96]{0:T(128)S(1)} %copy-done.2), kind=kOutput, calls=%fused_computation.53 | convolution fusion | flops 18886656 | bytes 229760 | tf_op jit(solution)/shard_map/dot_general | solution.py:137
  10.2 1.2 %collective-permute-done = f32[66,256]{1,0:T(8,128)S(1)} collective-permute-done((f32[66,256]{1,0:T(8,128)S(1)}, f32[66,256]{1,0:T(8,128)S(1)}, u32[]{:S(2)}, u32[]{:S(2)}) %collective-permute-start) | collective-permute-done | bytes 67616 | tf_op jit(solution)/shard_map/ppermute | solution.py:77
  11.5 2.1 %collective-permute-start.1 = (f32[68,256]{1,0:T(8,128)S(1)}, f32[68,256]{1,0:T(8,128)S(1)}, u32[]{:S(2)}, u32[]{:S(2)}) collective-permute-start(f32[68,256]{1,0:T(8,128)S(1)} %pad_maximum_fusion.3), channel_id=1, source_target_pairs={{0,2},{1,3},{2,0},{3,1},{4,6},{5,7},{6,4},{7,5},{8,10},{9,11},{10,... | collective-permute-start | bytes 208904 | tf_op jit(solution)/shard_map/ppermute | solution.py:77
  13.7 2.5 %collective-permute-done.1 = f32[68,256]{1,0:T(8,128)S(1)} collective-permute-done((f32[68,256]{1,0:T(8,128)S(1)}, f32[68,256]{1,0:T(8,128)S(1)}, u32[]{:S(2)}, u32[]{:S(2)}) %collective-permute-start.1) | collective-permute-done | bytes 69664 | tf_op jit(solution)/shard_map/ppermute | solution.py:77
  16.2 1.7 %collective-permute-start.2 = (f32[72,256]{1,0:T(8,128)S(1)}, f32[72,256]{1,0:T(8,128)S(1)}, u32[]{:S(2)}, u32[]{:S(2)}) collective-permute-start(f32[72,256]{1,0:T(8,128)S(1)} %pad_maximum_fusion.4), channel_id=1, source_target_pairs={{0,4},{1,5},{2,6},{3,7},{4,0},{5,1},{6,2},{7,3},{8,12},{9,13},{10,... | collective-permute-start | bytes 221192 | tf_op jit(solution)/shard_map/ppermute | solution.py:77
  17.9 2.8 %collective-permute-done.2 = f32[72,256]{1,0:T(8,128)S(1)} collective-permute-done((f32[72,256]{1,0:T(8,128)S(1)}, f32[72,256]{1,0:T(8,128)S(1)}, u32[]{:S(2)}, u32[]{:S(2)}) %collective-permute-start.2) | collective-permute-done | bytes 73760 | tf_op jit(solution)/shard_map/ppermute | solution.py:77
  20.7 3.3 %collective-permute-start.3 = (f32[80,256]{1,0:T(8,128)S(1)}, f32[80,256]{1,0:T(8,128)S(1)}, u32[]{:S(2)}, u32[]{:S(2)}) collective-permute-start(f32[80,256]{1,0:T(8,128)S(1)} %concatenate.55), channel_id=1, source_target_pairs={{0,8},{1,9},{2,10},{3,11},{4,12},{5,13},{6,14},{7,15},{8,0},{9,1},... | collective-permute-start | bytes 245768 | tf_op jit(solution)/shard_map/ppermute | solution.py:77
  24.2 2.5 %collective-permute-done.3 = f32[80,256]{1,0:T(8,128)S(1)} collective-permute-done((f32[80,256]{1,0:T(8,128)S(1)}, f32[80,256]{1,0:T(8,128)S(1)}, u32[]{:S(2)}, u32[]{:S(2)}) %collective-permute-start.3) | collective-permute-done | bytes 81952 | tf_op jit(solution)/shard_map/ppermute | solution.py:77
  26.8 0.2 rev.3
  27.1 0.9 %convolution_bitcast_fusion = f32[8,256]{1,0:T(8,128)S(1)} fusion(f32[8,256,256]{2,1,0:T(8,128)S(1)} %copy-done, f32[8,8,256]{2,1,0:T(8,128)S(1)} %bitcast.28), kind=kOutput, calls=%fused_computation.11 | convolution fusion | flops 25165824 | bytes 2170880 | tf_op jit(solution)/shard_map/qce,cde->qd/dot_general | solution.py:157
  28.0 1.6 %collective-permute-start.4 = (f32[72,256]{1,0:T(8,128)S(1)}, f32[72,256]{1,0:T(8,128)S(1)}, u32[]{:S(2)}, u32[]{:S(2)}) collective-permute-start(f32[72,256]{1,0:T(8,128)S(1)} %pad_maximum_fusion.5), channel_id=1, source_target_pairs={{0,16},{16,0},{32,48},{48,32},{64,80},{80,64},{96,112},{112,96},{1... | collective-permute-start | bytes 221192 | tf_op jit(solution)/shard_map/ppermute | solution.py:77
  29.6 0.1 convert_element_type.23
  29.9 0.6 %copy.17 = pred[128,27,16]{1,2,0:T(8,128)(4,1)S(1)} copy(pred[128,27,16]{0,2,1:T(8,128)(4,1)S(1)} %iota_compare_fusion) | data formatting | bytes 110592 | tf_op jit(solution)/shard_map/eq | solution.py:196
  30.5 0.9 %fusion = f32[128,16,192]{2,1,0:T(8,128)S(1)} fusion(pred[128,27,16]{1,2,0:T(8,128)(4,1)S(1)} %copy.17, s32[192]{0:T(256)S(1)} %add.138, s32[128,27]{1,0:T(8,128)S(1)} %get-tuple-element.4), kind=kOutput, calls=%fused_computation | convolution fusion | flops 21897216 | bytes 1642752 | tf_op jit(solution)/shard_map/blt,blj->btj/dot_general | solution.py:197
  31.5 1.0 %collective-permute-done.4 = f32[72,256]{1,0:T(8,128)S(1)} collective-permute-done((f32[72,256]{1,0:T(8,128)S(1)}, f32[72,256]{1,0:T(8,128)S(1)}, u32[]{:S(2)}, u32[]{:S(2)}) %collective-permute-start.4) | collective-permute-done | bytes 73760 | tf_op jit(solution)/shard_map/ppermute | solution.py:77
  32.5 3.8 %collective-permute-start.5 = (f32[80,256]{1,0:T(8,128)S(1)}, f32[80,256]{1,0:T(8,128)S(1)}, u32[]{:S(2)}, u32[]{:S(2)}) collective-permute-start(f32[80,256]{1,0:T(8,128)S(1)} %pad_maximum_fusion.1), channel_id=1, source_target_pairs={{0,32},{16,48},{32,0},{48,16},{64,96},{80,112},{96,64},{112,80},{1... | collective-permute-start | bytes 245768 | tf_op jit(solution)/shard_map/ppermute | solution.py:77
  36.3 2.4 %collective-permute-done.5 = f32[80,256]{1,0:T(8,128)S(1)} collective-permute-done((f32[80,256]{1,0:T(8,128)S(1)}, f32[80,256]{1,0:T(8,128)S(1)}, u32[]{:S(2)}, u32[]{:S(2)}) %collective-permute-start.5) | collective-permute-done | bytes 81952 | tf_op jit(solution)/shard_map/ppermute | solution.py:77
  38.8 3.9 %collective-permute-start.6 = (f32[96,256]{1,0:T(8,128)S(1)}, f32[96,256]{1,0:T(8,128)S(1)}, u32[]{:S(2)}, u32[]{:S(2)}) collective-permute-start(f32[96,256]{1,0:T(8,128)S(1)} %pad_maximum_fusion), channel_id=1, source_target_pairs={{0,64},{16,80},{32,96},{48,112},{64,0},{80,16},{96,32},{112,48},{1... | collective-permute-start | bytes 294920 | tf_op jit(solution)/shard_map/ppermute | solution.py:77
  42.7 0.2 fusion.13
  42.9 2.3 %collective-permute-done.6 = f32[96,256]{1,0:T(8,128)S(1)} collective-permute-done((f32[96,256]{1,0:T(8,128)S(1)}, f32[96,256]{1,0:T(8,128)S(1)}, u32[]{:S(2)}, u32[]{:S(2)}) %collective-permute-start.6) | collective-permute-done | bytes 98336 | tf_op jit(solution)/shard_map/ppermute | solution.py:77
  45.3 0.2 fusion.19
  45.6 2.1 %fusion.6 = f32[128,16,256]{2,0,1:T(8,128)S(1)} fusion(f32[128,16,192]{2,1,0:T(8,128)S(1)} %fusion, f32[64,256]{1,0:T(8,128)S(1)} %get-tuple-element.3, f32[64,256]{1,0:T(8,128)S(1)} %slice_add_fusion.1, f32[64,256]{1,0:T(8,128)S(1)} %get-tuple-element.2), kind=kOutput, calls=%fused_computation.6 | convolution fusion | flops 604078080 | bytes 3866624 | tf_op jit(solution)/shard_map/btj,jk->btk/dot_general | solution.py:198
  47.7 2.3 %fusion.10 = f32[144,256]{1,0:T(8,128)S(1)} fusion(f32[16,256,256]{2,1,0:T(8,128)S(1)} %copy-done.1, f32[16,16,256]{2,0,1:T(8,128)S(1)} %fusion.19, f32[128,16,256]{2,0,1:T(8,128)S(1)} %fusion.6), kind=kOutput, calls=%fused_computation.10 | convolution fusion | flops 906559488 | bytes 6701056 | tf_op jit(solution)/shard_map/btk,tlk->bl/dot_general | solution.py:204
  50.1 1.3 %collective-permute-done.7 = f32[144,256]{1,0:T(8,128)S(1)} collective-permute-done((f32[144,256]{1,0:T(8,128)S(1)}, f32[144,256]{1,0:T(8,128)S(1)}, u32[]{:S(2)}, u32[]{:S(2)}) %collective-permute-start.7) | collective-permute-done | bytes 147488 | tf_op jit(solution)/shard_map/ppermute | solution.py:77
  51.5 0.6 %fusion.36 = f32[16,8,256]{2,0,1:T(8,128)S(1)} fusion(f32[8,256,256]{2,1,0:T(8,128)S(1)} %copy-done, f32[144,256]{1,0:T(8,128)S(1)} %add.150), kind=kOutput, calls=%fused_computation.59 | convolution fusion | flops 50331648 | bytes 2244608 | tf_op jit(solution)/shard_map/qd,cds->qcs/dot_general | solution.py:208
  52.1 0.1 slice_add_fusion
  52.2 0.6 %constant_dynamic-slice_fusion = f32[8,256]{1,0:T(8,128)} fusion(f32[128,256]{1,0:T(8,128)S(1)} %slice_add_fusion, s32[]{:T(128)S(6)} %select_n.136), kind=kLoop, calls=%fused_computation.84 | loop fusion | bytes 16388 | tf_op jit(solution)/shard_map/dynamic_slice | solution.py:212
  52.8 0.8 %fusion.31.local_ref = f32[96,256]{1,0:T(8,128)} fusion(f32[128,256]{1,0:T(8,128)S(1)} %slice_add_fusion, s32[96]{0:T(128)S(1)} %fusion.44), kind=kOutput, calls=%fused_computation.52 | convolution fusion | flops 18886656 | bytes 229760 | tf_op jit(solution)/shard_map/dot_general | solution.py:217
  53.7 6.8 %shard_map.114 = bf16[96,128,128]{2,1,0:T(8,128)(2,1)} custom-call(bf16[96,128,256]{2,1,0:T(8,128)(2,1)} %bra_ref.3, bf16[96,128,256]{2,1,0:T(8,128)(2,1)} %ket_ref.3, f32[96,256]{1,0:T(8,128)} %fusion.31.local_ref), custom_call_target="tpu_custom_call" | custom-call | flops 805306368 | bytes 15826944 | tf_op jit(solution)/shard_map/pallas_call | solution.py:57
  (50 shorter events, 1.1 us)
Async XLA Ops:
  0.6 26.5 %copy-start = (f32[8,256,256]{2,1,0:T(8,128)S(1)}, f32[8,256,256]{2,1,0:T(8,128)}, u32[]{:S(2)}) copy-start(f32[8,256,256]{2,1,0:T(8,128)} %param.19) | copy-start | bytes 6291460
  1.7 7.2 %copy-start.2 = (s32[96]{0:T(128)S(1)}, s32[96]{0:T(128)}, u32[]{:S(2)}) copy-start(s32[96]{0:T(128)} %param.13) | copy-start | bytes 1156
  10.1 1.3 %collective-permute-start = (f32[66,256]{1,0:T(8,128)S(1)}, f32[66,256]{1,0:T(8,128)S(1)}, u32[]{:S(2)}, u32[]{:S(2)}) collective-permute-start(f32[66,256]{1,0:T(8,128)S(1)} %pad_maximum_fusion.2), channel_id=1, source_target_pairs={{0,1},{1,0},{2,3},{3,2},{4,5},{5,4},{6,7},{7,6},{8,9},{9,8},{10,11... | collective-permute-start | bytes 202760 | tf_op jit(solution)/shard_map/ppermute | solution.py:77
  11.5 4.7 %collective-permute-start.1 = (f32[68,256]{1,0:T(8,128)S(1)}, f32[68,256]{1,0:T(8,128)S(1)}, u32[]{:S(2)}, u32[]{:S(2)}) collective-permute-start(f32[68,256]{1,0:T(8,128)S(1)} %pad_maximum_fusion.3), channel_id=1, source_target_pairs={{0,2},{1,3},{2,0},{3,1},{4,6},{5,7},{6,4},{7,5},{8,10},{9,11},{10,... | collective-permute-start | bytes 208904 | tf_op jit(solution)/shard_map/ppermute | solution.py:77
  16.2 4.4 %collective-permute-start.2 = (f32[72,256]{1,0:T(8,128)S(1)}, f32[72,256]{1,0:T(8,128)S(1)}, u32[]{:S(2)}, u32[]{:S(2)}) collective-permute-start(f32[72,256]{1,0:T(8,128)S(1)} %pad_maximum_fusion.4), channel_id=1, source_target_pairs={{0,4},{1,5},{2,6},{3,7},{4,0},{5,1},{6,2},{7,3},{8,12},{9,13},{10,... | collective-permute-start | bytes 221192 | tf_op jit(solution)/shard_map/ppermute | solution.py:77
  20.7 6.0 %collective-permute-start.3 = (f32[80,256]{1,0:T(8,128)S(1)}, f32[80,256]{1,0:T(8,128)S(1)}, u32[]{:S(2)}, u32[]{:S(2)}) collective-permute-start(f32[80,256]{1,0:T(8,128)S(1)} %concatenate.55), channel_id=1, source_target_pairs={{0,8},{1,9},{2,10},{3,11},{4,12},{5,13},{6,14},{7,15},{8,0},{9,1},... | collective-permute-start | bytes 245768 | tf_op jit(solution)/shard_map/ppermute | solution.py:77
  28.0 4.4 %collective-permute-start.4 = (f32[72,256]{1,0:T(8,128)S(1)}, f32[72,256]{1,0:T(8,128)S(1)}, u32[]{:S(2)}, u32[]{:S(2)}) collective-permute-start(f32[72,256]{1,0:T(8,128)S(1)} %pad_maximum_fusion.5), channel_id=1, source_target_pairs={{0,16},{16,0},{32,48},{48,32},{64,80},{80,64},{96,112},{112,96},{1... | collective-permute-start | bytes 221192 | tf_op jit(solution)/shard_map/ppermute | solution.py:77
  32.5 6.2 %collective-permute-start.5 = (f32[80,256]{1,0:T(8,128)S(1)}, f32[80,256]{1,0:T(8,128)S(1)}, u32[]{:S(2)}, u32[]{:S(2)}) collective-permute-start(f32[80,256]{1,0:T(8,128)S(1)} %pad_maximum_fusion.1), channel_id=1, source_target_pairs={{0,32},{16,48},{32,0},{48,16},{64,96},{80,112},{96,64},{112,80},{1... | collective-permute-start | bytes 245768 | tf_op jit(solution)/shard_map/ppermute | solution.py:77
  38.8 6.5 %collective-permute-start.6 = (f32[96,256]{1,0:T(8,128)S(1)}, f32[96,256]{1,0:T(8,128)S(1)}, u32[]{:S(2)}, u32[]{:S(2)}) collective-permute-start(f32[96,256]{1,0:T(8,128)S(1)} %pad_maximum_fusion), channel_id=1, source_target_pairs={{0,64},{16,80},{32,96},{48,112},{64,0},{80,16},{96,32},{112,48},{1... | collective-permute-start | bytes 294920 | tf_op jit(solution)/shard_map/ppermute | solution.py:77
  45.5 2.2 %copy-start.1 = (f32[16,256,256]{2,1,0:T(8,128)S(1)}, f32[16,256,256]{2,1,0:T(8,128)}, u32[]{:S(2)}) copy-start(f32[16,256,256]{2,1,0:T(8,128)} %param.18) | copy-start | bytes 12582916
  50.0 1.5 %collective-permute-start.7 = (f32[144,256]{1,0:T(8,128)S(1)}, f32[144,256]{1,0:T(8,128)S(1)}, u32[]{:S(2)}, u32[]{:S(2)}) collective-permute-start(f32[144,256]{1,0:T(8,128)S(1)} %fusion.10), channel_id=1, source_target_pairs={{0,1},{1,0},{2,3},{3,2},{4,5},{5,4},{6,7},{7,6},{8,9},{9,8},{10,11... | collective-permute-start | bytes 442376 | tf_op jit(solution)/shard_map/ppermute | solution.py:77

commit v12 on v11

--- a/solution.py
+++ b/solution.py
@@ -70,6 +70,15 @@
             bytes_accessed=2 * blocks * (rows * cols + 2 * rows * coeffs) + 4 * blocks * coeffs,
         ),
     )(bra_table, ket_table, block_locals)
+
+
+def exact_left(spec, left, right):
+    high = right.astype(jnp.bfloat16)
+    low = (right - high.astype(jnp.float32)).astype(jnp.bfloat16)
+    left = left.astype(jnp.bfloat16)
+    return jnp.einsum(spec, left, high, preferred_element_type=jnp.float32) + jnp.einsum(
+        spec, left, low, preferred_element_type=jnp.float32
+    )
 
 
 def exchange(x, axis, mask):
@@ -134,9 +143,7 @@
     box_hot = (box_of_block[:, None] == jnp.arange(box_dom, dtype=jnp.int32)[None, :]).astype(
         jnp.float32
     )
-    partial_moments = lax.dot_general(
-        box_hot, moments, (((0,), (0,)), ((), ())), precision=top
-    )
+    partial_moments = exact_left("bj,bk->jk", box_hot, moments)
     first = partial_moments[:half]
     second = partial_moments[half:]
     got = exchange(jnp.concatenate([jnp.where(core0, second, first), slot], axis=0), "blk", 1)
@@ -195,11 +202,11 @@
     src_hot = (dom_src[..., None] == rows_held).astype(jnp.bfloat16)
     type_hot = (dom_type[..., None] == jnp.arange(n_types, dtype=jnp.int32)).astype(jnp.bfloat16)
     counts = jnp.einsum("blt,blj->btj", type_hot, src_hot, preferred_element_type=jnp.float32)
-    gathered = jnp.einsum("btj,jk->btk", counts, window, precision=top)
+    gathered = exact_left("btj,jk->btk", counts, window)
     csrc_hot = (dom_csrc[..., None] == parents_held).astype(jnp.bfloat16)
     ctype_hot = (dom_ctype[..., None] == jnp.arange(n_types, dtype=jnp.int32)).astype(jnp.bfloat16)
     ccounts = jnp.einsum("pet,peq->ptq", ctype_hot, csrc_hot, preferred_element_type=jnp.float32)
-    cgathered = jnp.einsum("ptq,qk->ptk", ccounts, parents, precision=top)
+    cgathered = exact_left("ptq,qk->ptk", ccounts, parents)
     rows = jnp.concatenate([gathered, cgathered], axis=0)
     far_part = jnp.einsum("btk,tlk->bl", rows, translation, precision=top)
     far = far_part + exchange(far_part, "blk", 1)
@@ -214,7 +221,7 @@
     slot_hot = (relabelled[:, None] == jnp.arange(box_dom, dtype=jnp.int32)[None, :]).astype(
         jnp.float32
     )
-    block_locals = jnp.dot(slot_hot, domain_local, precision=top)
+    block_locals = exact_left("bj,jk->bk", slot_hot, domain_local)
     coulomb = block_coulomb(bra_table, ket_table, block_locals)
     return (coulomb, box_locals)
 

time: 61.7 us -> 63.7 us (1.032)
  local copies, waits for them, and re-layouts: 2.14 us -> 4.99 us
  waiting for transfers between devices: 16.1 us -> 13.5 us
  matrix products: 9.39 us -> 11.2 us
    ppermute x8, waiting for transfers between devices: 16.1 us -> 13.5 us  [exchange(): return lax.ppermute(x, axis, [(i, i ^ mask) for i in range(count)])]
    convert_element_type x0 -> x1, local copies, waits for them, and re-layouts: none -> 1.93 us  [exact_left(): left = left.astype(jnp.bfloat16)]
    unnamed x6, local copies, waits for them, and re-layouts: 0.09 us -> 1.7 us
    dot_general x1, matrix products: 0.95 us -> 2.41 us  [shards(): jnp.einsum('blt,blj->btj', type_hot, src_hot, preferred_element_type=jnp....]
    eq x2 -> x1, local copies, waits for them, and re-layouts: 0.69 us -> 0.01 us  [shards(): dom_type[..., None] == jnp.arange(n_types, dtype=jnp.int32)]
    dot_general x4 -> x8, matrix products: 4.38 us -> 4.72 us  [the longest x4 2.62 us: exact_left(): jnp.einsum(spec, left, high, preferred_element_type=jnp.float32)]
  transfers between devices with their start and end apart: 8 -> 8, of which waited for: 8 -> 8; matrix products, arithmetic and copies ran while one was open for 4% -> 8% of each run, Pallas kernels for 0% -> 0%
where the time goes in v12:
time: 63.7 us; the launch traced here: 62.4 us
  starting transfers between devices  16.5 us (26%)
  Pallas kernels  14 us (22%)
  waiting for transfers between devices  13.5 us (21%)
  matrix products  11.2 us (18%)
  local copies, waits for them, and re-layouts  4.99 us (8%)
  other arithmetic  1.34 us (2%)
  between operations  0.95 us (1%)
    ppermute x8, starting transfers between devices, exchange(): return lax.ppermute(x, axis, [(i, i ^ mask) for i in range(count)])  16.5 us
    ppermute x8, waiting for transfers between devices, exchange(): return lax.ppermute(x, axis, [(i, i ^ mask) for i in range(count)])  13.5 us
    pallas_call x1, Pallas kernels, block_moments(): pl.pallas_call(moments_kernel, out_shape=jax.ShapeDtypeStruct((blocks, co...  7.2 us
    pallas_call x1, Pallas kernels, block_coulomb(): pl.pallas_call(coulomb_kernel, out_shape=jax.ShapeDtypeStruct((blocks, ro...  6.81 us
    dot_general x4, matrix products, exact_left(): jnp.einsum(spec, left, high, preferred_element_type=jnp.float32)  2.62 us
    dot_general x1, matrix products, shards(): jnp.einsum('blt,blj->btj', type_hot, src_hot, preferred_element_type=jnp....  2.41 us
    dot_general x1, matrix products, shards(): far_part = jnp.einsum('btk,tlk->bl', rows, translation, precision=top)  2.28 us
    dot_general x4, matrix products, exact_left(): jnp.einsum(spec, left, low, preferred_element_type=jnp.float32)  2.1 us
  transfers between devices with their start and end apart: 8, of which 8 were waited for; matrix products, arithmetic and copies ran while one was open for 8% of the time, Pallas kernels for 0%

profile of v12, /device:TPU:0, one launch (start us, length us, event | category | flops | bytes accessed | tf_op | source)
XLA Modules:
  0.0 62.4 jit_solution(4121399725759214346)
XLA Ops:
  0.7 0.9 %add_convert_fusion = f32[18,27]{1,0:T(8,128)S(1)} fusion(s32[1,27]{1,0:T(1,128)} %param.17, s32[1,27]{1,0:T(1,128)} %param.16, s32[8,27]{1,0:T(8,128)} %param.15, s32[8,27]{1,0:T(8,128)} %param.14), kind=kLoop, calls=%fused_computation.74 | loop fusion | flops 1944 | bytes 3888 | tf_op jit(solution)/shard_map/convert_element_type | solution.py:139
  1.7 7.2 %shard_map.113 = f32[96,256]{1,0:T(8,128)} custom-call(bf16[96,128,128]{2,1,0:T(8,128)(2,1)} %dens_ref.1, bf16[96,128,256]{2,1,0:T(8,128)(2,1)} %bra_ref.3, bf16[96,128,256]{2,1,0:T(8,128)(2,1)} %ket_ref.3), custom_call_target="tpu_custom_call" | custom-call | flops 805306368 | bytes 15826944 | tf_op jit(solution)/shard_map/pallas_call | solution.py:27
  8.9 1.2 %fusion.32 = f32[128,256]{1,0:T(8,128)S(1)} fusion(f32[96,256]{1,0:T(8,128)} %shard_map.113, s32[96]{0:T(128)S(1)} %copy-done.2), kind=kOutput, calls=%fused_computation.59 | convolution fusion | flops 6352896 | bytes 229760 | tf_op jit(solution)/shard_map/bj,bk->jk/dot_general | solution.py:79
  10.0 1.2 %convolution_add_fusion.2 = f32[128,256]{1,0:T(8,128)S(1)} fusion(f32[128,256]{1,0:T(8,128)S(1)} %fusion.32, f32[96,256]{1,0:T(8,128)} %shard_map.113, s32[96]{0:T(128)S(1)} %copy-done.2), kind=kOutput, calls=%fused_computation.12 | convolution fusion | flops 6459392 | bytes 360832 | tf_op jit(solution)/shard_map/bj,bk->jk/dot_general | solution.py:79
  11.4 1.2 %collective-permute-done = f32[66,256]{1,0:T(8,128)S(1)} collective-permute-done((f32[66,256]{1,0:T(8,128)S(1)}, f32[66,256]{1,0:T(8,128)S(1)}, u32[]{:S(2)}, u32[]{:S(2)}) %collective-permute-start) | collective-permute-done | bytes 67616 | tf_op jit(solution)/shard_map/ppermute | solution.py:86
  12.7 2.1 %collective-permute-start.1 = (f32[68,256]{1,0:T(8,128)S(1)}, f32[68,256]{1,0:T(8,128)S(1)}, u32[]{:S(2)}, u32[]{:S(2)}) collective-permute-start(f32[68,256]{1,0:T(8,128)S(1)} %pad_maximum_fusion.4), channel_id=1, source_target_pairs={{0,2},{1,3},{2,0},{3,1},{4,6},{5,7},{6,4},{7,5},{8,10},{9,11},{10,... | collective-permute-start | bytes 208904 | tf_op jit(solution)/shard_map/ppermute | solution.py:86
  14.9 2.5 %collective-permute-done.1 = f32[68,256]{1,0:T(8,128)S(1)} collective-permute-done((f32[68,256]{1,0:T(8,128)S(1)}, f32[68,256]{1,0:T(8,128)S(1)}, u32[]{:S(2)}, u32[]{:S(2)}) %collective-permute-start.1) | collective-permute-done | bytes 69664 | tf_op jit(solution)/shard_map/ppermute | solution.py:86
  17.4 1.7 %collective-permute-start.2 = (f32[72,256]{1,0:T(8,128)S(1)}, f32[72,256]{1,0:T(8,128)S(1)}, u32[]{:S(2)}, u32[]{:S(2)}) collective-permute-start(f32[72,256]{1,0:T(8,128)S(1)} %pad_maximum_fusion.5), channel_id=1, source_target_pairs={{0,4},{1,5},{2,6},{3,7},{4,0},{5,1},{6,2},{7,3},{8,12},{9,13},{10,... | collective-permute-start | bytes 221192 | tf_op jit(solution)/shard_map/ppermute | solution.py:86
  19.1 2.8 %collective-permute-done.2 = f32[72,256]{1,0:T(8,128)S(1)} collective-permute-done((f32[72,256]{1,0:T(8,128)S(1)}, f32[72,256]{1,0:T(8,128)S(1)}, u32[]{:S(2)}, u32[]{:S(2)}) %collective-permute-start.2) | collective-permute-done | bytes 73760 | tf_op jit(solution)/shard_map/ppermute | solution.py:86
  21.9 3.3 %collective-permute-start.3 = (f32[80,256]{1,0:T(8,128)S(1)}, f32[80,256]{1,0:T(8,128)S(1)}, u32[]{:S(2)}, u32[]{:S(2)}) collective-permute-start(f32[80,256]{1,0:T(8,128)S(1)} %concatenate.55), channel_id=1, source_target_pairs={{0,8},{1,9},{2,10},{3,11},{4,12},{5,13},{6,14},{7,15},{8,0},{9,1},... | collective-permute-start | bytes 245768 | tf_op jit(solution)/shard_map/ppermute | solution.py:86
  25.4 2.5 %collective-permute-done.3 = f32[80,256]{1,0:T(8,128)S(1)} collective-permute-done((f32[80,256]{1,0:T(8,128)S(1)}, f32[80,256]{1,0:T(8,128)S(1)}, u32[]{:S(2)}, u32[]{:S(2)}) %collective-permute-start.3) | collective-permute-done | bytes 81952 | tf_op jit(solution)/shard_map/ppermute | solution.py:86
  28.0 0.2 rev.3
  28.3 0.9 %convolution_bitcast_fusion = f32[8,256]{1,0:T(8,128)S(1)} fusion(f32[8,256,256]{2,1,0:T(8,128)S(1)} %copy-done, f32[8,8,256]{2,1,0:T(8,128)S(1)} %bitcast.33), kind=kOutput, calls=%fused_computation.15 | convolution fusion | flops 25165824 | bytes 2170880 | tf_op jit(solution)/shard_map/qce,cde->qd/dot_general | solution.py:164
  29.2 1.6 %collective-permute-start.4 = (f32[72,256]{1,0:T(8,128)S(1)}, f32[72,256]{1,0:T(8,128)S(1)}, u32[]{:S(2)}, u32[]{:S(2)}) collective-permute-start(f32[72,256]{1,0:T(8,128)S(1)} %pad_maximum_fusion.6), channel_id=1, source_target_pairs={{0,16},{16,0},{32,48},{48,32},{64,80},{80,64},{96,112},{112,96},{1... | collective-permute-start | bytes 221192 | tf_op jit(solution)/shard_map/ppermute | solution.py:86
  31.0 2.4 %fusion.8 = bf16[128,16,192]{2,1,0:T(8,128)(2,1)} fusion(s32[192]{0:T(256)S(1)} %add.151, s32[128,27]{1,0:T(8,128)S(1)} %get-tuple-element.5, s32[128,27]{1,0:T(8,128)S(1)} %get-tuple-element.4), kind=kOutput, calls=%fused_computation.9 | convolution fusion | flops 22345728 | bytes 814848 | tf_op jit(solution)/shard_map/blt,blj->btj/dot_general | solution.py:204
  33.4 0.3 collective-permute-done.4
  33.7 3.8 %collective-permute-start.5 = (f32[80,256]{1,0:T(8,128)S(1)}, f32[80,256]{1,0:T(8,128)S(1)}, u32[]{:S(2)}, u32[]{:S(2)}) collective-permute-start(f32[80,256]{1,0:T(8,128)S(1)} %pad_maximum_fusion.2), channel_id=1, source_target_pairs={{0,32},{16,48},{32,0},{48,16},{64,96},{80,112},{96,64},{112,80},{1... | collective-permute-start | bytes 245768 | tf_op jit(solution)/shard_map/ppermute | solution.py:86
  37.5 2.4 %collective-permute-done.5 = f32[80,256]{1,0:T(8,128)S(1)} collective-permute-done((f32[80,256]{1,0:T(8,128)S(1)}, f32[80,256]{1,0:T(8,128)S(1)}, u32[]{:S(2)}, u32[]{:S(2)}) %collective-permute-start.5) | collective-permute-done | bytes 81952 | tf_op jit(solution)/shard_map/ppermute | solution.py:86
  40.0 3.9 %collective-permute-start.6 = (f32[96,256]{1,0:T(8,128)S(1)}, f32[96,256]{1,0:T(8,128)S(1)}, u32[]{:S(2)}, u32[]{:S(2)}) collective-permute-start(f32[96,256]{1,0:T(8,128)S(1)} %pad_maximum_fusion.1), channel_id=1, source_target_pairs={{0,64},{16,80},{32,96},{48,112},{64,0},{80,16},{96,32},{112,48},{1... | collective-permute-start | bytes 294920 | tf_op jit(solution)/shard_map/ppermute | solution.py:86
  43.9 0.2 convolution_convert_fusion
  44.1 1.9 %copy.18 = bf16[128,16,192]{0,2,1:T(8,128)(2,1)S(1)} copy(bf16[128,16,192]{2,1,0:T(8,128)(2,1)} %fusion.8) | data formatting | bytes 1572864 | tf_op jit(solution)/shard_map/convert_element_type | solution.py:78
  46.0 0.4 collective-permute-done.6
  46.8 0.5 fusion.21
  47.3 0.5 convolution_add_fusion
  47.8 1.7 %copy-done.1 = f32[16,256,256]{2,1,0:T(8,128)S(1)} copy-done((f32[16,256,256]{2,1,0:T(8,128)S(1)}, f32[16,256,256]{2,1,0:T(8,128)}, u32[]{:S(2)}) %copy-start.1) | copy-done | bytes 4194328
  49.5 2.3 %fusion.11 = f32[144,256]{1,0:T(8,128)S(1)} fusion(f32[16,256,256]{2,1,0:T(8,128)S(1)} %copy-done.1, f32[16,16,256]{2,0,1:T(8,128)S(1)} %convolution_add_fusion.1, f32[128,16,256]{2,0,1:T(8,128)S(1)} %convolution_add_fusion), kind=kOutput, calls=%fused_computation.11 | convolution fusion | flops 906559488 | bytes 6701056 | tf_op jit(solution)/shard_map/btk,tlk->bl/dot_general | solution.py:211
  51.9 1.3 %collective-permute-done.7 = f32[144,256]{1,0:T(8,128)S(1)} collective-permute-done((f32[144,256]{1,0:T(8,128)S(1)}, f32[144,256]{1,0:T(8,128)S(1)}, u32[]{:S(2)}, u32[]{:S(2)}) %collective-permute-start.7) | collective-permute-done | bytes 147488 | tf_op jit(solution)/shard_map/ppermute | solution.py:86
  53.3 0.6 fusion.47
  54.0 0.6 constant_dynamic-slice_fusion
  54.6 0.2 fusion.25
  54.8 0.8 %convolution_add_fusion.3.local_ref = f32[96,256]{1,0:T(8,128)} fusion(f32[96,256]{1,0:T(8,128)S(1)} %fusion.25, f32[128,256]{1,0:T(8,128)S(1)} %slice_add_fusion, s32[96]{0:T(128)S(1)} %fusion.55), kind=kOutput, calls=%fused_computation.13 | convolution fusion | flops 6385664 | bytes 328064 | tf_op jit(solution)/shard_map/bj,jk->bk/dot_general | solution.py:79
  55.6 6.8 %shard_map.114 = bf16[96,128,128]{2,1,0:T(8,128)(2,1)} custom-call(bf16[96,128,256]{2,1,0:T(8,128)(2,1)} %bra_ref.3, bf16[96,128,256]{2,1,0:T(8,128)(2,1)} %ket_ref.3, f32[96,256]{1,0:T(8,128)} %convolution_add_fusion.3.local_ref), custom_call_target="tpu_custom_call" | custom-call | flops 805306368 | bytes 15826944 | tf_op jit(solution)/shard_map/pallas_call | solution.py:57
  (52 shorter events, 1.5 us)
Async XLA Ops:
  0.6 27.7 %copy-start = (f32[8,256,256]{2,1,0:T(8,128)S(1)}, f32[8,256,256]{2,1,0:T(8,128)}, u32[]{:S(2)}) copy-start(f32[8,256,256]{2,1,0:T(8,128)} %param.19) | copy-start | bytes 6291460
  1.7 7.2 %copy-start.2 = (s32[96]{0:T(128)S(1)}, s32[96]{0:T(128)}, u32[]{:S(2)}) copy-start(s32[96]{0:T(128)} %param.13) | copy-start | bytes 1156
  11.3 1.3 %collective-permute-start = (f32[66,256]{1,0:T(8,128)S(1)}, f32[66,256]{1,0:T(8,128)S(1)}, u32[]{:S(2)}, u32[]{:S(2)}) collective-permute-start(f32[66,256]{1,0:T(8,128)S(1)} %pad_maximum_fusion.3), channel_id=1, source_target_pairs={{0,1},{1,0},{2,3},{3,2},{4,5},{5,4},{6,7},{7,6},{8,9},{9,8},{10,11... | collective-permute-start | bytes 202760 | tf_op jit(solution)/shard_map/ppermute | solution.py:86
  12.7 4.7 %collective-permute-start.1 = (f32[68,256]{1,0:T(8,128)S(1)}, f32[68,256]{1,0:T(8,128)S(1)}, u32[]{:S(2)}, u32[]{:S(2)}) collective-permute-start(f32[68,256]{1,0:T(8,128)S(1)} %pad_maximum_fusion.4), channel_id=1, source_target_pairs={{0,2},{1,3},{2,0},{3,1},{4,6},{5,7},{6,4},{7,5},{8,10},{9,11},{10,... | collective-permute-start | bytes 208904 | tf_op jit(solution)/shard_map/ppermute | solution.py:86
  17.4 4.4 %collective-permute-start.2 = (f32[72,256]{1,0:T(8,128)S(1)}, f32[72,256]{1,0:T(8,128)S(1)}, u32[]{:S(2)}, u32[]{:S(2)}) collective-permute-start(f32[72,256]{1,0:T(8,128)S(1)} %pad_maximum_fusion.5), channel_id=1, source_target_pairs={{0,4},{1,5},{2,6},{3,7},{4,0},{5,1},{6,2},{7,3},{8,12},{9,13},{10,... | collective-permute-start | bytes 221192 | tf_op jit(solution)/shard_map/ppermute | solution.py:86
  21.9 6.0 %collective-permute-start.3 = (f32[80,256]{1,0:T(8,128)S(1)}, f32[80,256]{1,0:T(8,128)S(1)}, u32[]{:S(2)}, u32[]{:S(2)}) collective-permute-start(f32[80,256]{1,0:T(8,128)S(1)} %concatenate.55), channel_id=1, source_target_pairs={{0,8},{1,9},{2,10},{3,11},{4,12},{5,13},{6,14},{7,15},{8,0},{9,1},... | collective-permute-start | bytes 245768 | tf_op jit(solution)/shard_map/ppermute | solution.py:86
  29.2 4.4 %collective-permute-start.4 = (f32[72,256]{1,0:T(8,128)S(1)}, f32[72,256]{1,0:T(8,128)S(1)}, u32[]{:S(2)}, u32[]{:S(2)}) collective-permute-start(f32[72,256]{1,0:T(8,128)S(1)} %pad_maximum_fusion.6), channel_id=1, source_target_pairs={{0,16},{16,0},{32,48},{48,32},{64,80},{80,64},{96,112},{112,96},{1... | collective-permute-start | bytes 221192 | tf_op jit(solution)/shard_map/ppermute | solution.py:86
  33.7 6.2 %collective-permute-start.5 = (f32[80,256]{1,0:T(8,128)S(1)}, f32[80,256]{1,0:T(8,128)S(1)}, u32[]{:S(2)}, u32[]{:S(2)}) collective-permute-start(f32[80,256]{1,0:T(8,128)S(1)} %pad_maximum_fusion.2), channel_id=1, source_target_pairs={{0,32},{16,48},{32,0},{48,16},{64,96},{80,112},{96,64},{112,80},{1... | collective-permute-start | bytes 245768 | tf_op jit(solution)/shard_map/ppermute | solution.py:86
  40.0 6.5 %collective-permute-start.6 = (f32[96,256]{1,0:T(8,128)S(1)}, f32[96,256]{1,0:T(8,128)S(1)}, u32[]{:S(2)}, u32[]{:S(2)}) collective-permute-start(f32[96,256]{1,0:T(8,128)S(1)} %pad_maximum_fusion.1), channel_id=1, source_target_pairs={{0,64},{16,80},{32,96},{48,112},{64,0},{80,16},{96,32},{112,48},{1... | collective-permute-start | bytes 294920 | tf_op jit(solution)/shard_map/ppermute | solution.py:86
  47.3 2.2 %copy-start.1 = (f32[16,256,256]{2,1,0:T(8,128)S(1)}, f32[16,256,256]{2,1,0:T(8,128)}, u32[]{:S(2)}) copy-start(f32[16,256,256]{2,1,0:T(8,128)} %param.18) | copy-start | bytes 12582916
  51.8 1.5 %collective-permute-start.7 = (f32[144,256]{1,0:T(8,128)S(1)}, f32[144,256]{1,0:T(8,128)S(1)}, u32[]{:S(2)}, u32[]{:S(2)}) collective-permute-start(f32[144,256]{1,0:T(8,128)S(1)} %fusion.11), channel_id=1, source_target_pairs={{0,1},{1,0},{2,3},{3,2},{4,5},{5,4},{6,7},{7,6},{8,9},{9,8},{10,11... | collective-permute-start | bytes 442376 | tf_op jit(solution)/shard_map/ppermute | solution.py:86

commit v13 on v11

--- a/solution.py
+++ b/solution.py
@@ -42,34 +42,41 @@
     )(density, bra_table, ket_table)
 
 
-def coulomb_kernel(bra_ref, ket_ref, local_ref, out_ref):
-    for j in range(out_ref.shape[0]):
-        scaled = (bra_ref[j].astype(jnp.float32) * local_ref[pl.ds(j, 1), :]).astype(jnp.bfloat16)
+def coulomb_kernel(ids_ref, bra_ref, ket_ref, local_ref, out_ref):
+    tile = out_ref.shape[0]
+    first = pl.program_id(0) * tile
+    for j in range(tile):
+        local = local_ref[pl.ds(ids_ref[first + j], 1), :]
+        scaled = (bra_ref[j].astype(jnp.float32) * local).astype(jnp.bfloat16)
         out_ref[j] = lax.dot_general(
             scaled, ket_ref[j], (((1,), (1,)), ((), ())), preferred_element_type=jnp.float32
         ).astype(jnp.bfloat16)
 
 
-def block_coulomb(bra_table, ket_table, block_locals):
+def block_coulomb(bra_table, ket_table, domain_local, box_ids):
     blocks, rows, coeffs = bra_table.shape
     cols = ket_table.shape[1]
+    boxes = domain_local.shape[0]
     tile = tile_of(blocks)
     return pl.pallas_call(
         coulomb_kernel,
         out_shape=jax.ShapeDtypeStruct((blocks, rows, cols), jnp.bfloat16),
-        grid=(blocks // tile,),
-        in_specs=[
-            pl.BlockSpec((tile, rows, coeffs), lambda i: (i, 0, 0)),
-            pl.BlockSpec((tile, cols, coeffs), lambda i: (i, 0, 0)),
-            pl.BlockSpec((tile, coeffs), lambda i: (i, 0)),
-        ],
-        out_specs=pl.BlockSpec((tile, rows, cols), lambda i: (i, 0, 0)),
+        grid_spec=pltpu.PrefetchScalarGridSpec(
+            num_scalar_prefetch=1,
+            grid=(blocks // tile,),
+            in_specs=[
+                pl.BlockSpec((tile, rows, coeffs), lambda i, ids: (i, 0, 0)),
+                pl.BlockSpec((tile, cols, coeffs), lambda i, ids: (i, 0, 0)),
+                pl.BlockSpec((boxes, coeffs), lambda i, ids: (0, 0)),
+            ],
+            out_specs=pl.BlockSpec((tile, rows, cols), lambda i, ids: (i, 0, 0)),
+        ),
         cost_estimate=pl.CostEstimate(
             flops=2 * blocks * rows * cols * coeffs,
             transcendentals=0,
-            bytes_accessed=2 * blocks * (rows * cols + 2 * rows * coeffs) + 4 * blocks * coeffs,
+            bytes_accessed=2 * blocks * (rows * cols + 2 * rows * coeffs) + 4 * boxes * coeffs,
         ),
-    )(bra_table, ket_table, block_locals)
+    )(box_ids, bra_table, ket_table, domain_local)
 
 
 def exchange(x, axis, mask):
@@ -211,11 +218,7 @@
     domain_local = leaf_far + downward
     box_locals = lax.dynamic_slice_in_dim(domain_local, core * leaves, leaves, axis=0)
     relabelled = ((box_of_block // leaves) ^ base) * leaves + box_of_block % leaves
-    slot_hot = (relabelled[:, None] == jnp.arange(box_dom, dtype=jnp.int32)[None, :]).astype(
-        jnp.float32
-    )
-    block_locals = jnp.dot(slot_hot, domain_local, precision=top)
-    coulomb = block_coulomb(bra_table, ket_table, block_locals)
+    coulomb = block_coulomb(bra_table, ket_table, domain_local, relabelled)
     return (coulomb, box_locals)
 
 

time: 61.7 us -> 61.6 us (level)
  matrix products: 9.39 us -> 8.54 us
  Pallas kernels: 14 us -> 14.7 us
    dot_general x1 -> x0, matrix products: 0.84 us -> none  [shards(): block_locals = jnp.dot(slot_hot, domain_local, precision=top)]
    pallas_call x1, Pallas kernels: 6.81 us -> 7.51 us  [block_coulomb(): pl.pallas_call(coulomb_kernel, out_shape=jax.ShapeDtypeStruct((blocks, ro...]
  transfers between devices with their start and end apart: 8 -> 8, of which waited for: 8 -> 8; matrix products, arithmetic and copies ran while one was open for 4% -> 5% of each run, Pallas kernels for 0% -> 0%
where the time goes in v13:
time: 61.6 us; the launch traced here: 60.4 us
  starting transfers between devices  16.5 us (27%)
  waiting for transfers between devices  15.6 us (25%)
  Pallas kernels  14.7 us (24%)
  matrix products  8.54 us (14%)
  local copies, waits for them, and re-layouts  2.17 us (4%)
  other arithmetic  1.94 us (3%)
  between operations  0.95 us (2%)
    ppermute x8, starting transfers between devices, exchange(): return lax.ppermute(x, axis, [(i, i ^ mask) for i in range(count)])  16.5 us
    ppermute x8, waiting for transfers between devices, exchange(): return lax.ppermute(x, axis, [(i, i ^ mask) for i in range(count)])  15.6 us
    pallas_call x1, Pallas kernels, block_coulomb(): pl.pallas_call(coulomb_kernel, out_shape=jax.ShapeDtypeStruct((blocks, ro...  7.51 us
    pallas_call x1, Pallas kernels, block_moments(): pl.pallas_call(moments_kernel, out_shape=jax.ShapeDtypeStruct((blocks, co...  7.2 us
    dot_general x1, matrix products, shards(): far_part = jnp.einsum('btk,tlk->bl', rows, translation, precision=top)  2.29 us
    dot_general x1, matrix products, shards(): gathered = jnp.einsum('btj,jk->btk', counts, window, precision=top)  2.1 us
  transfers between devices with their start and end apart: 8, of which 8 were waited for; matrix products, arithmetic and copies ran while one was open for 5% of the time, Pallas kernels for 0%

profile of v13, /device:TPU:0, one launch (start us, length us, event | category | flops | bytes accessed | tf_op | source)
XLA Modules:
  0.0 60.4 jit_solution(9009907925458176252)
XLA Ops:
  0.7 0.9 %add_convert_fusion = f32[18,27]{1,0:T(8,128)S(1)} fusion(s32[1,27]{1,0:T(1,128)} %param.17, s32[1,27]{1,0:T(1,128)} %param.16, s32[8,27]{1,0:T(8,128)} %param.15, s32[8,27]{1,0:T(8,128)} %param.14), kind=kLoop, calls=%fused_computation.57 | loop fusion | flops 1944 | bytes 3888 | tf_op jit(solution)/shard_map/convert_element_type | solution.py:137
  1.6 0.1 convert_element_type.20
  1.7 7.2 %shard_map.113 = f32[96,256]{1,0:T(8,128)} custom-call(bf16[96,128,128]{2,1,0:T(8,128)(2,1)} %dens_ref.1, bf16[96,128,256]{2,1,0:T(8,128)(2,1)} %bra_ref.3, bf16[96,128,256]{2,1,0:T(8,128)(2,1)} %ket_ref.3), custom_call_target="tpu_custom_call" | custom-call | flops 805306368 | bytes 15826944 | tf_op jit(solution)/shard_map/pallas_call | solution.py:27
  8.9 1.2 %fusion.31 = f32[128,256]{1,0:T(8,128)S(1)} fusion(f32[96,256]{1,0:T(8,128)} %shard_map.113, s32[96]{0:T(128)S(1)} %copy-done.3), kind=kOutput, calls=%fused_computation.51 | convolution fusion | flops 18886656 | bytes 229760 | tf_op jit(solution)/shard_map/dot_general | solution.py:144
  10.2 1.2 %collective-permute-done = f32[66,256]{1,0:T(8,128)S(1)} collective-permute-done((f32[66,256]{1,0:T(8,128)S(1)}, f32[66,256]{1,0:T(8,128)S(1)}, u32[]{:S(2)}, u32[]{:S(2)}) %collective-permute-start) | collective-permute-done | bytes 67616 | tf_op jit(solution)/shard_map/ppermute | solution.py:84
  11.5 2.1 %collective-permute-start.1 = (f32[68,256]{1,0:T(8,128)S(1)}, f32[68,256]{1,0:T(8,128)S(1)}, u32[]{:S(2)}, u32[]{:S(2)}) collective-permute-start(f32[68,256]{1,0:T(8,128)S(1)} %pad_maximum_fusion.3), channel_id=1, source_target_pairs={{0,2},{1,3},{2,0},{3,1},{4,6},{5,7},{6,4},{7,5},{8,10},{9,11},{10,... | collective-permute-start | bytes 208904 | tf_op jit(solution)/shard_map/ppermute | solution.py:84
  13.7 2.5 %collective-permute-done.1 = f32[68,256]{1,0:T(8,128)S(1)} collective-permute-done((f32[68,256]{1,0:T(8,128)S(1)}, f32[68,256]{1,0:T(8,128)S(1)}, u32[]{:S(2)}, u32[]{:S(2)}) %collective-permute-start.1) | collective-permute-done | bytes 69664 | tf_op jit(solution)/shard_map/ppermute | solution.py:84
  16.2 1.7 %collective-permute-start.2 = (f32[72,256]{1,0:T(8,128)S(1)}, f32[72,256]{1,0:T(8,128)S(1)}, u32[]{:S(2)}, u32[]{:S(2)}) collective-permute-start(f32[72,256]{1,0:T(8,128)S(1)} %pad_maximum_fusion.4), channel_id=1, source_target_pairs={{0,4},{1,5},{2,6},{3,7},{4,0},{5,1},{6,2},{7,3},{8,12},{9,13},{10,... | collective-permute-start | bytes 221192 | tf_op jit(solution)/shard_map/ppermute | solution.py:84
  17.9 2.8 %collective-permute-done.2 = f32[72,256]{1,0:T(8,128)S(1)} collective-permute-done((f32[72,256]{1,0:T(8,128)S(1)}, f32[72,256]{1,0:T(8,128)S(1)}, u32[]{:S(2)}, u32[]{:S(2)}) %collective-permute-start.2) | collective-permute-done | bytes 73760 | tf_op jit(solution)/shard_map/ppermute | solution.py:84
  20.7 3.3 %collective-permute-start.3 = (f32[80,256]{1,0:T(8,128)S(1)}, f32[80,256]{1,0:T(8,128)S(1)}, u32[]{:S(2)}, u32[]{:S(2)}) collective-permute-start(f32[80,256]{1,0:T(8,128)S(1)} %concatenate.55), channel_id=1, source_target_pairs={{0,8},{1,9},{2,10},{3,11},{4,12},{5,13},{6,14},{7,15},{8,0},{9,1},... | collective-permute-start | bytes 245768 | tf_op jit(solution)/shard_map/ppermute | solution.py:84
  24.2 2.5 %collective-permute-done.3 = f32[80,256]{1,0:T(8,128)S(1)} collective-permute-done((f32[80,256]{1,0:T(8,128)S(1)}, f32[80,256]{1,0:T(8,128)S(1)}, u32[]{:S(2)}, u32[]{:S(2)}) %collective-permute-start.3) | collective-permute-done | bytes 81952 | tf_op jit(solution)/shard_map/ppermute | solution.py:84
  26.8 0.2 rev.3
  27.1 0.9 %convolution_bitcast_fusion = f32[8,256]{1,0:T(8,128)S(1)} fusion(f32[8,256,256]{2,1,0:T(8,128)S(1)} %copy-done, f32[8,8,256]{2,1,0:T(8,128)S(1)} %bitcast.27), kind=kOutput, calls=%fused_computation.11 | convolution fusion | flops 25165824 | bytes 2170880 | tf_op jit(solution)/shard_map/qce,cde->qd/dot_general | solution.py:164
  28.0 1.6 %collective-permute-start.4 = (f32[72,256]{1,0:T(8,128)S(1)}, f32[72,256]{1,0:T(8,128)S(1)}, u32[]{:S(2)}, u32[]{:S(2)}) collective-permute-start(f32[72,256]{1,0:T(8,128)S(1)} %pad_maximum_fusion.5), channel_id=1, source_target_pairs={{0,16},{16,0},{32,48},{48,32},{64,80},{80,64},{96,112},{112,96},{1... | collective-permute-start | bytes 221192 | tf_op jit(solution)/shard_map/ppermute | solution.py:84
  29.6 0.1 convert_element_type.22
  29.9 0.6 %copy.17 = pred[128,27,16]{1,2,0:T(8,128)(4,1)S(1)} copy(pred[128,27,16]{0,2,1:T(8,128)(4,1)S(1)} %iota_compare_fusion) | data formatting | bytes 110592 | tf_op jit(solution)/shard_map/eq | solution.py:203
  30.5 0.9 %fusion = f32[128,16,192]{2,1,0:T(8,128)S(1)} fusion(pred[128,27,16]{1,2,0:T(8,128)(4,1)S(1)} %copy.17, s32[192]{0:T(256)S(1)} %add.138, s32[128,27]{1,0:T(8,128)S(1)} %get-tuple-element.4), kind=kOutput, calls=%fused_computation | convolution fusion | flops 21897216 | bytes 1642752 | tf_op jit(solution)/shard_map/blt,blj->btj/dot_general | solution.py:204
  31.5 1.0 %collective-permute-done.4 = f32[72,256]{1,0:T(8,128)S(1)} collective-permute-done((f32[72,256]{1,0:T(8,128)S(1)}, f32[72,256]{1,0:T(8,128)S(1)}, u32[]{:S(2)}, u32[]{:S(2)}) %collective-permute-start.4) | collective-permute-done | bytes 73760 | tf_op jit(solution)/shard_map/ppermute | solution.py:84
  32.5 3.8 %collective-permute-start.5 = (f32[80,256]{1,0:T(8,128)S(1)}, f32[80,256]{1,0:T(8,128)S(1)}, u32[]{:S(2)}, u32[]{:S(2)}) collective-permute-start(f32[80,256]{1,0:T(8,128)S(1)} %pad_maximum_fusion.1), channel_id=1, source_target_pairs={{0,32},{16,48},{32,0},{48,16},{64,96},{80,112},{96,64},{112,80},{1... | collective-permute-start | bytes 245768 | tf_op jit(solution)/shard_map/ppermute | solution.py:84
  36.3 2.4 %collective-permute-done.5 = f32[80,256]{1,0:T(8,128)S(1)} collective-permute-done((f32[80,256]{1,0:T(8,128)S(1)}, f32[80,256]{1,0:T(8,128)S(1)}, u32[]{:S(2)}, u32[]{:S(2)}) %collective-permute-start.5) | collective-permute-done | bytes 81952 | tf_op jit(solution)/shard_map/ppermute | solution.py:84
  38.8 3.9 %collective-permute-start.6 = (f32[96,256]{1,0:T(8,128)S(1)}, f32[96,256]{1,0:T(8,128)S(1)}, u32[]{:S(2)}, u32[]{:S(2)}) collective-permute-start(f32[96,256]{1,0:T(8,128)S(1)} %pad_maximum_fusion), channel_id=1, source_target_pairs={{0,64},{16,80},{32,96},{48,112},{64,0},{80,16},{96,32},{112,48},{1... | collective-permute-start | bytes 294920 | tf_op jit(solution)/shard_map/ppermute | solution.py:84
  42.7 0.2 fusion.13
  42.9 2.3 %collective-permute-done.6 = f32[96,256]{1,0:T(8,128)S(1)} collective-permute-done((f32[96,256]{1,0:T(8,128)S(1)}, f32[96,256]{1,0:T(8,128)S(1)}, u32[]{:S(2)}, u32[]{:S(2)}) %collective-permute-start.6) | collective-permute-done | bytes 98336 | tf_op jit(solution)/shard_map/ppermute | solution.py:84
  45.3 0.2 fusion.19
  45.6 2.1 %fusion.6 = f32[128,16,256]{2,0,1:T(8,128)S(1)} fusion(f32[128,16,192]{2,1,0:T(8,128)S(1)} %fusion, f32[64,256]{1,0:T(8,128)S(1)} %get-tuple-element.3, f32[64,256]{1,0:T(8,128)S(1)} %slice_add_fusion.1, f32[64,256]{1,0:T(8,128)S(1)} %get-tuple-element.2), kind=kOutput, calls=%fused_computation.6 | convolution fusion | flops 604078080 | bytes 3866624 | tf_op jit(solution)/shard_map/btj,jk->btk/dot_general | solution.py:205
  47.7 2.3 %fusion.10 = f32[144,256]{1,0:T(8,128)S(1)} fusion(f32[16,256,256]{2,1,0:T(8,128)S(1)} %copy-done.1, f32[16,16,256]{2,0,1:T(8,128)S(1)} %fusion.19, f32[128,16,256]{2,0,1:T(8,128)S(1)} %fusion.6), kind=kOutput, calls=%fused_computation.10 | convolution fusion | flops 906559488 | bytes 6701056 | tf_op jit(solution)/shard_map/btk,tlk->bl/dot_general | solution.py:211
  50.1 0.6 fusion.42.ids_ref
  50.7 0.8 %collective-permute-done.7 = f32[144,256]{1,0:T(8,128)S(1)} collective-permute-done((f32[144,256]{1,0:T(8,128)S(1)}, f32[144,256]{1,0:T(8,128)S(1)}, u32[]{:S(2)}, u32[]{:S(2)}) %collective-permute-start.7) | collective-permute-done | bytes 147488 | tf_op jit(solution)/shard_map/ppermute | solution.py:84
  51.5 0.6 %fusion.34 = f32[16,8,256]{2,0,1:T(8,128)S(1)} fusion(f32[8,256,256]{2,1,0:T(8,128)S(1)} %copy-done, f32[144,256]{1,0:T(8,128)S(1)} %add.150), kind=kOutput, calls=%fused_computation.56 | convolution fusion | flops 50331648 | bytes 2244608 | tf_op jit(solution)/shard_map/qd,cds->qcs/dot_general | solution.py:215
  52.1 0.1 slice_add_fusion.local_ref
  52.2 0.6 %constant_dynamic-slice_fusion = f32[8,256]{1,0:T(8,128)} fusion(f32[128,256]{1,0:T(8,128)S(1)} %slice_add_fusion.local_ref, s32[]{:T(128)S(6)} %select_n.136), kind=kLoop, calls=%fused_computation.81 | loop fusion | bytes 16388 | tf_op jit(solution)/shard_map/dynamic_slice | solution.py:219
  52.9 7.5 %shard_map.114 = bf16[96,128,128]{2,1,0:T(8,128)(2,1)} custom-call(s32[96]{0:T(128)} %fusion.42.ids_ref, bf16[96,128,256]{2,1,0:T(8,128)(2,1)} %bra_ref.3, bf16[96,128,256]{2,1,0:T(8,128)(2,1)} %ket_ref.3, f32[128,256]{1,0:T(8,128)} %copy-done.2), custom_call_target="tpu_custom_call" | custom-call | flops 805306368 | bytes 15859712 | tf_op jit(solution)/shard_map/pallas_call | solution.py:61
  (51 shorter events, 1.1 us)
Async XLA Ops:
  0.6 26.5 %copy-start = (f32[8,256,256]{2,1,0:T(8,128)S(1)}, f32[8,256,256]{2,1,0:T(8,128)}, u32[]{:S(2)}) copy-start(f32[8,256,256]{2,1,0:T(8,128)} %param.19) | copy-start | bytes 6291460
  1.7 7.2 %copy-start.3 = (s32[96]{0:T(128)S(1)}, s32[96]{0:T(128)}, u32[]{:S(2)}) copy-start(s32[96]{0:T(128)} %param.13) | copy-start | bytes 1156
  10.1 1.3 %collective-permute-start = (f32[66,256]{1,0:T(8,128)S(1)}, f32[66,256]{1,0:T(8,128)S(1)}, u32[]{:S(2)}, u32[]{:S(2)}) collective-permute-start(f32[66,256]{1,0:T(8,128)S(1)} %pad_maximum_fusion.2), channel_id=1, source_target_pairs={{0,1},{1,0},{2,3},{3,2},{4,5},{5,4},{6,7},{7,6},{8,9},{9,8},{10,11... | collective-permute-start | bytes 202760 | tf_op jit(solution)/shard_map/ppermute | solution.py:84
  11.5 4.7 %collective-permute-start.1 = (f32[68,256]{1,0:T(8,128)S(1)}, f32[68,256]{1,0:T(8,128)S(1)}, u32[]{:S(2)}, u32[]{:S(2)}) collective-permute-start(f32[68,256]{1,0:T(8,128)S(1)} %pad_maximum_fusion.3), channel_id=1, source_target_pairs={{0,2},{1,3},{2,0},{3,1},{4,6},{5,7},{6,4},{7,5},{8,10},{9,11},{10,... | collective-permute-start | bytes 208904 | tf_op jit(solution)/shard_map/ppermute | solution.py:84
  16.2 4.4 %collective-permute-start.2 = (f32[72,256]{1,0:T(8,128)S(1)}, f32[72,256]{1,0:T(8,128)S(1)}, u32[]{:S(2)}, u32[]{:S(2)}) collective-permute-start(f32[72,256]{1,0:T(8,128)S(1)} %pad_maximum_fusion.4), channel_id=1, source_target_pairs={{0,4},{1,5},{2,6},{3,7},{4,0},{5,1},{6,2},{7,3},{8,12},{9,13},{10,... | collective-permute-start | bytes 221192 | tf_op jit(solution)/shard_map/ppermute | solution.py:84
  20.7 6.0 %collective-permute-start.3 = (f32[80,256]{1,0:T(8,128)S(1)}, f32[80,256]{1,0:T(8,128)S(1)}, u32[]{:S(2)}, u32[]{:S(2)}) collective-permute-start(f32[80,256]{1,0:T(8,128)S(1)} %concatenate.55), channel_id=1, source_target_pairs={{0,8},{1,9},{2,10},{3,11},{4,12},{5,13},{6,14},{7,15},{8,0},{9,1},... | collective-permute-start | bytes 245768 | tf_op jit(solution)/shard_map/ppermute | solution.py:84
  28.0 4.4 %collective-permute-start.4 = (f32[72,256]{1,0:T(8,128)S(1)}, f32[72,256]{1,0:T(8,128)S(1)}, u32[]{:S(2)}, u32[]{:S(2)}) collective-permute-start(f32[72,256]{1,0:T(8,128)S(1)} %pad_maximum_fusion.5), channel_id=1, source_target_pairs={{0,16},{16,0},{32,48},{48,32},{64,80},{80,64},{96,112},{112,96},{1... | collective-permute-start | bytes 221192 | tf_op jit(solution)/shard_map/ppermute | solution.py:84
  32.5 6.2 %collective-permute-start.5 = (f32[80,256]{1,0:T(8,128)S(1)}, f32[80,256]{1,0:T(8,128)S(1)}, u32[]{:S(2)}, u32[]{:S(2)}) collective-permute-start(f32[80,256]{1,0:T(8,128)S(1)} %pad_maximum_fusion.1), channel_id=1, source_target_pairs={{0,32},{16,48},{32,0},{48,16},{64,96},{80,112},{96,64},{112,80},{1... | collective-permute-start | bytes 245768 | tf_op jit(solution)/shard_map/ppermute | solution.py:84
  38.8 6.5 %collective-permute-start.6 = (f32[96,256]{1,0:T(8,128)S(1)}, f32[96,256]{1,0:T(8,128)S(1)}, u32[]{:S(2)}, u32[]{:S(2)}) collective-permute-start(f32[96,256]{1,0:T(8,128)S(1)} %pad_maximum_fusion), channel_id=1, source_target_pairs={{0,64},{16,80},{32,96},{48,112},{64,0},{80,16},{96,32},{112,48},{1... | collective-permute-start | bytes 294920 | tf_op jit(solution)/shard_map/ppermute | solution.py:84
  45.5 2.2 %copy-start.1 = (f32[16,256,256]{2,1,0:T(8,128)S(1)}, f32[16,256,256]{2,1,0:T(8,128)}, u32[]{:S(2)}) copy-start(f32[16,256,256]{2,1,0:T(8,128)} %param.18) | copy-start | bytes 12582916
  50.0 1.5 %collective-permute-start.7 = (f32[144,256]{1,0:T(8,128)S(1)}, f32[144,256]{1,0:T(8,128)S(1)}, u32[]{:S(2)}, u32[]{:S(2)}) collective-permute-start(f32[144,256]{1,0:T(8,128)S(1)} %fusion.10), channel_id=1, source_target_pairs={{0,1},{1,0},{2,3},{3,2},{4,5},{5,4},{6,7},{7,6},{8,9},{9,8},{10,11... | collective-permute-start | bytes 442376 | tf_op jit(solution)/shard_map/ppermute | solution.py:84
  52.2 0.7 %copy-start.2 = (f32[128,256]{1,0:T(8,128)}, f32[128,256]{1,0:T(8,128)S(1)}, u32[]{:S(2)}) copy-start(f32[128,256]{1,0:T(8,128)S(1)} %slice_add_fusion.local_ref) | copy-start | bytes 393220

commit v14 on v13

--- a/solution.py
+++ b/solution.py
@@ -1,3 +1,5 @@
+import functools
+
 import jax
 import jax.numpy as jnp
 from jax import lax
@@ -42,41 +44,44 @@
     )(density, bra_table, ket_table)
 
 
-def coulomb_kernel(ids_ref, bra_ref, ket_ref, local_ref, out_ref):
+def coulomb_kernel(leaves, ids_ref, base_ref, bra_ref, ket_ref, local_ref, out_ref):
     tile = out_ref.shape[0]
     first = pl.program_id(0) * tile
+    base = base_ref[0]
     for j in range(tile):
-        local = local_ref[pl.ds(ids_ref[first + j], 1), :]
+        box = ids_ref[first + j]
+        row = ((box // leaves) ^ base) * leaves + box % leaves
+        local = local_ref[pl.ds(row, 1), :]
         scaled = (bra_ref[j].astype(jnp.float32) * local).astype(jnp.bfloat16)
         out_ref[j] = lax.dot_general(
             scaled, ket_ref[j], (((1,), (1,)), ((), ())), preferred_element_type=jnp.float32
         ).astype(jnp.bfloat16)
 
 
-def block_coulomb(bra_table, ket_table, domain_local, box_ids):
+def block_coulomb(bra_table, ket_table, domain_local, box_ids, base, leaves):
     blocks, rows, coeffs = bra_table.shape
     cols = ket_table.shape[1]
     boxes = domain_local.shape[0]
     tile = tile_of(blocks)
     return pl.pallas_call(
-        coulomb_kernel,
+        functools.partial(coulomb_kernel, leaves),
         out_shape=jax.ShapeDtypeStruct((blocks, rows, cols), jnp.bfloat16),
         grid_spec=pltpu.PrefetchScalarGridSpec(
-            num_scalar_prefetch=1,
+            num_scalar_prefetch=2,
             grid=(blocks // tile,),
             in_specs=[
-                pl.BlockSpec((tile, rows, coeffs), lambda i, ids: (i, 0, 0)),
-                pl.BlockSpec((tile, cols, coeffs), lambda i, ids: (i, 0, 0)),
-                pl.BlockSpec((boxes, coeffs), lambda i, ids: (0, 0)),
+                pl.BlockSpec((tile, rows, coeffs), lambda i, ids, base: (i, 0, 0)),
+                pl.BlockSpec((tile, cols, coeffs), lambda i, ids, base: (i, 0, 0)),
+                pl.BlockSpec((boxes, coeffs), lambda i, ids, base: (0, 0)),
             ],
-            out_specs=pl.BlockSpec((tile, rows, cols), lambda i, ids: (i, 0, 0)),
+            out_specs=pl.BlockSpec((tile, rows, cols), lambda i, ids, base: (i, 0, 0)),
         ),
         cost_estimate=pl.CostEstimate(
             flops=2 * blocks * rows * cols * coeffs,
             transcendentals=0,
             bytes_accessed=2 * blocks * (rows * cols + 2 * rows * coeffs) + 4 * boxes * coeffs,
         ),
-    )(box_ids, bra_table, ket_table, domain_local)
+    )(box_ids, base, bra_table, ket_table, domain_local)
 
 
 def exchange(x, axis, mask):
@@ -217,8 +222,9 @@
     ).reshape(box_dom, coeffs)
     domain_local = leaf_far + downward
     box_locals = lax.dynamic_slice_in_dim(domain_local, core * leaves, leaves, axis=0)
-    relabelled = ((box_of_block // leaves) ^ base) * leaves + box_of_block % leaves
-    coulomb = block_coulomb(bra_table, ket_table, domain_local, relabelled)
+    coulomb = block_coulomb(
+        bra_table, ket_table, domain_local, box_of_block, base.reshape(1).astype(jnp.int32), leaves
+    )
     return (coulomb, box_locals)
 
 

time: 61.6 us -> 61.6 us (level)
  transfers between devices with their start and end apart: 8 -> 8, of which waited for: 8 -> 8; matrix products, arithmetic and copies ran while one was open for 5% -> 4% of each run, Pallas kernels for 0% -> 0%
where the time goes in v14:
time: 61.6 us; the launch traced here: 60.4 us
  starting transfers between devices  16.5 us (27%)
  waiting for transfers between devices  16.1 us (26%)
  Pallas kernels  14.7 us (24%)
  matrix products  8.55 us (14%)
  local copies, waits for them, and re-layouts  2.17 us (4%)
  other arithmetic  1.38 us (2%)
  between operations  0.96 us (2%)
    ppermute x8, starting transfers between devices, exchange(): return lax.ppermute(x, axis, [(i, i ^ mask) for i in range(count)])  16.5 us
    ppermute x8, waiting for transfers between devices, exchange(): return lax.ppermute(x, axis, [(i, i ^ mask) for i in range(count)])  16.1 us
    pallas_call x1, Pallas kernels, block_coulomb(): pl.pallas_call(functools.partial(coulomb_kernel, leaves), out_shape=jax.S...  7.51 us
    pallas_call x1, Pallas kernels, block_moments(): pl.pallas_call(moments_kernel, out_shape=jax.ShapeDtypeStruct((blocks, co...  7.2 us
    dot_general x1, matrix products, shards(): far_part = jnp.einsum('btk,tlk->bl', rows, translation, precision=top)  2.29 us
    dot_general x1, matrix products, shards(): gathered = jnp.einsum('btj,jk->btk', counts, window, precision=top)  2.1 us
  transfers between devices with their start and end apart: 8, of which 8 were waited for; matrix products, arithmetic and copies ran while one was open for 4% of the time, Pallas kernels for 0%

profile of v14, /device:TPU:0, one launch (start us, length us, event | category | flops | bytes accessed | tf_op | source)
XLA Modules:
  0.0 60.4 jit_solution(1008376249786122300)
XLA Ops:
  0.7 0.9 %add_convert_fusion = f32[18,27]{1,0:T(8,128)S(1)} fusion(s32[1,27]{1,0:T(1,128)} %param.17, s32[1,27]{1,0:T(1,128)} %param.16, s32[8,27]{1,0:T(8,128)} %param.15, s32[8,27]{1,0:T(8,128)} %param.14), kind=kLoop, calls=%fused_computation.57 | loop fusion | flops 1944 | bytes 3888 | tf_op jit(solution)/shard_map/convert_element_type | solution.py:142
  1.6 0.1 convert_element_type.20
  1.7 7.2 %shard_map.113 = f32[96,256]{1,0:T(8,128)} custom-call(bf16[96,128,128]{2,1,0:T(8,128)(2,1)} %dens_ref.1, bf16[96,128,256]{2,1,0:T(8,128)(2,1)} %bra_ref.3, bf16[96,128,256]{2,1,0:T(8,128)(2,1)} %ket_ref.3), custom_call_target="tpu_custom_call" | custom-call | flops 805306368 | bytes 15826944 | tf_op jit(solution)/shard_map/pallas_call | solution.py:29
  8.9 1.2 %fusion.31 = f32[128,256]{1,0:T(8,128)S(1)} fusion(f32[96,256]{1,0:T(8,128)} %shard_map.113, s32[96]{0:T(128)S(1)} %copy-done.3), kind=kOutput, calls=%fused_computation.51 | convolution fusion | flops 18886656 | bytes 229760 | tf_op jit(solution)/shard_map/dot_general | solution.py:149
  10.1 0.1 collective-permute-start
  10.2 1.2 %collective-permute-done = f32[66,256]{1,0:T(8,128)S(1)} collective-permute-done((f32[66,256]{1,0:T(8,128)S(1)}, f32[66,256]{1,0:T(8,128)S(1)}, u32[]{:S(2)}, u32[]{:S(2)}) %collective-permute-start) | collective-permute-done | bytes 67616 | tf_op jit(solution)/shard_map/ppermute | solution.py:89
  11.5 2.1 %collective-permute-start.1 = (f32[68,256]{1,0:T(8,128)S(1)}, f32[68,256]{1,0:T(8,128)S(1)}, u32[]{:S(2)}, u32[]{:S(2)}) collective-permute-start(f32[68,256]{1,0:T(8,128)S(1)} %pad_maximum_fusion.3), channel_id=1, source_target_pairs={{0,2},{1,3},{2,0},{3,1},{4,6},{5,7},{6,4},{7,5},{8,10},{9,11},{10,... | collective-permute-start | bytes 208904 | tf_op jit(solution)/shard_map/ppermute | solution.py:89
  13.7 2.5 %collective-permute-done.1 = f32[68,256]{1,0:T(8,128)S(1)} collective-permute-done((f32[68,256]{1,0:T(8,128)S(1)}, f32[68,256]{1,0:T(8,128)S(1)}, u32[]{:S(2)}, u32[]{:S(2)}) %collective-permute-start.1) | collective-permute-done | bytes 69664 | tf_op jit(solution)/shard_map/ppermute | solution.py:89
  16.2 1.7 %collective-permute-start.2 = (f32[72,256]{1,0:T(8,128)S(1)}, f32[72,256]{1,0:T(8,128)S(1)}, u32[]{:S(2)}, u32[]{:S(2)}) collective-permute-start(f32[72,256]{1,0:T(8,128)S(1)} %pad_maximum_fusion.4), channel_id=1, source_target_pairs={{0,4},{1,5},{2,6},{3,7},{4,0},{5,1},{6,2},{7,3},{8,12},{9,13},{10,... | collective-permute-start | bytes 221192 | tf_op jit(solution)/shard_map/ppermute | solution.py:89
  17.9 2.8 %collective-permute-done.2 = f32[72,256]{1,0:T(8,128)S(1)} collective-permute-done((f32[72,256]{1,0:T(8,128)S(1)}, f32[72,256]{1,0:T(8,128)S(1)}, u32[]{:S(2)}, u32[]{:S(2)}) %collective-permute-start.2) | collective-permute-done | bytes 73760 | tf_op jit(solution)/shard_map/ppermute | solution.py:89
  20.7 3.3 %collective-permute-start.3 = (f32[80,256]{1,0:T(8,128)S(1)}, f32[80,256]{1,0:T(8,128)S(1)}, u32[]{:S(2)}, u32[]{:S(2)}) collective-permute-start(f32[80,256]{1,0:T(8,128)S(1)} %concatenate.55), channel_id=1, source_target_pairs={{0,8},{1,9},{2,10},{3,11},{4,12},{5,13},{6,14},{7,15},{8,0},{9,1},... | collective-permute-start | bytes 245768 | tf_op jit(solution)/shard_map/ppermute | solution.py:89
  24.2 2.5 %collective-permute-done.3 = f32[80,256]{1,0:T(8,128)S(1)} collective-permute-done((f32[80,256]{1,0:T(8,128)S(1)}, f32[80,256]{1,0:T(8,128)S(1)}, u32[]{:S(2)}, u32[]{:S(2)}) %collective-permute-start.3) | collective-permute-done | bytes 81952 | tf_op jit(solution)/shard_map/ppermute | solution.py:89
  26.8 0.2 rev.3
  27.1 0.9 %convolution_bitcast_fusion = f32[8,256]{1,0:T(8,128)S(1)} fusion(f32[8,256,256]{2,1,0:T(8,128)S(1)} %copy-done, f32[8,8,256]{2,1,0:T(8,128)S(1)} %bitcast.28), kind=kOutput, calls=%fused_computation.11 | convolution fusion | flops 25165824 | bytes 2170880 | tf_op jit(solution)/shard_map/qce,cde->qd/dot_general | solution.py:169
  28.0 1.6 %collective-permute-start.4 = (f32[72,256]{1,0:T(8,128)S(1)}, f32[72,256]{1,0:T(8,128)S(1)}, u32[]{:S(2)}, u32[]{:S(2)}) collective-permute-start(f32[72,256]{1,0:T(8,128)S(1)} %pad_maximum_fusion.5), channel_id=1, source_target_pairs={{0,16},{16,0},{32,48},{48,32},{64,80},{80,64},{96,112},{112,96},{1... | collective-permute-start | bytes 221192 | tf_op jit(solution)/shard_map/ppermute | solution.py:89
  29.6 0.1 convert_element_type.22
  29.9 0.6 %copy.17 = pred[128,27,16]{1,2,0:T(8,128)(4,1)S(1)} copy(pred[128,27,16]{0,2,1:T(8,128)(4,1)S(1)} %iota_compare_fusion) | data formatting | bytes 110592 | tf_op jit(solution)/shard_map/eq | solution.py:208
  30.5 0.9 %fusion = f32[128,16,192]{2,1,0:T(8,128)S(1)} fusion(pred[128,27,16]{1,2,0:T(8,128)(4,1)S(1)} %copy.17, s32[192]{0:T(256)S(1)} %add.126, s32[128,27]{1,0:T(8,128)S(1)} %get-tuple-element.4), kind=kOutput, calls=%fused_computation | convolution fusion | flops 21897216 | bytes 1642752 | tf_op jit(solution)/shard_map/blt,blj->btj/dot_general | solution.py:209
  31.5 1.0 %collective-permute-done.4 = f32[72,256]{1,0:T(8,128)S(1)} collective-permute-done((f32[72,256]{1,0:T(8,128)S(1)}, f32[72,256]{1,0:T(8,128)S(1)}, u32[]{:S(2)}, u32[]{:S(2)}) %collective-permute-start.4) | collective-permute-done | bytes 73760 | tf_op jit(solution)/shard_map/ppermute | solution.py:89
  32.5 3.8 %collective-permute-start.5 = (f32[80,256]{1,0:T(8,128)S(1)}, f32[80,256]{1,0:T(8,128)S(1)}, u32[]{:S(2)}, u32[]{:S(2)}) collective-permute-start(f32[80,256]{1,0:T(8,128)S(1)} %pad_maximum_fusion.1), channel_id=1, source_target_pairs={{0,32},{16,48},{32,0},{48,16},{64,96},{80,112},{96,64},{112,80},{1... | collective-permute-start | bytes 245768 | tf_op jit(solution)/shard_map/ppermute | solution.py:89
  36.3 2.4 %collective-permute-done.5 = f32[80,256]{1,0:T(8,128)S(1)} collective-permute-done((f32[80,256]{1,0:T(8,128)S(1)}, f32[80,256]{1,0:T(8,128)S(1)}, u32[]{:S(2)}, u32[]{:S(2)}) %collective-permute-start.5) | collective-permute-done | bytes 81952 | tf_op jit(solution)/shard_map/ppermute | solution.py:89
  38.8 3.9 %collective-permute-start.6 = (f32[96,256]{1,0:T(8,128)S(1)}, f32[96,256]{1,0:T(8,128)S(1)}, u32[]{:S(2)}, u32[]{:S(2)}) collective-permute-start(f32[96,256]{1,0:T(8,128)S(1)} %pad_maximum_fusion), channel_id=1, source_target_pairs={{0,64},{16,80},{32,96},{48,112},{64,0},{80,16},{96,32},{112,48},{1... | collective-permute-start | bytes 294920 | tf_op jit(solution)/shard_map/ppermute | solution.py:89
  42.7 0.2 fusion.13
  42.9 2.3 %collective-permute-done.6 = f32[96,256]{1,0:T(8,128)S(1)} collective-permute-done((f32[96,256]{1,0:T(8,128)S(1)}, f32[96,256]{1,0:T(8,128)S(1)}, u32[]{:S(2)}, u32[]{:S(2)}) %collective-permute-start.6) | collective-permute-done | bytes 98336 | tf_op jit(solution)/shard_map/ppermute | solution.py:89
  45.3 0.2 fusion.19
  45.6 2.1 %fusion.6 = f32[128,16,256]{2,0,1:T(8,128)S(1)} fusion(f32[128,16,192]{2,1,0:T(8,128)S(1)} %fusion, f32[64,256]{1,0:T(8,128)S(1)} %get-tuple-element.3, f32[64,256]{1,0:T(8,128)S(1)} %slice_add_fusion.1, f32[64,256]{1,0:T(8,128)S(1)} %get-tuple-element.2), kind=kOutput, calls=%fused_computation.6 | convolution fusion | flops 604078080 | bytes 3866624 | tf_op jit(solution)/shard_map/btj,jk->btk/dot_general | solution.py:210
  47.7 2.3 %fusion.10 = f32[144,256]{1,0:T(8,128)S(1)} fusion(f32[16,256,256]{2,1,0:T(8,128)S(1)} %copy-done.1, f32[16,16,256]{2,0,1:T(8,128)S(1)} %fusion.19, f32[128,16,256]{2,0,1:T(8,128)S(1)} %fusion.6), kind=kOutput, calls=%fused_computation.10 | convolution fusion | flops 906559488 | bytes 6701056 | tf_op jit(solution)/shard_map/btk,tlk->bl/dot_general | solution.py:216
  50.1 1.3 %collective-permute-done.7 = f32[144,256]{1,0:T(8,128)S(1)} collective-permute-done((f32[144,256]{1,0:T(8,128)S(1)}, f32[144,256]{1,0:T(8,128)S(1)}, u32[]{:S(2)}, u32[]{:S(2)}) %collective-permute-start.7) | collective-permute-done | bytes 147488 | tf_op jit(solution)/shard_map/ppermute | solution.py:89
  51.5 0.6 %fusion.34 = f32[16,8,256]{2,0,1:T(8,128)S(1)} fusion(f32[8,256,256]{2,1,0:T(8,128)S(1)} %copy-done, f32[144,256]{1,0:T(8,128)S(1)} %add.138), kind=kOutput, calls=%fused_computation.56 | convolution fusion | flops 50331648 | bytes 2244608 | tf_op jit(solution)/shard_map/qd,cds->qcs/dot_general | solution.py:220
  52.1 0.1 slice_add_fusion.local_ref
  52.2 0.6 %constant_dynamic-slice_fusion = f32[8,256]{1,0:T(8,128)} fusion(f32[128,256]{1,0:T(8,128)S(1)} %slice_add_fusion.local_ref, s32[]{:T(128)S(6)} %select_n.123), kind=kLoop, calls=%fused_computation.75 | loop fusion | bytes 16388 | tf_op jit(solution)/shard_map/dynamic_slice | solution.py:224
  52.9 7.5 %shard_map.114 = bf16[96,128,128]{2,1,0:T(8,128)(2,1)} custom-call(s32[96]{0:T(128)} %ids_ref.1, s32[1]{0:T(128)} %bitcast.base_ref, bf16[96,128,256]{2,1,0:T(8,128)(2,1)} %bra_ref.3, bf16[96,128,256]{2,1,0:T(8,128)(2,1)} %ket_ref.3, f32[128,256]{1,0:T(8,128)} %copy-done.2), custom_call_target="tpu_custom_call" | custom-call | flops 805306368 | bytes 15859712 | tf_op jit(solution)/shard_map/pallas_call | solution.py:66
  (50 shorter events, 1.0 us)
Async XLA Ops:
  0.6 26.5 %copy-start = (f32[8,256,256]{2,1,0:T(8,128)S(1)}, f32[8,256,256]{2,1,0:T(8,128)}, u32[]{:S(2)}) copy-start(f32[8,256,256]{2,1,0:T(8,128)} %param.19) | copy-start | bytes 6291460
  1.7 7.2 %copy-start.3 = (s32[96]{0:T(128)S(1)}, s32[96]{0:T(128)}, u32[]{:S(2)}) copy-start(s32[96]{0:T(128)} %ids_ref.1) | copy-start | bytes 1156
  10.1 1.3 %collective-permute-start = (f32[66,256]{1,0:T(8,128)S(1)}, f32[66,256]{1,0:T(8,128)S(1)}, u32[]{:S(2)}, u32[]{:S(2)}) collective-permute-start(f32[66,256]{1,0:T(8,128)S(1)} %pad_maximum_fusion.2), channel_id=1, source_target_pairs={{0,1},{1,0},{2,3},{3,2},{4,5},{5,4},{6,7},{7,6},{8,9},{9,8},{10,11... | collective-permute-start | bytes 202760 | tf_op jit(solution)/shard_map/ppermute | solution.py:89
  11.5 4.7 %collective-permute-start.1 = (f32[68,256]{1,0:T(8,128)S(1)}, f32[68,256]{1,0:T(8,128)S(1)}, u32[]{:S(2)}, u32[]{:S(2)}) collective-permute-start(f32[68,256]{1,0:T(8,128)S(1)} %pad_maximum_fusion.3), channel_id=1, source_target_pairs={{0,2},{1,3},{2,0},{3,1},{4,6},{5,7},{6,4},{7,5},{8,10},{9,11},{10,... | collective-permute-start | bytes 208904 | tf_op jit(solution)/shard_map/ppermute | solution.py:89
  16.2 4.4 %collective-permute-start.2 = (f32[72,256]{1,0:T(8,128)S(1)}, f32[72,256]{1,0:T(8,128)S(1)}, u32[]{:S(2)}, u32[]{:S(2)}) collective-permute-start(f32[72,256]{1,0:T(8,128)S(1)} %pad_maximum_fusion.4), channel_id=1, source_target_pairs={{0,4},{1,5},{2,6},{3,7},{4,0},{5,1},{6,2},{7,3},{8,12},{9,13},{10,... | collective-permute-start | bytes 221192 | tf_op jit(solution)/shard_map/ppermute | solution.py:89
  20.7 6.0 %collective-permute-start.3 = (f32[80,256]{1,0:T(8,128)S(1)}, f32[80,256]{1,0:T(8,128)S(1)}, u32[]{:S(2)}, u32[]{:S(2)}) collective-permute-start(f32[80,256]{1,0:T(8,128)S(1)} %concatenate.55), channel_id=1, source_target_pairs={{0,8},{1,9},{2,10},{3,11},{4,12},{5,13},{6,14},{7,15},{8,0},{9,1},... | collective-permute-start | bytes 245768 | tf_op jit(solution)/shard_map/ppermute | solution.py:89
  28.0 4.4 %collective-permute-start.4 = (f32[72,256]{1,0:T(8,128)S(1)}, f32[72,256]{1,0:T(8,128)S(1)}, u32[]{:S(2)}, u32[]{:S(2)}) collective-permute-start(f32[72,256]{1,0:T(8,128)S(1)} %pad_maximum_fusion.5), channel_id=1, source_target_pairs={{0,16},{16,0},{32,48},{48,32},{64,80},{80,64},{96,112},{112,96},{1... | collective-permute-start | bytes 221192 | tf_op jit(solution)/shard_map/ppermute | solution.py:89
  32.5 6.2 %collective-permute-start.5 = (f32[80,256]{1,0:T(8,128)S(1)}, f32[80,256]{1,0:T(8,128)S(1)}, u32[]{:S(2)}, u32[]{:S(2)}) collective-permute-start(f32[80,256]{1,0:T(8,128)S(1)} %pad_maximum_fusion.1), channel_id=1, source_target_pairs={{0,32},{16,48},{32,0},{48,16},{64,96},{80,112},{96,64},{112,80},{1... | collective-permute-start | bytes 245768 | tf_op jit(solution)/shard_map/ppermute | solution.py:89
  38.8 6.5 %collective-permute-start.6 = (f32[96,256]{1,0:T(8,128)S(1)}, f32[96,256]{1,0:T(8,128)S(1)}, u32[]{:S(2)}, u32[]{:S(2)}) collective-permute-start(f32[96,256]{1,0:T(8,128)S(1)} %pad_maximum_fusion), channel_id=1, source_target_pairs={{0,64},{16,80},{32,96},{48,112},{64,0},{80,16},{96,32},{112,48},{1... | collective-permute-start | bytes 294920 | tf_op jit(solution)/shard_map/ppermute | solution.py:89
  45.5 2.2 %copy-start.1 = (f32[16,256,256]{2,1,0:T(8,128)S(1)}, f32[16,256,256]{2,1,0:T(8,128)}, u32[]{:S(2)}) copy-start(f32[16,256,256]{2,1,0:T(8,128)} %param.18) | copy-start | bytes 12582916
  50.0 1.5 %collective-permute-start.7 = (f32[144,256]{1,0:T(8,128)S(1)}, f32[144,256]{1,0:T(8,128)S(1)}, u32[]{:S(2)}, u32[]{:S(2)}) collective-permute-start(f32[144,256]{1,0:T(8,128)S(1)} %fusion.10), channel_id=1, source_target_pairs={{0,1},{1,0},{2,3},{3,2},{4,5},{5,4},{6,7},{7,6},{8,9},{9,8},{10,11... | collective-permute-start | bytes 442376 | tf_op jit(solution)/shard_map/ppermute | solution.py:89
  52.2 0.7 %copy-start.2 = (f32[128,256]{1,0:T(8,128)}, f32[128,256]{1,0:T(8,128)S(1)}, u32[]{:S(2)}) copy-start(f32[128,256]{1,0:T(8,128)S(1)} %slice_add_fusion.local_ref) | copy-start | bytes 393220

commit v15 on v13

--- a/solution.py
+++ b/solution.py
@@ -216,7 +216,7 @@
         "qd,cds->qcs", parent_locals, upward_translation_table, precision=top
     ).reshape(box_dom, coeffs)
     domain_local = leaf_far + downward
-    box_locals = lax.dynamic_slice_in_dim(domain_local, core * leaves, leaves, axis=0)
+    box_locals = jnp.where(core0, domain_local[:leaves], domain_local[leaves : 2 * leaves])
     relabelled = ((box_of_block // leaves) ^ base) * leaves + box_of_block % leaves
     coulomb = block_coulomb(bra_table, ket_table, domain_local, relabelled)
     return (coulomb, box_locals)

time: 61.6 us -> 61.6 us (level)
  other arithmetic: 1.94 us -> 2.57 us
  local copies, waits for them, and re-layouts: 2.17 us -> 1.54 us
    select_n x0 -> x1, other arithmetic: none -> 0.63 us  [shards(): jnp.where(core0, domain_local[:leaves], domain_local[leaves:2 * leaves])]
    dynamic_slice x1 -> x0, local copies, waits for them, and re-layouts: 0.63 us -> none  [shards(): lax.dynamic_slice_in_dim(domain_local, core * leaves, leaves, axis=0)]
where the time goes in v15:
time: 61.6 us; the launch traced here: 60.4 us
  starting transfers between devices  16.5 us (27%)
  waiting for transfers between devices  15.6 us (25%)
  Pallas kernels  14.7 us (24%)
  matrix products  8.54 us (14%)
  other arithmetic  2.57 us (4%)
  local copies, waits for them, and re-layouts  1.54 us (2%)
  between operations  0.95 us (2%)
    ppermute x8, starting transfers between devices, exchange(): return lax.ppermute(x, axis, [(i, i ^ mask) for i in range(count)])  16.5 us
    ppermute x8, waiting for transfers between devices, exchange(): return lax.ppermute(x, axis, [(i, i ^ mask) for i in range(count)])  15.6 us
    pallas_call x1, Pallas kernels, block_coulomb(): pl.pallas_call(coulomb_kernel, out_shape=jax.ShapeDtypeStruct((blocks, ro...  7.51 us
    pallas_call x1, Pallas kernels, block_moments(): pl.pallas_call(moments_kernel, out_shape=jax.ShapeDtypeStruct((blocks, co...  7.2 us
    dot_general x1, matrix products, shards(): far_part = jnp.einsum('btk,tlk->bl', rows, translation, precision=top)  2.29 us
    dot_general x1, matrix products, shards(): gathered = jnp.einsum('btj,jk->btk', counts, window, precision=top)  2.1 us
  transfers between devices with their start and end apart: 8, of which 8 were waited for; matrix products, arithmetic and copies ran while one was open for 5% of the time, Pallas kernels for 0%

profile of v15, /device:TPU:0, one launch (start us, length us, event | category | flops | bytes accessed | tf_op | source)
XLA Modules:
  0.0 60.4 jit_solution(1311086794318238775)
XLA Ops:
  0.7 0.9 %add_convert_fusion = f32[18,27]{1,0:T(8,128)S(1)} fusion(s32[1,27]{1,0:T(1,128)} %param.17, s32[1,27]{1,0:T(1,128)} %param.16, s32[8,27]{1,0:T(8,128)} %param.15, s32[8,27]{1,0:T(8,128)} %param.14), kind=kLoop, calls=%fused_computation.57 | loop fusion | flops 1944 | bytes 3888 | tf_op jit(solution)/shard_map/convert_element_type | solution.py:137
  1.6 0.1 convert_element_type.20
  1.7 7.2 %shard_map.113 = f32[96,256]{1,0:T(8,128)} custom-call(bf16[96,128,128]{2,1,0:T(8,128)(2,1)} %dens_ref.1, bf16[96,128,256]{2,1,0:T(8,128)(2,1)} %bra_ref.3, bf16[96,128,256]{2,1,0:T(8,128)(2,1)} %ket_ref.3), custom_call_target="tpu_custom_call" | custom-call | flops 805306368 | bytes 15826944 | tf_op jit(solution)/shard_map/pallas_call | solution.py:27
  8.9 1.2 %fusion.31 = f32[128,256]{1,0:T(8,128)S(1)} fusion(f32[96,256]{1,0:T(8,128)} %shard_map.113, s32[96]{0:T(128)S(1)} %copy-done.3), kind=kOutput, calls=%fused_computation.51 | convolution fusion | flops 18886656 | bytes 229760 | tf_op jit(solution)/shard_map/dot_general | solution.py:144
  10.2 1.2 %collective-permute-done = f32[66,256]{1,0:T(8,128)S(1)} collective-permute-done((f32[66,256]{1,0:T(8,128)S(1)}, f32[66,256]{1,0:T(8,128)S(1)}, u32[]{:S(2)}, u32[]{:S(2)}) %collective-permute-start) | collective-permute-done | bytes 67616 | tf_op jit(solution)/shard_map/ppermute | solution.py:84
  11.5 2.1 %collective-permute-start.1 = (f32[68,256]{1,0:T(8,128)S(1)}, f32[68,256]{1,0:T(8,128)S(1)}, u32[]{:S(2)}, u32[]{:S(2)}) collective-permute-start(f32[68,256]{1,0:T(8,128)S(1)} %pad_maximum_fusion.3), channel_id=1, source_target_pairs={{0,2},{1,3},{2,0},{3,1},{4,6},{5,7},{6,4},{7,5},{8,10},{9,11},{10,... | collective-permute-start | bytes 208904 | tf_op jit(solution)/shard_map/ppermute | solution.py:84
  13.7 2.5 %collective-permute-done.1 = f32[68,256]{1,0:T(8,128)S(1)} collective-permute-done((f32[68,256]{1,0:T(8,128)S(1)}, f32[68,256]{1,0:T(8,128)S(1)}, u32[]{:S(2)}, u32[]{:S(2)}) %collective-permute-start.1) | collective-permute-done | bytes 69664 | tf_op jit(solution)/shard_map/ppermute | solution.py:84
  16.2 1.7 %collective-permute-start.2 = (f32[72,256]{1,0:T(8,128)S(1)}, f32[72,256]{1,0:T(8,128)S(1)}, u32[]{:S(2)}, u32[]{:S(2)}) collective-permute-start(f32[72,256]{1,0:T(8,128)S(1)} %pad_maximum_fusion.4), channel_id=1, source_target_pairs={{0,4},{1,5},{2,6},{3,7},{4,0},{5,1},{6,2},{7,3},{8,12},{9,13},{10,... | collective-permute-start | bytes 221192 | tf_op jit(solution)/shard_map/ppermute | solution.py:84
  17.9 2.8 %collective-permute-done.2 = f32[72,256]{1,0:T(8,128)S(1)} collective-permute-done((f32[72,256]{1,0:T(8,128)S(1)}, f32[72,256]{1,0:T(8,128)S(1)}, u32[]{:S(2)}, u32[]{:S(2)}) %collective-permute-start.2) | collective-permute-done | bytes 73760 | tf_op jit(solution)/shard_map/ppermute | solution.py:84
  20.7 3.3 %collective-permute-start.3 = (f32[80,256]{1,0:T(8,128)S(1)}, f32[80,256]{1,0:T(8,128)S(1)}, u32[]{:S(2)}, u32[]{:S(2)}) collective-permute-start(f32[80,256]{1,0:T(8,128)S(1)} %concatenate.55), channel_id=1, source_target_pairs={{0,8},{1,9},{2,10},{3,11},{4,12},{5,13},{6,14},{7,15},{8,0},{9,1},... | collective-permute-start | bytes 245768 | tf_op jit(solution)/shard_map/ppermute | solution.py:84
  24.2 2.5 %collective-permute-done.3 = f32[80,256]{1,0:T(8,128)S(1)} collective-permute-done((f32[80,256]{1,0:T(8,128)S(1)}, f32[80,256]{1,0:T(8,128)S(1)}, u32[]{:S(2)}, u32[]{:S(2)}) %collective-permute-start.3) | collective-permute-done | bytes 81952 | tf_op jit(solution)/shard_map/ppermute | solution.py:84
  26.8 0.2 rev.3
  27.1 0.9 %convolution_bitcast_fusion = f32[8,256]{1,0:T(8,128)S(1)} fusion(f32[8,256,256]{2,1,0:T(8,128)S(1)} %copy-done, f32[8,8,256]{2,1,0:T(8,128)S(1)} %bitcast.27), kind=kOutput, calls=%fused_computation.11 | convolution fusion | flops 25165824 | bytes 2170880 | tf_op jit(solution)/shard_map/qce,cde->qd/dot_general | solution.py:164
  28.0 1.6 %collective-permute-start.4 = (f32[72,256]{1,0:T(8,128)S(1)}, f32[72,256]{1,0:T(8,128)S(1)}, u32[]{:S(2)}, u32[]{:S(2)}) collective-permute-start(f32[72,256]{1,0:T(8,128)S(1)} %pad_maximum_fusion.5), channel_id=1, source_target_pairs={{0,16},{16,0},{32,48},{48,32},{64,80},{80,64},{96,112},{112,96},{1... | collective-permute-start | bytes 221192 | tf_op jit(solution)/shard_map/ppermute | solution.py:84
  29.6 0.1 convert_element_type.22
  29.9 0.6 %copy.17 = pred[128,27,16]{1,2,0:T(8,128)(4,1)S(1)} copy(pred[128,27,16]{0,2,1:T(8,128)(4,1)S(1)} %iota_compare_fusion) | data formatting | bytes 110592 | tf_op jit(solution)/shard_map/eq | solution.py:203
  30.5 0.9 %fusion = f32[128,16,192]{2,1,0:T(8,128)S(1)} fusion(pred[128,27,16]{1,2,0:T(8,128)(4,1)S(1)} %copy.17, s32[192]{0:T(256)S(1)} %add.135, s32[128,27]{1,0:T(8,128)S(1)} %get-tuple-element.4), kind=kOutput, calls=%fused_computation | convolution fusion | flops 21897216 | bytes 1642752 | tf_op jit(solution)/shard_map/blt,blj->btj/dot_general | solution.py:204
  31.5 1.0 %collective-permute-done.4 = f32[72,256]{1,0:T(8,128)S(1)} collective-permute-done((f32[72,256]{1,0:T(8,128)S(1)}, f32[72,256]{1,0:T(8,128)S(1)}, u32[]{:S(2)}, u32[]{:S(2)}) %collective-permute-start.4) | collective-permute-done | bytes 73760 | tf_op jit(solution)/shard_map/ppermute | solution.py:84
  32.5 3.8 %collective-permute-start.5 = (f32[80,256]{1,0:T(8,128)S(1)}, f32[80,256]{1,0:T(8,128)S(1)}, u32[]{:S(2)}, u32[]{:S(2)}) collective-permute-start(f32[80,256]{1,0:T(8,128)S(1)} %pad_maximum_fusion.1), channel_id=1, source_target_pairs={{0,32},{16,48},{32,0},{48,16},{64,96},{80,112},{96,64},{112,80},{1... | collective-permute-start | bytes 245768 | tf_op jit(solution)/shard_map/ppermute | solution.py:84
  36.3 2.4 %collective-permute-done.5 = f32[80,256]{1,0:T(8,128)S(1)} collective-permute-done((f32[80,256]{1,0:T(8,128)S(1)}, f32[80,256]{1,0:T(8,128)S(1)}, u32[]{:S(2)}, u32[]{:S(2)}) %collective-permute-start.5) | collective-permute-done | bytes 81952 | tf_op jit(solution)/shard_map/ppermute | solution.py:84
  38.8 3.9 %collective-permute-start.6 = (f32[96,256]{1,0:T(8,128)S(1)}, f32[96,256]{1,0:T(8,128)S(1)}, u32[]{:S(2)}, u32[]{:S(2)}) collective-permute-start(f32[96,256]{1,0:T(8,128)S(1)} %pad_maximum_fusion), channel_id=1, source_target_pairs={{0,64},{16,80},{32,96},{48,112},{64,0},{80,16},{96,32},{112,48},{1... | collective-permute-start | bytes 294920 | tf_op jit(solution)/shard_map/ppermute | solution.py:84
  42.7 0.2 fusion.13
  42.9 2.3 %collective-permute-done.6 = f32[96,256]{1,0:T(8,128)S(1)} collective-permute-done((f32[96,256]{1,0:T(8,128)S(1)}, f32[96,256]{1,0:T(8,128)S(1)}, u32[]{:S(2)}, u32[]{:S(2)}) %collective-permute-start.6) | collective-permute-done | bytes 98336 | tf_op jit(solution)/shard_map/ppermute | solution.py:84
  45.3 0.2 fusion.19
  45.6 2.1 %fusion.6 = f32[128,16,256]{2,0,1:T(8,128)S(1)} fusion(f32[128,16,192]{2,1,0:T(8,128)S(1)} %fusion, f32[64,256]{1,0:T(8,128)S(1)} %get-tuple-element.3, f32[64,256]{1,0:T(8,128)S(1)} %slice_add_fusion.1, f32[64,256]{1,0:T(8,128)S(1)} %get-tuple-element.2), kind=kOutput, calls=%fused_computation.6 | convolution fusion | flops 604078080 | bytes 3866624 | tf_op jit(solution)/shard_map/btj,jk->btk/dot_general | solution.py:205
  47.7 2.3 %fusion.10 = f32[144,256]{1,0:T(8,128)S(1)} fusion(f32[16,256,256]{2,1,0:T(8,128)S(1)} %copy-done.1, f32[16,16,256]{2,0,1:T(8,128)S(1)} %fusion.19, f32[128,16,256]{2,0,1:T(8,128)S(1)} %fusion.6), kind=kOutput, calls=%fused_computation.10 | convolution fusion | flops 906559488 | bytes 6701056 | tf_op jit(solution)/shard_map/btk,tlk->bl/dot_general | solution.py:211
  50.1 0.6 fusion.42.ids_ref
  50.7 0.8 %collective-permute-done.7 = f32[144,256]{1,0:T(8,128)S(1)} collective-permute-done((f32[144,256]{1,0:T(8,128)S(1)}, f32[144,256]{1,0:T(8,128)S(1)}, u32[]{:S(2)}, u32[]{:S(2)}) %collective-permute-start.7) | collective-permute-done | bytes 147488 | tf_op jit(solution)/shard_map/ppermute | solution.py:84
  51.5 0.6 %fusion.34 = f32[16,8,256]{2,0,1:T(8,128)S(1)} fusion(f32[8,256,256]{2,1,0:T(8,128)S(1)} %copy-done, f32[144,256]{1,0:T(8,128)S(1)} %add.147), kind=kOutput, calls=%fused_computation.56 | convolution fusion | flops 50331648 | bytes 2244608 | tf_op jit(solution)/shard_map/qd,cds->qcs/dot_general | solution.py:215
  52.1 0.1 slice_add_fusion.local_ref
  52.2 0.6 %slice_select_fusion.2 = f32[8,256]{1,0:T(8,128)} fusion(f32[128,256]{1,0:T(8,128)S(1)} %slice_add_fusion.local_ref, pred[]{:T(512)S(6)} %eq.98), kind=kLoop, calls=%fused_computation.66 | loop fusion | flops 2048 | bytes 24577 | tf_op jit(solution)/shard_map/jit(_where)/select_n | solution.py:219
  52.9 7.5 %shard_map.114 = bf16[96,128,128]{2,1,0:T(8,128)(2,1)} custom-call(s32[96]{0:T(128)} %fusion.42.ids_ref, bf16[96,128,256]{2,1,0:T(8,128)(2,1)} %bra_ref.3, bf16[96,128,256]{2,1,0:T(8,128)(2,1)} %ket_ref.3, f32[128,256]{1,0:T(8,128)} %copy-done.2), custom_call_target="tpu_custom_call" | custom-call | flops 805306368 | bytes 15859712 | tf_op jit(solution)/shard_map/pallas_call | solution.py:61
  (51 shorter events, 1.1 us)
Async XLA Ops:
  0.6 26.5 %copy-start = (f32[8,256,256]{2,1,0:T(8,128)S(1)}, f32[8,256,256]{2,1,0:T(8,128)}, u32[]{:S(2)}) copy-start(f32[8,256,256]{2,1,0:T(8,128)} %param.19) | copy-start | bytes 6291460
  1.7 7.2 %copy-start.3 = (s32[96]{0:T(128)S(1)}, s32[96]{0:T(128)}, u32[]{:S(2)}) copy-start(s32[96]{0:T(128)} %param.13) | copy-start | bytes 1156
  10.1 1.3 %collective-permute-start = (f32[66,256]{1,0:T(8,128)S(1)}, f32[66,256]{1,0:T(8,128)S(1)}, u32[]{:S(2)}, u32[]{:S(2)}) collective-permute-start(f32[66,256]{1,0:T(8,128)S(1)} %pad_maximum_fusion.2), channel_id=1, source_target_pairs={{0,1},{1,0},{2,3},{3,2},{4,5},{5,4},{6,7},{7,6},{8,9},{9,8},{10,11... | collective-permute-start | bytes 202760 | tf_op jit(solution)/shard_map/ppermute | solution.py:84
  11.5 4.7 %collective-permute-start.1 = (f32[68,256]{1,0:T(8,128)S(1)}, f32[68,256]{1,0:T(8,128)S(1)}, u32[]{:S(2)}, u32[]{:S(2)}) collective-permute-start(f32[68,256]{1,0:T(8,128)S(1)} %pad_maximum_fusion.3), channel_id=1, source_target_pairs={{0,2},{1,3},{2,0},{3,1},{4,6},{5,7},{6,4},{7,5},{8,10},{9,11},{10,... | collective-permute-start | bytes 208904 | tf_op jit(solution)/shard_map/ppermute | solution.py:84
  16.2 4.4 %collective-permute-start.2 = (f32[72,256]{1,0:T(8,128)S(1)}, f32[72,256]{1,0:T(8,128)S(1)}, u32[]{:S(2)}, u32[]{:S(2)}) collective-permute-start(f32[72,256]{1,0:T(8,128)S(1)} %pad_maximum_fusion.4), channel_id=1, source_target_pairs={{0,4},{1,5},{2,6},{3,7},{4,0},{5,1},{6,2},{7,3},{8,12},{9,13},{10,... | collective-permute-start | bytes 221192 | tf_op jit(solution)/shard_map/ppermute | solution.py:84
  20.7 6.0 %collective-permute-start.3 = (f32[80,256]{1,0:T(8,128)S(1)}, f32[80,256]{1,0:T(8,128)S(1)}, u32[]{:S(2)}, u32[]{:S(2)}) collective-permute-start(f32[80,256]{1,0:T(8,128)S(1)} %concatenate.55), channel_id=1, source_target_pairs={{0,8},{1,9},{2,10},{3,11},{4,12},{5,13},{6,14},{7,15},{8,0},{9,1},... | collective-permute-start | bytes 245768 | tf_op jit(solution)/shard_map/ppermute | solution.py:84
  28.0 4.4 %collective-permute-start.4 = (f32[72,256]{1,0:T(8,128)S(1)}, f32[72,256]{1,0:T(8,128)S(1)}, u32[]{:S(2)}, u32[]{:S(2)}) collective-permute-start(f32[72,256]{1,0:T(8,128)S(1)} %pad_maximum_fusion.5), channel_id=1, source_target_pairs={{0,16},{16,0},{32,48},{48,32},{64,80},{80,64},{96,112},{112,96},{1... | collective-permute-start | bytes 221192 | tf_op jit(solution)/shard_map/ppermute | solution.py:84
  32.5 6.2 %collective-permute-start.5 = (f32[80,256]{1,0:T(8,128)S(1)}, f32[80,256]{1,0:T(8,128)S(1)}, u32[]{:S(2)}, u32[]{:S(2)}) collective-permute-start(f32[80,256]{1,0:T(8,128)S(1)} %pad_maximum_fusion.1), channel_id=1, source_target_pairs={{0,32},{16,48},{32,0},{48,16},{64,96},{80,112},{96,64},{112,80},{1... | collective-permute-start | bytes 245768 | tf_op jit(solution)/shard_map/ppermute | solution.py:84
  38.8 6.5 %collective-permute-start.6 = (f32[96,256]{1,0:T(8,128)S(1)}, f32[96,256]{1,0:T(8,128)S(1)}, u32[]{:S(2)}, u32[]{:S(2)}) collective-permute-start(f32[96,256]{1,0:T(8,128)S(1)} %pad_maximum_fusion), channel_id=1, source_target_pairs={{0,64},{16,80},{32,96},{48,112},{64,0},{80,16},{96,32},{112,48},{1... | collective-permute-start | bytes 294920 | tf_op jit(solution)/shard_map/ppermute | solution.py:84
  45.5 2.2 %copy-start.1 = (f32[16,256,256]{2,1,0:T(8,128)S(1)}, f32[16,256,256]{2,1,0:T(8,128)}, u32[]{:S(2)}) copy-start(f32[16,256,256]{2,1,0:T(8,128)} %param.18) | copy-start | bytes 12582916
  50.0 1.5 %collective-permute-start.7 = (f32[144,256]{1,0:T(8,128)S(1)}, f32[144,256]{1,0:T(8,128)S(1)}, u32[]{:S(2)}, u32[]{:S(2)}) collective-permute-start(f32[144,256]{1,0:T(8,128)S(1)} %fusion.10), channel_id=1, source_target_pairs={{0,1},{1,0},{2,3},{3,2},{4,5},{5,4},{6,7},{7,6},{8,9},{9,8},{10,11... | collective-permute-start | bytes 442376 | tf_op jit(solution)/shard_map/ppermute | solution.py:84
  52.2 0.7 %copy-start.2 = (f32[128,256]{1,0:T(8,128)}, f32[128,256]{1,0:T(8,128)S(1)}, u32[]{:S(2)}) copy-start(f32[128,256]{1,0:T(8,128)S(1)} %slice_add_fusion.local_ref) | copy-start | bytes 393220

commit v16 on v13

--- a/solution.py
+++ b/solution.py
@@ -13,11 +13,11 @@
 
 
 def moments_kernel(dens_ref, bra_ref, ket_ref, out_ref):
+    rows = []
     for j in range(out_ref.shape[0]):
         mixed = jnp.dot(dens_ref[j], ket_ref[j], preferred_element_type=jnp.float32)
-        out_ref[pl.ds(j, 1), :] = jnp.sum(
-            bra_ref[j].astype(jnp.float32) * mixed, axis=0, keepdims=True
-        )
+        rows.append(jnp.sum(bra_ref[j].astype(jnp.float32) * mixed, axis=0, keepdims=True))
+    out_ref[...] = jnp.concatenate(rows, axis=0)
 
 
 def block_moments(density, bra_table, ket_table):

time: 61.6 us -> 61.6 us (level)
  no operation moved by 1% of the time
where the time goes in v16:
time: 61.6 us; the launch traced here: 60.4 us
  starting transfers between devices  16.5 us (27%)
  waiting for transfers between devices  15.6 us (25%)
  Pallas kernels  14.7 us (24%)
  matrix products  8.54 us (14%)
  local copies, waits for them, and re-layouts  2.17 us (4%)
  other arithmetic  1.94 us (3%)
  between operations  0.95 us (2%)
    ppermute x8, starting transfers between devices, exchange(): return lax.ppermute(x, axis, [(i, i ^ mask) for i in range(count)])  16.5 us
    ppermute x8, waiting for transfers between devices, exchange(): return lax.ppermute(x, axis, [(i, i ^ mask) for i in range(count)])  15.6 us
    pallas_call x1, Pallas kernels, block_coulomb(): pl.pallas_call(coulomb_kernel, out_shape=jax.ShapeDtypeStruct((blocks, ro...  7.51 us
    pallas_call x1, Pallas kernels, block_moments(): pl.pallas_call(moments_kernel, out_shape=jax.ShapeDtypeStruct((blocks, co...  7.2 us
    dot_general x1, matrix products, shards(): far_part = jnp.einsum('btk,tlk->bl', rows, translation, precision=top)  2.29 us
    dot_general x1, matrix products, shards(): gathered = jnp.einsum('btj,jk->btk', counts, window, precision=top)  2.1 us
  transfers between devices with their start and end apart: 8, of which 8 were waited for; matrix products, arithmetic and copies ran while one was open for 5% of the time, Pallas kernels for 0%

profile of v16, /device:TPU:0, one launch (start us, length us, event | category | flops | bytes accessed | tf_op | source)
XLA Modules:
  0.0 60.4 jit_solution(16880298179706869586)
XLA Ops:
  0.7 0.9 %add_convert_fusion = f32[18,27]{1,0:T(8,128)S(1)} fusion(s32[1,27]{1,0:T(1,128)} %param.17, s32[1,27]{1,0:T(1,128)} %param.16, s32[8,27]{1,0:T(8,128)} %param.15, s32[8,27]{1,0:T(8,128)} %param.14), kind=kLoop, calls=%fused_computation.57 | loop fusion | flops 1944 | bytes 3888 | tf_op jit(solution)/shard_map/convert_element_type | solution.py:137
  1.6 0.1 convert_element_type.20
  1.7 7.2 %shard_map.113 = f32[96,256]{1,0:T(8,128)} custom-call(bf16[96,128,128]{2,1,0:T(8,128)(2,1)} %dens_ref.1, bf16[96,128,256]{2,1,0:T(8,128)(2,1)} %bra_ref.3, bf16[96,128,256]{2,1,0:T(8,128)(2,1)} %ket_ref.3), custom_call_target="tpu_custom_call" | custom-call | flops 805306368 | bytes 15826944 | tf_op jit(solution)/shard_map/pallas_call | solution.py:27
  8.9 1.2 %fusion.31 = f32[128,256]{1,0:T(8,128)S(1)} fusion(f32[96,256]{1,0:T(8,128)} %shard_map.113, s32[96]{0:T(128)S(1)} %copy-done.3), kind=kOutput, calls=%fused_computation.51 | convolution fusion | flops 18886656 | bytes 229760 | tf_op jit(solution)/shard_map/dot_general | solution.py:144
  10.2 1.2 %collective-permute-done = f32[66,256]{1,0:T(8,128)S(1)} collective-permute-done((f32[66,256]{1,0:T(8,128)S(1)}, f32[66,256]{1,0:T(8,128)S(1)}, u32[]{:S(2)}, u32[]{:S(2)}) %collective-permute-start) | collective-permute-done | bytes 67616 | tf_op jit(solution)/shard_map/ppermute | solution.py:84
  11.5 2.1 %collective-permute-start.1 = (f32[68,256]{1,0:T(8,128)S(1)}, f32[68,256]{1,0:T(8,128)S(1)}, u32[]{:S(2)}, u32[]{:S(2)}) collective-permute-start(f32[68,256]{1,0:T(8,128)S(1)} %pad_maximum_fusion.3), channel_id=1, source_target_pairs={{0,2},{1,3},{2,0},{3,1},{4,6},{5,7},{6,4},{7,5},{8,10},{9,11},{10,... | collective-permute-start | bytes 208904 | tf_op jit(solution)/shard_map/ppermute | solution.py:84
  13.7 2.5 %collective-permute-done.1 = f32[68,256]{1,0:T(8,128)S(1)} collective-permute-done((f32[68,256]{1,0:T(8,128)S(1)}, f32[68,256]{1,0:T(8,128)S(1)}, u32[]{:S(2)}, u32[]{:S(2)}) %collective-permute-start.1) | collective-permute-done | bytes 69664 | tf_op jit(solution)/shard_map/ppermute | solution.py:84
  16.2 1.7 %collective-permute-start.2 = (f32[72,256]{1,0:T(8,128)S(1)}, f32[72,256]{1,0:T(8,128)S(1)}, u32[]{:S(2)}, u32[]{:S(2)}) collective-permute-start(f32[72,256]{1,0:T(8,128)S(1)} %pad_maximum_fusion.4), channel_id=1, source_target_pairs={{0,4},{1,5},{2,6},{3,7},{4,0},{5,1},{6,2},{7,3},{8,12},{9,13},{10,... | collective-permute-start | bytes 221192 | tf_op jit(solution)/shard_map/ppermute | solution.py:84
  17.9 2.8 %collective-permute-done.2 = f32[72,256]{1,0:T(8,128)S(1)} collective-permute-done((f32[72,256]{1,0:T(8,128)S(1)}, f32[72,256]{1,0:T(8,128)S(1)}, u32[]{:S(2)}, u32[]{:S(2)}) %collective-permute-start.2) | collective-permute-done | bytes 73760 | tf_op jit(solution)/shard_map/ppermute | solution.py:84
  20.7 3.3 %collective-permute-start.3 = (f32[80,256]{1,0:T(8,128)S(1)}, f32[80,256]{1,0:T(8,128)S(1)}, u32[]{:S(2)}, u32[]{:S(2)}) collective-permute-start(f32[80,256]{1,0:T(8,128)S(1)} %concatenate.55), channel_id=1, source_target_pairs={{0,8},{1,9},{2,10},{3,11},{4,12},{5,13},{6,14},{7,15},{8,0},{9,1},... | collective-permute-start | bytes 245768 | tf_op jit(solution)/shard_map/ppermute | solution.py:84
  24.2 2.5 %collective-permute-done.3 = f32[80,256]{1,0:T(8,128)S(1)} collective-permute-done((f32[80,256]{1,0:T(8,128)S(1)}, f32[80,256]{1,0:T(8,128)S(1)}, u32[]{:S(2)}, u32[]{:S(2)}) %collective-permute-start.3) | collective-permute-done | bytes 81952 | tf_op jit(solution)/shard_map/ppermute | solution.py:84
  26.8 0.2 rev.3
  27.1 0.9 %convolution_bitcast_fusion = f32[8,256]{1,0:T(8,128)S(1)} fusion(f32[8,256,256]{2,1,0:T(8,128)S(1)} %copy-done, f32[8,8,256]{2,1,0:T(8,128)S(1)} %bitcast.27), kind=kOutput, calls=%fused_computation.11 | convolution fusion | flops 25165824 | bytes 2170880 | tf_op jit(solution)/shard_map/qce,cde->qd/dot_general | solution.py:164
  28.0 1.6 %collective-permute-start.4 = (f32[72,256]{1,0:T(8,128)S(1)}, f32[72,256]{1,0:T(8,128)S(1)}, u32[]{:S(2)}, u32[]{:S(2)}) collective-permute-start(f32[72,256]{1,0:T(8,128)S(1)} %pad_maximum_fusion.5), channel_id=1, source_target_pairs={{0,16},{16,0},{32,48},{48,32},{64,80},{80,64},{96,112},{112,96},{1... | collective-permute-start | bytes 221192 | tf_op jit(solution)/shard_map/ppermute | solution.py:84
  29.6 0.1 convert_element_type.22
  29.9 0.6 %copy.17 = pred[128,27,16]{1,2,0:T(8,128)(4,1)S(1)} copy(pred[128,27,16]{0,2,1:T(8,128)(4,1)S(1)} %iota_compare_fusion) | data formatting | bytes 110592 | tf_op jit(solution)/shard_map/eq | solution.py:203
  30.5 0.9 %fusion = f32[128,16,192]{2,1,0:T(8,128)S(1)} fusion(pred[128,27,16]{1,2,0:T(8,128)(4,1)S(1)} %copy.17, s32[192]{0:T(256)S(1)} %add.138, s32[128,27]{1,0:T(8,128)S(1)} %get-tuple-element.4), kind=kOutput, calls=%fused_computation | convolution fusion | flops 21897216 | bytes 1642752 | tf_op jit(solution)/shard_map/blt,blj->btj/dot_general | solution.py:204
  31.5 1.0 %collective-permute-done.4 = f32[72,256]{1,0:T(8,128)S(1)} collective-permute-done((f32[72,256]{1,0:T(8,128)S(1)}, f32[72,256]{1,0:T(8,128)S(1)}, u32[]{:S(2)}, u32[]{:S(2)}) %collective-permute-start.4) | collective-permute-done | bytes 73760 | tf_op jit(solution)/shard_map/ppermute | solution.py:84
  32.5 3.8 %collective-permute-start.5 = (f32[80,256]{1,0:T(8,128)S(1)}, f32[80,256]{1,0:T(8,128)S(1)}, u32[]{:S(2)}, u32[]{:S(2)}) collective-permute-start(f32[80,256]{1,0:T(8,128)S(1)} %pad_maximum_fusion.1), channel_id=1, source_target_pairs={{0,32},{16,48},{32,0},{48,16},{64,96},{80,112},{96,64},{112,80},{1... | collective-permute-start | bytes 245768 | tf_op jit(solution)/shard_map/ppermute | solution.py:84
  36.3 2.4 %collective-permute-done.5 = f32[80,256]{1,0:T(8,128)S(1)} collective-permute-done((f32[80,256]{1,0:T(8,128)S(1)}, f32[80,256]{1,0:T(8,128)S(1)}, u32[]{:S(2)}, u32[]{:S(2)}) %collective-permute-start.5) | collective-permute-done | bytes 81952 | tf_op jit(solution)/shard_map/ppermute | solution.py:84
  38.8 3.9 %collective-permute-start.6 = (f32[96,256]{1,0:T(8,128)S(1)}, f32[96,256]{1,0:T(8,128)S(1)}, u32[]{:S(2)}, u32[]{:S(2)}) collective-permute-start(f32[96,256]{1,0:T(8,128)S(1)} %pad_maximum_fusion), channel_id=1, source_target_pairs={{0,64},{16,80},{32,96},{48,112},{64,0},{80,16},{96,32},{112,48},{1... | collective-permute-start | bytes 294920 | tf_op jit(solution)/shard_map/ppermute | solution.py:84
  42.7 0.2 fusion.13
  42.9 2.3 %collective-permute-done.6 = f32[96,256]{1,0:T(8,128)S(1)} collective-permute-done((f32[96,256]{1,0:T(8,128)S(1)}, f32[96,256]{1,0:T(8,128)S(1)}, u32[]{:S(2)}, u32[]{:S(2)}) %collective-permute-start.6) | collective-permute-done | bytes 98336 | tf_op jit(solution)/shard_map/ppermute | solution.py:84
  45.3 0.2 fusion.19
  45.6 2.1 %fusion.6 = f32[128,16,256]{2,0,1:T(8,128)S(1)} fusion(f32[128,16,192]{2,1,0:T(8,128)S(1)} %fusion, f32[64,256]{1,0:T(8,128)S(1)} %get-tuple-element.3, f32[64,256]{1,0:T(8,128)S(1)} %slice_add_fusion.1, f32[64,256]{1,0:T(8,128)S(1)} %get-tuple-element.2), kind=kOutput, calls=%fused_computation.6 | convolution fusion | flops 604078080 | bytes 3866624 | tf_op jit(solution)/shard_map/btj,jk->btk/dot_general | solution.py:205
  47.7 2.3 %fusion.10 = f32[144,256]{1,0:T(8,128)S(1)} fusion(f32[16,256,256]{2,1,0:T(8,128)S(1)} %copy-done.1, f32[16,16,256]{2,0,1:T(8,128)S(1)} %fusion.19, f32[128,16,256]{2,0,1:T(8,128)S(1)} %fusion.6), kind=kOutput, calls=%fused_computation.10 | convolution fusion | flops 906559488 | bytes 6701056 | tf_op jit(solution)/shard_map/btk,tlk->bl/dot_general | solution.py:211
  50.1 0.6 fusion.42.ids_ref
  50.7 0.8 %collective-permute-done.7 = f32[144,256]{1,0:T(8,128)S(1)} collective-permute-done((f32[144,256]{1,0:T(8,128)S(1)}, f32[144,256]{1,0:T(8,128)S(1)}, u32[]{:S(2)}, u32[]{:S(2)}) %collective-permute-start.7) | collective-permute-done | bytes 147488 | tf_op jit(solution)/shard_map/ppermute | solution.py:84
  51.5 0.6 %fusion.34 = f32[16,8,256]{2,0,1:T(8,128)S(1)} fusion(f32[8,256,256]{2,1,0:T(8,128)S(1)} %copy-done, f32[144,256]{1,0:T(8,128)S(1)} %add.150), kind=kOutput, calls=%fused_computation.56 | convolution fusion | flops 50331648 | bytes 2244608 | tf_op jit(solution)/shard_map/qd,cds->qcs/dot_general | solution.py:215
  52.1 0.1 slice_add_fusion.local_ref
  52.2 0.6 %constant_dynamic-slice_fusion = f32[8,256]{1,0:T(8,128)} fusion(f32[128,256]{1,0:T(8,128)S(1)} %slice_add_fusion.local_ref, s32[]{:T(128)S(6)} %select_n.136), kind=kLoop, calls=%fused_computation.81 | loop fusion | bytes 16388 | tf_op jit(solution)/shard_map/dynamic_slice | solution.py:219
  52.9 7.5 %shard_map.114 = bf16[96,128,128]{2,1,0:T(8,128)(2,1)} custom-call(s32[96]{0:T(128)} %fusion.42.ids_ref, bf16[96,128,256]{2,1,0:T(8,128)(2,1)} %bra_ref.3, bf16[96,128,256]{2,1,0:T(8,128)(2,1)} %ket_ref.3, f32[128,256]{1,0:T(8,128)} %copy-done.2), custom_call_target="tpu_custom_call" | custom-call | flops 805306368 | bytes 15859712 | tf_op jit(solution)/shard_map/pallas_call | solution.py:61
  (51 shorter events, 1.1 us)
Async XLA Ops:
  0.6 26.5 %copy-start = (f32[8,256,256]{2,1,0:T(8,128)S(1)}, f32[8,256,256]{2,1,0:T(8,128)}, u32[]{:S(2)}) copy-start(f32[8,256,256]{2,1,0:T(8,128)} %param.19) | copy-start | bytes 6291460
  1.7 7.2 %copy-start.3 = (s32[96]{0:T(128)S(1)}, s32[96]{0:T(128)}, u32[]{:S(2)}) copy-start(s32[96]{0:T(128)} %param.13) | copy-start | bytes 1156
  10.1 1.3 %collective-permute-start = (f32[66,256]{1,0:T(8,128)S(1)}, f32[66,256]{1,0:T(8,128)S(1)}, u32[]{:S(2)}, u32[]{:S(2)}) collective-permute-start(f32[66,256]{1,0:T(8,128)S(1)} %pad_maximum_fusion.2), channel_id=1, source_target_pairs={{0,1},{1,0},{2,3},{3,2},{4,5},{5,4},{6,7},{7,6},{8,9},{9,8},{10,11... | collective-permute-start | bytes 202760 | tf_op jit(solution)/shard_map/ppermute | solution.py:84
  11.5 4.7 %collective-permute-start.1 = (f32[68,256]{1,0:T(8,128)S(1)}, f32[68,256]{1,0:T(8,128)S(1)}, u32[]{:S(2)}, u32[]{:S(2)}) collective-permute-start(f32[68,256]{1,0:T(8,128)S(1)} %pad_maximum_fusion.3), channel_id=1, source_target_pairs={{0,2},{1,3},{2,0},{3,1},{4,6},{5,7},{6,4},{7,5},{8,10},{9,11},{10,... | collective-permute-start | bytes 208904 | tf_op jit(solution)/shard_map/ppermute | solution.py:84
  16.2 4.4 %collective-permute-start.2 = (f32[72,256]{1,0:T(8,128)S(1)}, f32[72,256]{1,0:T(8,128)S(1)}, u32[]{:S(2)}, u32[]{:S(2)}) collective-permute-start(f32[72,256]{1,0:T(8,128)S(1)} %pad_maximum_fusion.4), channel_id=1, source_target_pairs={{0,4},{1,5},{2,6},{3,7},{4,0},{5,1},{6,2},{7,3},{8,12},{9,13},{10,... | collective-permute-start | bytes 221192 | tf_op jit(solution)/shard_map/ppermute | solution.py:84
  20.7 6.0 %collective-permute-start.3 = (f32[80,256]{1,0:T(8,128)S(1)}, f32[80,256]{1,0:T(8,128)S(1)}, u32[]{:S(2)}, u32[]{:S(2)}) collective-permute-start(f32[80,256]{1,0:T(8,128)S(1)} %concatenate.55), channel_id=1, source_target_pairs={{0,8},{1,9},{2,10},{3,11},{4,12},{5,13},{6,14},{7,15},{8,0},{9,1},... | collective-permute-start | bytes 245768 | tf_op jit(solution)/shard_map/ppermute | solution.py:84
  28.0 4.4 %collective-permute-start.4 = (f32[72,256]{1,0:T(8,128)S(1)}, f32[72,256]{1,0:T(8,128)S(1)}, u32[]{:S(2)}, u32[]{:S(2)}) collective-permute-start(f32[72,256]{1,0:T(8,128)S(1)} %pad_maximum_fusion.5), channel_id=1, source_target_pairs={{0,16},{16,0},{32,48},{48,32},{64,80},{80,64},{96,112},{112,96},{1... | collective-permute-start | bytes 221192 | tf_op jit(solution)/shard_map/ppermute | solution.py:84
  32.5 6.2 %collective-permute-start.5 = (f32[80,256]{1,0:T(8,128)S(1)}, f32[80,256]{1,0:T(8,128)S(1)}, u32[]{:S(2)}, u32[]{:S(2)}) collective-permute-start(f32[80,256]{1,0:T(8,128)S(1)} %pad_maximum_fusion.1), channel_id=1, source_target_pairs={{0,32},{16,48},{32,0},{48,16},{64,96},{80,112},{96,64},{112,80},{1... | collective-permute-start | bytes 245768 | tf_op jit(solution)/shard_map/ppermute | solution.py:84
  38.8 6.5 %collective-permute-start.6 = (f32[96,256]{1,0:T(8,128)S(1)}, f32[96,256]{1,0:T(8,128)S(1)}, u32[]{:S(2)}, u32[]{:S(2)}) collective-permute-start(f32[96,256]{1,0:T(8,128)S(1)} %pad_maximum_fusion), channel_id=1, source_target_pairs={{0,64},{16,80},{32,96},{48,112},{64,0},{80,16},{96,32},{112,48},{1... | collective-permute-start | bytes 294920 | tf_op jit(solution)/shard_map/ppermute | solution.py:84
  45.5 2.2 %copy-start.1 = (f32[16,256,256]{2,1,0:T(8,128)S(1)}, f32[16,256,256]{2,1,0:T(8,128)}, u32[]{:S(2)}) copy-start(f32[16,256,256]{2,1,0:T(8,128)} %param.18) | copy-start | bytes 12582916
  50.0 1.5 %collective-permute-start.7 = (f32[144,256]{1,0:T(8,128)S(1)}, f32[144,256]{1,0:T(8,128)S(1)}, u32[]{:S(2)}, u32[]{:S(2)}) collective-permute-start(f32[144,256]{1,0:T(8,128)S(1)} %fusion.10), channel_id=1, source_target_pairs={{0,1},{1,0},{2,3},{3,2},{4,5},{5,4},{6,7},{7,6},{8,9},{9,8},{10,11... | collective-permute-start | bytes 442376 | tf_op jit(solution)/shard_map/ppermute | solution.py:84
  52.2 0.7 %copy-start.2 = (f32[128,256]{1,0:T(8,128)}, f32[128,256]{1,0:T(8,128)S(1)}, u32[]{:S(2)}) copy-start(f32[128,256]{1,0:T(8,128)S(1)} %slice_add_fusion.local_ref) | copy-start | bytes 393220

commit v17 on v13

--- a/solution.py
+++ b/solution.py
@@ -57,7 +57,7 @@
     blocks, rows, coeffs = bra_table.shape
     cols = ket_table.shape[1]
     boxes = domain_local.shape[0]
-    tile = tile_of(blocks)
+    tile = tile_of(blocks, most=96)
     return pl.pallas_call(
         coulomb_kernel,
         out_shape=jax.ShapeDtypeStruct((blocks, rows, cols), jnp.bfloat16),

time: 61.6 us -> 63 us (1.023)
  Pallas kernels: 14.7 us -> 16 us
    pallas_call x1, Pallas kernels: 7.51 us -> 8.75 us  [block_coulomb(): pl.pallas_call(coulomb_kernel, out_shape=jax.ShapeDtypeStruct((blocks, ro...]
where the time goes in v17:
time: 63 us; the launch traced here: 61.8 us
  starting transfers between devices  16.7 us (27%)
  Pallas kernels  16 us (25%)
  waiting for transfers between devices  15.6 us (25%)
  matrix products  8.54 us (14%)
  local copies, waits for them, and re-layouts  2.17 us (3%)
  other arithmetic  1.94 us (3%)
  between operations  0.96 us (2%)
    ppermute x8, starting transfers between devices, exchange(): return lax.ppermute(x, axis, [(i, i ^ mask) for i in range(count)])  16.7 us
    ppermute x8, waiting for transfers between devices, exchange(): return lax.ppermute(x, axis, [(i, i ^ mask) for i in range(count)])  15.6 us
    pallas_call x1, Pallas kernels, block_coulomb(): pl.pallas_call(coulomb_kernel, out_shape=jax.ShapeDtypeStruct((blocks, ro...  8.75 us
    pallas_call x1, Pallas kernels, block_moments(): pl.pallas_call(moments_kernel, out_shape=jax.ShapeDtypeStruct((blocks, co...  7.2 us
    dot_general x1, matrix products, shards(): far_part = jnp.einsum('btk,tlk->bl', rows, translation, precision=top)  2.28 us
    dot_general x1, matrix products, shards(): gathered = jnp.einsum('btj,jk->btk', counts, window, precision=top)  2.1 us
  transfers between devices with their start and end apart: 8, of which 8 were waited for; matrix products, arithmetic and copies ran while one was open for 5% of the time, Pallas kernels for 0%

profile of v17, /device:TPU:0, one launch (start us, length us, event | category | flops | bytes accessed | tf_op | source)
XLA Modules:
  0.0 61.8 jit_solution(17772204081109547811)
XLA Ops:
  0.7 0.9 %add_convert_fusion = f32[18,27]{1,0:T(8,128)S(1)} fusion(s32[1,27]{1,0:T(1,128)} %param.17, s32[1,27]{1,0:T(1,128)} %param.16, s32[8,27]{1,0:T(8,128)} %param.15, s32[8,27]{1,0:T(8,128)} %param.14), kind=kLoop, calls=%fused_computation.57 | loop fusion | flops 1944 | bytes 3888 | tf_op jit(solution)/shard_map/convert_element_type | solution.py:137
  1.7 7.2 %shard_map.113 = f32[96,256]{1,0:T(8,128)} custom-call(bf16[96,128,128]{2,1,0:T(8,128)(2,1)} %dens_ref.1, bf16[96,128,256]{2,1,0:T(8,128)(2,1)} %bra_ref.3, bf16[96,128,256]{2,1,0:T(8,128)(2,1)} %ket_ref.3), custom_call_target="tpu_custom_call" | custom-call | flops 805306368 | bytes 15826944 | tf_op jit(solution)/shard_map/pallas_call | solution.py:27
  8.9 1.2 %fusion.31 = f32[128,256]{1,0:T(8,128)S(1)} fusion(f32[96,256]{1,0:T(8,128)} %shard_map.113, s32[96]{0:T(128)S(1)} %copy-done.3), kind=kOutput, calls=%fused_computation.51 | convolution fusion | flops 18886656 | bytes 229760 | tf_op jit(solution)/shard_map/dot_general | solution.py:144
  10.2 1.2 %collective-permute-done = f32[66,256]{1,0:T(8,128)S(1)} collective-permute-done((f32[66,256]{1,0:T(8,128)S(1)}, f32[66,256]{1,0:T(8,128)S(1)}, u32[]{:S(2)}, u32[]{:S(2)}) %collective-permute-start) | collective-permute-done | bytes 67616 | tf_op jit(solution)/shard_map/ppermute | solution.py:84
  11.5 2.1 %collective-permute-start.1 = (f32[68,256]{1,0:T(8,128)S(1)}, f32[68,256]{1,0:T(8,128)S(1)}, u32[]{:S(2)}, u32[]{:S(2)}) collective-permute-start(f32[68,256]{1,0:T(8,128)S(1)} %pad_maximum_fusion.3), channel_id=1, source_target_pairs={{0,2},{1,3},{2,0},{3,1},{4,6},{5,7},{6,4},{7,5},{8,10},{9,11},{10,... | collective-permute-start | bytes 208904 | tf_op jit(solution)/shard_map/ppermute | solution.py:84
  13.7 2.5 %collective-permute-done.1 = f32[68,256]{1,0:T(8,128)S(1)} collective-permute-done((f32[68,256]{1,0:T(8,128)S(1)}, f32[68,256]{1,0:T(8,128)S(1)}, u32[]{:S(2)}, u32[]{:S(2)}) %collective-permute-start.1) | collective-permute-done | bytes 69664 | tf_op jit(solution)/shard_map/ppermute | solution.py:84
  16.2 1.7 %collective-permute-start.2 = (f32[72,256]{1,0:T(8,128)S(1)}, f32[72,256]{1,0:T(8,128)S(1)}, u32[]{:S(2)}, u32[]{:S(2)}) collective-permute-start(f32[72,256]{1,0:T(8,128)S(1)} %pad_maximum_fusion.4), channel_id=1, source_target_pairs={{0,4},{1,5},{2,6},{3,7},{4,0},{5,1},{6,2},{7,3},{8,12},{9,13},{10,... | collective-permute-start | bytes 221192 | tf_op jit(solution)/shard_map/ppermute | solution.py:84
  17.9 2.8 %collective-permute-done.2 = f32[72,256]{1,0:T(8,128)S(1)} collective-permute-done((f32[72,256]{1,0:T(8,128)S(1)}, f32[72,256]{1,0:T(8,128)S(1)}, u32[]{:S(2)}, u32[]{:S(2)}) %collective-permute-start.2) | collective-permute-done | bytes 73760 | tf_op jit(solution)/shard_map/ppermute | solution.py:84
  20.7 3.3 %collective-permute-start.3 = (f32[80,256]{1,0:T(8,128)S(1)}, f32[80,256]{1,0:T(8,128)S(1)}, u32[]{:S(2)}, u32[]{:S(2)}) collective-permute-start(f32[80,256]{1,0:T(8,128)S(1)} %concatenate.55), channel_id=1, source_target_pairs={{0,8},{1,9},{2,10},{3,11},{4,12},{5,13},{6,14},{7,15},{8,0},{9,1},... | collective-permute-start | bytes 245768 | tf_op jit(solution)/shard_map/ppermute | solution.py:84
  24.2 2.5 %collective-permute-done.3 = f32[80,256]{1,0:T(8,128)S(1)} collective-permute-done((f32[80,256]{1,0:T(8,128)S(1)}, f32[80,256]{1,0:T(8,128)S(1)}, u32[]{:S(2)}, u32[]{:S(2)}) %collective-permute-start.3) | collective-permute-done | bytes 81952 | tf_op jit(solution)/shard_map/ppermute | solution.py:84
  26.8 0.2 rev.3
  27.1 0.9 %convolution_bitcast_fusion = f32[8,256]{1,0:T(8,128)S(1)} fusion(f32[8,256,256]{2,1,0:T(8,128)S(1)} %copy-done, f32[8,8,256]{2,1,0:T(8,128)S(1)} %bitcast.27), kind=kOutput, calls=%fused_computation.11 | convolution fusion | flops 25165824 | bytes 2170880 | tf_op jit(solution)/shard_map/qce,cde->qd/dot_general | solution.py:164
  28.0 1.6 %collective-permute-start.4 = (f32[72,256]{1,0:T(8,128)S(1)}, f32[72,256]{1,0:T(8,128)S(1)}, u32[]{:S(2)}, u32[]{:S(2)}) collective-permute-start(f32[72,256]{1,0:T(8,128)S(1)} %pad_maximum_fusion.5), channel_id=1, source_target_pairs={{0,16},{16,0},{32,48},{48,32},{64,80},{80,64},{96,112},{112,96},{1... | collective-permute-start | bytes 221192 | tf_op jit(solution)/shard_map/ppermute | solution.py:84
  29.6 0.1 convert_element_type.22
  29.9 0.6 %copy.17 = pred[128,27,16]{1,2,0:T(8,128)(4,1)S(1)} copy(pred[128,27,16]{0,2,1:T(8,128)(4,1)S(1)} %iota_compare_fusion) | data formatting | bytes 110592 | tf_op jit(solution)/shard_map/eq | solution.py:203
  30.5 0.9 %fusion = f32[128,16,192]{2,1,0:T(8,128)S(1)} fusion(pred[128,27,16]{1,2,0:T(8,128)(4,1)S(1)} %copy.17, s32[192]{0:T(256)S(1)} %add.138, s32[128,27]{1,0:T(8,128)S(1)} %get-tuple-element.4), kind=kOutput, calls=%fused_computation | convolution fusion | flops 21897216 | bytes 1642752 | tf_op jit(solution)/shard_map/blt,blj->btj/dot_general | solution.py:204
  31.5 1.0 %collective-permute-done.4 = f32[72,256]{1,0:T(8,128)S(1)} collective-permute-done((f32[72,256]{1,0:T(8,128)S(1)}, f32[72,256]{1,0:T(8,128)S(1)}, u32[]{:S(2)}, u32[]{:S(2)}) %collective-permute-start.4) | collective-permute-done | bytes 73760 | tf_op jit(solution)/shard_map/ppermute | solution.py:84
  32.5 3.8 %collective-permute-start.5 = (f32[80,256]{1,0:T(8,128)S(1)}, f32[80,256]{1,0:T(8,128)S(1)}, u32[]{:S(2)}, u32[]{:S(2)}) collective-permute-start(f32[80,256]{1,0:T(8,128)S(1)} %pad_maximum_fusion.1), channel_id=1, source_target_pairs={{0,32},{16,48},{32,0},{48,16},{64,96},{80,112},{96,64},{112,80},{1... | collective-permute-start | bytes 245768 | tf_op jit(solution)/shard_map/ppermute | solution.py:84
  36.3 2.4 %collective-permute-done.5 = f32[80,256]{1,0:T(8,128)S(1)} collective-permute-done((f32[80,256]{1,0:T(8,128)S(1)}, f32[80,256]{1,0:T(8,128)S(1)}, u32[]{:S(2)}, u32[]{:S(2)}) %collective-permute-start.5) | collective-permute-done | bytes 81952 | tf_op jit(solution)/shard_map/ppermute | solution.py:84
  38.8 3.9 %collective-permute-start.6 = (f32[96,256]{1,0:T(8,128)S(1)}, f32[96,256]{1,0:T(8,128)S(1)}, u32[]{:S(2)}, u32[]{:S(2)}) collective-permute-start(f32[96,256]{1,0:T(8,128)S(1)} %pad_maximum_fusion), channel_id=1, source_target_pairs={{0,64},{16,80},{32,96},{48,112},{64,0},{80,16},{96,32},{112,48},{1... | collective-permute-start | bytes 294920 | tf_op jit(solution)/shard_map/ppermute | solution.py:84
  42.7 0.2 fusion.13
  42.9 2.3 %collective-permute-done.6 = f32[96,256]{1,0:T(8,128)S(1)} collective-permute-done((f32[96,256]{1,0:T(8,128)S(1)}, f32[96,256]{1,0:T(8,128)S(1)}, u32[]{:S(2)}, u32[]{:S(2)}) %collective-permute-start.6) | collective-permute-done | bytes 98336 | tf_op jit(solution)/shard_map/ppermute | solution.py:84
  45.3 0.2 fusion.19
  45.6 2.1 %fusion.6 = f32[128,16,256]{2,0,1:T(8,128)S(1)} fusion(f32[128,16,192]{2,1,0:T(8,128)S(1)} %fusion, f32[64,256]{1,0:T(8,128)S(1)} %get-tuple-element.3, f32[64,256]{1,0:T(8,128)S(1)} %slice_add_fusion.1, f32[64,256]{1,0:T(8,128)S(1)} %get-tuple-element.2), kind=kOutput, calls=%fused_computation.6 | convolution fusion | flops 604078080 | bytes 3866624 | tf_op jit(solution)/shard_map/btj,jk->btk/dot_general | solution.py:205
  47.7 2.3 %fusion.10 = f32[144,256]{1,0:T(8,128)S(1)} fusion(f32[16,256,256]{2,1,0:T(8,128)S(1)} %copy-done.1, f32[16,16,256]{2,0,1:T(8,128)S(1)} %fusion.19, f32[128,16,256]{2,0,1:T(8,128)S(1)} %fusion.6), kind=kOutput, calls=%fused_computation.10 | convolution fusion | flops 906559488 | bytes 6701056 | tf_op jit(solution)/shard_map/btk,tlk->bl/dot_general | solution.py:211
  50.0 0.3 collective-permute-start.7
  50.3 0.6 fusion.42.ids_ref
  50.9 0.8 %collective-permute-done.7 = f32[144,256]{1,0:T(8,128)S(1)} collective-permute-done((f32[144,256]{1,0:T(8,128)S(1)}, f32[144,256]{1,0:T(8,128)S(1)}, u32[]{:S(2)}, u32[]{:S(2)}) %collective-permute-start.7) | collective-permute-done | bytes 147488 | tf_op jit(solution)/shard_map/ppermute | solution.py:84
  51.7 0.6 fusion.34
  52.3 0.1 slice_add_fusion.local_ref
  52.4 0.6 %constant_dynamic-slice_fusion = f32[8,256]{1,0:T(8,128)} fusion(f32[128,256]{1,0:T(8,128)S(1)} %slice_add_fusion.local_ref, s32[]{:T(128)S(6)} %select_n.136), kind=kLoop, calls=%fused_computation.81 | loop fusion | bytes 16388 | tf_op jit(solution)/shard_map/dynamic_slice | solution.py:219
  53.0 8.7 %shard_map.114 = bf16[96,128,128]{2,1,0:T(8,128)(2,1)} custom-call(s32[96]{0:T(128)} %fusion.42.ids_ref, bf16[96,128,256]{2,1,0:T(8,128)(2,1)} %bra_ref.3, bf16[96,128,256]{2,1,0:T(8,128)(2,1)} %ket_ref.3, f32[128,256]{1,0:T(8,128)} %copy-done.2), custom_call_target="tpu_custom_call" | custom-call | flops 805306368 | bytes 15859712 | tf_op jit(solution)/shard_map/pallas_call | solution.py:61
  (51 shorter events, 1.1 us)
Async XLA Ops:
  0.6 26.5 %copy-start = (f32[8,256,256]{2,1,0:T(8,128)S(1)}, f32[8,256,256]{2,1,0:T(8,128)}, u32[]{:S(2)}) copy-start(f32[8,256,256]{2,1,0:T(8,128)} %param.19) | copy-start | bytes 6291460
  1.7 7.2 %copy-start.3 = (s32[96]{0:T(128)S(1)}, s32[96]{0:T(128)}, u32[]{:S(2)}) copy-start(s32[96]{0:T(128)} %param.13) | copy-start | bytes 1156
  10.1 1.3 %collective-permute-start = (f32[66,256]{1,0:T(8,128)S(1)}, f32[66,256]{1,0:T(8,128)S(1)}, u32[]{:S(2)}, u32[]{:S(2)}) collective-permute-start(f32[66,256]{1,0:T(8,128)S(1)} %pad_maximum_fusion.2), channel_id=1, source_target_pairs={{0,1},{1,0},{2,3},{3,2},{4,5},{5,4},{6,7},{7,6},{8,9},{9,8},{10,11... | collective-permute-start | bytes 202760 | tf_op jit(solution)/shard_map/ppermute | solution.py:84
  11.5 4.7 %collective-permute-start.1 = (f32[68,256]{1,0:T(8,128)S(1)}, f32[68,256]{1,0:T(8,128)S(1)}, u32[]{:S(2)}, u32[]{:S(2)}) collective-permute-start(f32[68,256]{1,0:T(8,128)S(1)} %pad_maximum_fusion.3), channel_id=1, source_target_pairs={{0,2},{1,3},{2,0},{3,1},{4,6},{5,7},{6,4},{7,5},{8,10},{9,11},{10,... | collective-permute-start | bytes 208904 | tf_op jit(solution)/shard_map/ppermute | solution.py:84
  16.2 4.4 %collective-permute-start.2 = (f32[72,256]{1,0:T(8,128)S(1)}, f32[72,256]{1,0:T(8,128)S(1)}, u32[]{:S(2)}, u32[]{:S(2)}) collective-permute-start(f32[72,256]{1,0:T(8,128)S(1)} %pad_maximum_fusion.4), channel_id=1, source_target_pairs={{0,4},{1,5},{2,6},{3,7},{4,0},{5,1},{6,2},{7,3},{8,12},{9,13},{10,... | collective-permute-start | bytes 221192 | tf_op jit(solution)/shard_map/ppermute | solution.py:84
  20.7 6.0 %collective-permute-start.3 = (f32[80,256]{1,0:T(8,128)S(1)}, f32[80,256]{1,0:T(8,128)S(1)}, u32[]{:S(2)}, u32[]{:S(2)}) collective-permute-start(f32[80,256]{1,0:T(8,128)S(1)} %concatenate.55), channel_id=1, source_target_pairs={{0,8},{1,9},{2,10},{3,11},{4,12},{5,13},{6,14},{7,15},{8,0},{9,1},... | collective-permute-start | bytes 245768 | tf_op jit(solution)/shard_map/ppermute | solution.py:84
  28.0 4.4 %collective-permute-start.4 = (f32[72,256]{1,0:T(8,128)S(1)}, f32[72,256]{1,0:T(8,128)S(1)}, u32[]{:S(2)}, u32[]{:S(2)}) collective-permute-start(f32[72,256]{1,0:T(8,128)S(1)} %pad_maximum_fusion.5), channel_id=1, source_target_pairs={{0,16},{16,0},{32,48},{48,32},{64,80},{80,64},{96,112},{112,96},{1... | collective-permute-start | bytes 221192 | tf_op jit(solution)/shard_map/ppermute | solution.py:84
  32.5 6.2 %collective-permute-start.5 = (f32[80,256]{1,0:T(8,128)S(1)}, f32[80,256]{1,0:T(8,128)S(1)}, u32[]{:S(2)}, u32[]{:S(2)}) collective-permute-start(f32[80,256]{1,0:T(8,128)S(1)} %pad_maximum_fusion.1), channel_id=1, source_target_pairs={{0,32},{16,48},{32,0},{48,16},{64,96},{80,112},{96,64},{112,80},{1... | collective-permute-start | bytes 245768 | tf_op jit(solution)/shard_map/ppermute | solution.py:84
  38.8 6.5 %collective-permute-start.6 = (f32[96,256]{1,0:T(8,128)S(1)}, f32[96,256]{1,0:T(8,128)S(1)}, u32[]{:S(2)}, u32[]{:S(2)}) collective-permute-start(f32[96,256]{1,0:T(8,128)S(1)} %pad_maximum_fusion), channel_id=1, source_target_pairs={{0,64},{16,80},{32,96},{48,112},{64,0},{80,16},{96,32},{112,48},{1... | collective-permute-start | bytes 294920 | tf_op jit(solution)/shard_map/ppermute | solution.py:84
  45.5 2.2 %copy-start.1 = (f32[16,256,256]{2,1,0:T(8,128)S(1)}, f32[16,256,256]{2,1,0:T(8,128)}, u32[]{:S(2)}) copy-start(f32[16,256,256]{2,1,0:T(8,128)} %param.18) | copy-start | bytes 12582916
  50.0 1.6 %collective-permute-start.7 = (f32[144,256]{1,0:T(8,128)S(1)}, f32[144,256]{1,0:T(8,128)S(1)}, u32[]{:S(2)}, u32[]{:S(2)}) collective-permute-start(f32[144,256]{1,0:T(8,128)S(1)} %fusion.10), channel_id=1, source_target_pairs={{0,1},{1,0},{2,3},{3,2},{4,5},{5,4},{6,7},{7,6},{8,9},{9,8},{10,11... | collective-permute-start | bytes 442376 | tf_op jit(solution)/shard_map/ppermute | solution.py:84
  52.4 0.7 %copy-start.2 = (f32[128,256]{1,0:T(8,128)}, f32[128,256]{1,0:T(8,128)S(1)}, u32[]{:S(2)}) copy-start(f32[128,256]{1,0:T(8,128)S(1)} %slice_add_fusion.local_ref) | copy-start | bytes 393220
